TPU v7x, 256 devices: a whole 4x4x8 slice. The times are simulated.
256 devices in a mesh: head: 8 (over y, z_lo), blk: 32 (over z_hi, x, core).
Axes of the slice: x: 4, y: 4, z: 8 (z_hi: 4, z_lo: 2; z = z_hi * 2 + z_lo), core: 2. Of those that a mesh axis runs over, the one named last changes fastest.
Arguments:
- queries: bfloat16 [32768, 6144], P(('blk', 'head')), may hold values from -4.5 to 4.5
- key_states: bfloat16 [32768, 6144], P(('blk', 'head')), may hold values from -4.5 to 4.5
- value_states: bfloat16 [32768, 6144], P(('blk', 'head')), may hold values from -6 to 6
- block_lists: int32 [256, 8], P('blk'), may hold values from 0 to 255, as said below
- block_counts: int32 [256], P('blk'), may hold values from 1 to 8
- tile_order: int32 [256], replicated, may hold values from 0 to 255, each once
Outputs:
- attended: bfloat16 [32768, 6144], P(('blk', 'head'))
Inputs may be any that keep to these rules, and one draw needn't show every extreme that they name: `block_lists`: entry 0 of row t is t itself; the entries of a row are distinct, and each names a tile whose shard of 8 tiles lies at most 3 shards from the shard of t, counted cyclically over the clip.
All inputs are finite; a program needn't handle non-finite values.
Results may differ from a plain program's by a relative error of at most 0.0095.
Values may be sent and summed in bfloat16 or wider, within the bound.
No kernel may reach another device: no remote copies, remote signals or barrier semaphores. Data moves between devices by JAX's collectives and lax.ppermute only.
A program may use at most 128 MiB of HBM per device.

v0:
```python
import jax
import jax.numpy as jnp
from jax import lax
from jax.sharding import PartitionSpec as P

H = 48
DH = 128
TILE = 128
REACH = 3
SLOTS = 8


def shifted(block, axis, distance):
    devices = range(lax.axis_size(axis))
    route = [((i - distance) % len(devices), i) for i in devices]
    return lax.ppermute(block, axis, route)


def body(queries, key_states, value_states, block_lists, block_counts, tile_order):
    cycle_size = lax.axis_size("blk")
    group_size = lax.axis_size("head")
    heads_local = H // group_size
    q_heads, k_heads, v_heads = (
        lax.all_to_all(queries, "head", split_axis=1, concat_axis=0, tiled=True),
        lax.all_to_all(key_states, "head", split_axis=1, concat_axis=0, tiled=True),
        lax.all_to_all(value_states, "head", split_axis=1, concat_axis=0, tiled=True),
    )
    shard_tok = q_heads.shape[0]
    tile_count = shard_tok // TILE
    tile_shape = (tile_count, TILE, heads_local, DH)
    q_tiles = q_heads.reshape(tile_shape)
    local_pair = jnp.stack((k_heads.reshape(tile_shape), v_heads.reshape(tile_shape)))
    pieces = {0: local_pair}
    current = shifted(local_pair, "blk", -REACH)
    pieces[REACH] = current
    for hop_index in range(2 * REACH):
        current = shifted(current, "blk", 1)
        offset = REACH - 1 - hop_index
        if offset != 0:
            pieces[offset] = current
    window = jnp.concatenate([pieces[offset] for offset in range(-REACH, REACH + 1)], axis=1)
    blk_index = lax.axis_index("blk")
    shard_of = block_lists // tile_count
    slot_window = (
        shard_of - blk_index + REACH
    ) % cycle_size * tile_count + block_lists % tile_count
    query_tile = blk_index * tile_count + jnp.arange(tile_count, dtype=jnp.int32)
    distance = (
        jnp.abs(tile_order[query_tile][:, None] - tile_order[block_lists]).astype(jnp.float32)
        / tile_order.shape[0]
    )
    valid = jnp.arange(SLOTS, dtype=jnp.int32)[None, :] < block_counts[:, None]
    head_index = lax.axis_index("head") * heads_local + jnp.arange(heads_local, dtype=jnp.int32)
    slopes = 8.0 * jnp.power(2.0, -8.0 * head_index.astype(jnp.float32) / H)
    scale = DH ** (-0.5)

    def one_tile(items):
        q_tile, where_index, dist_row, valid_row = items
        chosen = window[:, where_index]
        scores = (
            jnp.einsum("ihd,cjhd->hicj", q_tile, chosen[0], preferred_element_type=jnp.float32)
            * scale
        )
        scores = scores - slopes[:, None, None, None] * dist_row[None, None, :, None]
        scores = jnp.where(valid_row[None, None, :, None], scores, -1e30).reshape(
            heads_local, TILE, SLOTS * TILE
        )
        top = jnp.max(scores, axis=-1)
        weights = jnp.exp(scores - top[..., None]).astype(jnp.bfloat16)
        total = jnp.sum(weights.astype(jnp.float32), axis=-1)
        mixed = jnp.einsum(
            "hik,khd->ihd",
            weights,
            chosen[1].reshape(SLOTS * TILE, heads_local, DH),
            preferred_element_type=jnp.float32,
        )
        return (mixed / total.T[:, :, None]).astype(jnp.bfloat16)

    out_tiles = lax.map(one_tile, (q_tiles, slot_window, distance, valid))
    return lax.all_to_all(
        out_tiles.reshape(shard_tok, heads_local * DH),
        "head",
        split_axis=0,
        concat_axis=1,
        tiled=True,
    )


def solution(mesh):
    in_specs = (
        P(("blk", "head"), None),
        P(("blk", "head"), None),
        P(("blk", "head"), None),
        P("blk", None),
        P("blk"),
        P(),
    )
    out_specs = P(("blk", "head"), None)
    return jax.shard_map(body, mesh=mesh, in_specs=in_specs, out_specs=out_specs, check_vma=False)
```

profile of v0, /device:TPU:128, one launch (start us, length us, event | category | flops | bytes accessed | tf_op | source)
XLA Modules:
  0.0 854.5 jit_solution(15599572577048918496)
XLA Ops:
  2.7 4.9 all-to-all-start
  9.2 19.8 %all-to-all-done = bf16[128,8,768]{0,2,1:T(8,128)(2,1)S(1)} async-done(((bf16[128,8,768]{0,2,1:T(8,128)(2,1)}), bf16[128,8,768]{0,2,1:T(8,128)(2,1)S(1)}, u32[]{:S(2)}, u32[]{:S(2)}) %all-to-all-start) | async-done | bytes 1572896 | tf_op jit(solution)/shard_map/all_to_all | solution.py:25
  29.0 24.2 %all_to_all.67 = bf16[128,8,768]{0,2,1:T(8,128)(2,1)S(1)} all-to-all(bf16[128,8,768]{0,2,1:T(8,128)(2,1)} %bitcast.102), channel_id=1, replica_groups=mesh['head'=8,'blk'=32] {'head'}, dimensions={1} | all-to-all | bytes 3145728 | tf_op jit(solution)/shard_map/all_to_all | solution.py:26
  54.2 135.8 %collective-permute-done = bf16[2,8,128,6,128]{2,4,3,1,0:T(8,128)(2,1)S(1)} collective-permute-done((bf16[2,8,128,6,128]{2,4,3,1,0:T(8,128)(2,1)S(1)}, bf16[2,8,128,6,128]{2,4,3,1,0:T(8,128)(2,1)S(1)}, u32[]{:S(2)}, u32[]{:S(2)}) %collective-permute-start) | collective-permute-done | bytes 3145760 | tf_op jit(solution)/shard_map/ppermute | solution.py:16
  192.0 57.5 %collective-permute-done.1 = bf16[2,8,128,6,128]{2,4,3,1,0:T(8,128)(2,1)S(1)} collective-permute-done((bf16[2,8,128,6,128]{2,4,3,1,0:T(8,128)(2,1)S(1)}, bf16[2,8,128,6,128]{2,4,3,1,0:T(8,128)(2,1)S(1)}, u32[]{:S(2)}, u32[]{:S(2)}) %collective-permute-start.1) | collective-permute-done | bytes 3145760 | tf_op jit(solution)/shard_map/ppermute | solution.py:16
  251.1 71.7 %collective-permute-done.2 = bf16[2,8,128,6,128]{2,4,3,1,0:T(8,128)(2,1)S(1)} collective-permute-done((bf16[2,8,128,6,128]{2,4,3,1,0:T(8,128)(2,1)S(1)}, bf16[2,8,128,6,128]{2,4,3,1,0:T(8,128)(2,1)S(1)}, u32[]{:S(2)}, u32[]{:S(2)}) %collective-permute-start.2) | collective-permute-done | bytes 3145760 | tf_op jit(solution)/shard_map/ppermute | solution.py:16
  324.6 71.0 %collective-permute-done.3 = bf16[2,8,128,6,128]{2,4,3,1,0:T(8,128)(2,1)S(1)} collective-permute-done((bf16[2,8,128,6,128]{2,4,3,1,0:T(8,128)(2,1)S(1)}, bf16[2,8,128,6,128]{2,4,3,1,0:T(8,128)(2,1)S(1)}, u32[]{:S(2)}, u32[]{:S(2)}) %collective-permute-start.3) | collective-permute-done | bytes 3145760 | tf_op jit(solution)/shard_map/ppermute | solution.py:16
  395.5 52.5 %collective-permute-done.4 = bf16[2,8,128,6,128]{2,4,3,1,0:T(8,128)(2,1)S(1)} collective-permute-done((bf16[2,8,128,6,128]{2,4,3,1,0:T(8,128)(2,1)S(1)}, bf16[2,8,128,6,128]{2,4,3,1,0:T(8,128)(2,1)S(1)}, u32[]{:S(2)}, u32[]{:S(2)}) %collective-permute-start.4) | collective-permute-done | bytes 3145760 | tf_op jit(solution)/shard_map/ppermute | solution.py:16
  449.7 67.0 %collective-permute-done.5 = bf16[2,8,128,6,128]{2,4,3,1,0:T(8,128)(2,1)} collective-permute-done((bf16[2,8,128,6,128]{2,4,3,1,0:T(8,128)(2,1)S(1)}, bf16[2,8,128,6,128]{2,4,3,1,0:T(8,128)(2,1)}, u32[]{:S(2)}, u32[]{:S(2)}) %collective-permute-start.5) | collective-permute-done | bytes 3145760 | tf_op jit(solution)/shard_map/ppermute | solution.py:16
  519.2 72.9 %all-to-all-start.2 = ((bf16[128,8,768]{0,2,1:T(8,128)(2,1)}), bf16[128,8,768]{0,2,1:T(8,128)(2,1)}, u32[]{:S(2)}, u32[]{:S(2)}) async-start(bf16[128,8,768]{0,2,1:T(8,128)(2,1)} %bitcast.101), calls=%async_computation.2 | async-start | bytes 3145728 | tf_op jit(solution)/shard_map/all_to_all | solution.py:24
  594.0 4.6 constant_dynamic-update-slice_fusion.6
  598.6 4.7 constant_dynamic-update-slice_fusion.5
  617.1 28.6 %copy.36 = bf16[2,56,128,6,128]{4,2,3,1,0:T(8,128)(2,1)} copy(bf16[2,56,128,6,128]{2,4,3,1,0:T(8,128)(2,1)} %constant_dynamic-update-slice_fusion) | data formatting | bytes 44040192
  645.7 153.6 %while.11 = (s32[]{:T(128)}, bf16[8,128,6,128]{1,3,2,0:T(8,128)(2,1)}, s32[8,8]{1,0:T(8,128)S(1)}, bf16[2,56,128,6,128]{4,2,3,1,0:T(8,128)(2,1)}, pred[8,8]{1,0:...) while((s32[]{:T(128)}, ...), condition=%wide.region_3.4_spmd.clone, body=%wide.region_0.3_spmd.clone.sunk | while | flops 410713696 | bytes 44454676 | solution.py:79
  645.7 8.4 gather_fusion
  664.9 8.4 gather_fusion
  684.1 8.4 gather_fusion
  703.3 8.4 gather_fusion
  722.5 8.4 gather_fusion
  741.7 8.4 gather_fusion
  756.9 3.9 fusion.44
  760.9 8.4 gather_fusion
  780.1 8.4 gather_fusion
  801.0 51.0 %all_to_all.68 = bf16[8,128,768]{2,1,0:T(8,128)(2,1)S(1)} all-to-all(bf16[8,128,768]{2,1,0:T(8,128)(2,1)S(1)} %copy.38), channel_id=1, replica_groups=mesh['head'=8,'blk'=32] {'head'}, dimensions={0} | all-to-all | bytes 3145728 | tf_op jit(solution)/shard_map/all_to_all | solution.py:80
  (160 shorter events, 116.7 us)
Async XLA Ops:
  0.0 592.3 %copy-start = (s32[256]{0:T(256)S(1)}, s32[256]{0:T(256)}, u32[]{:S(2)}) copy-start(s32[256]{0:T(256)} %param.13) | copy-start | bytes 3076
  0.0 7.7 copy-start.10
  2.7 26.3 %all-to-all-start = ((bf16[128,8,768]{0,2,1:T(8,128)(2,1)}), bf16[128,8,768]{0,2,1:T(8,128)(2,1)S(1)}, u32[]{:S(2)}, u32[]{:S(2)}) async-start(bf16[128,8,768]{0,2,1:T(8,128)(2,1)} %bitcast), calls=%async_computation | async-start | bytes 3145728 | tf_op jit(solution)/shard_map/all_to_all | solution.py:25
  53.5 538.6 %copy-start.11 = (s32[8,8]{1,0:T(8,128)S(1)}, s32[8,8]{1,0:T(8,128)}, u32[]{:S(2)}) copy-start(s32[8,8]{1,0:T(8,128)} %param.11) | copy-start | bytes 772
  53.5 136.5 %collective-permute-start = (bf16[2,8,128,6,128]{2,4,3,1,0:T(8,128)(2,1)S(1)}, bf16[2,8,128,6,128]{2,4,3,1,0:T(8,128)(2,1)S(1)}, u32[]{:S(2)}, u32[]{:S(2)}) collective-permute-start(bf16[2,8,128,6,128]{2,4,3,1,0:T(8,128)(2,1)S(1)} %pad_maximum_fusion), channel_id=1, source_target_pairs={{3,0},{4,1},{5,2},{6,3},{7,4},{8,5},{9,6},{10,7},{11,8},{12,9},{13... | collective-permute-start | bytes 9437192 | tf_op jit(solution)/shard_map/ppermute | solution.py:16
  190.0 1.6 copy-start.2
  191.6 57.8 %collective-permute-start.1 = (bf16[2,8,128,6,128]{2,4,3,1,0:T(8,128)(2,1)S(1)}, bf16[2,8,128,6,128]{2,4,3,1,0:T(8,128)(2,1)S(1)}, u32[]{:S(2)}, u32[]{:S(2)}) collective-permute-start(bf16[2,8,128,6,128]{2,4,3,1,0:T(8,128)(2,1)S(1)} %collective-permute-done), channel_id=1, source_target_pairs={{31,0},{0,1},{1,2},{2,3},{3,4},{4,5},{5,6},{6,7},{7,8},{8,9},{9,10... | collective-permute-start | bytes 9437192 | tf_op jit(solution)/shard_map/ppermute | solution.py:16
  249.5 1.7 copy-start.4
  251.1 71.7 %collective-permute-start.2 = (bf16[2,8,128,6,128]{2,4,3,1,0:T(8,128)(2,1)S(1)}, bf16[2,8,128,6,128]{2,4,3,1,0:T(8,128)(2,1)S(1)}, u32[]{:S(2)}, u32[]{:S(2)}) collective-permute-start(bf16[2,8,128,6,128]{2,4,3,1,0:T(8,128)(2,1)S(1)} %collective-permute-done.1), channel_id=1, source_target_pairs={{31,0},{0,1},{1,2},{2,3},{3,4},{4,5},{5,6},{6,7},{7,8},{8,9},{9,10... | collective-permute-start | bytes 9437192 | tf_op jit(solution)/shard_map/ppermute | solution.py:16
  322.9 1.7 copy-start.6
  324.6 71.0 %collective-permute-start.3 = (bf16[2,8,128,6,128]{2,4,3,1,0:T(8,128)(2,1)S(1)}, bf16[2,8,128,6,128]{2,4,3,1,0:T(8,128)(2,1)S(1)}, u32[]{:S(2)}, u32[]{:S(2)}) collective-permute-start(bf16[2,8,128,6,128]{2,4,3,1,0:T(8,128)(2,1)S(1)} %collective-permute-done.2), channel_id=1, source_target_pairs={{31,0},{0,1},{1,2},{2,3},{3,4},{4,5},{5,6},{6,7},{7,8},{8,9},{9,10... | collective-permute-start | bytes 9437192 | tf_op jit(solution)/shard_map/ppermute | solution.py:16
  395.5 52.5 %collective-permute-start.4 = (bf16[2,8,128,6,128]{2,4,3,1,0:T(8,128)(2,1)S(1)}, bf16[2,8,128,6,128]{2,4,3,1,0:T(8,128)(2,1)S(1)}, u32[]{:S(2)}, u32[]{:S(2)}) collective-permute-start(bf16[2,8,128,6,128]{2,4,3,1,0:T(8,128)(2,1)S(1)} %collective-permute-done.3), channel_id=1, source_target_pairs={{31,0},{0,1},{1,2},{2,3},{3,4},{4,5},{5,6},{6,7},{7,8},{8,9},{9,10... | collective-permute-start | bytes 9437192 | tf_op jit(solution)/shard_map/ppermute | solution.py:16
  448.0 1.7 copy-start.8
  449.7 67.0 %collective-permute-start.5 = (bf16[2,8,128,6,128]{2,4,3,1,0:T(8,128)(2,1)S(1)}, bf16[2,8,128,6,128]{2,4,3,1,0:T(8,128)(2,1)}, u32[]{:S(2)}, u32[]{:S(2)}) collective-permute-start(bf16[2,8,128,6,128]{2,4,3,1,0:T(8,128)(2,1)S(1)} %collective-permute-done.4), channel_id=1, source_target_pairs={{31,0},{0,1},{1,2},{2,3},{3,4},{4,5},{5,6},{6,7},{7,8},{8,9},{9,10... | collective-permute-start | bytes 9437192 | tf_op jit(solution)/shard_map/ppermute | solution.py:16
  516.6 77.3 %collective-permute-start.6 = (bf16[2,8,128,6,128]{2,4,3,1,0:T(8,128)(2,1)}, bf16[2,8,128,6,128]{2,4,3,1,0:T(8,128)(2,1)}, u32[]{:S(2)}, u32[]{:S(2)}) collective-permute-start(bf16[2,8,128,6,128]{2,4,3,1,0:T(8,128)(2,1)} %collective-permute-done.5), channel_id=1, source_target_pairs={{31,0},{0,1},{1,2},{2,3},{3,4},{4,5},{5,6},{6,7},{7,8},{8,9},{9,10... | collective-permute-start | bytes 9437192 | tf_op jit(solution)/shard_map/ppermute | solution.py:16
  519.2 126.5 %all-to-all-start.2 = ((bf16[128,8,768]{0,2,1:T(8,128)(2,1)}), bf16[128,8,768]{0,2,1:T(8,128)(2,1)}, u32[]{:S(2)}, u32[]{:S(2)}) async-start(bf16[128,8,768]{0,2,1:T(8,128)(2,1)} %bitcast.101), calls=%async_computation.2 | async-start | bytes 3145728 | tf_op jit(solution)/shard_map/all_to_all | solution.py:24
  592.1 1.7 copy-start.12
  598.6 4.7 copy-start.9
  606.1 2.8 copy-start.7
  608.9 2.7 copy-start.5
  611.7 2.7 copy-start.3
  801.0 53.5 %copy-start.1 = (s32[256]{0:T(256)S(1)}, s32[256]{0:T(256)}, u32[]{:S(2)}) copy-start(s32[256]{0:T(256)} %param.13) | copy-start | bytes 3076
where the time goes:
time: 870 us; the launch traced here: 854 us
  waiting for transfers between devices  475 us (55%)
  local copies, waits for them, and re-layouts  169 us (19%)
  starting transfers between devices  78.9 us (9%)
  blocking collectives  75.2 us (9%)
  matrix products  43.4 us (5%)
  other arithmetic  12 us (1%)
    ppermute x7, waiting for transfers between devices, shifted(): return lax.ppermute(block, axis, route)  455 us
    all_to_all x1, starting transfers between devices, body(): lax.all_to_all(queries, 'head', split_axis=1, concat_axis=0, tiled=True)  72.9 us
    gather x16, local copies, waits for them, and re-layouts, one_tile(): chosen = window[:, where_index]  69.1 us
    unnamed x35, local copies, waits for them, and re-layouts  60.4 us
    all_to_all x1, blocking collectives, body(): lax.all_to_all(out_tiles.reshape(shard_tok, heads_local * DH), 'head', sp...  51 us
    dot_general x8, matrix products, one_tile(): jnp.einsum('hik,khd->ihd', weights, chosen[1].reshape(SLOTS * TILE, heads...  31.6 us
    all_to_all x1, blocking collectives, body(): lax.all_to_all(value_states, 'head', split_axis=1, concat_axis=0, tiled=T...  24.2 us
    all_to_all x1, waiting for transfers between devices, body(): lax.all_to_all(key_states, 'head', split_axis=1, concat_axis=0, tiled=True)  19.8 us
  transfers between devices with their start and end apart: 9, of which 7 were waited for; matrix products, arithmetic and copies ran while one was open for 7% of the time, Pallas kernels for 0%

commit v1 on v0

v1 whole, which is shorter than its diff:
```python
import jax
import jax.numpy as jnp
from jax import lax
from jax.experimental import pallas as pl
from jax.experimental.pallas import tpu as pltpu
from jax.sharding import PartitionSpec as P

H = 48
DH = 128
TILE = 128
REACH = 3
SLOTS = 8

PIECE_OF_OFFSET = ((4, 1, 5, 0, 3, 2, 6), (5, 1, 3, 0, 6, 2, 4))


def permute(block, axis, route):
    return lax.ppermute(block, axis, route)


def shift_pairs(n, distance):
    return [(i, (i + distance) % n) for i in range(n)]


def attention_kernel(sw_ref, cnt_ref, bias_ref, q_ref, *refs, heads_local, scale):
    k_refs = refs[:SLOTS]
    v_refs = refs[SLOTS:2 * SLOTS]
    o_ref = refs[2 * SLOTS]
    i = pl.program_id(0)
    count = cnt_ref[i]
    for h in range(heads_local):
        cols = slice(h * DH, (h + 1) * DH)
        q = q_ref[:, cols]
        scores = []
        for c in range(SLOTS):
            k = k_refs[c][:, cols]
            s = lax.dot_general(q, k, (((1,), (1,)), ((), ())), preferred_element_type=jnp.float32)
            s = s * scale
            s = s - bias_ref[(i * SLOTS + c) * heads_local + h]
            s = jnp.where(c < count, s, -1e30)
            scores.append(s)
        top = scores[0].max(axis=1, keepdims=True)
        for c in range(1, SLOTS):
            top = jnp.maximum(top, scores[c].max(axis=1, keepdims=True))
        total = jnp.zeros((TILE, 1), jnp.float32)
        acc = jnp.zeros((TILE, DH), jnp.float32)
        for c in range(SLOTS):
            w = jnp.exp(scores[c] - top).astype(jnp.bfloat16)
            total = total + w.astype(jnp.float32).sum(axis=1, keepdims=True)
            acc = acc + jnp.dot(w, v_refs[c][:, cols], preferred_element_type=jnp.float32)
        o_ref[:, cols] = (acc / total).astype(o_ref.dtype)


def body(queries, key_states, value_states, block_lists, block_counts, tile_order):
    cycle_size = lax.axis_size("blk")
    group_size = lax.axis_size("head")
    heads_local = H // group_size
    k_heads, v_heads = (
        lax.all_to_all(key_states, "head", split_axis=1, concat_axis=0, tiled=True),
        lax.all_to_all(value_states, "head", split_axis=1, concat_axis=0, tiled=True),
    )
    q_heads = lax.all_to_all(queries, "head", split_axis=1, concat_axis=0, tiled=True)
    shard_tok = q_heads.shape[0]
    tile_count = shard_tok // TILE
    width = heads_local * DH
    local_pair = jnp.stack((k_heads, v_heads))

    n = cycle_size
    from_left2 = permute(local_pair, "blk", shift_pairs(n, 2))
    from_right2 = permute(local_pair, "blk", shift_pairs(n, -2))
    other_core = permute(local_pair, "blk", [(i, i ^ 1) for i in range(n)])
    blk_index = lax.axis_index("blk")
    core = blk_index % 2
    forward = jnp.where(core == 1, from_left2, from_right2)
    cross_route = [(i, i + 1) if i % 2 == 1 else (i, i - 1) for i in range(n)]
    cross_route = [(s, d % n) for s, d in cross_route]
    across = permute(forward, "blk", cross_route)
    other_left2 = permute(from_left2, "blk", [(i, i ^ 1) for i in range(n)])
    other_right2 = permute(from_right2, "blk", [(i, i ^ 1) for i in range(n)])
    window = jnp.concatenate(
        [local_pair, from_left2, from_right2, other_core, across, other_left2, other_right2], axis=1
    )

    shard_of = block_lists // tile_count
    offset = (shard_of - blk_index + REACH) % cycle_size
    table = jnp.array(PIECE_OF_OFFSET, dtype=jnp.int32)[core]
    slot_window = (table[offset] * tile_count + block_lists % tile_count).astype(jnp.int32)
    query_tile = blk_index * tile_count + jnp.arange(tile_count, dtype=jnp.int32)
    distance = (
        jnp.abs(tile_order[query_tile][:, None] - tile_order[block_lists]).astype(jnp.float32)
        / tile_order.shape[0]
    )
    head_index = lax.axis_index("head") * heads_local + jnp.arange(heads_local, dtype=jnp.int32)
    slopes = 8.0 * jnp.power(2.0, -8.0 * head_index.astype(jnp.float32) / H)
    bias = (slopes[None, None, :] * distance[:, :, None]).reshape(-1)
    scale = DH ** (-0.5)

    def kv_spec(which, c):
        return pl.BlockSpec((None, TILE, width), lambda i, sw, cnt, which=which, c=c: (which, sw[i * SLOTS + c], 0))

    in_specs = (
        [pl.BlockSpec(memory_space=pltpu.SMEM), pl.BlockSpec((TILE, width), lambda i, sw, cnt: (i, 0))]
        + [kv_spec(0, c) for c in range(SLOTS)]
        + [kv_spec(1, c) for c in range(SLOTS)]
    )
    grid_spec = pltpu.PrefetchScalarGridSpec(
        num_scalar_prefetch=2,
        grid=(tile_count,),
        in_specs=in_specs,
        out_specs=pl.BlockSpec((TILE, width), lambda i, sw, cnt: (i, 0)),
    )
    kernel = lambda *args: attention_kernel(*args, heads_local=heads_local, scale=scale)
    out = pl.pallas_call(
        kernel,
        grid_spec=grid_spec,
        out_shape=jax.ShapeDtypeStruct((shard_tok, width), jnp.bfloat16),
    )(slot_window.reshape(-1), block_counts.astype(jnp.int32), bias, q_heads, *([window] * (2 * SLOTS)))
    return lax.all_to_all(out, "head", split_axis=0, concat_axis=1, tiled=True)


def solution(mesh):
    in_specs = (
        P(("blk", "head"), None),
        P(("blk", "head"), None),
        P(("blk", "head"), None),
        P("blk", None),
        P("blk"),
        P(),
    )
    out_specs = P(("blk", "head"), None)
    return jax.shard_map(body, mesh=mesh, in_specs=in_specs, out_specs=out_specs, check_vma=False)
```

time: 870 us -> 347 us (0.40); the launches traced: 854 us -> 346 us
  waiting for transfers between devices: 475 us -> 192 us
  local copies, waits for them, and re-layouts: 169 us -> 27.7 us
  matrix products: 43.4 us -> 0 us
  blocking collectives: 75.2 us -> 42 us
  starting transfers between devices: 78.9 us -> 47.6 us
  Pallas kernels: 0 us -> 28.2 us
    ppermute x7 -> x6, waiting for transfers between devices: 455 us -> 172 us  [permute(): return lax.ppermute(block, axis, route)]
    gather x16 -> x1, local copies, waits for them, and re-layouts: 69.1 us -> 0.77 us  [body(): table[offset] * tile_count + block_lists % tile_count]
    unnamed x35 -> x12, local copies, waits for them, and re-layouts: 60.4 us -> 13.3 us
    all_to_all x1, starting transfers between devices: 72.9 us -> 33 us  [body(): lax.all_to_all(queries, 'head', split_axis=1, concat_axis=0, tiled=True)]
    all_to_all x1, blocking collectives: 51 us -> 17.8 us  [body(): return lax.all_to_all(out, 'head', split_axis=0, concat_axis=1, tiled=True)]
    dot_general x8 -> x0, matrix products: 31.6 us -> none  [one_tile(): jnp.einsum('hik,khd->ihd', weights, chosen[1].reshape(SLOTS * TILE, heads...]
    pallas_call x0 -> x1, Pallas kernels: none -> 28.2 us  [body(): pl.pallas_call(kernel, grid_spec=grid_spec, out_shape=jax.ShapeDtypeStruc...]
    reshape x8 -> x1, local copies, waits for them, and re-layouts: 19.2 us -> 0.62 us  [body(): slot_window.reshape(-1)]
  transfers between devices with their start and end apart: 9 -> 8, of which waited for: 7 -> 3; matrix products, arithmetic and copies ran while one was open for 7% -> 9% of each run, Pallas kernels for 0% -> 0%
where the time goes in v1:
time: 347 us; the launch traced here: 346 us
  waiting for transfers between devices  192 us (55%)
  starting transfers between devices  47.6 us (14%)
  blocking collectives  42 us (12%)
  Pallas kernels  28.2 us (8%)
  local copies, waits for them, and re-layouts  27.7 us (8%)
  other arithmetic  9.19 us (3%)
    ppermute x6, waiting for transfers between devices, permute(): return lax.ppermute(block, axis, route)  172 us
    all_to_all x1, starting transfers between devices, body(): lax.all_to_all(queries, 'head', split_axis=1, concat_axis=0, tiled=True)  33 us
    pallas_call x1, Pallas kernels, body(): pl.pallas_call(kernel, grid_spec=grid_spec, out_shape=jax.ShapeDtypeStruc...  28.2 us
    all_to_all x1, blocking collectives, body(): lax.all_to_all(value_states, 'head', split_axis=1, concat_axis=0, tiled=T...  24.2 us
    all_to_all x1, waiting for transfers between devices, body(): lax.all_to_all(key_states, 'head', split_axis=1, concat_axis=0, tiled=True)  19.8 us
    all_to_all x1, blocking collectives, body(): return lax.all_to_all(out, 'head', split_axis=0, concat_axis=1, tiled=True)  17.8 us
    unnamed x12, local copies, waits for them, and re-layouts  13.3 us
    ppermute x6, starting transfers between devices, permute(): return lax.ppermute(block, axis, route)  9.74 us
  transfers between devices with their start and end apart: 8, of which 3 were waited for; matrix products, arithmetic and copies ran while one was open for 9% of the time, Pallas kernels for 0%

profile of v1, /device:TPU:128, one launch (start us, length us, event | category | flops | bytes accessed | tf_op | source)
XLA Modules:
  0.0 346.4 jit_solution(18419283522788297083)
XLA Ops:
  0.0 2.7 copy.24
  2.7 4.9 %all-to-all-start.1 = ((bf16[128,8,768]{2,0,1:T(8,128)(2,1)}), bf16[128,8,768]{2,0,1:T(8,128)(2,1)S(1)}, u32[]{:S(2)}, u32[]{:S(2)}) async-start(bf16[128,8,768]{2,0,1:T(8,128)(2,1)} %bitcast.27), calls=%async_computation.1 | async-start | bytes 3145728 | tf_op jit(solution)/shard_map/all_to_all | solution.py:59
  7.6 1.5 copy.23
  9.1 19.8 %all-to-all-done.1 = bf16[128,8,768]{2,0,1:T(8,128)(2,1)S(1)} async-done(((bf16[128,8,768]{2,0,1:T(8,128)(2,1)}), bf16[128,8,768]{2,0,1:T(8,128)(2,1)S(1)}, u32[]{:S(2)}, u32[]{:S(2)}) %all-to-all-start.1) | async-done | bytes 1572896 | tf_op jit(solution)/shard_map/all_to_all | solution.py:59
  29.0 24.2 %all_to_all.70 = bf16[128,8,768]{2,0,1:T(8,128)(2,1)S(1)} all-to-all(bf16[128,8,768]{2,0,1:T(8,128)(2,1)S(1)} %bitcast.32), channel_id=1, replica_groups=mesh['head'=8,'blk'=32] {'head'}, dimensions={1} | all-to-all | bytes 3145728 | tf_op jit(solution)/shard_map/all_to_all | solution.py:60
  53.2 3.3 pad_maximum_fusion
  56.4 1.5 collective-permute-start
  57.9 4.8 %collective-permute-start.1 = (bf16[2,1024,768]{2,1,0:T(8,128)(2,1)}, bf16[2,1024,768]{2,1,0:T(8,128)(2,1)}, u32[]{:S(2)}, u32[]{:S(2)}) collective-permute-start(bf16[2,1024,768]{2,1,0:T(8,128)(2,1)} %get-tuple-element.7), channel_id=1, source_target_pairs={{0,30},{1,31},{2,0},{3,1},{4,2},{5,3},{6,4},{7,5},{8,6},{9,7},{10,... | collective-permute-start | bytes 9437192 | tf_op jit(solution)/shard_map/ppermute | solution.py:18
  62.7 134.1 %collective-permute-done = bf16[2,1024,768]{2,1,0:T(8,128)(2,1)S(1)} collective-permute-done((bf16[2,1024,768]{2,1,0:T(8,128)(2,1)}, bf16[2,1024,768]{2,1,0:T(8,128)(2,1)S(1)}, u32[]{:S(2)}, u32[]{:S(2)}) %collective-permute-start) | collective-permute-done | bytes 3145760 | tf_op jit(solution)/shard_map/ppermute | solution.py:18
  196.8 1.9 constant_dynamic-update-slice_fusion.5
  198.7 5.7 %broadcast_select_fusion = (bf16[2,1024,768]{2,1,0:T(8,128)(2,1)}, bf16[2,7168,768]{2,1,0:T(8,128)(2,1)}) fusion(bf16[2,1024,768]{2,1,0:T(8,128)(2,1)S(1)} %collective-permute-done, bf16[2,1024,768]{2,1,0:T(8,128)(2,1)} %collective-permute-done.1, pred[]{:T(512)S(6)} %eq.8, bf16[2,7168,768]{2,1,0:T(8,128)(2,1)} %constant_dynamic-update-slice_fusion.5), kind=kLoop, calls=%fused_computation.4 | loop fusion | flops 1572864 | bytes 12582913 | tf_op jit(solution)/shard_map/jit(_where)/select_n | solution.py:74
  204.4 3.0 collective-permute-start.3
  207.9 1.2 copy.25
  209.1 33.0 %all-to-all-start = ((bf16[128,8,768]{2,0,1:T(8,128)(2,1)}), bf16[128,8,768]{2,0,1:T(8,128)(2,1)}, u32[]{:S(2)}, u32[]{:S(2)}) async-start(bf16[128,8,768]{2,0,1:T(8,128)(2,1)} %bitcast.30), calls=%async_computation | async-start | bytes 3145728 | tf_op jit(solution)/shard_map/all_to_all | solution.py:62
  242.2 0.8 gather_fusion
  243.8 0.8 gather_fusion.2
  246.3 3.8 %constant_dynamic-update-slice_fusion.3 = bf16[2,7168,768]{2,1,0:T(8,128)(2,1)} fusion(bf16[2,7168,768]{2,1,0:T(8,128)(2,1)} %get-tuple-element.6, bf16[2,1024,768]{2,1,0:T(8,128)(2,1)} %collective-permute-done.2), kind=kLoop, calls=%fused_computation.12 | loop fusion | bytes 6291456
  250.0 37.6 %collective-permute-done.3 = bf16[2,1024,768]{2,1,0:T(8,128)(2,1)} collective-permute-done((bf16[2,1024,768]{2,1,0:T(8,128)(2,1)}, bf16[2,1024,768]{2,1,0:T(8,128)(2,1)}, u32[]{:S(2)}, u32[]{:S(2)}) %collective-permute-start.3) | collective-permute-done | bytes 3145760 | tf_op jit(solution)/shard_map/ppermute | solution.py:18
  287.7 3.8 %constant_dynamic-update-slice_fusion.2 = bf16[2,7168,768]{2,1,0:T(8,128)(2,1)} fusion(bf16[2,7168,768]{2,1,0:T(8,128)(2,1)} %constant_dynamic-update-slice_fusion.3, bf16[2,1024,768]{2,1,0:T(8,128)(2,1)} %collective-permute-done.3), kind=kLoop, calls=%fused_computation.11 | loop fusion | bytes 6291456
  291.5 3.8 %constant_dynamic-update-slice_fusion.1 = bf16[2,7168,768]{2,1,0:T(8,128)(2,1)} fusion(bf16[2,7168,768]{2,1,0:T(8,128)(2,1)} %constant_dynamic-update-slice_fusion.2, bf16[2,1024,768]{2,1,0:T(8,128)(2,1)} %collective-permute-done.4), kind=kLoop, calls=%fused_computation.10 | loop fusion | bytes 6291456
  295.3 3.8 %constant_dynamic-update-slice_fusion.args_4_.args_5_.args_6_.args_7_.args_8_.args_9_.args_10_.args_11_.args_12_.args_13_.args_14_.args_15_.args_16_.args_17_.args_18_.args_19_ = bf16[2,7168,768]{2,1,0:T(8,128)(2,1)} fusion(bf16[2,7168,768]{2,1,0:T(8,128)(2,1)} %constant_dynamic-update-slice_fusion.1, bf16[2,1024,768]{2,1,0:T(8,128)(2,1)} %collective-permute-done.5), kind=kLoop, calls=%fused_computation.9 | loop fusion | bytes 6291456 | tf_op jit(solution)/shard_map/concatenate | solution.py:80
  299.1 28.2 %shard_map.73 = bf16[1024,768]{1,0:T(8,128)(2,1)} custom-call(s32[64]{0:T(128)} %reshape.66.args_0_, s32[8]{0:T(128)} %args_1_.4, f32[384]{0:T(512)} %mul.43.args_2_, bf16[1024,768]{1,0:T(8,128)(2,1)} %bitcast.3.args_3_, ...), custom_call_target="tpu_custom_call" | custom-call | tf_op jit(solution)/shard_map/pallas_call | solution.py:113
  327.3 17.8 %all_to_all.71 = bf16[8,128,768]{2,1,0:T(8,128)(2,1)S(1)} all-to-all(bf16[8,128,768]{2,1,0:T(8,128)(2,1)} %bitcast.29), channel_id=1, replica_groups=mesh['head'=8,'blk'=32] {'head'}, dimensions={0} | all-to-all | bytes 3145728 | tf_op jit(solution)/shard_map/all_to_all | solution.py:118
  345.1 1.3 copy.19
  (33 shorter events, 3.1 us)
Async XLA Ops:
  0.0 243.8 %copy-start = (s32[256]{0:T(256)S(1)}, s32[256]{0:T(256)}, u32[]{:S(2)}) copy-start(s32[256]{0:T(256)} %param.12) | copy-start | bytes 3076
  2.7 26.3 %all-to-all-start.1 = ((bf16[128,8,768]{2,0,1:T(8,128)(2,1)}), bf16[128,8,768]{2,0,1:T(8,128)(2,1)S(1)}, u32[]{:S(2)}, u32[]{:S(2)}) async-start(bf16[128,8,768]{2,0,1:T(8,128)(2,1)} %bitcast.27), calls=%async_computation.1 | async-start | bytes 3145728 | tf_op jit(solution)/shard_map/all_to_all | solution.py:59
  56.4 140.3 %collective-permute-start = (bf16[2,1024,768]{2,1,0:T(8,128)(2,1)}, bf16[2,1024,768]{2,1,0:T(8,128)(2,1)S(1)}, u32[]{:S(2)}, u32[]{:S(2)}) collective-permute-start(bf16[2,1024,768]{2,1,0:T(8,128)(2,1)} %get-tuple-element.7), channel_id=1, source_target_pairs={{0,2},{1,3},{2,4},{3,5},{4,6},{5,7},{6,8},{7,9},{8,10},{9,11},{10,... | collective-permute-start | bytes 9437192 | tf_op jit(solution)/shard_map/ppermute | solution.py:18
  57.9 140.7 %collective-permute-start.1 = (bf16[2,1024,768]{2,1,0:T(8,128)(2,1)}, bf16[2,1024,768]{2,1,0:T(8,128)(2,1)}, u32[]{:S(2)}, u32[]{:S(2)}) collective-permute-start(bf16[2,1024,768]{2,1,0:T(8,128)(2,1)} %get-tuple-element.7), channel_id=1, source_target_pairs={{0,30},{1,31},{2,0},{3,1},{4,2},{5,3},{6,4},{7,5},{8,6},{9,7},{10,... | collective-permute-start | bytes 9437192 | tf_op jit(solution)/shard_map/ppermute | solution.py:18
  62.7 183.6 %collective-permute-start.2 = (bf16[2,1024,768]{2,1,0:T(8,128)(2,1)}, bf16[2,1024,768]{2,1,0:T(8,128)(2,1)}, u32[]{:S(2)}, u32[]{:S(2)}) collective-permute-start(bf16[2,1024,768]{2,1,0:T(8,128)(2,1)} %get-tuple-element.7), channel_id=1, source_target_pairs={{0,1},{1,0},{2,3},{3,2},{4,5},{5,4},{6,7},{7,6},{8,9},{9,8},{10,11... | collective-permute-start | bytes 9437192 | tf_op jit(solution)/shard_map/ppermute | solution.py:18
  198.7 9.2 %copy-start.1 = (bf16[128,6144]{1,0:T(8,128)(2,1)S(1)}, bf16[128,6144]{1,0:T(8,128)(2,1)}, u32[]{:S(2)}) copy-start(bf16[128,6144]{1,0:T(8,128)(2,1)} %param.7) | copy-start | bytes 4718596
  204.4 83.3 %collective-permute-start.3 = (bf16[2,1024,768]{2,1,0:T(8,128)(2,1)}, bf16[2,1024,768]{2,1,0:T(8,128)(2,1)}, u32[]{:S(2)}, u32[]{:S(2)}) collective-permute-start(bf16[2,1024,768]{2,1,0:T(8,128)(2,1)} %get-tuple-element.5), channel_id=1, source_target_pairs={{0,31},{1,2},{2,1},{3,4},{4,3},{5,6},{6,5},{7,8},{8,7},{9,10},{10,... | collective-permute-start | bytes 9437192 | tf_op jit(solution)/shard_map/ppermute | solution.py:18
  207.3 84.1 %collective-permute-start.4 = (bf16[2,1024,768]{2,1,0:T(8,128)(2,1)S(1)}, bf16[2,1024,768]{2,1,0:T(8,128)(2,1)}, u32[]{:S(2)}, u32[]{:S(2)}) collective-permute-start(bf16[2,1024,768]{2,1,0:T(8,128)(2,1)S(1)} %collective-permute-done), channel_id=1, source_target_pairs={{0,1},{1,0},{2,3},{3,2},{4,5},{5,4},{6,7},{7,6},{8,9},{9,8},{10,11... | collective-permute-start | bytes 9437192 | tf_op jit(solution)/shard_map/ppermute | solution.py:18
  207.3 88.0 %collective-permute-start.5 = (bf16[2,1024,768]{2,1,0:T(8,128)(2,1)}, bf16[2,1024,768]{2,1,0:T(8,128)(2,1)}, u32[]{:S(2)}, u32[]{:S(2)}) collective-permute-start(bf16[2,1024,768]{2,1,0:T(8,128)(2,1)} %collective-permute-done.1), channel_id=1, source_target_pairs={{0,1},{1,0},{2,3},{3,2},{4,5},{5,4},{6,7},{7,6},{8,9},{9,8},{10,11... | collective-permute-start | bytes 9437192 | tf_op jit(solution)/shard_map/ppermute | solution.py:18
  207.9 34.2 %copy-start.2 = (s32[8,8]{1,0:T(8,128)S(1)}, s32[8,8]{1,0:T(8,128)}, u32[]{:S(2)}) copy-start(s32[8,8]{1,0:T(8,128)} %param.10) | copy-start | bytes 772
  207.9 34.3 %copy-start.3 = (s32[2,7]{1,0:T(2,128)S(1)}, s32[2,7]{1,0:T(2,128)}, u32[]{:S(2)}) copy-start(s32[2,7]{1,0:T(2,128)} %constant.85.clone) | copy-start | bytes 172
  209.1 90.0 %all-to-all-start = ((bf16[128,8,768]{2,0,1:T(8,128)(2,1)}), bf16[128,8,768]{2,0,1:T(8,128)(2,1)}, u32[]{:S(2)}, u32[]{:S(2)}) async-start(bf16[128,8,768]{2,0,1:T(8,128)(2,1)} %bitcast.30), calls=%async_computation | async-start | bytes 3145728 | tf_op jit(solution)/shard_map/all_to_all | solution.py:62

commit v2 on v1

--- a/solution.py
+++ b/solution.py
@@ -33,8 +33,7 @@
         q = q_ref[:, cols]
         scores = []
         for c in range(SLOTS):
-            k = k_refs[c][:, cols]
-            s = lax.dot_general(q, k, (((1,), (1,)), ((), ())), preferred_element_type=jnp.float32)
+            s = jnp.dot(q, k_refs[c][cols, :], preferred_element_type=jnp.float32)
             s = s * scale
             s = s - bias_ref[(i * SLOTS + c) * heads_local + h]
             s = jnp.where(c < count, s, -1e30)
@@ -51,36 +50,36 @@
         o_ref[:, cols] = (acc / total).astype(o_ref.dtype)
 
 
+def exchange(local, axis, n):
+    swap = [(i, i ^ 1) for i in range(n)]
+    from_left2 = permute(local, "blk", shift_pairs(n, 2))
+    from_right2 = permute(local, "blk", shift_pairs(n, -2))
+    other_core = permute(local, "blk", swap)
+    core = lax.axis_index("blk") % 2
+    forward = jnp.where(core == 1, from_left2, from_right2)
+    cross_route = [((i, (i + 1) % n) if i % 2 == 1 else (i, (i - 1) % n)) for i in range(n)]
+    across = permute(forward, "blk", cross_route)
+    other_left2 = permute(from_left2, "blk", swap)
+    other_right2 = permute(from_right2, "blk", swap)
+    pieces = [local, from_left2, from_right2, other_core, across, other_left2, other_right2]
+    return jnp.concatenate(pieces, axis=axis)
+
+
 def body(queries, key_states, value_states, block_lists, block_counts, tile_order):
     cycle_size = lax.axis_size("blk")
     group_size = lax.axis_size("head")
     heads_local = H // group_size
-    k_heads, v_heads = (
-        lax.all_to_all(key_states, "head", split_axis=1, concat_axis=0, tiled=True),
-        lax.all_to_all(value_states, "head", split_axis=1, concat_axis=0, tiled=True),
-    )
+    k_heads = lax.all_to_all(key_states, "head", split_axis=1, concat_axis=0, tiled=True)
+    k_window = exchange(k_heads.T, 1, cycle_size)
+    v_heads = lax.all_to_all(value_states, "head", split_axis=1, concat_axis=0, tiled=True)
+    v_window = exchange(v_heads, 0, cycle_size)
     q_heads = lax.all_to_all(queries, "head", split_axis=1, concat_axis=0, tiled=True)
     shard_tok = q_heads.shape[0]
     tile_count = shard_tok // TILE
     width = heads_local * DH
-    local_pair = jnp.stack((k_heads, v_heads))
 
-    n = cycle_size
-    from_left2 = permute(local_pair, "blk", shift_pairs(n, 2))
-    from_right2 = permute(local_pair, "blk", shift_pairs(n, -2))
-    other_core = permute(local_pair, "blk", [(i, i ^ 1) for i in range(n)])
     blk_index = lax.axis_index("blk")
     core = blk_index % 2
-    forward = jnp.where(core == 1, from_left2, from_right2)
-    cross_route = [(i, i + 1) if i % 2 == 1 else (i, i - 1) for i in range(n)]
-    cross_route = [(s, d % n) for s, d in cross_route]
-    across = permute(forward, "blk", cross_route)
-    other_left2 = permute(from_left2, "blk", [(i, i ^ 1) for i in range(n)])
-    other_right2 = permute(from_right2, "blk", [(i, i ^ 1) for i in range(n)])
-    window = jnp.concatenate(
-        [local_pair, from_left2, from_right2, other_core, across, other_left2, other_right2], axis=1
-    )
-
     shard_of = block_lists // tile_count
     offset = (shard_of - blk_index + REACH) % cycle_size
     table = jnp.array(PIECE_OF_OFFSET, dtype=jnp.int32)[core]
@@ -95,13 +94,16 @@
     bias = (slopes[None, None, :] * distance[:, :, None]).reshape(-1)
     scale = DH ** (-0.5)
 
-    def kv_spec(which, c):
-        return pl.BlockSpec((None, TILE, width), lambda i, sw, cnt, which=which, c=c: (which, sw[i * SLOTS + c], 0))
-
+    k_specs = [
+        pl.BlockSpec((width, TILE), lambda i, sw, cnt, c=c: (0, sw[i * SLOTS + c])) for c in range(SLOTS)
+    ]
+    v_specs = [
+        pl.BlockSpec((TILE, width), lambda i, sw, cnt, c=c: (sw[i * SLOTS + c], 0)) for c in range(SLOTS)
+    ]
     in_specs = (
         [pl.BlockSpec(memory_space=pltpu.SMEM), pl.BlockSpec((TILE, width), lambda i, sw, cnt: (i, 0))]
-        + [kv_spec(0, c) for c in range(SLOTS)]
-        + [kv_spec(1, c) for c in range(SLOTS)]
+        + k_specs
+        + v_specs
     )
     grid_spec = pltpu.PrefetchScalarGridSpec(
         num_scalar_prefetch=2,
@@ -114,7 +116,14 @@
         kernel,
         grid_spec=grid_spec,
         out_shape=jax.ShapeDtypeStruct((shard_tok, width), jnp.bfloat16),
-    )(slot_window.reshape(-1), block_counts.astype(jnp.int32), bias, q_heads, *([window] * (2 * SLOTS)))
+    )(
+        slot_window.reshape(-1),
+        block_counts.astype(jnp.int32),
+        bias,
+        q_heads,
+        *([k_window] * SLOTS),
+        *([v_window] * SLOTS),
+    )
     return lax.all_to_all(out, "head", split_axis=0, concat_axis=1, tiled=True)
 
 

time: 347 us -> 331 us (0.954); the launches traced: 346 us -> 325 us
  blocking collectives: 42 us -> 18.8 us
  starting transfers between devices: 47.6 us -> 26.3 us
  local copies, waits for them, and re-layouts: 27.7 us -> 44.8 us
  waiting for transfers between devices: 192 us -> 204 us
  Pallas kernels: 28.2 us -> 24.2 us
    ppermute x6 -> x12, waiting for transfers between devices: 172 us -> 135 us  [permute(): return lax.ppermute(block, axis, route)]
    all_to_all x1, starting transfers between devices: 33 us -> 3.58 us  [body(): lax.all_to_all(queries, 'head', split_axis=1, concat_axis=0, tiled=True)]
    all_to_all x1, waiting for transfers between devices: 19.8 us -> 48.9 us  [body(): lax.all_to_all(key_states, 'head', split_axis=1, concat_axis=0, tiled=True)]
    all_to_all x1 -> x0, blocking collectives: 24.2 us -> none  [body(): lax.all_to_all(value_states, 'head', split_axis=1, concat_axis=0, tiled=T...]
    all_to_all x0 -> x1, waiting for transfers between devices: none -> 19.9 us  [body(): lax.all_to_all(value_states, 'head', split_axis=1, concat_axis=0, tiled=T...]
    unnamed x12 -> x25, local copies, waits for them, and re-layouts: 13.3 us -> 29 us
    all_to_all x0 -> x1, starting transfers between devices: none -> 5.06 us  [body(): lax.all_to_all(value_states, 'head', split_axis=1, concat_axis=0, tiled=T...]
    ppermute x6 -> x12, starting transfers between devices: 9.74 us -> 13.9 us  [permute(): return lax.ppermute(block, axis, route)]
  transfers between devices with their start and end apart: 8 -> 15, of which waited for: 3 -> 6; matrix products, arithmetic and copies ran while one was open for 9% -> 13% of each run, Pallas kernels for 0% -> 0%
where the time goes in v2:
time: 331 us; the launch traced here: 325 us
  waiting for transfers between devices  204 us (62%)
  local copies, waits for them, and re-layouts  44.8 us (14%)
  starting transfers between devices  26.3 us (8%)
  Pallas kernels  24.2 us (7%)
  blocking collectives  18.8 us (6%)
  other arithmetic  7.18 us (2%)
    ppermute x12, waiting for transfers between devices, permute(): return lax.ppermute(block, axis, route)  135 us
    all_to_all x1, waiting for transfers between devices, body(): lax.all_to_all(key_states, 'head', split_axis=1, concat_axis=0, tiled=True)  48.9 us
    unnamed x25, local copies, waits for them, and re-layouts  29 us
    pallas_call x1, Pallas kernels, body(): pl.pallas_call(kernel, grid_spec=grid_spec, out_shape=jax.ShapeDtypeStruc...  24.2 us
    all_to_all x1, waiting for transfers between devices, body(): lax.all_to_all(value_states, 'head', split_axis=1, concat_axis=0, tiled=T...  19.9 us
    all_to_all x1, blocking collectives, body(): return lax.all_to_all(out, 'head', split_axis=0, concat_axis=1, tiled=True)  18.8 us
    ppermute x12, starting transfers between devices, permute(): return lax.ppermute(block, axis, route)  13.9 us
    select_n x2, other arithmetic, exchange(): forward = jnp.where(core == 1, from_left2, from_right2)  6.97 us
  transfers between devices with their start and end apart: 15, of which 6 were waited for; matrix products, arithmetic and copies ran while one was open for 13% of the time, Pallas kernels for 0%

profile of v2, /device:TPU:128, one launch (start us, length us, event | category | flops | bytes accessed | tf_op | source)
XLA Modules:
  0.0 325.4 jit_solution(8813473545174700759)
XLA Ops:
  0.0 2.7 copy.30
  2.7 5.1 %all-to-all-start.2 = ((bf16[128,8,768]{2,0,1:T(8,128)(2,1)}), bf16[128,8,768]{2,0,1:T(8,128)(2,1)}, u32[]{:S(2)}, u32[]{:S(2)}) async-start(bf16[128,8,768]{2,0,1:T(8,128)(2,1)} %bitcast.35), calls=%async_computation.2 | async-start | bytes 3145728 | tf_op jit(solution)/shard_map/all_to_all | solution.py:74
  9.3 19.9 %all-to-all-done.2 = bf16[128,8,768]{2,0,1:T(8,128)(2,1)} async-done(((bf16[128,8,768]{2,0,1:T(8,128)(2,1)}), bf16[128,8,768]{2,0,1:T(8,128)(2,1)}, u32[]{:S(2)}, u32[]{:S(2)}) %all-to-all-start.2) | async-done | bytes 1572896 | tf_op jit(solution)/shard_map/all_to_all | solution.py:74
  29.2 3.7 %all-to-all-start.1 = ((bf16[128,8,768]{0,2,1:T(8,128)(2,1)}), bf16[128,8,768]{0,2,1:T(8,128)(2,1)S(1)}, u32[]{:S(2)}, u32[]{:S(2)}) async-start(bf16[128,8,768]{0,2,1:T(8,128)(2,1)} %bitcast.4), calls=%async_computation.1 | async-start | bytes 3145728 | tf_op jit(solution)/shard_map/all_to_all | solution.py:72
  34.5 4.8 %collective-permute-start.7 = (bf16[1024,768]{1,0:T(8,128)(2,1)}, bf16[1024,768]{1,0:T(8,128)(2,1)}, u32[]{:S(2)}, u32[]{:S(2)}) collective-permute-start(bf16[1024,768]{1,0:T(8,128)(2,1)} %bitcast.8), channel_id=1, source_target_pairs={{0,30},{1,31},{2,0},{3,1},{4,2},{5,3},{6,4},{7,5},{8,6},{9,7},{10,... | collective-permute-start | bytes 4718600 | tf_op jit(solution)/shard_map/ppermute | solution.py:18
  40.5 48.9 %all-to-all-done.1 = bf16[128,8,768]{0,2,1:T(8,128)(2,1)S(1)} async-done(((bf16[128,8,768]{0,2,1:T(8,128)(2,1)}), bf16[128,8,768]{0,2,1:T(8,128)(2,1)S(1)}, u32[]{:S(2)}, u32[]{:S(2)}) %all-to-all-start.1) | async-done | bytes 1572896 | tf_op jit(solution)/shard_map/all_to_all | solution.py:72
  89.4 3.6 %all-to-all-start = ((bf16[128,8,768]{2,0,1:T(8,128)(2,1)}), bf16[128,8,768]{2,0,1:T(8,128)(2,1)S(1)}, u32[]{:S(2)}, u32[]{:S(2)}) async-start(bf16[128,8,768]{2,0,1:T(8,128)(2,1)} %bitcast.39), calls=%async_computation | async-start | bytes 3145728 | tf_op jit(solution)/shard_map/all_to_all | solution.py:76
  94.4 6.3 %collective-permute-start.1 = (bf16[768,1024]{1,0:T(8,128)(2,1)}, bf16[768,1024]{1,0:T(8,128)(2,1)}, u32[]{:S(2)}, u32[]{:S(2)}) collective-permute-start(bf16[768,1024]{1,0:T(8,128)(2,1)} %bitcast_bitcast_fusion), channel_id=1, source_target_pairs={{0,30},{1,31},{2,0},{3,1},{4,2},{5,3},{6,4},{7,5},{8,6},{9,7},{10,... | collective-permute-start | bytes 4718600 | tf_op jit(solution)/shard_map/ppermute | solution.py:18
  102.2 53.3 %collective-permute-done.6 = bf16[1024,768]{1,0:T(8,128)(2,1)} collective-permute-done((bf16[1024,768]{1,0:T(8,128)(2,1)}, bf16[1024,768]{1,0:T(8,128)(2,1)}, u32[]{:S(2)}, u32[]{:S(2)}) %collective-permute-start.6) | collective-permute-done | bytes 1572896 | tf_op jit(solution)/shard_map/ppermute | solution.py:18
  157.1 3.0 broadcast_select_fusion
  160.1 4.2 %copy-done.1 = bf16[7168,768]{1,0:T(8,128)(2,1)} copy-done((bf16[7168,768]{1,0:T(8,128)(2,1)}, bf16[7168,768]{1,0:T(8,128)(2,1)S(1)}, u32[]{:S(2)}) %copy-start.1) | copy-done | bytes 11010072
  166.8 56.2 %collective-permute-done = bf16[768,1024]{1,0:T(8,128)(2,1)} collective-permute-done((bf16[768,1024]{1,0:T(8,128)(2,1)}, bf16[768,1024]{1,0:T(8,128)(2,1)}, u32[]{:S(2)}, u32[]{:S(2)}) %collective-permute-start) | collective-permute-done | bytes 1572896 | tf_op jit(solution)/shard_map/ppermute | solution.py:18
  223.0 2.7 constant_dynamic-update-slice_fusion.5
  225.7 3.9 %broadcast_select_fusion.1 = (bf16[768,1024]{1,0:T(8,128)(2,1)}, bf16[768,7168]{1,0:T(8,128)(2,1)}) fusion(bf16[768,1024]{1,0:T(8,128)(2,1)} %collective-permute-done, bf16[768,1024]{1,0:T(8,128)(2,1)} %collective-permute-done.1, pred[]{:T(512)S(6)} %eq.11, bf16[768,7168]{1,0:T(8,128)(2,1)} %constant_dynamic-update-slice_fusion.5), kind=kLoop, calls=%fused_computation.7 | loop fusion | flops 786432 | bytes 6291457 | tf_op jit(solution)/shard_map/jit(_where)/select_n | solution.py:59
  233.2 5.0 %collective-permute-done.9 = bf16[1024,768]{1,0:T(8,128)(2,1)} collective-permute-done((bf16[1024,768]{1,0:T(8,128)(2,1)}, bf16[1024,768]{1,0:T(8,128)(2,1)}, u32[]{:S(2)}, u32[]{:S(2)}) %collective-permute-start.9) | collective-permute-done | bytes 1572896 | tf_op jit(solution)/shard_map/ppermute | solution.py:18
  239.0 2.7 constant_dynamic-update-slice_fusion.10
  241.7 2.7 constant_dynamic-update-slice_fusion.3
  244.4 2.7 constant_dynamic-update-slice_fusion.9
  251.1 20.7 %collective-permute-done.3 = bf16[768,1024]{1,0:T(8,128)(2,1)} collective-permute-done((bf16[768,1024]{1,0:T(8,128)(2,1)}, bf16[768,1024]{1,0:T(8,128)(2,1)}, u32[]{:S(2)}, u32[]{:S(2)}) %collective-permute-start.3) | collective-permute-done | bytes 1572896 | tf_op jit(solution)/shard_map/ppermute | solution.py:18
  271.8 2.7 constant_dynamic-update-slice_fusion.2
  274.5 2.7 constant_dynamic-update-slice_fusion.1
  277.3 2.7 constant_dynamic-update-slice_fusion.args_4_.args_5_.args_6_.args_7_.args_8_.args_9_.args_10_.args_11_
  281.1 24.2 %shard_map.73 = bf16[1024,768]{1,0:T(8,128)(2,1)} custom-call(s32[64]{0:T(128)} %reshape.64.args_0_, s32[8]{0:T(128)} %args_1_.4, f32[384]{0:T(512)} %mul.43.args_2_, bf16[1024,768]{1,0:T(8,128)(2,1)} %bitcast.37, bf16[768,7168]{1,0:T(8,128)(2,1)} %constant_dynamic-update-slice_fusion.args_4_.args_5_.args_6_.args_7_.args_8_.args_9_.args_10_.args_11_, ...), custom_call_target="tpu_custom_call" | custom-call | tf_op jit(solution)/shard_map/pallas_call | solution.py:115
  305.3 18.8 %all_to_all.76 = bf16[8,128,768]{2,1,0:T(8,128)(2,1)S(1)} all-to-all(bf16[8,128,768]{2,1,0:T(8,128)(2,1)} %bitcast.38), channel_id=1, replica_groups=mesh['head'=8,'blk'=32] {'head'}, dimensions={0} | all-to-all | bytes 3145728 | tf_op jit(solution)/shard_map/all_to_all | solution.py:127
  (60 shorter events, 22.2 us)
Async XLA Ops:
  0.0 231.6 %copy-start = (s32[256]{0:T(256)S(1)}, s32[256]{0:T(256)}, u32[]{:S(2)}) copy-start(s32[256]{0:T(256)} %param.12) | copy-start | bytes 3076
  2.7 5.1 %copy-start.3 = (bf16[128,6144]{1,0:T(8,128)(2,1)S(1)}, bf16[128,6144]{1,0:T(8,128)(2,1)}, u32[]{:S(2)}) copy-start(bf16[128,6144]{1,0:T(8,128)(2,1)} %param.8) | copy-start | bytes 4718596
  2.7 26.5 %all-to-all-start.2 = ((bf16[128,8,768]{2,0,1:T(8,128)(2,1)}), bf16[128,8,768]{2,0,1:T(8,128)(2,1)}, u32[]{:S(2)}, u32[]{:S(2)}) async-start(bf16[128,8,768]{2,0,1:T(8,128)(2,1)} %bitcast.35), calls=%async_computation.2 | async-start | bytes 3145728 | tf_op jit(solution)/shard_map/all_to_all | solution.py:74
  29.2 10.0 %copy-start.4 = (bf16[128,6144]{1,0:T(8,128)(2,1)S(1)}, bf16[128,6144]{1,0:T(8,128)(2,1)}, u32[]{:S(2)}) copy-start(bf16[128,6144]{1,0:T(8,128)(2,1)} %param.7) | copy-start | bytes 4718596
  29.2 60.2 %all-to-all-start.1 = ((bf16[128,8,768]{0,2,1:T(8,128)(2,1)}), bf16[128,8,768]{0,2,1:T(8,128)(2,1)S(1)}, u32[]{:S(2)}, u32[]{:S(2)}) async-start(bf16[128,8,768]{0,2,1:T(8,128)(2,1)} %bitcast.4), calls=%async_computation.1 | async-start | bytes 3145728 | tf_op jit(solution)/shard_map/all_to_all | solution.py:72
  32.9 122.7 %collective-permute-start.6 = (bf16[1024,768]{1,0:T(8,128)(2,1)}, bf16[1024,768]{1,0:T(8,128)(2,1)}, u32[]{:S(2)}, u32[]{:S(2)}) collective-permute-start(bf16[1024,768]{1,0:T(8,128)(2,1)} %bitcast.8), channel_id=1, source_target_pairs={{0,2},{1,3},{2,4},{3,5},{4,6},{5,7},{6,8},{7,9},{8,10},{9,11},{10,... | collective-permute-start | bytes 4718600 | tf_op jit(solution)/shard_map/ppermute | solution.py:18
  34.5 122.6 %collective-permute-start.7 = (bf16[1024,768]{1,0:T(8,128)(2,1)}, bf16[1024,768]{1,0:T(8,128)(2,1)}, u32[]{:S(2)}, u32[]{:S(2)}) collective-permute-start(bf16[1024,768]{1,0:T(8,128)(2,1)} %bitcast.8), channel_id=1, source_target_pairs={{0,30},{1,31},{2,0},{3,1},{4,2},{5,3},{6,4},{7,5},{8,6},{9,7},{10,... | collective-permute-start | bytes 4718600 | tf_op jit(solution)/shard_map/ppermute | solution.py:18
  89.4 190.6 %all-to-all-start = ((bf16[128,8,768]{2,0,1:T(8,128)(2,1)}), bf16[128,8,768]{2,0,1:T(8,128)(2,1)S(1)}, u32[]{:S(2)}, u32[]{:S(2)}) async-start(bf16[128,8,768]{2,0,1:T(8,128)(2,1)} %bitcast.39), calls=%async_computation | async-start | bytes 3145728 | tf_op jit(solution)/shard_map/all_to_all | solution.py:76
  92.9 1.4 copy-start.5
  94.3 128.7 %collective-permute-start = (bf16[768,1024]{1,0:T(8,128)(2,1)}, bf16[768,1024]{1,0:T(8,128)(2,1)}, u32[]{:S(2)}, u32[]{:S(2)}) collective-permute-start(bf16[768,1024]{1,0:T(8,128)(2,1)} %bitcast_bitcast_fusion), channel_id=1, source_target_pairs={{0,2},{1,3},{2,4},{3,5},{4,6},{5,7},{6,8},{7,9},{8,10},{9,11},{10,... | collective-permute-start | bytes 4718600 | tf_op jit(solution)/shard_map/ppermute | solution.py:18
  94.4 131.3 %collective-permute-start.1 = (bf16[768,1024]{1,0:T(8,128)(2,1)}, bf16[768,1024]{1,0:T(8,128)(2,1)}, u32[]{:S(2)}, u32[]{:S(2)}) collective-permute-start(bf16[768,1024]{1,0:T(8,128)(2,1)} %bitcast_bitcast_fusion), channel_id=1, source_target_pairs={{0,30},{1,31},{2,0},{3,1},{4,2},{5,3},{6,4},{7,5},{8,6},{9,7},{10,... | collective-permute-start | bytes 4718600 | tf_op jit(solution)/shard_map/ppermute | solution.py:18
  100.7 129.1 %collective-permute-start.8 = (bf16[1024,768]{1,0:T(8,128)(2,1)}, bf16[1024,768]{1,0:T(8,128)(2,1)}, u32[]{:S(2)}, u32[]{:S(2)}) collective-permute-start(bf16[1024,768]{1,0:T(8,128)(2,1)} %bitcast.8), channel_id=1, source_target_pairs={{0,1},{1,0},{2,3},{3,2},{4,5},{5,4},{6,7},{7,6},{8,9},{9,8},{10,11... | collective-permute-start | bytes 4718600 | tf_op jit(solution)/shard_map/ppermute | solution.py:18
  155.6 75.9 %collective-permute-start.2 = (bf16[768,1024]{1,0:T(8,128)(2,1)}, bf16[768,1024]{1,0:T(8,128)(2,1)}, u32[]{:S(2)}, u32[]{:S(2)}) collective-permute-start(bf16[768,1024]{1,0:T(8,128)(2,1)} %bitcast_bitcast_fusion), channel_id=1, source_target_pairs={{0,1},{1,0},{2,3},{3,2},{4,5},{5,4},{6,7},{7,6},{8,9},{9,8},{10,11... | collective-permute-start | bytes 4718600 | tf_op jit(solution)/shard_map/ppermute | solution.py:18
  157.1 7.4 %copy-start.6 = (s32[2,7]{1,0:T(2,128)S(1)}, s32[2,7]{1,0:T(2,128)}, u32[]{:S(2)}) copy-start(s32[2,7]{1,0:T(2,128)} %constant.89.clone) | copy-start | bytes 172
  160.1 4.2 %copy-start.1 = (bf16[7168,768]{1,0:T(8,128)(2,1)}, bf16[7168,768]{1,0:T(8,128)(2,1)S(1)}, u32[]{:S(2)}) copy-start(bf16[7168,768]{1,0:T(8,128)(2,1)S(1)} %get-tuple-element.6) | copy-start | bytes 33030148
  164.3 73.8 %collective-permute-start.9 = (bf16[1024,768]{1,0:T(8,128)(2,1)}, bf16[1024,768]{1,0:T(8,128)(2,1)}, u32[]{:S(2)}, u32[]{:S(2)}) collective-permute-start(bf16[1024,768]{1,0:T(8,128)(2,1)} %get-tuple-element.5), channel_id=1, source_target_pairs={{0,31},{1,2},{2,1},{3,4},{4,3},{5,6},{6,5},{7,8},{8,7},{9,10},{10,... | collective-permute-start | bytes 4718600 | tf_op jit(solution)/shard_map/ppermute | solution.py:18
  223.0 24.1 %collective-permute-start.10 = (bf16[1024,768]{1,0:T(8,128)(2,1)}, bf16[1024,768]{1,0:T(8,128)(2,1)S(1)}, u32[]{:S(2)}, u32[]{:S(2)}) collective-permute-start(bf16[1024,768]{1,0:T(8,128)(2,1)} %collective-permute-done.6), channel_id=1, source_target_pairs={{0,1},{1,0},{2,3},{3,2},{4,5},{5,4},{6,7},{7,6},{8,9},{9,8},{10,11... | collective-permute-start | bytes 4718600 | tf_op jit(solution)/shard_map/ppermute | solution.py:18
  229.7 42.2 %collective-permute-start.3 = (bf16[768,1024]{1,0:T(8,128)(2,1)}, bf16[768,1024]{1,0:T(8,128)(2,1)}, u32[]{:S(2)}, u32[]{:S(2)}) collective-permute-start(bf16[768,1024]{1,0:T(8,128)(2,1)} %get-tuple-element.7), channel_id=1, source_target_pairs={{0,31},{1,2},{2,1},{3,4},{4,3},{5,6},{6,5},{7,8},{8,7},{9,10},{10,... | collective-permute-start | bytes 4718600 | tf_op jit(solution)/shard_map/ppermute | solution.py:18
  229.8 18.6 %collective-permute-start.11 = (bf16[1024,768]{1,0:T(8,128)(2,1)}, bf16[1024,768]{1,0:T(8,128)(2,1)}, u32[]{:S(2)}, u32[]{:S(2)}) collective-permute-start(bf16[1024,768]{1,0:T(8,128)(2,1)} %collective-permute-done.7), channel_id=1, source_target_pairs={{0,1},{1,0},{2,3},{3,2},{4,5},{5,4},{6,7},{7,6},{8,9},{9,8},{10,11... | collective-permute-start | bytes 4718600 | tf_op jit(solution)/shard_map/ppermute | solution.py:18
  231.5 43.0 %collective-permute-start.4 = (bf16[768,1024]{1,0:T(8,128)(2,1)}, bf16[768,1024]{1,0:T(8,128)(2,1)}, u32[]{:S(2)}, u32[]{:S(2)}) collective-permute-start(bf16[768,1024]{1,0:T(8,128)(2,1)} %collective-permute-done), channel_id=1, source_target_pairs={{0,1},{1,0},{2,3},{3,2},{4,5},{5,4},{6,7},{7,6},{8,9},{9,8},{10,11... | collective-permute-start | bytes 4718600 | tf_op jit(solution)/shard_map/ppermute | solution.py:18
  238.2 39.1 %collective-permute-start.5 = (bf16[768,1024]{1,0:T(8,128)(2,1)}, bf16[768,1024]{1,0:T(8,128)(2,1)}, u32[]{:S(2)}, u32[]{:S(2)}) collective-permute-start(bf16[768,1024]{1,0:T(8,128)(2,1)} %collective-permute-done.1), channel_id=1, source_target_pairs={{0,1},{1,0},{2,3},{3,2},{4,5},{5,4},{6,7},{7,6},{8,9},{9,8},{10,11... | collective-permute-start | bytes 4718600 | tf_op jit(solution)/shard_map/ppermute | solution.py:18
  280.0 1.1 copy-start.2

commit v3 on v2

--- a/solution.py
+++ b/solution.py
@@ -50,10 +50,22 @@
         o_ref[:, cols] = (acc / total).astype(o_ref.dtype)
 
 
+def detour(local, n, distance):
+    group = 8
+    crossing = group - 1 if distance > 0 else 1
+    direct = [(i, (i + distance) % n) for i in range(n) if i % group != crossing]
+    moved = permute(local, "blk", direct)
+    step = group if distance > 0 else -group
+    hop1 = permute(local, "blk", [(i, (i + step) % n) for i in range(n) if i % group == crossing])
+    hop2 = permute(hop1, "blk", [(i, (i + distance - step) % n) for i in range(n) if i % group == crossing])
+    arrived = (lax.axis_index("blk") - distance) % group == crossing
+    return jnp.where(arrived, hop2, moved)
+
+
 def exchange(local, axis, n):
     swap = [(i, i ^ 1) for i in range(n)]
-    from_left2 = permute(local, "blk", shift_pairs(n, 2))
-    from_right2 = permute(local, "blk", shift_pairs(n, -2))
+    from_left2 = detour(local, n, 2)
+    from_right2 = detour(local, n, -2)
     other_core = permute(local, "blk", swap)
     core = lax.axis_index("blk") % 2
     forward = jnp.where(core == 1, from_left2, from_right2)

time: 331 us -> 344 us (1.039)
  starting transfers between devices: 26.3 us -> 80.4 us
  waiting for transfers between devices: 204 us -> 164 us
  local copies, waits for them, and re-layouts: 44.8 us -> 36.5 us
  blocking collectives: 18.8 us -> 25.6 us
    ppermute x12 -> x20, starting transfers between devices: 13.9 us -> 64.4 us  [permute(): return lax.ppermute(block, axis, route)]
    ppermute x12 -> x20, waiting for transfers between devices: 135 us -> 102 us  [permute(): return lax.ppermute(block, axis, route)]
    all_to_all x1, blocking collectives: 18.8 us -> 25.6 us  [body(): return lax.all_to_all(out, 'head', split_axis=0, concat_axis=1, tiled=True)]
    all_to_all x1, waiting for transfers between devices: 48.9 us -> 42.7 us  [body(): lax.all_to_all(key_states, 'head', split_axis=1, concat_axis=0, tiled=True)]
    unnamed x25 -> x35, local copies, waits for them, and re-layouts: 29 us -> 23.3 us
    all_to_all x1, starting transfers between devices: 3.58 us -> 7.33 us  [body(): lax.all_to_all(queries, 'head', split_axis=1, concat_axis=0, tiled=True)]
  transfers between devices with their start and end apart: 15 -> 23, of which waited for: 6 -> 6; matrix products, arithmetic and copies ran while one was open for 13% -> 11% of each run, Pallas kernels for 0% -> 0%
where the time goes in v3:
time: 344 us; the launch traced here: 338 us
  waiting for transfers between devices  164 us (48%)
  starting transfers between devices  80.4 us (23%)
  local copies, waits for them, and re-layouts  36.5 us (11%)
  blocking collectives  25.6 us (7%)
  Pallas kernels  23.9 us (7%)
  other arithmetic  6.84 us (2%)
    ppermute x20, waiting for transfers between devices, permute(): return lax.ppermute(block, axis, route)  102 us
    ppermute x20, starting transfers between devices, permute(): return lax.ppermute(block, axis, route)  64.4 us
    all_to_all x1, waiting for transfers between devices, body(): lax.all_to_all(key_states, 'head', split_axis=1, concat_axis=0, tiled=True)  42.7 us
    all_to_all x1, blocking collectives, body(): return lax.all_to_all(out, 'head', split_axis=0, concat_axis=1, tiled=True)  25.6 us
    pallas_call x1, Pallas kernels, body(): pl.pallas_call(kernel, grid_spec=grid_spec, out_shape=jax.ShapeDtypeStruc...  23.9 us
    unnamed x35, local copies, waits for them, and re-layouts  23.3 us
    all_to_all x1, waiting for transfers between devices, body(): lax.all_to_all(value_states, 'head', split_axis=1, concat_axis=0, tiled=T...  19.8 us
    all_to_all x1, starting transfers between devices, body(): lax.all_to_all(queries, 'head', split_axis=1, concat_axis=0, tiled=True)  7.33 us
  transfers between devices with their start and end apart: 23, of which 6 were waited for; matrix products, arithmetic and copies ran while one was open for 11% of the time, Pallas kernels for 0%

profile of v3, /device:TPU:128, one launch (start us, length us, event | category | flops | bytes accessed | tf_op | source)
XLA Modules:
  0.0 337.7 jit_solution(454619018791135853)
XLA Ops:
  0.0 2.7 copy.30
  2.7 5.1 %all-to-all-start.2 = ((bf16[128,8,768]{2,0,1:T(8,128)(2,1)}), bf16[128,8,768]{2,0,1:T(8,128)(2,1)S(1)}, u32[]{:S(2)}, u32[]{:S(2)}) async-start(bf16[128,8,768]{2,0,1:T(8,128)(2,1)} %bitcast.35), calls=%async_computation.2 | async-start | bytes 3145728 | tf_op jit(solution)/shard_map/all_to_all | solution.py:86
  9.3 19.8 %all-to-all-done.2 = bf16[128,8,768]{2,0,1:T(8,128)(2,1)S(1)} async-done(((bf16[128,8,768]{2,0,1:T(8,128)(2,1)}), bf16[128,8,768]{2,0,1:T(8,128)(2,1)S(1)}, u32[]{:S(2)}, u32[]{:S(2)}) %all-to-all-start.2) | async-done | bytes 1572896 | tf_op jit(solution)/shard_map/all_to_all | solution.py:86
  29.1 3.6 %all-to-all-start.1 = ((bf16[128,8,768]{0,2,1:T(8,128)(2,1)}), bf16[128,8,768]{0,2,1:T(8,128)(2,1)S(1)}, u32[]{:S(2)}, u32[]{:S(2)}) async-start(bf16[128,8,768]{0,2,1:T(8,128)(2,1)} %bitcast.46), calls=%async_computation.1 | async-start | bytes 3145728 | tf_op jit(solution)/shard_map/all_to_all | solution.py:84
  36.4 3.4 %collective-permute-start.12 = (bf16[1024,768]{1,0:T(8,128)(2,1)S(1)}, bf16[1024,768]{1,0:T(8,128)(2,1)}, u32[]{:S(2)}, u32[]{:S(2)}) collective-permute-start(bf16[1024,768]{1,0:T(8,128)(2,1)S(1)} %bitcast.41), channel_id=1, source_target_pairs={{0,2},{1,3},{2,4},{3,5},{4,6},{5,7},{6,8},{8,10},{9,11},{10,12},{1... | collective-permute-start | bytes 4718600 | tf_op jit(solution)/shard_map/ppermute | solution.py:18
  39.8 6.7 %collective-permute-start.15 = (bf16[1024,768]{1,0:T(8,128)(2,1)S(1)}, bf16[1024,768]{1,0:T(8,128)(2,1)}, u32[]{:S(2)}, u32[]{:S(2)}) collective-permute-start(bf16[1024,768]{1,0:T(8,128)(2,1)S(1)} %bitcast.42), channel_id=1, source_target_pairs={{0,30},{2,0},{3,1},{4,2},{5,3},{6,4},{7,5},{8,6},{10,8},{11,9},{12... | collective-permute-start | bytes 4718600 | tf_op jit(solution)/shard_map/ppermute | solution.py:18
  46.5 42.7 %all-to-all-done.1 = bf16[128,8,768]{0,2,1:T(8,128)(2,1)S(1)} async-done(((bf16[128,8,768]{0,2,1:T(8,128)(2,1)}), bf16[128,8,768]{0,2,1:T(8,128)(2,1)S(1)}, u32[]{:S(2)}, u32[]{:S(2)}) %all-to-all-start.1) | async-done | bytes 1572896 | tf_op jit(solution)/shard_map/all_to_all | solution.py:84
  94.2 1.9 collective-permute-start.2
  96.1 25.9 %collective-permute-done.12 = bf16[1024,768]{1,0:T(8,128)(2,1)} collective-permute-done((bf16[1024,768]{1,0:T(8,128)(2,1)S(1)}, bf16[1024,768]{1,0:T(8,128)(2,1)}, u32[]{:S(2)}, u32[]{:S(2)}) %collective-permute-start.12) | collective-permute-done | bytes 1572896 | tf_op jit(solution)/shard_map/ppermute | solution.py:18
  122.0 1.9 collective-permute-start.11
  125.7 1.9 collective-permute-start.5
  128.9 7.3 %all-to-all-start = ((bf16[128,8,768]{2,0,1:T(8,128)(2,1)}), bf16[128,8,768]{2,0,1:T(8,128)(2,1)S(1)}, u32[]{:S(2)}, u32[]{:S(2)}) async-start(bf16[128,8,768]{2,0,1:T(8,128)(2,1)} %bitcast.45), calls=%async_computation | async-start | bytes 3145728 | tf_op jit(solution)/shard_map/all_to_all | solution.py:88
  137.1 1.9 collective-permute-start.1
  139.0 48.3 %collective-permute-done.2 = bf16[768,1024]{1,0:T(8,128)(2,1)} collective-permute-done((bf16[768,1024]{1,0:T(8,128)(2,1)}, bf16[768,1024]{1,0:T(8,128)(2,1)}, u32[]{:S(2)}, u32[]{:S(2)}) %collective-permute-start.2) | collective-permute-done | bytes 1572896 | tf_op jit(solution)/shard_map/ppermute | solution.py:18
  189.3 13.2 %collective-permute-start.16 = (bf16[1024,768]{1,0:T(8,128)(2,1)}, bf16[1024,768]{1,0:T(8,128)(2,1)}, u32[]{:S(2)}, u32[]{:S(2)}) collective-permute-start(bf16[1024,768]{1,0:T(8,128)(2,1)} %bitcast.43), channel_id=1, source_target_pairs={{0,1},{1,0},{2,3},{3,2},{4,5},{5,4},{6,7},{7,6},{8,9},{9,8},{10,11... | collective-permute-start | bytes 4718600 | tf_op jit(solution)/shard_map/ppermute | solution.py:18
  202.6 4.4 %broadcast_select_fusion = (bf16[1024,768]{1,0:T(8,128)(2,1)}, bf16[1024,768]{1,0:T(8,128)(2,1)}, bf16[1024,768]{1,0:T(8,128)(2,1)}) fusion(pred[]{:T(512)S(6)} %eq.25, bf16[1024,768]{1,0:T(8,128)(2,1)} %collective-permute-done.14, bf16[1024,768]{1,0:T(8,128)(2,1)} %collective-permute-done.15, pred[]{:T(512)S(6)} %eq.24, ...), kind=kLoop, calls=%fused_computation.6 | loop fusion | flops 2359296 | bytes 11010051 | tf_op jit(solution)/shard_map/jit(_where)/select_n | solution.py:71
  210.0 21.9 %collective-permute-start.18 = (bf16[1024,768]{1,0:T(8,128)(2,1)}, bf16[1024,768]{1,0:T(8,128)(2,1)S(1)}, u32[]{:S(2)}, u32[]{:S(2)}) collective-permute-start(bf16[1024,768]{1,0:T(8,128)(2,1)} %get-tuple-element.7), channel_id=1, source_target_pairs={{0,1},{1,0},{2,3},{3,2},{4,5},{5,4},{6,7},{7,6},{8,9},{9,8},{10,11... | collective-permute-start | bytes 4718600 | tf_op jit(solution)/shard_map/ppermute | solution.py:18
  231.9 2.2 broadcast_select_fusion.3
  237.7 27.3 %collective-permute-done.17 = bf16[1024,768]{1,0:T(8,128)(2,1)} collective-permute-done((bf16[1024,768]{1,0:T(8,128)(2,1)}, bf16[1024,768]{1,0:T(8,128)(2,1)}, u32[]{:S(2)}, u32[]{:S(2)}) %collective-permute-start.17) | collective-permute-done | bytes 1572896 | tf_op jit(solution)/shard_map/ppermute | solution.py:18
  270.9 2.6 constant_dynamic-update-slice_fusion.10
  273.6 2.7 constant_dynamic-update-slice_fusion.3
  276.3 2.7 constant_dynamic-update-slice_fusion.9
  286.9 23.9 %shard_map.73 = bf16[1024,768]{1,0:T(8,128)(2,1)} custom-call(s32[64]{0:T(128)} %reshape.64.args_0_, s32[8]{0:T(128)} %args_1_.4, f32[384]{0:T(512)} %mul.43.args_2_, bf16[1024,768]{1,0:T(8,128)(2,1)} %bitcast.37, bf16[768,7168]{1,0:T(8,128)(2,1)} %constant_dynamic-update-slice_fusion.args_4_.args_5_.args_6_.args_7_.args_8_.args_9_.args_10_.args_11_, ...), custom_call_target="tpu_custom_call" | custom-call | tf_op jit(solution)/shard_map/pallas_call | solution.py:127
  310.9 25.6 %all_to_all.76 = bf16[8,128,768]{2,1,0:T(8,128)(2,1)S(1)} all-to-all(bf16[8,128,768]{2,1,0:T(8,128)(2,1)} %bitcast.38), channel_id=1, replica_groups=mesh['head'=8,'blk'=32] {'head'}, dimensions={0} | all-to-all | bytes 3145728 | tf_op jit(solution)/shard_map/all_to_all | solution.py:139
  (86 shorter events, 38.0 us)
Async XLA Ops:
  0.0 207.7 %copy-start = (s32[256]{0:T(256)S(1)}, s32[256]{0:T(256)}, u32[]{:S(2)}) copy-start(s32[256]{0:T(256)} %param.12) | copy-start | bytes 3076
  2.7 26.4 %all-to-all-start.2 = ((bf16[128,8,768]{2,0,1:T(8,128)(2,1)}), bf16[128,8,768]{2,0,1:T(8,128)(2,1)S(1)}, u32[]{:S(2)}, u32[]{:S(2)}) async-start(bf16[128,8,768]{2,0,1:T(8,128)(2,1)} %bitcast.35), calls=%async_computation.2 | async-start | bytes 3145728 | tf_op jit(solution)/shard_map/all_to_all | solution.py:86
  29.1 60.0 %all-to-all-start.1 = ((bf16[128,8,768]{0,2,1:T(8,128)(2,1)}), bf16[128,8,768]{0,2,1:T(8,128)(2,1)S(1)}, u32[]{:S(2)}, u32[]{:S(2)}) async-start(bf16[128,8,768]{0,2,1:T(8,128)(2,1)} %bitcast.46), calls=%async_computation.1 | async-start | bytes 3145728 | tf_op jit(solution)/shard_map/all_to_all | solution.py:84
  32.7 59.6 %collective-permute-start.10 = (bf16[1024,768]{1,0:T(8,128)(2,1)S(1)}, bf16[1024,768]{1,0:T(8,128)(2,1)}, u32[]{:S(2)}, u32[]{:S(2)}) collective-permute-start(bf16[1024,768]{1,0:T(8,128)(2,1)S(1)} %bitcast.39), channel_id=1, source_target_pairs={{7,15},{15,23},{23,31},{31,7},{39,47},{47,55},{55,63},{63,39},{71,... | collective-permute-start | bytes 4718600 | tf_op jit(solution)/shard_map/ppermute | solution.py:18
  34.6 59.6 %collective-permute-start.13 = (bf16[1024,768]{1,0:T(8,128)(2,1)S(1)}, bf16[1024,768]{1,0:T(8,128)(2,1)}, u32[]{:S(2)}, u32[]{:S(2)}) collective-permute-start(bf16[1024,768]{1,0:T(8,128)(2,1)S(1)} %bitcast.40), channel_id=1, source_target_pairs={{1,25},{9,1},{17,9},{25,17},{33,57},{41,33},{49,41},{57,49},{65,89... | collective-permute-start | bytes 4718600 | tf_op jit(solution)/shard_map/ppermute | solution.py:18
  36.4 85.6 %collective-permute-start.12 = (bf16[1024,768]{1,0:T(8,128)(2,1)S(1)}, bf16[1024,768]{1,0:T(8,128)(2,1)}, u32[]{:S(2)}, u32[]{:S(2)}) collective-permute-start(bf16[1024,768]{1,0:T(8,128)(2,1)S(1)} %bitcast.41), channel_id=1, source_target_pairs={{0,2},{1,3},{2,4},{3,5},{4,6},{5,7},{6,8},{8,10},{9,11},{10,12},{1... | collective-permute-start | bytes 4718600 | tf_op jit(solution)/shard_map/ppermute | solution.py:18
  39.8 84.1 %collective-permute-start.15 = (bf16[1024,768]{1,0:T(8,128)(2,1)S(1)}, bf16[1024,768]{1,0:T(8,128)(2,1)}, u32[]{:S(2)}, u32[]{:S(2)}) collective-permute-start(bf16[1024,768]{1,0:T(8,128)(2,1)S(1)} %bitcast.42), channel_id=1, source_target_pairs={{0,30},{2,0},{3,1},{4,2},{5,3},{6,4},{7,5},{8,6},{10,8},{11,9},{12... | collective-permute-start | bytes 4718600 | tf_op jit(solution)/shard_map/ppermute | solution.py:18
  90.5 35.1 %collective-permute-start = (bf16[768,1024]{1,0:T(8,128)(2,1)}, bf16[768,1024]{1,0:T(8,128)(2,1)}, u32[]{:S(2)}, u32[]{:S(2)}) collective-permute-start(bf16[768,1024]{1,0:T(8,128)(2,1)} %bitcast_bitcast_fusion), channel_id=1, source_target_pairs={{7,15},{15,23},{23,31},{31,7},{39,47},{47,55},{55,63},{63,39},{71,... | collective-permute-start | bytes 4718600 | tf_op jit(solution)/shard_map/ppermute | solution.py:18
  92.3 44.8 %collective-permute-start.3 = (bf16[768,1024]{1,0:T(8,128)(2,1)}, bf16[768,1024]{1,0:T(8,128)(2,1)}, u32[]{:S(2)}, u32[]{:S(2)}) collective-permute-start(bf16[768,1024]{1,0:T(8,128)(2,1)} %bitcast_bitcast_fusion), channel_id=1, source_target_pairs={{1,25},{9,1},{17,9},{25,17},{33,57},{41,33},{49,41},{57,49},{65,89... | collective-permute-start | bytes 4718600 | tf_op jit(solution)/shard_map/ppermute | solution.py:18
  94.2 93.1 %collective-permute-start.2 = (bf16[768,1024]{1,0:T(8,128)(2,1)}, bf16[768,1024]{1,0:T(8,128)(2,1)}, u32[]{:S(2)}, u32[]{:S(2)}) collective-permute-start(bf16[768,1024]{1,0:T(8,128)(2,1)} %bitcast_bitcast_fusion), channel_id=1, source_target_pairs={{0,2},{1,3},{2,4},{3,5},{4,6},{5,7},{6,8},{8,10},{9,11},{10,12},{1... | collective-permute-start | bytes 4718600 | tf_op jit(solution)/shard_map/ppermute | solution.py:18
  122.0 67.3 %collective-permute-start.11 = (bf16[1024,768]{1,0:T(8,128)(2,1)}, bf16[1024,768]{1,0:T(8,128)(2,1)}, u32[]{:S(2)}, u32[]{:S(2)}) collective-permute-start(bf16[1024,768]{1,0:T(8,128)(2,1)} %collective-permute-done.10), channel_id=1, source_target_pairs={{7,1},{15,9},{23,17},{31,25},{39,33},{47,41},{55,49},{63,57},{71,6... | collective-permute-start | bytes 4718600 | tf_op jit(solution)/shard_map/ppermute | solution.py:18
  123.9 78.6 %collective-permute-start.14 = (bf16[1024,768]{1,0:T(8,128)(2,1)}, bf16[1024,768]{1,0:T(8,128)(2,1)}, u32[]{:S(2)}, u32[]{:S(2)}) collective-permute-start(bf16[1024,768]{1,0:T(8,128)(2,1)} %collective-permute-done.13), channel_id=1, source_target_pairs={{1,7},{9,15},{17,23},{25,31},{33,39},{41,47},{49,55},{57,63},{65,7... | collective-permute-start | bytes 4718600 | tf_op jit(solution)/shard_map/ppermute | solution.py:18
  125.7 81.3 %collective-permute-start.5 = (bf16[768,1024]{1,0:T(8,128)(2,1)}, bf16[768,1024]{1,0:T(8,128)(2,1)}, u32[]{:S(2)}, u32[]{:S(2)}) collective-permute-start(bf16[768,1024]{1,0:T(8,128)(2,1)} %bitcast_bitcast_fusion), channel_id=1, source_target_pairs={{0,30},{2,0},{3,1},{4,2},{5,3},{6,4},{7,5},{8,6},{10,8},{11,9},{12... | collective-permute-start | bytes 4718600 | tf_op jit(solution)/shard_map/ppermute | solution.py:18
  128.9 156.9 %all-to-all-start = ((bf16[128,8,768]{2,0,1:T(8,128)(2,1)}), bf16[128,8,768]{2,0,1:T(8,128)(2,1)S(1)}, u32[]{:S(2)}, u32[]{:S(2)}) async-start(bf16[128,8,768]{2,0,1:T(8,128)(2,1)} %bitcast.45), calls=%async_computation | async-start | bytes 3145728 | tf_op jit(solution)/shard_map/all_to_all | solution.py:88
  137.1 72.9 %collective-permute-start.1 = (bf16[768,1024]{1,0:T(8,128)(2,1)}, bf16[768,1024]{1,0:T(8,128)(2,1)}, u32[]{:S(2)}, u32[]{:S(2)}) collective-permute-start(bf16[768,1024]{1,0:T(8,128)(2,1)} %collective-permute-done), channel_id=1, source_target_pairs={{7,1},{15,9},{23,17},{31,25},{39,33},{47,41},{55,49},{63,57},{71,6... | collective-permute-start | bytes 4718600 | tf_op jit(solution)/shard_map/ppermute | solution.py:18
  187.3 44.6 %collective-permute-start.4 = (bf16[768,1024]{1,0:T(8,128)(2,1)}, bf16[768,1024]{1,0:T(8,128)(2,1)}, u32[]{:S(2)}, u32[]{:S(2)}) collective-permute-start(bf16[768,1024]{1,0:T(8,128)(2,1)} %collective-permute-done.3), channel_id=1, source_target_pairs={{1,7},{9,15},{17,23},{25,31},{33,39},{41,47},{49,55},{57,63},{65,7... | collective-permute-start | bytes 4718600 | tf_op jit(solution)/shard_map/ppermute | solution.py:18
  189.3 44.9 %collective-permute-start.16 = (bf16[1024,768]{1,0:T(8,128)(2,1)}, bf16[1024,768]{1,0:T(8,128)(2,1)}, u32[]{:S(2)}, u32[]{:S(2)}) collective-permute-start(bf16[1024,768]{1,0:T(8,128)(2,1)} %bitcast.43), channel_id=1, source_target_pairs={{0,1},{1,0},{2,3},{3,2},{4,5},{5,4},{6,7},{7,6},{8,9},{9,8},{10,11... | collective-permute-start | bytes 4718600 | tf_op jit(solution)/shard_map/ppermute | solution.py:18
  202.5 33.9 %collective-permute-start.6 = (bf16[768,1024]{1,0:T(8,128)(2,1)}, bf16[768,1024]{1,0:T(8,128)(2,1)}, u32[]{:S(2)}, u32[]{:S(2)}) collective-permute-start(bf16[768,1024]{1,0:T(8,128)(2,1)} %bitcast_bitcast_fusion), channel_id=1, source_target_pairs={{0,1},{1,0},{2,3},{3,2},{4,5},{5,4},{6,7},{7,6},{8,9},{9,8},{10,11... | collective-permute-start | bytes 4718600 | tf_op jit(solution)/shard_map/ppermute | solution.py:18
  207.0 58.1 %collective-permute-start.17 = (bf16[1024,768]{1,0:T(8,128)(2,1)}, bf16[1024,768]{1,0:T(8,128)(2,1)}, u32[]{:S(2)}, u32[]{:S(2)}) collective-permute-start(bf16[1024,768]{1,0:T(8,128)(2,1)} %get-tuple-element.5), channel_id=1, source_target_pairs={{0,31},{1,2},{2,1},{3,4},{4,3},{5,6},{6,5},{7,8},{8,7},{9,10},{10,... | collective-permute-start | bytes 4718600 | tf_op jit(solution)/shard_map/ppermute | solution.py:18
  210.0 69.0 %collective-permute-start.18 = (bf16[1024,768]{1,0:T(8,128)(2,1)}, bf16[1024,768]{1,0:T(8,128)(2,1)S(1)}, u32[]{:S(2)}, u32[]{:S(2)}) collective-permute-start(bf16[1024,768]{1,0:T(8,128)(2,1)} %get-tuple-element.7), channel_id=1, source_target_pairs={{0,1},{1,0},{2,3},{3,2},{4,5},{5,4},{6,7},{7,6},{8,9},{9,8},{10,11... | collective-permute-start | bytes 4718600 | tf_op jit(solution)/shard_map/ppermute | solution.py:18
  231.9 48.4 %collective-permute-start.19 = (bf16[1024,768]{1,0:T(8,128)(2,1)}, bf16[1024,768]{1,0:T(8,128)(2,1)S(1)}, u32[]{:S(2)}, u32[]{:S(2)}) collective-permute-start(bf16[1024,768]{1,0:T(8,128)(2,1)} %get-tuple-element.6), channel_id=1, source_target_pairs={{0,1},{1,0},{2,3},{3,2},{4,5},{5,4},{6,7},{7,6},{8,9},{9,8},{10,11... | collective-permute-start | bytes 4718600 | tf_op jit(solution)/shard_map/ppermute | solution.py:18
  234.2 47.6 %collective-permute-start.7 = (bf16[768,1024]{1,0:T(8,128)(2,1)S(1)}, bf16[768,1024]{1,0:T(8,128)(2,1)S(1)}, u32[]{:S(2)}, u32[]{:S(2)}) collective-permute-start(bf16[768,1024]{1,0:T(8,128)(2,1)S(1)} %get-tuple-element.8), channel_id=1, source_target_pairs={{0,31},{1,2},{2,1},{3,4},{4,3},{5,6},{6,5},{7,8},{8,7},{9,10},{10,... | collective-permute-start | bytes 4718600 | tf_op jit(solution)/shard_map/ppermute | solution.py:18
  236.4 46.7 %collective-permute-start.8 = (bf16[768,1024]{1,0:T(8,128)(2,1)S(1)}, bf16[768,1024]{1,0:T(8,128)(2,1)S(1)}, u32[]{:S(2)}, u32[]{:S(2)}) collective-permute-start(bf16[768,1024]{1,0:T(8,128)(2,1)S(1)} %get-tuple-element.10), channel_id=1, source_target_pairs={{0,1},{1,0},{2,3},{3,2},{4,5},{5,4},{6,7},{7,6},{8,9},{9,8},{10,11... | collective-permute-start | bytes 4718600 | tf_op jit(solution)/shard_map/ppermute | solution.py:18
  265.1 19.4 %collective-permute-start.9 = (bf16[768,1024]{1,0:T(8,128)(2,1)S(1)}, bf16[768,1024]{1,0:T(8,128)(2,1)S(1)}, u32[]{:S(2)}, u32[]{:S(2)}) collective-permute-start(bf16[768,1024]{1,0:T(8,128)(2,1)S(1)} %get-tuple-element.9), channel_id=1, source_target_pairs={{0,1},{1,0},{2,3},{3,2},{4,5},{5,4},{6,7},{7,6},{8,9},{9,8},{10,11... | collective-permute-start | bytes 4718600 | tf_op jit(solution)/shard_map/ppermute | solution.py:18
  (10 other events, 104.3 us)

commit v4 on v2

--- a/solution.py
+++ b/solution.py
@@ -10,6 +10,7 @@
 TILE = 128
 REACH = 3
 SLOTS = 8
+TILE_COUNT = 8
 
 PIECE_OF_OFFSET = ((4, 1, 5, 0, 3, 2, 6), (5, 1, 3, 0, 6, 2, 4))
 
@@ -22,18 +23,49 @@
     return [(i, (i + distance) % n) for i in range(n)]
 
 
-def attention_kernel(sw_ref, cnt_ref, bias_ref, q_ref, *refs, heads_local, scale):
-    k_refs = refs[:SLOTS]
-    v_refs = refs[SLOTS:2 * SLOTS]
-    o_ref = refs[2 * SLOTS]
+def attention_kernel(sw_ref, cnt_ref, bias_ref, q_ref, *refs, heads_local, scale, pieces):
+    k_hbm = refs[:pieces]
+    v_hbm = refs[pieces:2 * pieces]
+    o_ref, k_buf, v_buf, sem = refs[2 * pieces:]
     i = pl.program_id(0)
+    steps = pl.num_programs(0)
+    parity = i % 2
+
+    def copies(step, slot, c, p, j):
+        k_copy = pltpu.make_async_copy(k_hbm[p].at[:, pl.ds(j * TILE, TILE)], k_buf.at[slot, c], sem.at[0, slot, c])
+        v_copy = pltpu.make_async_copy(v_hbm[p].at[pl.ds(j * TILE, TILE), :], v_buf.at[slot, c], sem.at[1, slot, c])
+        return k_copy, v_copy
+
+    def start(step, slot):
+        for c in range(SLOTS):
+            code = sw_ref[step * SLOTS + c]
+            p_code = code // TILE_COUNT
+            j = code % TILE_COUNT
+            for p in range(pieces):
+                @pl.when(p_code == p)
+                def _():
+                    for copy in copies(step, slot, c, p, j):
+                        copy.start()
+
+    @pl.when(i == 0)
+    def _():
+        start(0, 0)
+
+    @pl.when(i + 1 < steps)
+    def _():
+        start(i + 1, 1 - parity)
+
+    for c in range(SLOTS):
+        for copy in copies(i, parity, c, 0, 0):
+            copy.wait()
+
     count = cnt_ref[i]
     for h in range(heads_local):
         cols = slice(h * DH, (h + 1) * DH)
         q = q_ref[:, cols]
         scores = []
         for c in range(SLOTS):
-            s = jnp.dot(q, k_refs[c][cols, :], preferred_element_type=jnp.float32)
+            s = jnp.dot(q, k_buf[parity, c, cols, :], preferred_element_type=jnp.float32)
             s = s * scale
             s = s - bias_ref[(i * SLOTS + c) * heads_local + h]
             s = jnp.where(c < count, s, -1e30)
@@ -46,7 +78,7 @@
         for c in range(SLOTS):
             w = jnp.exp(scores[c] - top).astype(jnp.bfloat16)
             total = total + w.astype(jnp.float32).sum(axis=1, keepdims=True)
-            acc = acc + jnp.dot(w, v_refs[c][:, cols], preferred_element_type=jnp.float32)
+            acc = acc + jnp.dot(w, v_buf[parity, c, :, cols], preferred_element_type=jnp.float32)
         o_ref[:, cols] = (acc / total).astype(o_ref.dtype)
 
 
@@ -61,8 +93,7 @@
     across = permute(forward, "blk", cross_route)
     other_left2 = permute(from_left2, "blk", swap)
     other_right2 = permute(from_right2, "blk", swap)
-    pieces = [local, from_left2, from_right2, other_core, across, other_left2, other_right2]
-    return jnp.concatenate(pieces, axis=axis)
+    return [local, from_left2, from_right2, other_core, across, other_left2, other_right2]
 
 
 def body(queries, key_states, value_states, block_lists, block_counts, tile_order):
@@ -94,35 +125,37 @@
     bias = (slopes[None, None, :] * distance[:, :, None]).reshape(-1)
     scale = DH ** (-0.5)
 
-    k_specs = [
-        pl.BlockSpec((width, TILE), lambda i, sw, cnt, c=c: (0, sw[i * SLOTS + c])) for c in range(SLOTS)
-    ]
-    v_specs = [
-        pl.BlockSpec((TILE, width), lambda i, sw, cnt, c=c: (sw[i * SLOTS + c], 0)) for c in range(SLOTS)
-    ]
+    assert tile_count == TILE_COUNT
+    pieces = len(k_window)
+    any_spec = pl.BlockSpec(memory_space=pl.ANY)
     in_specs = (
         [pl.BlockSpec(memory_space=pltpu.SMEM), pl.BlockSpec((TILE, width), lambda i, sw, cnt: (i, 0))]
-        + k_specs
-        + v_specs
+        + [any_spec] * (2 * pieces)
     )
     grid_spec = pltpu.PrefetchScalarGridSpec(
         num_scalar_prefetch=2,
         grid=(tile_count,),
         in_specs=in_specs,
         out_specs=pl.BlockSpec((TILE, width), lambda i, sw, cnt: (i, 0)),
+        scratch_shapes=[
+            pltpu.VMEM((2, SLOTS, width, TILE), jnp.bfloat16),
+            pltpu.VMEM((2, SLOTS, TILE, width), jnp.bfloat16),
+            pltpu.SemaphoreType.DMA((2, 2, SLOTS)),
+        ],
     )
-    kernel = lambda *args: attention_kernel(*args, heads_local=heads_local, scale=scale)
+    kernel = lambda *args: attention_kernel(*args, heads_local=heads_local, scale=scale, pieces=pieces)
     out = pl.pallas_call(
         kernel,
         grid_spec=grid_spec,
         out_shape=jax.ShapeDtypeStruct((shard_tok, width), jnp.bfloat16),
+        compiler_params=pltpu.CompilerParams(dimension_semantics=("arbitrary",)),
     )(
         slot_window.reshape(-1),
         block_counts.astype(jnp.int32),
         bias,
         q_heads,
-        *([k_window] * SLOTS),
-        *([v_window] * SLOTS),
+        *k_window,
+        *v_window,
     )
     return lax.all_to_all(out, "head", split_axis=0, concat_axis=1, tiled=True)
 

time: 331 us -> 323 us (0.976)
  local copies, waits for them, and re-layouts: 44.8 us -> 14.9 us
  waiting for transfers between devices: 204 us -> 228 us
    all_to_all x1, waiting for transfers between devices: 0.01 us -> 41.5 us  [body(): lax.all_to_all(queries, 'head', split_axis=1, concat_axis=0, tiled=True)]
    unnamed x25 -> x17, local copies, waits for them, and re-layouts: 29 us -> 2.74 us
    ppermute x12, waiting for transfers between devices: 135 us -> 113 us  [permute(): return lax.ppermute(block, axis, route)]
    concatenate x2 -> x0, local copies, waits for them, and re-layouts: 5.36 us -> none  [exchange(): return jnp.concatenate(pieces, axis=axis)]
    all_to_all x1, waiting for transfers between devices: 48.9 us -> 53.7 us  [body(): lax.all_to_all(key_states, 'head', split_axis=1, concat_axis=0, tiled=True)]
  transfers between devices with their start and end apart: 15 -> 15, of which waited for: 6 -> 7; matrix products, arithmetic and copies ran while one was open for 13% -> 4% of each run, Pallas kernels for 0% -> 0%
where the time goes in v4:
time: 323 us; the launch traced here: 318 us
  waiting for transfers between devices  228 us (71%)
  starting transfers between devices  26.6 us (8%)
  Pallas kernels  24.5 us (8%)
  blocking collectives  18.8 us (6%)
  local copies, waits for them, and re-layouts  14.9 us (5%)
  other arithmetic  4.36 us (1%)
    ppermute x12, waiting for transfers between devices, permute(): return lax.ppermute(block, axis, route)  113 us
    all_to_all x1, waiting for transfers between devices, body(): lax.all_to_all(key_states, 'head', split_axis=1, concat_axis=0, tiled=True)  53.7 us
    all_to_all x1, waiting for transfers between devices, body(): lax.all_to_all(queries, 'head', split_axis=1, concat_axis=0, tiled=True)  41.5 us
    pallas_call x1, Pallas kernels, body(): pl.pallas_call(kernel, grid_spec=grid_spec, out_shape=jax.ShapeDtypeStruc...  24.5 us
    all_to_all x1, waiting for transfers between devices, body(): lax.all_to_all(value_states, 'head', split_axis=1, concat_axis=0, tiled=T...  19.9 us
    all_to_all x1, blocking collectives, body(): return lax.all_to_all(out, 'head', split_axis=0, concat_axis=1, tiled=True)  18.8 us
    ppermute x12, starting transfers between devices, permute(): return lax.ppermute(block, axis, route)  12.5 us
  transfers between devices with their start and end apart: 15, of which 7 were waited for; matrix products, arithmetic and copies ran while one was open for 4% of the time, Pallas kernels for 0%

profile of v4, /device:TPU:128, one launch (start us, length us, event | category | flops | bytes accessed | tf_op | source)
XLA Modules:
  0.0 317.7 jit_solution(8046042662711833141)
XLA Ops:
  0.0 2.7 copy.28
  2.7 5.1 %all-to-all-start.2 = ((bf16[128,8,768]{2,0,1:T(8,128)(2,1)}), bf16[128,8,768]{2,0,1:T(8,128)(2,1)}, u32[]{:S(2)}, u32[]{:S(2)}) async-start(bf16[128,8,768]{2,0,1:T(8,128)(2,1)} %bitcast.29), calls=%async_computation.2 | async-start | bytes 3145728 | tf_op jit(solution)/shard_map/all_to_all | solution.py:105
  7.7 1.6 copy.17
  9.3 19.9 %all-to-all-done.2 = bf16[128,8,768]{2,0,1:T(8,128)(2,1)} async-done(((bf16[128,8,768]{2,0,1:T(8,128)(2,1)}), bf16[128,8,768]{2,0,1:T(8,128)(2,1)}, u32[]{:S(2)}, u32[]{:S(2)}) %all-to-all-start.2) | async-done | bytes 1572896 | tf_op jit(solution)/shard_map/all_to_all | solution.py:105
  29.2 4.3 %all-to-all-start.1 = ((bf16[128,8,768]{0,2,1:T(8,128)(2,1)}), bf16[128,8,768]{0,2,1:T(8,128)(2,1)}, u32[]{:S(2)}, u32[]{:S(2)}) async-start(bf16[128,8,768]{0,2,1:T(8,128)(2,1)} %bitcast.4), calls=%async_computation.1 | async-start | bytes 3145728 | tf_op jit(solution)/shard_map/all_to_all | solution.py:103
  33.5 2.8 collective-permute-start.7
  36.3 53.7 %all-to-all-done.1 = bf16[128,8,768]{0,2,1:T(8,128)(2,1)} async-done(((bf16[128,8,768]{0,2,1:T(8,128)(2,1)}), bf16[128,8,768]{0,2,1:T(8,128)(2,1)}, u32[]{:S(2)}, u32[]{:S(2)}) %all-to-all-start.1) | async-done | bytes 1572896 | tf_op jit(solution)/shard_map/all_to_all | solution.py:103
  90.0 2.9 bitcast_bitcast_fusion.args_4_
  92.9 2.0 collective-permute-start
  95.4 27.0 %collective-permute-done.6.args_12_ = bf16[1024,768]{1,0:T(8,128)(2,1)S(1)} collective-permute-done((bf16[1024,768]{1,0:T(8,128)(2,1)}, bf16[1024,768]{1,0:T(8,128)(2,1)S(1)}, u32[]{:S(2)}, u32[]{:S(2)}) %collective-permute-start.6) | collective-permute-done | bytes 1572896 | tf_op jit(solution)/shard_map/ppermute | solution.py:19
  122.4 1.4 copy.29
  123.8 4.8 %all-to-all-start = ((bf16[128,8,768]{2,0,1:T(8,128)(2,1)}), bf16[128,8,768]{2,0,1:T(8,128)(2,1)}, u32[]{:S(2)}, u32[]{:S(2)}) async-start(bf16[128,8,768]{2,0,1:T(8,128)(2,1)} %bitcast.31), calls=%async_computation | async-start | bytes 3145728 | tf_op jit(solution)/shard_map/all_to_all | solution.py:107
  128.6 1.3 broadcast_select_fusion
  129.9 53.8 %collective-permute-done.1.args_6_ = bf16[768,1024]{1,0:T(8,128)(2,1)} collective-permute-done((bf16[768,1024]{1,0:T(8,128)(2,1)}, bf16[768,1024]{1,0:T(8,128)(2,1)}, u32[]{:S(2)}, u32[]{:S(2)}) %collective-permute-start.1) | collective-permute-done | bytes 1572896 | tf_op jit(solution)/shard_map/ppermute | solution.py:19
  183.7 6.3 %collective-permute-start.9 = (bf16[1024,768]{1,0:T(8,128)(2,1)}, bf16[1024,768]{1,0:T(8,128)(2,1)}, u32[]{:S(2)}, u32[]{:S(2)}) collective-permute-start(bf16[1024,768]{1,0:T(8,128)(2,1)} %broadcast_select_fusion), channel_id=1, source_target_pairs={{0,31},{1,2},{2,1},{3,4},{4,3},{5,6},{6,5},{7,8},{8,7},{9,10},{10,... | collective-permute-start | bytes 4718600 | tf_op jit(solution)/shard_map/ppermute | solution.py:19
  190.0 2.8 broadcast_select_fusion.1
  196.1 0.8 gather_fusion.2
  197.9 41.5 %all-to-all-done = bf16[128,8,768]{2,0,1:T(8,128)(2,1)} async-done(((bf16[128,8,768]{2,0,1:T(8,128)(2,1)}), bf16[128,8,768]{2,0,1:T(8,128)(2,1)}, u32[]{:S(2)}, u32[]{:S(2)}) %all-to-all-start) | async-done | bytes 1572896 | tf_op jit(solution)/shard_map/all_to_all | solution.py:107
  239.3 15.8 %collective-permute-done.9.args_15_ = bf16[1024,768]{1,0:T(8,128)(2,1)} collective-permute-done((bf16[1024,768]{1,0:T(8,128)(2,1)}, bf16[1024,768]{1,0:T(8,128)(2,1)}, u32[]{:S(2)}, u32[]{:S(2)}) %collective-permute-start.9) | collective-permute-done | bytes 1572896 | tf_op jit(solution)/shard_map/ppermute | solution.py:19
  255.1 16.8 %collective-permute-done.3.args_8_ = bf16[768,1024]{1,0:T(8,128)(2,1)} collective-permute-done((bf16[768,1024]{1,0:T(8,128)(2,1)}, bf16[768,1024]{1,0:T(8,128)(2,1)}, u32[]{:S(2)}, u32[]{:S(2)}) %collective-permute-start.3) | collective-permute-done | bytes 1572896 | tf_op jit(solution)/shard_map/ppermute | solution.py:19
  272.0 1.1 copy-done.3
  273.1 24.5 %shard_map.73 = bf16[1024,768]{1,0:T(8,128)(2,1)} custom-call(s32[64]{0:T(128)} %reshape.64.args_0_, s32[8]{0:T(128)} %args_1_.4, f32[384]{0:T(512)} %mul.43.args_2_, bf16[1024,768]{1,0:T(8,128)(2,1)} %bitcast.3.args_3_, bf16[768,1024]{1,0:T(8,128)(2,1)} %bitcast_bitcast_fusion.args_4_, bf16[768,1024]{1,0:T(8,128)(2,1)} %collective-permute-done.args_5_, ...), custom_call_target="tpu_custom_call" | custom-call | tf_op jit(solution)/shard_map/pallas_call | solution.py:147
  297.6 18.8 %all_to_all.76 = bf16[8,128,768]{2,1,0:T(8,128)(2,1)S(1)} all-to-all(bf16[8,128,768]{2,1,0:T(8,128)(2,1)} %bitcast.32), channel_id=1, replica_groups=mesh['head'=8,'blk'=32] {'head'}, dimensions={0} | all-to-all | bytes 3145728 | tf_op jit(solution)/shard_map/all_to_all | solution.py:160
  316.4 1.3 copy.24
  (51 shorter events, 4.8 us)
Async XLA Ops:
  0.0 195.4 %copy-start = (s32[256]{0:T(256)S(1)}, s32[256]{0:T(256)}, u32[]{:S(2)}) copy-start(s32[256]{0:T(256)} %param.12) | copy-start | bytes 3076
  2.7 5.1 %copy-start.4 = (bf16[128,6144]{1,0:T(8,128)(2,1)S(1)}, bf16[128,6144]{1,0:T(8,128)(2,1)}, u32[]{:S(2)}) copy-start(bf16[128,6144]{1,0:T(8,128)(2,1)} %param.8) | copy-start | bytes 4718596
  2.7 26.5 %all-to-all-start.2 = ((bf16[128,8,768]{2,0,1:T(8,128)(2,1)}), bf16[128,8,768]{2,0,1:T(8,128)(2,1)}, u32[]{:S(2)}, u32[]{:S(2)}) async-start(bf16[128,8,768]{2,0,1:T(8,128)(2,1)} %bitcast.29), calls=%async_computation.2 | async-start | bytes 3145728 | tf_op jit(solution)/shard_map/all_to_all | solution.py:105
  29.2 60.8 %all-to-all-start.1 = ((bf16[128,8,768]{0,2,1:T(8,128)(2,1)}), bf16[128,8,768]{0,2,1:T(8,128)(2,1)}, u32[]{:S(2)}, u32[]{:S(2)}) async-start(bf16[128,8,768]{0,2,1:T(8,128)(2,1)} %bitcast.4), calls=%async_computation.1 | async-start | bytes 3145728 | tf_op jit(solution)/shard_map/all_to_all | solution.py:103
  33.5 61.5 %collective-permute-start.7 = (bf16[1024,768]{1,0:T(8,128)(2,1)}, bf16[1024,768]{1,0:T(8,128)(2,1)S(1)}, u32[]{:S(2)}, u32[]{:S(2)}) collective-permute-start(bf16[1024,768]{1,0:T(8,128)(2,1)} %bitcast.8.args_11_), channel_id=1, source_target_pairs={{0,30},{1,31},{2,0},{3,1},{4,2},{5,3},{6,4},{7,5},{8,6},{9,7},{10,... | collective-permute-start | bytes 4718600 | tf_op jit(solution)/shard_map/ppermute | solution.py:19
  36.3 86.1 %collective-permute-start.6 = (bf16[1024,768]{1,0:T(8,128)(2,1)}, bf16[1024,768]{1,0:T(8,128)(2,1)S(1)}, u32[]{:S(2)}, u32[]{:S(2)}) collective-permute-start(bf16[1024,768]{1,0:T(8,128)(2,1)} %bitcast.8.args_11_), channel_id=1, source_target_pairs={{0,2},{1,3},{2,4},{3,5},{4,6},{5,7},{6,8},{7,9},{8,10},{9,11},{10,... | collective-permute-start | bytes 4718600 | tf_op jit(solution)/shard_map/ppermute | solution.py:19
  90.0 32.4 %copy-start.5 = (bf16[128,6144]{1,0:T(8,128)(2,1)S(1)}, bf16[128,6144]{1,0:T(8,128)(2,1)}, u32[]{:S(2)}) copy-start(bf16[128,6144]{1,0:T(8,128)(2,1)} %param.7) | copy-start | bytes 4718596
  92.9 90.8 %collective-permute-start.1 = (bf16[768,1024]{1,0:T(8,128)(2,1)}, bf16[768,1024]{1,0:T(8,128)(2,1)}, u32[]{:S(2)}, u32[]{:S(2)}) collective-permute-start(bf16[768,1024]{1,0:T(8,128)(2,1)} %bitcast_bitcast_fusion.args_4_), channel_id=1, source_target_pairs={{0,30},{1,31},{2,0},{3,1},{4,2},{5,3},{6,4},{7,5},{8,6},{9,7},{10,... | collective-permute-start | bytes 4718600 | tf_op jit(solution)/shard_map/ppermute | solution.py:19
  92.9 97.1 %collective-permute-start = (bf16[768,1024]{1,0:T(8,128)(2,1)}, bf16[768,1024]{1,0:T(8,128)(2,1)}, u32[]{:S(2)}, u32[]{:S(2)}) collective-permute-start(bf16[768,1024]{1,0:T(8,128)(2,1)} %bitcast_bitcast_fusion.args_4_), channel_id=1, source_target_pairs={{0,2},{1,3},{2,4},{3,5},{4,6},{5,7},{6,8},{7,9},{8,10},{9,11},{10,... | collective-permute-start | bytes 4718600 | tf_op jit(solution)/shard_map/ppermute | solution.py:19
  94.9 97.9 %collective-permute-start.8 = (bf16[1024,768]{1,0:T(8,128)(2,1)}, bf16[1024,768]{1,0:T(8,128)(2,1)}, u32[]{:S(2)}, u32[]{:S(2)}) collective-permute-start(bf16[1024,768]{1,0:T(8,128)(2,1)} %bitcast.8.args_11_), channel_id=1, source_target_pairs={{0,1},{1,0},{2,3},{3,2},{4,5},{5,4},{6,7},{7,6},{8,9},{9,8},{10,11... | collective-permute-start | bytes 4718600 | tf_op jit(solution)/shard_map/ppermute | solution.py:19
  94.9 33.7 %copy-start.1 = (bf16[1024,768]{1,0:T(8,128)(2,1)}, bf16[1024,768]{1,0:T(8,128)(2,1)S(1)}, u32[]{:S(2)}) copy-start(bf16[1024,768]{1,0:T(8,128)(2,1)S(1)} %collective-permute-done.7.args_13_) | copy-start | bytes 4718596
  94.9 98.0 %collective-permute-start.2 = (bf16[768,1024]{1,0:T(8,128)(2,1)}, bf16[768,1024]{1,0:T(8,128)(2,1)}, u32[]{:S(2)}, u32[]{:S(2)}) collective-permute-start(bf16[768,1024]{1,0:T(8,128)(2,1)} %bitcast_bitcast_fusion.args_4_), channel_id=1, source_target_pairs={{0,1},{1,0},{2,3},{3,2},{4,5},{5,4},{6,7},{7,6},{8,9},{9,8},{10,11... | collective-permute-start | bytes 4718600 | tf_op jit(solution)/shard_map/ppermute | solution.py:19
  122.4 70.4 %copy-start.2 = (bf16[1024,768]{1,0:T(8,128)(2,1)}, bf16[1024,768]{1,0:T(8,128)(2,1)S(1)}, u32[]{:S(2)}) copy-start(bf16[1024,768]{1,0:T(8,128)(2,1)S(1)} %collective-permute-done.6.args_12_) | copy-start | bytes 4718596
  122.4 71.0 %collective-permute-start.11 = (bf16[1024,768]{1,0:T(8,128)(2,1)S(1)}, bf16[1024,768]{1,0:T(8,128)(2,1)}, u32[]{:S(2)}, u32[]{:S(2)}) collective-permute-start(bf16[1024,768]{1,0:T(8,128)(2,1)S(1)} %collective-permute-done.7.args_13_), channel_id=1, source_target_pairs={{0,1},{1,0},{2,3},{3,2},{4,5},{5,4},{6,7},{7,6},{8,9},{9,8},{10,11... | collective-permute-start | bytes 4718600 | tf_op jit(solution)/shard_map/ppermute | solution.py:19
  123.8 115.5 %all-to-all-start = ((bf16[128,8,768]{2,0,1:T(8,128)(2,1)}), bf16[128,8,768]{2,0,1:T(8,128)(2,1)}, u32[]{:S(2)}, u32[]{:S(2)}) async-start(bf16[128,8,768]{2,0,1:T(8,128)(2,1)} %bitcast.31), calls=%async_computation | async-start | bytes 3145728 | tf_op jit(solution)/shard_map/all_to_all | solution.py:107
  129.9 63.8 %copy-start.6 = (s32[8,8]{1,0:T(8,128)S(1)}, s32[8,8]{1,0:T(8,128)}, u32[]{:S(2)}) copy-start(s32[8,8]{1,0:T(8,128)} %param.10) | copy-start | bytes 772
  129.9 64.0 %copy-start.7 = (s32[2,7]{1,0:T(2,128)S(1)}, s32[2,7]{1,0:T(2,128)}, u32[]{:S(2)}) copy-start(s32[2,7]{1,0:T(2,128)} %constant.89.clone) | copy-start | bytes 172
  183.7 71.4 %collective-permute-start.9 = (bf16[1024,768]{1,0:T(8,128)(2,1)}, bf16[1024,768]{1,0:T(8,128)(2,1)}, u32[]{:S(2)}, u32[]{:S(2)}) collective-permute-start(bf16[1024,768]{1,0:T(8,128)(2,1)} %broadcast_select_fusion), channel_id=1, source_target_pairs={{0,31},{1,2},{2,1},{3,4},{4,3},{5,6},{6,5},{7,8},{8,7},{9,10},{10,... | collective-permute-start | bytes 4718600 | tf_op jit(solution)/shard_map/ppermute | solution.py:19
  192.8 79.2 %collective-permute-start.3 = (bf16[768,1024]{1,0:T(8,128)(2,1)}, bf16[768,1024]{1,0:T(8,128)(2,1)}, u32[]{:S(2)}, u32[]{:S(2)}) collective-permute-start(bf16[768,1024]{1,0:T(8,128)(2,1)} %broadcast_select_fusion.1), channel_id=1, source_target_pairs={{0,31},{1,2},{2,1},{3,4},{4,3},{5,6},{6,5},{7,8},{8,7},{9,10},{10,... | collective-permute-start | bytes 4718600 | tf_op jit(solution)/shard_map/ppermute | solution.py:19
  192.8 62.3 %collective-permute-start.10 = (bf16[1024,768]{1,0:T(8,128)(2,1)S(1)}, bf16[1024,768]{1,0:T(8,128)(2,1)}, u32[]{:S(2)}, u32[]{:S(2)}) collective-permute-start(bf16[1024,768]{1,0:T(8,128)(2,1)S(1)} %collective-permute-done.6.args_12_), channel_id=1, source_target_pairs={{0,1},{1,0},{2,3},{3,2},{4,5},{5,4},{6,7},{7,6},{8,9},{9,8},{10,11... | collective-permute-start | bytes 4718600 | tf_op jit(solution)/shard_map/ppermute | solution.py:19
  192.9 62.2 %collective-permute-start.5 = (bf16[768,1024]{1,0:T(8,128)(2,1)}, bf16[768,1024]{1,0:T(8,128)(2,1)}, u32[]{:S(2)}, u32[]{:S(2)}) collective-permute-start(bf16[768,1024]{1,0:T(8,128)(2,1)} %collective-permute-done.1.args_6_), channel_id=1, source_target_pairs={{0,1},{1,0},{2,3},{3,2},{4,5},{5,4},{6,7},{7,6},{8,9},{9,8},{10,11... | collective-permute-start | bytes 4718600 | tf_op jit(solution)/shard_map/ppermute | solution.py:19
  193.4 78.6 %collective-permute-start.4 = (bf16[768,1024]{1,0:T(8,128)(2,1)}, bf16[768,1024]{1,0:T(8,128)(2,1)S(1)}, u32[]{:S(2)}, u32[]{:S(2)}) collective-permute-start(bf16[768,1024]{1,0:T(8,128)(2,1)} %collective-permute-done.args_5_), channel_id=1, source_target_pairs={{0,1},{1,0},{2,3},{3,2},{4,5},{5,4},{6,7},{7,6},{8,9},{9,8},{10,11... | collective-permute-start | bytes 4718600 | tf_op jit(solution)/shard_map/ppermute | solution.py:19
  272.0 1.1 copy-start.3

commit v5 on v4

--- a/solution.py
+++ b/solution.py
@@ -32,8 +32,12 @@
     parity = i % 2
 
     def copies(step, slot, c, p, j):
-        k_copy = pltpu.make_async_copy(k_hbm[p].at[:, pl.ds(j * TILE, TILE)], k_buf.at[slot, c], sem.at[0, slot, c])
-        v_copy = pltpu.make_async_copy(v_hbm[p].at[pl.ds(j * TILE, TILE), :], v_buf.at[slot, c], sem.at[1, slot, c])
+        k_copy = pltpu.make_async_copy(
+            k_hbm[p].at[:, pl.ds(j * TILE, TILE)], k_buf.at[slot, :, pl.ds(c * TILE, TILE)], sem.at[0, slot, c]
+        )
+        v_copy = pltpu.make_async_copy(
+            v_hbm[p].at[pl.ds(j * TILE, TILE), :], v_buf.at[slot, pl.ds(c * TILE, TILE), :], sem.at[1, slot, c]
+        )
         return k_copy, v_copy
 
     def start(step, slot):
@@ -60,25 +64,20 @@
             copy.wait()
 
     count = cnt_ref[i]
+    keys = SLOTS * TILE
+    valid = lax.broadcasted_iota(jnp.int32, (TILE, keys), 1) < count * TILE
+    k_all = k_buf.at[parity]
+    v_all = v_buf.at[parity]
     for h in range(heads_local):
         cols = slice(h * DH, (h + 1) * DH)
-        q = q_ref[:, cols]
-        scores = []
-        for c in range(SLOTS):
-            s = jnp.dot(q, k_buf[parity, c, cols, :], preferred_element_type=jnp.float32)
-            s = s * scale
-            s = s - bias_ref[(i * SLOTS + c) * heads_local + h]
-            s = jnp.where(c < count, s, -1e30)
-            scores.append(s)
-        top = scores[0].max(axis=1, keepdims=True)
-        for c in range(1, SLOTS):
-            top = jnp.maximum(top, scores[c].max(axis=1, keepdims=True))
-        total = jnp.zeros((TILE, 1), jnp.float32)
-        acc = jnp.zeros((TILE, DH), jnp.float32)
-        for c in range(SLOTS):
-            w = jnp.exp(scores[c] - top).astype(jnp.bfloat16)
-            total = total + w.astype(jnp.float32).sum(axis=1, keepdims=True)
-            acc = acc + jnp.dot(w, v_buf[parity, c, :, cols], preferred_element_type=jnp.float32)
+        s = jnp.dot(q_ref[:, cols], k_all[cols, :], preferred_element_type=jnp.float32)
+        s = s * scale
+        s = s - bias_ref[h : h + 1, :]
+        s = jnp.where(valid, s, -1e30)
+        top = s.max(axis=1, keepdims=True)
+        w = jnp.exp(s - top).astype(jnp.bfloat16)
+        total = w.astype(jnp.float32).sum(axis=1, keepdims=True)
+        acc = jnp.dot(w, v_all[:, cols], preferred_element_type=jnp.float32)
         o_ref[:, cols] = (acc / total).astype(o_ref.dtype)
 
 
@@ -122,14 +121,18 @@
     )
     head_index = lax.axis_index("head") * heads_local + jnp.arange(heads_local, dtype=jnp.int32)
     slopes = 8.0 * jnp.power(2.0, -8.0 * head_index.astype(jnp.float32) / H)
-    bias = (slopes[None, None, :] * distance[:, :, None]).reshape(-1)
+    bias = slopes[None, :, None, None] * distance[:, None, :, None]
+    bias = jnp.broadcast_to(bias, (tile_count, heads_local, SLOTS, TILE)).reshape(tile_count, heads_local, SLOTS * TILE)
     scale = DH ** (-0.5)
 
     assert tile_count == TILE_COUNT
     pieces = len(k_window)
     any_spec = pl.BlockSpec(memory_space=pl.ANY)
     in_specs = (
-        [pl.BlockSpec(memory_space=pltpu.SMEM), pl.BlockSpec((TILE, width), lambda i, sw, cnt: (i, 0))]
+        [
+            pl.BlockSpec((None, heads_local, SLOTS * TILE), lambda i, sw, cnt: (i, 0, 0)),
+            pl.BlockSpec((TILE, width), lambda i, sw, cnt: (i, 0)),
+        ]
         + [any_spec] * (2 * pieces)
     )
     grid_spec = pltpu.PrefetchScalarGridSpec(
@@ -138,8 +141,8 @@
         in_specs=in_specs,
         out_specs=pl.BlockSpec((TILE, width), lambda i, sw, cnt: (i, 0)),
         scratch_shapes=[
-            pltpu.VMEM((2, SLOTS, width, TILE), jnp.bfloat16),
-            pltpu.VMEM((2, SLOTS, TILE, width), jnp.bfloat16),
+            pltpu.VMEM((2, width, SLOTS * TILE), jnp.bfloat16),
+            pltpu.VMEM((2, SLOTS * TILE, width), jnp.bfloat16),
             pltpu.SemaphoreType.DMA((2, 2, SLOTS)),
         ],
     )

time: 323 us -> 323 us (level)
  transfers between devices with their start and end apart: 15 -> 15, of which waited for: 7 -> 7; matrix products, arithmetic and copies ran while one was open for 4% -> 5% of each run, Pallas kernels for 0% -> 0%
where the time goes in v5:
time: 323 us; the launch traced here: 318 us
  waiting for transfers between devices  228 us (71%)
  starting transfers between devices  26.6 us (8%)
  Pallas kernels  24.4 us (8%)
  blocking collectives  18.8 us (6%)
  local copies, waits for them, and re-layouts  15.2 us (5%)
  other arithmetic  4.36 us (1%)
    ppermute x12, waiting for transfers between devices, permute(): return lax.ppermute(block, axis, route)  113 us
    all_to_all x1, waiting for transfers between devices, body(): lax.all_to_all(key_states, 'head', split_axis=1, concat_axis=0, tiled=True)  53.7 us
    all_to_all x1, waiting for transfers between devices, body(): lax.all_to_all(queries, 'head', split_axis=1, concat_axis=0, tiled=True)  41.1 us
    pallas_call x1, Pallas kernels, body(): pl.pallas_call(kernel, grid_spec=grid_spec, out_shape=jax.ShapeDtypeStruc...  24.4 us
    all_to_all x1, waiting for transfers between devices, body(): lax.all_to_all(value_states, 'head', split_axis=1, concat_axis=0, tiled=T...  19.9 us
    all_to_all x1, blocking collectives, body(): return lax.all_to_all(out, 'head', split_axis=0, concat_axis=1, tiled=True)  18.8 us
    ppermute x12, starting transfers between devices, permute(): return lax.ppermute(block, axis, route)  12.5 us
  transfers between devices with their start and end apart: 15, of which 7 were waited for; matrix products, arithmetic and copies ran while one was open for 5% of the time, Pallas kernels for 0%

profile of v5, /device:TPU:128, one launch (start us, length us, event | category | flops | bytes accessed | tf_op | source)
XLA Modules:
  0.0 317.6 jit_solution(5192126115428913124)
XLA Ops:
  0.0 2.7 copy.30
  2.7 5.1 %all-to-all-start.2 = ((bf16[128,8,768]{2,0,1:T(8,128)(2,1)}), bf16[128,8,768]{2,0,1:T(8,128)(2,1)}, u32[]{:S(2)}, u32[]{:S(2)}) async-start(bf16[128,8,768]{2,0,1:T(8,128)(2,1)} %bitcast.33), calls=%async_computation.2 | async-start | bytes 3145728 | tf_op jit(solution)/shard_map/all_to_all | solution.py:104
  7.7 1.6 copy.18
  9.3 19.9 %all-to-all-done.2 = bf16[128,8,768]{2,0,1:T(8,128)(2,1)} async-done(((bf16[128,8,768]{2,0,1:T(8,128)(2,1)}), bf16[128,8,768]{2,0,1:T(8,128)(2,1)}, u32[]{:S(2)}, u32[]{:S(2)}) %all-to-all-start.2) | async-done | bytes 1572896 | tf_op jit(solution)/shard_map/all_to_all | solution.py:104
  29.2 4.3 %all-to-all-start.1 = ((bf16[128,8,768]{0,2,1:T(8,128)(2,1)}), bf16[128,8,768]{0,2,1:T(8,128)(2,1)}, u32[]{:S(2)}, u32[]{:S(2)}) async-start(bf16[128,8,768]{0,2,1:T(8,128)(2,1)} %bitcast.4), calls=%async_computation.1 | async-start | bytes 3145728 | tf_op jit(solution)/shard_map/all_to_all | solution.py:102
  33.5 2.8 collective-permute-start.7
  36.3 53.7 %all-to-all-done.1 = bf16[128,8,768]{0,2,1:T(8,128)(2,1)} async-done(((bf16[128,8,768]{0,2,1:T(8,128)(2,1)}), bf16[128,8,768]{0,2,1:T(8,128)(2,1)}, u32[]{:S(2)}, u32[]{:S(2)}) %all-to-all-start.1) | async-done | bytes 1572896 | tf_op jit(solution)/shard_map/all_to_all | solution.py:102
  90.0 2.9 bitcast_bitcast_fusion.args_4_
  92.9 2.0 collective-permute-start
  95.4 27.0 %collective-permute-done.6.args_12_ = bf16[1024,768]{1,0:T(8,128)(2,1)S(1)} collective-permute-done((bf16[1024,768]{1,0:T(8,128)(2,1)}, bf16[1024,768]{1,0:T(8,128)(2,1)S(1)}, u32[]{:S(2)}, u32[]{:S(2)}) %collective-permute-start.6) | collective-permute-done | bytes 1572896 | tf_op jit(solution)/shard_map/ppermute | solution.py:19
  122.4 1.4 copy.31
  123.8 4.8 %all-to-all-start = ((bf16[128,8,768]{2,0,1:T(8,128)(2,1)}), bf16[128,8,768]{2,0,1:T(8,128)(2,1)}, u32[]{:S(2)}, u32[]{:S(2)}) async-start(bf16[128,8,768]{2,0,1:T(8,128)(2,1)} %bitcast.35), calls=%async_computation | async-start | bytes 3145728 | tf_op jit(solution)/shard_map/all_to_all | solution.py:106
  128.6 1.3 broadcast_select_fusion
  129.9 53.8 %collective-permute-done.1.args_6_ = bf16[768,1024]{1,0:T(8,128)(2,1)} collective-permute-done((bf16[768,1024]{1,0:T(8,128)(2,1)}, bf16[768,1024]{1,0:T(8,128)(2,1)}, u32[]{:S(2)}, u32[]{:S(2)}) %collective-permute-start.1) | collective-permute-done | bytes 1572896 | tf_op jit(solution)/shard_map/ppermute | solution.py:19
  183.7 6.3 %collective-permute-start.9 = (bf16[1024,768]{1,0:T(8,128)(2,1)}, bf16[1024,768]{1,0:T(8,128)(2,1)}, u32[]{:S(2)}, u32[]{:S(2)}) collective-permute-start(bf16[1024,768]{1,0:T(8,128)(2,1)} %broadcast_select_fusion), channel_id=1, source_target_pairs={{0,31},{1,2},{2,1},{3,4},{4,3},{5,6},{6,5},{7,8},{8,7},{9,10},{10,... | collective-permute-start | bytes 4718600 | tf_op jit(solution)/shard_map/ppermute | solution.py:19
  190.0 2.8 broadcast_select_fusion.1
  197.4 0.8 copy.21.args_2_
  198.2 41.1 %all-to-all-done = bf16[128,8,768]{2,0,1:T(8,128)(2,1)} async-done(((bf16[128,8,768]{2,0,1:T(8,128)(2,1)}), bf16[128,8,768]{2,0,1:T(8,128)(2,1)}, u32[]{:S(2)}, u32[]{:S(2)}) %all-to-all-start) | async-done | bytes 1572896 | tf_op jit(solution)/shard_map/all_to_all | solution.py:106
  239.3 15.8 %collective-permute-done.9.args_15_ = bf16[1024,768]{1,0:T(8,128)(2,1)} collective-permute-done((bf16[1024,768]{1,0:T(8,128)(2,1)}, bf16[1024,768]{1,0:T(8,128)(2,1)}, u32[]{:S(2)}, u32[]{:S(2)}) %collective-permute-start.9) | collective-permute-done | bytes 1572896 | tf_op jit(solution)/shard_map/ppermute | solution.py:19
  255.1 16.8 %collective-permute-done.3.args_8_ = bf16[768,1024]{1,0:T(8,128)(2,1)} collective-permute-done((bf16[768,1024]{1,0:T(8,128)(2,1)}, bf16[768,1024]{1,0:T(8,128)(2,1)}, u32[]{:S(2)}, u32[]{:S(2)}) %collective-permute-start.3) | collective-permute-done | bytes 1572896 | tf_op jit(solution)/shard_map/ppermute | solution.py:19
  272.0 1.1 copy-done.3
  273.1 24.4 %shard_map.73 = bf16[1024,768]{1,0:T(8,128)(2,1)} custom-call(s32[64]{0:T(128)} %reshape.68.args_0_, s32[8]{0:T(128)} %args_1_.4, f32[8,6,1024]{2,1,0:T(8,128)} %copy.21.args_2_, bf16[1024,768]{1,0:T(8,128)(2,1)} %bitcast.3.args_3_, bf16[768,1024]{1,0:T(8,128)(2,1)} %bitcast_bitcast_fusion.args_4_, bf16[768,1024]{1,0:T(8,128)(2,1)} %collective-permute-done.args_5_, ...), custom_call_target="tpu_custom_call" | custom-call | tf_op jit(solution)/shard_map/pallas_call | solution.py:150
  297.5 18.8 %all_to_all.76 = bf16[8,128,768]{2,1,0:T(8,128)(2,1)S(1)} all-to-all(bf16[8,128,768]{2,1,0:T(8,128)(2,1)} %bitcast.36), channel_id=1, replica_groups=mesh['head'=8,'blk'=32] {'head'}, dimensions={0} | all-to-all | bytes 3145728 | tf_op jit(solution)/shard_map/all_to_all | solution.py:163
  316.3 1.3 copy.26
  (53 shorter events, 5.0 us)
Async XLA Ops:
  0.0 195.5 %copy-start = (s32[256]{0:T(256)S(1)}, s32[256]{0:T(256)}, u32[]{:S(2)}) copy-start(s32[256]{0:T(256)} %param.12) | copy-start | bytes 3076
  2.7 5.1 %copy-start.4 = (bf16[128,6144]{1,0:T(8,128)(2,1)S(1)}, bf16[128,6144]{1,0:T(8,128)(2,1)}, u32[]{:S(2)}) copy-start(bf16[128,6144]{1,0:T(8,128)(2,1)} %param.8) | copy-start | bytes 4718596
  2.7 26.5 %all-to-all-start.2 = ((bf16[128,8,768]{2,0,1:T(8,128)(2,1)}), bf16[128,8,768]{2,0,1:T(8,128)(2,1)}, u32[]{:S(2)}, u32[]{:S(2)}) async-start(bf16[128,8,768]{2,0,1:T(8,128)(2,1)} %bitcast.33), calls=%async_computation.2 | async-start | bytes 3145728 | tf_op jit(solution)/shard_map/all_to_all | solution.py:104
  29.2 60.8 %all-to-all-start.1 = ((bf16[128,8,768]{0,2,1:T(8,128)(2,1)}), bf16[128,8,768]{0,2,1:T(8,128)(2,1)}, u32[]{:S(2)}, u32[]{:S(2)}) async-start(bf16[128,8,768]{0,2,1:T(8,128)(2,1)} %bitcast.4), calls=%async_computation.1 | async-start | bytes 3145728 | tf_op jit(solution)/shard_map/all_to_all | solution.py:102
  33.5 61.5 %collective-permute-start.7 = (bf16[1024,768]{1,0:T(8,128)(2,1)}, bf16[1024,768]{1,0:T(8,128)(2,1)S(1)}, u32[]{:S(2)}, u32[]{:S(2)}) collective-permute-start(bf16[1024,768]{1,0:T(8,128)(2,1)} %bitcast.8.args_11_), channel_id=1, source_target_pairs={{0,30},{1,31},{2,0},{3,1},{4,2},{5,3},{6,4},{7,5},{8,6},{9,7},{10,... | collective-permute-start | bytes 4718600 | tf_op jit(solution)/shard_map/ppermute | solution.py:19
  36.3 86.1 %collective-permute-start.6 = (bf16[1024,768]{1,0:T(8,128)(2,1)}, bf16[1024,768]{1,0:T(8,128)(2,1)S(1)}, u32[]{:S(2)}, u32[]{:S(2)}) collective-permute-start(bf16[1024,768]{1,0:T(8,128)(2,1)} %bitcast.8.args_11_), channel_id=1, source_target_pairs={{0,2},{1,3},{2,4},{3,5},{4,6},{5,7},{6,8},{7,9},{8,10},{9,11},{10,... | collective-permute-start | bytes 4718600 | tf_op jit(solution)/shard_map/ppermute | solution.py:19
  90.0 32.4 %copy-start.5 = (bf16[128,6144]{1,0:T(8,128)(2,1)S(1)}, bf16[128,6144]{1,0:T(8,128)(2,1)}, u32[]{:S(2)}) copy-start(bf16[128,6144]{1,0:T(8,128)(2,1)} %param.7) | copy-start | bytes 4718596
  92.9 90.8 %collective-permute-start.1 = (bf16[768,1024]{1,0:T(8,128)(2,1)}, bf16[768,1024]{1,0:T(8,128)(2,1)}, u32[]{:S(2)}, u32[]{:S(2)}) collective-permute-start(bf16[768,1024]{1,0:T(8,128)(2,1)} %bitcast_bitcast_fusion.args_4_), channel_id=1, source_target_pairs={{0,30},{1,31},{2,0},{3,1},{4,2},{5,3},{6,4},{7,5},{8,6},{9,7},{10,... | collective-permute-start | bytes 4718600 | tf_op jit(solution)/shard_map/ppermute | solution.py:19
  92.9 97.1 %collective-permute-start = (bf16[768,1024]{1,0:T(8,128)(2,1)}, bf16[768,1024]{1,0:T(8,128)(2,1)}, u32[]{:S(2)}, u32[]{:S(2)}) collective-permute-start(bf16[768,1024]{1,0:T(8,128)(2,1)} %bitcast_bitcast_fusion.args_4_), channel_id=1, source_target_pairs={{0,2},{1,3},{2,4},{3,5},{4,6},{5,7},{6,8},{7,9},{8,10},{9,11},{10,... | collective-permute-start | bytes 4718600 | tf_op jit(solution)/shard_map/ppermute | solution.py:19
  94.9 97.9 %collective-permute-start.8 = (bf16[1024,768]{1,0:T(8,128)(2,1)}, bf16[1024,768]{1,0:T(8,128)(2,1)}, u32[]{:S(2)}, u32[]{:S(2)}) collective-permute-start(bf16[1024,768]{1,0:T(8,128)(2,1)} %bitcast.8.args_11_), channel_id=1, source_target_pairs={{0,1},{1,0},{2,3},{3,2},{4,5},{5,4},{6,7},{7,6},{8,9},{9,8},{10,11... | collective-permute-start | bytes 4718600 | tf_op jit(solution)/shard_map/ppermute | solution.py:19
  94.9 33.7 %copy-start.1 = (bf16[1024,768]{1,0:T(8,128)(2,1)}, bf16[1024,768]{1,0:T(8,128)(2,1)S(1)}, u32[]{:S(2)}) copy-start(bf16[1024,768]{1,0:T(8,128)(2,1)S(1)} %collective-permute-done.7.args_13_) | copy-start | bytes 4718596
  94.9 98.0 %collective-permute-start.2 = (bf16[768,1024]{1,0:T(8,128)(2,1)}, bf16[768,1024]{1,0:T(8,128)(2,1)}, u32[]{:S(2)}, u32[]{:S(2)}) collective-permute-start(bf16[768,1024]{1,0:T(8,128)(2,1)} %bitcast_bitcast_fusion.args_4_), channel_id=1, source_target_pairs={{0,1},{1,0},{2,3},{3,2},{4,5},{5,4},{6,7},{7,6},{8,9},{9,8},{10,11... | collective-permute-start | bytes 4718600 | tf_op jit(solution)/shard_map/ppermute | solution.py:19
  122.4 70.4 %copy-start.2 = (bf16[1024,768]{1,0:T(8,128)(2,1)}, bf16[1024,768]{1,0:T(8,128)(2,1)S(1)}, u32[]{:S(2)}) copy-start(bf16[1024,768]{1,0:T(8,128)(2,1)S(1)} %collective-permute-done.6.args_12_) | copy-start | bytes 4718596
  122.4 71.0 %collective-permute-start.11 = (bf16[1024,768]{1,0:T(8,128)(2,1)S(1)}, bf16[1024,768]{1,0:T(8,128)(2,1)}, u32[]{:S(2)}, u32[]{:S(2)}) collective-permute-start(bf16[1024,768]{1,0:T(8,128)(2,1)S(1)} %collective-permute-done.7.args_13_), channel_id=1, source_target_pairs={{0,1},{1,0},{2,3},{3,2},{4,5},{5,4},{6,7},{7,6},{8,9},{9,8},{10,11... | collective-permute-start | bytes 4718600 | tf_op jit(solution)/shard_map/ppermute | solution.py:19
  123.8 115.5 %all-to-all-start = ((bf16[128,8,768]{2,0,1:T(8,128)(2,1)}), bf16[128,8,768]{2,0,1:T(8,128)(2,1)}, u32[]{:S(2)}, u32[]{:S(2)}) async-start(bf16[128,8,768]{2,0,1:T(8,128)(2,1)} %bitcast.35), calls=%async_computation | async-start | bytes 3145728 | tf_op jit(solution)/shard_map/all_to_all | solution.py:106
  129.9 63.8 %copy-start.6 = (s32[8,8]{1,0:T(8,128)S(1)}, s32[8,8]{1,0:T(8,128)}, u32[]{:S(2)}) copy-start(s32[8,8]{1,0:T(8,128)} %param.10) | copy-start | bytes 772
  129.9 64.0 %copy-start.7 = (s32[2,7]{1,0:T(2,128)S(1)}, s32[2,7]{1,0:T(2,128)}, u32[]{:S(2)}) copy-start(s32[2,7]{1,0:T(2,128)} %constant.89.clone) | copy-start | bytes 172
  183.7 71.4 %collective-permute-start.9 = (bf16[1024,768]{1,0:T(8,128)(2,1)}, bf16[1024,768]{1,0:T(8,128)(2,1)}, u32[]{:S(2)}, u32[]{:S(2)}) collective-permute-start(bf16[1024,768]{1,0:T(8,128)(2,1)} %broadcast_select_fusion), channel_id=1, source_target_pairs={{0,31},{1,2},{2,1},{3,4},{4,3},{5,6},{6,5},{7,8},{8,7},{9,10},{10,... | collective-permute-start | bytes 4718600 | tf_op jit(solution)/shard_map/ppermute | solution.py:19
  192.8 79.2 %collective-permute-start.3 = (bf16[768,1024]{1,0:T(8,128)(2,1)}, bf16[768,1024]{1,0:T(8,128)(2,1)}, u32[]{:S(2)}, u32[]{:S(2)}) collective-permute-start(bf16[768,1024]{1,0:T(8,128)(2,1)} %broadcast_select_fusion.1), channel_id=1, source_target_pairs={{0,31},{1,2},{2,1},{3,4},{4,3},{5,6},{6,5},{7,8},{8,7},{9,10},{10,... | collective-permute-start | bytes 4718600 | tf_op jit(solution)/shard_map/ppermute | solution.py:19
  192.8 62.3 %collective-permute-start.10 = (bf16[1024,768]{1,0:T(8,128)(2,1)S(1)}, bf16[1024,768]{1,0:T(8,128)(2,1)}, u32[]{:S(2)}, u32[]{:S(2)}) collective-permute-start(bf16[1024,768]{1,0:T(8,128)(2,1)S(1)} %collective-permute-done.6.args_12_), channel_id=1, source_target_pairs={{0,1},{1,0},{2,3},{3,2},{4,5},{5,4},{6,7},{7,6},{8,9},{9,8},{10,11... | collective-permute-start | bytes 4718600 | tf_op jit(solution)/shard_map/ppermute | solution.py:19
  192.9 62.2 %collective-permute-start.5 = (bf16[768,1024]{1,0:T(8,128)(2,1)}, bf16[768,1024]{1,0:T(8,128)(2,1)}, u32[]{:S(2)}, u32[]{:S(2)}) collective-permute-start(bf16[768,1024]{1,0:T(8,128)(2,1)} %collective-permute-done.1.args_6_), channel_id=1, source_target_pairs={{0,1},{1,0},{2,3},{3,2},{4,5},{5,4},{6,7},{7,6},{8,9},{9,8},{10,11... | collective-permute-start | bytes 4718600 | tf_op jit(solution)/shard_map/ppermute | solution.py:19
  193.4 78.6 %collective-permute-start.4 = (bf16[768,1024]{1,0:T(8,128)(2,1)}, bf16[768,1024]{1,0:T(8,128)(2,1)S(1)}, u32[]{:S(2)}, u32[]{:S(2)}) collective-permute-start(bf16[768,1024]{1,0:T(8,128)(2,1)} %collective-permute-done.args_5_), channel_id=1, source_target_pairs={{0,1},{1,0},{2,3},{3,2},{4,5},{5,4},{6,7},{7,6},{8,9},{9,8},{10,11... | collective-permute-start | bytes 4718600 | tf_op jit(solution)/shard_map/ppermute | solution.py:19
  272.0 1.1 copy-start.3

commit v6 on v5

--- a/solution.py
+++ b/solution.py
@@ -12,7 +12,7 @@
 SLOTS = 8
 TILE_COUNT = 8
 
-PIECE_OF_OFFSET = ((4, 1, 5, 0, 3, 2, 6), (5, 1, 3, 0, 6, 2, 4))
+PIECE_OF_OFFSET = ((4, 1, 6, 0, 3, 2, 7), (6, 1, 3, 0, 7, 2, 5))
 
 
 def permute(block, axis, route):
@@ -86,13 +86,11 @@
     from_left2 = permute(local, "blk", shift_pairs(n, 2))
     from_right2 = permute(local, "blk", shift_pairs(n, -2))
     other_core = permute(local, "blk", swap)
-    core = lax.axis_index("blk") % 2
-    forward = jnp.where(core == 1, from_left2, from_right2)
-    cross_route = [((i, (i + 1) % n) if i % 2 == 1 else (i, (i - 1) % n)) for i in range(n)]
-    across = permute(forward, "blk", cross_route)
+    odd_ahead = permute(from_left2, "blk", [(i, (i + 1) % n) for i in range(1, n, 2)])
+    even_back = permute(from_right2, "blk", [(i, (i - 1) % n) for i in range(0, n, 2)])
     other_left2 = permute(from_left2, "blk", swap)
     other_right2 = permute(from_right2, "blk", swap)
-    return [local, from_left2, from_right2, other_core, across, other_left2, other_right2]
+    return [local, from_left2, from_right2, other_core, odd_ahead, even_back, other_left2, other_right2]
 
 
 def body(queries, key_states, value_states, block_lists, block_counts, tile_order):

time: 323 us -> 335 us (1.037)
  the two profiles are of different devices: /device:TPU:128 before, /device:TPU:64 now
where the time goes in v6:
time: 335 us; the launch traced here: 334 us
  waiting for transfers between devices  219 us (65%)
  starting transfers between devices  39.1 us (12%)
  blocking collectives  36.4 us (11%)
  Pallas kernels  24.6 us (7%)
  local copies, waits for them, and re-layouts  15.2 us (5%)
    ppermute x14, waiting for transfers between devices, permute(): return lax.ppermute(block, axis, route)  96.1 us
    all_to_all x1, waiting for transfers between devices, body(): lax.all_to_all(key_states, 'head', split_axis=1, concat_axis=0, tiled=True)  54.3 us
    all_to_all x1, waiting for transfers between devices, body(): lax.all_to_all(queries, 'head', split_axis=1, concat_axis=0, tiled=True)  48.5 us
    all_to_all x1, blocking collectives, body(): return lax.all_to_all(out, 'head', split_axis=0, concat_axis=1, tiled=True)  36.4 us
    pallas_call x1, Pallas kernels, body(): pl.pallas_call(kernel, grid_spec=grid_spec, out_shape=jax.ShapeDtypeStruc...  24.6 us
    all_to_all x1, waiting for transfers between devices, body(): lax.all_to_all(value_states, 'head', split_axis=1, concat_axis=0, tiled=T...  19.8 us
    ppermute x14, starting transfers between devices, permute(): return lax.ppermute(block, axis, route)  19 us
    all_to_all x1, starting transfers between devices, body(): lax.all_to_all(queries, 'head', split_axis=1, concat_axis=0, tiled=True)  9.86 us
  transfers between devices with their start and end apart: 17, of which 7 were waited for; matrix products, arithmetic and copies ran while one was open for 3% of the time, Pallas kernels for 0%

profile of v6, /device:TPU:64, one launch (start us, length us, event | category | flops | bytes accessed | tf_op | source)
XLA Modules:
  0.0 334.4 jit_solution(13914662641742892976)
XLA Ops:
  0.0 2.7 copy.30
  2.7 6.0 %all-to-all-start.2 = ((bf16[128,8,768]{2,0,1:T(8,128)(2,1)}), bf16[128,8,768]{2,0,1:T(8,128)(2,1)S(1)}, u32[]{:S(2)}, u32[]{:S(2)}) async-start(bf16[128,8,768]{2,0,1:T(8,128)(2,1)} %bitcast.33), calls=%async_computation.2 | async-start | bytes 3145728 | tf_op jit(solution)/shard_map/all_to_all | solution.py:102
  8.7 1.6 copy.18
  10.2 19.8 %all-to-all-done.2 = bf16[128,8,768]{2,0,1:T(8,128)(2,1)S(1)} async-done(((bf16[128,8,768]{2,0,1:T(8,128)(2,1)}), bf16[128,8,768]{2,0,1:T(8,128)(2,1)S(1)}, u32[]{:S(2)}, u32[]{:S(2)}) %all-to-all-start.2) | async-done | bytes 1572896 | tf_op jit(solution)/shard_map/all_to_all | solution.py:102
  30.0 4.3 %all-to-all-start.1 = ((bf16[128,8,768]{0,2,1:T(8,128)(2,1)}), bf16[128,8,768]{0,2,1:T(8,128)(2,1)}, u32[]{:S(2)}, u32[]{:S(2)}) async-start(bf16[128,8,768]{0,2,1:T(8,128)(2,1)} %bitcast.4), calls=%async_computation.1 | async-start | bytes 3145728 | tf_op jit(solution)/shard_map/all_to_all | solution.py:100
  34.4 1.9 collective-permute-start.8
  36.5 54.3 %all-to-all-done.1 = bf16[128,8,768]{0,2,1:T(8,128)(2,1)} async-done(((bf16[128,8,768]{0,2,1:T(8,128)(2,1)}), bf16[128,8,768]{0,2,1:T(8,128)(2,1)}, u32[]{:S(2)}, u32[]{:S(2)}) %all-to-all-start.1) | async-done | bytes 1572896 | tf_op jit(solution)/shard_map/all_to_all | solution.py:100
  90.9 1.6 bitcast_bitcast_fusion.args_4_
  92.7 2.0 collective-permute-start
  94.7 27.8 %collective-permute-done.7.args_13_ = bf16[1024,768]{1,0:T(8,128)(2,1)} collective-permute-done((bf16[1024,768]{1,0:T(8,128)(2,1)S(1)}, bf16[1024,768]{1,0:T(8,128)(2,1)}, u32[]{:S(2)}, u32[]{:S(2)}) %collective-permute-start.7) | collective-permute-done | bytes 1572896 | tf_op jit(solution)/shard_map/ppermute | solution.py:19
  122.5 2.5 collective-permute-start.11
  126.1 2.7 copy.31
  128.8 9.9 %all-to-all-start = ((bf16[128,8,768]{2,0,1:T(8,128)(2,1)}), bf16[128,8,768]{2,0,1:T(8,128)(2,1)S(1)}, u32[]{:S(2)}, u32[]{:S(2)}) async-start(bf16[128,8,768]{2,0,1:T(8,128)(2,1)} %bitcast.40), calls=%async_computation | async-start | bytes 3145728 | tf_op jit(solution)/shard_map/all_to_all | solution.py:104
  138.7 47.1 %collective-permute-done.1.args_6_ = bf16[768,1024]{1,0:T(8,128)(2,1)} collective-permute-done((bf16[768,1024]{1,0:T(8,128)(2,1)S(1)}, bf16[768,1024]{1,0:T(8,128)(2,1)}, u32[]{:S(2)}, u32[]{:S(2)}) %collective-permute-start.1) | collective-permute-done | bytes 1572896 | tf_op jit(solution)/shard_map/ppermute | solution.py:19
  185.7 1.3 collective-permute-start.10
  187.0 1.2 collective-permute-start.6
  188.2 8.4 %collective-permute-start.4 = (bf16[768,1024]{1,0:T(8,128)(2,1)}, bf16[768,1024]{1,0:T(8,128)(2,1)}, u32[]{:S(2)}, u32[]{:S(2)}) collective-permute-start(bf16[768,1024]{1,0:T(8,128)(2,1)} %collective-permute-done.1.args_6_), channel_id=1, source_target_pairs={{0,31},{2,1},{4,3},{6,5},{8,7},{10,9},{12,11},{14,13},{16,15},{18,... | collective-permute-start | bytes 4718600 | tf_op jit(solution)/shard_map/ppermute | solution.py:19
  196.6 6.0 %collective-permute-done.11.args_17_ = bf16[1024,768]{1,0:T(8,128)(2,1)} collective-permute-done((bf16[1024,768]{1,0:T(8,128)(2,1)}, bf16[1024,768]{1,0:T(8,128)(2,1)}, u32[]{:S(2)}, u32[]{:S(2)}) %collective-permute-start.11) | collective-permute-done | bytes 1572896 | tf_op jit(solution)/shard_map/ppermute | solution.py:19
  202.7 1.3 collective-permute-start.3
  208.4 48.5 %all-to-all-done = bf16[128,8,768]{2,0,1:T(8,128)(2,1)S(1)} async-done(((bf16[128,8,768]{2,0,1:T(8,128)(2,1)}), bf16[128,8,768]{2,0,1:T(8,128)(2,1)S(1)}, u32[]{:S(2)}, u32[]{:S(2)}) %all-to-all-start) | async-done | bytes 1572896 | tf_op jit(solution)/shard_map/all_to_all | solution.py:104
  257.0 15.2 %collective-permute-done.3.args_8_ = bf16[768,1024]{1,0:T(8,128)(2,1)} collective-permute-done((bf16[768,1024]{1,0:T(8,128)(2,1)}, bf16[768,1024]{1,0:T(8,128)(2,1)}, u32[]{:S(2)}, u32[]{:S(2)}) %collective-permute-start.3) | collective-permute-done | bytes 1572896 | tf_op jit(solution)/shard_map/ppermute | solution.py:19
  272.1 24.6 %shard_map.73 = bf16[1024,768]{1,0:T(8,128)(2,1)} custom-call(s32[64]{0:T(128)} %reshape.68.args_0_, s32[8]{0:T(128)} %args_1_.4, f32[8,6,1024]{2,1,0:T(8,128)} %copy.21.args_2_, bf16[1024,768]{1,0:T(8,128)(2,1)} %bitcast.39, bf16[768,1024]{1,0:T(8,128)(2,1)} %copy-done.2, bf16[768,1024]{1,0:T(8,128)(2,1)} %collective-permute-done.args_5_, ...), custom_call_target="tpu_custom_call" | custom-call | tf_op jit(solution)/shard_map/pallas_call | solution.py:148
  296.7 36.4 %all_to_all.76 = bf16[8,128,768]{2,1,0:T(8,128)(2,1)S(1)} all-to-all(bf16[8,128,768]{2,1,0:T(8,128)(2,1)} %bitcast.41), channel_id=1, replica_groups=mesh['head'=8,'blk'=32] {'head'}, dimensions={0} | all-to-all | bytes 3145728 | tf_op jit(solution)/shard_map/all_to_all | solution.py:161
  333.1 1.3 copy.26
  (57 shorter events, 6.1 us)
Async XLA Ops:
  0.0 205.7 %copy-start = (s32[256]{0:T(256)S(1)}, s32[256]{0:T(256)}, u32[]{:S(2)}) copy-start(s32[256]{0:T(256)} %param.12) | copy-start | bytes 3076
  2.7 27.3 %all-to-all-start.2 = ((bf16[128,8,768]{2,0,1:T(8,128)(2,1)}), bf16[128,8,768]{2,0,1:T(8,128)(2,1)S(1)}, u32[]{:S(2)}, u32[]{:S(2)}) async-start(bf16[128,8,768]{2,0,1:T(8,128)(2,1)} %bitcast.33), calls=%async_computation.2 | async-start | bytes 3145728 | tf_op jit(solution)/shard_map/all_to_all | solution.py:102
  30.0 6.3 %copy-start.1 = (bf16[128,8,768]{2,0,1:T(8,128)(2,1)}, bf16[128,8,768]{2,0,1:T(8,128)(2,1)S(1)}, u32[]{:S(2)}) copy-start(bf16[128,8,768]{2,0,1:T(8,128)(2,1)S(1)} %all-to-all-done.2) | copy-start | bytes 4718596
  30.0 60.8 %all-to-all-start.1 = ((bf16[128,8,768]{0,2,1:T(8,128)(2,1)}), bf16[128,8,768]{0,2,1:T(8,128)(2,1)}, u32[]{:S(2)}, u32[]{:S(2)}) async-start(bf16[128,8,768]{0,2,1:T(8,128)(2,1)} %bitcast.4), calls=%async_computation.1 | async-start | bytes 3145728 | tf_op jit(solution)/shard_map/all_to_all | solution.py:100
  34.3 58.4 %collective-permute-start.9 = (bf16[1024,768]{1,0:T(8,128)(2,1)S(1)}, bf16[1024,768]{1,0:T(8,128)(2,1)}, u32[]{:S(2)}, u32[]{:S(2)}) collective-permute-start(bf16[1024,768]{1,0:T(8,128)(2,1)S(1)} %bitcast.35), channel_id=1, source_target_pairs={{0,1},{1,0},{2,3},{3,2},{4,5},{5,4},{6,7},{7,6},{8,9},{9,8},{10,11... | collective-permute-start | bytes 4718600 | tf_op jit(solution)/shard_map/ppermute | solution.py:19
  34.4 60.3 %collective-permute-start.8 = (bf16[1024,768]{1,0:T(8,128)(2,1)S(1)}, bf16[1024,768]{1,0:T(8,128)(2,1)}, u32[]{:S(2)}, u32[]{:S(2)}) collective-permute-start(bf16[1024,768]{1,0:T(8,128)(2,1)S(1)} %bitcast.36), channel_id=1, source_target_pairs={{0,30},{1,31},{2,0},{3,1},{4,2},{5,3},{6,4},{7,5},{8,6},{9,7},{10,... | collective-permute-start | bytes 4718600 | tf_op jit(solution)/shard_map/ppermute | solution.py:19
  36.4 86.1 %collective-permute-start.7 = (bf16[1024,768]{1,0:T(8,128)(2,1)S(1)}, bf16[1024,768]{1,0:T(8,128)(2,1)}, u32[]{:S(2)}, u32[]{:S(2)}) collective-permute-start(bf16[1024,768]{1,0:T(8,128)(2,1)S(1)} %bitcast.37), channel_id=1, source_target_pairs={{0,2},{1,3},{2,4},{3,5},{4,6},{5,7},{6,8},{7,9},{8,10},{9,11},{10,... | collective-permute-start | bytes 4718600 | tf_op jit(solution)/shard_map/ppermute | solution.py:19
  92.5 36.3 %copy-start.2 = (bf16[768,1024]{1,0:T(8,128)(2,1)}, bf16[768,1024]{1,0:T(8,128)(2,1)S(1)}, u32[]{:S(2)}) copy-start(bf16[768,1024]{1,0:T(8,128)(2,1)S(1)} %bitcast_bitcast_fusion.args_4_) | copy-start | bytes 4718596
  92.5 32.5 %collective-permute-start.2 = (bf16[768,1024]{1,0:T(8,128)(2,1)S(1)}, bf16[768,1024]{1,0:T(8,128)(2,1)S(1)}, u32[]{:S(2)}, u32[]{:S(2)}) collective-permute-start(bf16[768,1024]{1,0:T(8,128)(2,1)S(1)} %bitcast_bitcast_fusion.args_4_), channel_id=1, source_target_pairs={{0,1},{1,0},{2,3},{3,2},{4,5},{5,4},{6,7},{7,6},{8,9},{9,8},{10,11... | collective-permute-start | bytes 4718600 | tf_op jit(solution)/shard_map/ppermute | solution.py:19
  92.6 93.1 %collective-permute-start.1 = (bf16[768,1024]{1,0:T(8,128)(2,1)S(1)}, bf16[768,1024]{1,0:T(8,128)(2,1)}, u32[]{:S(2)}, u32[]{:S(2)}) collective-permute-start(bf16[768,1024]{1,0:T(8,128)(2,1)S(1)} %bitcast_bitcast_fusion.args_4_), channel_id=1, source_target_pairs={{0,30},{1,31},{2,0},{3,1},{4,2},{5,3},{6,4},{7,5},{8,6},{9,7},{10,... | collective-permute-start | bytes 4718600 | tf_op jit(solution)/shard_map/ppermute | solution.py:19
  92.7 94.3 %collective-permute-start = (bf16[768,1024]{1,0:T(8,128)(2,1)S(1)}, bf16[768,1024]{1,0:T(8,128)(2,1)}, u32[]{:S(2)}, u32[]{:S(2)}) collective-permute-start(bf16[768,1024]{1,0:T(8,128)(2,1)S(1)} %bitcast_bitcast_fusion.args_4_), channel_id=1, source_target_pairs={{0,2},{1,3},{2,4},{3,5},{4,6},{5,7},{6,8},{7,9},{8,10},{9,11},{10,... | collective-permute-start | bytes 4718600 | tf_op jit(solution)/shard_map/ppermute | solution.py:19
  94.7 93.5 %collective-permute-start.13 = (bf16[1024,768]{1,0:T(8,128)(2,1)}, bf16[1024,768]{1,0:T(8,128)(2,1)}, u32[]{:S(2)}, u32[]{:S(2)}) collective-permute-start(bf16[1024,768]{1,0:T(8,128)(2,1)} %collective-permute-done.8.args_14_), channel_id=1, source_target_pairs={{0,1},{1,0},{2,3},{3,2},{4,5},{5,4},{6,7},{7,6},{8,9},{9,8},{10,11... | collective-permute-start | bytes 4718600 | tf_op jit(solution)/shard_map/ppermute | solution.py:19
  122.5 80.2 %collective-permute-start.11 = (bf16[1024,768]{1,0:T(8,128)(2,1)}, bf16[1024,768]{1,0:T(8,128)(2,1)}, u32[]{:S(2)}, u32[]{:S(2)}) collective-permute-start(bf16[1024,768]{1,0:T(8,128)(2,1)} %collective-permute-done.8.args_14_), channel_id=1, source_target_pairs={{0,31},{2,1},{4,3},{6,5},{8,7},{10,9},{12,11},{14,13},{16,15},{18,... | collective-permute-start | bytes 4718600 | tf_op jit(solution)/shard_map/ppermute | solution.py:19
  126.1 76.5 %collective-permute-start.12 = (bf16[1024,768]{1,0:T(8,128)(2,1)}, bf16[1024,768]{1,0:T(8,128)(2,1)}, u32[]{:S(2)}, u32[]{:S(2)}) collective-permute-start(bf16[1024,768]{1,0:T(8,128)(2,1)} %collective-permute-done.7.args_13_), channel_id=1, source_target_pairs={{0,1},{1,0},{2,3},{3,2},{4,5},{5,4},{6,7},{7,6},{8,9},{9,8},{10,11... | collective-permute-start | bytes 4718600 | tf_op jit(solution)/shard_map/ppermute | solution.py:19
  128.8 75.2 %copy-start.7 = (s32[8,8]{1,0:T(8,128)S(1)}, s32[8,8]{1,0:T(8,128)}, u32[]{:S(2)}) copy-start(s32[8,8]{1,0:T(8,128)} %param.10) | copy-start | bytes 772
  128.8 75.4 %copy-start.8 = (s32[2,7]{1,0:T(2,128)S(1)}, s32[2,7]{1,0:T(2,128)}, u32[]{:S(2)}) copy-start(s32[2,7]{1,0:T(2,128)} %constant.84.clone) | copy-start | bytes 172
  128.8 128.1 %all-to-all-start = ((bf16[128,8,768]{2,0,1:T(8,128)(2,1)}), bf16[128,8,768]{2,0,1:T(8,128)(2,1)S(1)}, u32[]{:S(2)}, u32[]{:S(2)}) async-start(bf16[128,8,768]{2,0,1:T(8,128)(2,1)} %bitcast.40), calls=%async_computation | async-start | bytes 3145728 | tf_op jit(solution)/shard_map/all_to_all | solution.py:104
  185.7 71.2 %collective-permute-start.10 = (bf16[1024,768]{1,0:T(8,128)(2,1)}, bf16[1024,768]{1,0:T(8,128)(2,1)}, u32[]{:S(2)}, u32[]{:S(2)}) collective-permute-start(bf16[1024,768]{1,0:T(8,128)(2,1)} %collective-permute-done.7.args_13_), channel_id=1, source_target_pairs={{1,2},{3,4},{5,6},{7,8},{9,10},{11,12},{13,14},{15,16},{17,18},{19... | collective-permute-start | bytes 4718600 | tf_op jit(solution)/shard_map/ppermute | solution.py:19
  187.0 69.9 %collective-permute-start.6 = (bf16[768,1024]{1,0:T(8,128)(2,1)}, bf16[768,1024]{1,0:T(8,128)(2,1)S(1)}, u32[]{:S(2)}, u32[]{:S(2)}) collective-permute-start(bf16[768,1024]{1,0:T(8,128)(2,1)} %collective-permute-done.1.args_6_), channel_id=1, source_target_pairs={{0,1},{1,0},{2,3},{3,2},{4,5},{5,4},{6,7},{7,6},{8,9},{9,8},{10,11... | collective-permute-start | bytes 4718600 | tf_op jit(solution)/shard_map/ppermute | solution.py:19
  188.2 68.7 %collective-permute-start.4 = (bf16[768,1024]{1,0:T(8,128)(2,1)}, bf16[768,1024]{1,0:T(8,128)(2,1)}, u32[]{:S(2)}, u32[]{:S(2)}) collective-permute-start(bf16[768,1024]{1,0:T(8,128)(2,1)} %collective-permute-done.1.args_6_), channel_id=1, source_target_pairs={{0,31},{2,1},{4,3},{6,5},{8,7},{10,9},{12,11},{14,13},{16,15},{18,... | collective-permute-start | bytes 4718600 | tf_op jit(solution)/shard_map/ppermute | solution.py:19
  202.7 54.3 %collective-permute-start.5 = (bf16[768,1024]{1,0:T(8,128)(2,1)}, bf16[768,1024]{1,0:T(8,128)(2,1)}, u32[]{:S(2)}, u32[]{:S(2)}) collective-permute-start(bf16[768,1024]{1,0:T(8,128)(2,1)} %collective-permute-done.args_5_), channel_id=1, source_target_pairs={{0,1},{1,0},{2,3},{3,2},{4,5},{5,4},{6,7},{7,6},{8,9},{9,8},{10,11... | collective-permute-start | bytes 4718600 | tf_op jit(solution)/shard_map/ppermute | solution.py:19
  202.7 69.5 %collective-permute-start.3 = (bf16[768,1024]{1,0:T(8,128)(2,1)}, bf16[768,1024]{1,0:T(8,128)(2,1)}, u32[]{:S(2)}, u32[]{:S(2)}) collective-permute-start(bf16[768,1024]{1,0:T(8,128)(2,1)} %collective-permute-done.args_5_), channel_id=1, source_target_pairs={{1,2},{3,4},{5,6},{7,8},{9,10},{11,12},{13,14},{15,16},{17,18},{19... | collective-permute-start | bytes 4718600 | tf_op jit(solution)/shard_map/ppermute | solution.py:19
  256.9 15.2 %copy-start.3 = (bf16[128,8,768]{2,0,1:T(8,128)(2,1)}, bf16[128,8,768]{2,0,1:T(8,128)(2,1)S(1)}, u32[]{:S(2)}) copy-start(bf16[128,8,768]{2,0,1:T(8,128)(2,1)S(1)} %all-to-all-done) | copy-start | bytes 4718596
  256.9 15.2 %copy-start.5 = (bf16[768,1024]{1,0:T(8,128)(2,1)}, bf16[768,1024]{1,0:T(8,128)(2,1)S(1)}, u32[]{:S(2)}) copy-start(bf16[768,1024]{1,0:T(8,128)(2,1)S(1)} %collective-permute-done.6.args_11_) | copy-start | bytes 4718596
  (2 other events, 7.1 us)

commit v7 on v6

--- a/solution.py
+++ b/solution.py
@@ -97,11 +97,12 @@
     cycle_size = lax.axis_size("blk")
     group_size = lax.axis_size("head")
     heads_local = H // group_size
+    q_heads = lax.all_to_all(queries, "head", split_axis=1, concat_axis=0, tiled=True)
+    q_heads, key_states = lax.optimization_barrier((q_heads, key_states))
     k_heads = lax.all_to_all(key_states, "head", split_axis=1, concat_axis=0, tiled=True)
     k_window = exchange(k_heads.T, 1, cycle_size)
     v_heads = lax.all_to_all(value_states, "head", split_axis=1, concat_axis=0, tiled=True)
     v_window = exchange(v_heads, 0, cycle_size)
-    q_heads = lax.all_to_all(queries, "head", split_axis=1, concat_axis=0, tiled=True)
     shard_tok = q_heads.shape[0]
     tile_count = shard_tok // TILE
     width = heads_local * DH

time: 335 us -> 367 us (1.096)
  the two profiles are of different devices: /device:TPU:64 before, /device:TPU:128 now
where the time goes in v7:
time: 367 us
  waiting for transfers between devices  269 us (73%)
  starting transfers between devices  39.7 us (11%)
  Pallas kernels  24.5 us (7%)
  blocking collectives  18.6 us (5%)
  local copies, waits for them, and re-layouts  14.2 us (4%)
    ppermute x14, waiting for transfers between devices, permute(): return lax.ppermute(block, axis, route)  147 us
    all_to_all x1, waiting for transfers between devices, body(): lax.all_to_all(queries, 'head', split_axis=1, concat_axis=0, tiled=True)  53.6 us
    all_to_all x1, waiting for transfers between devices, body(): lax.all_to_all(key_states, 'head', split_axis=1, concat_axis=0, tiled=True)  48.3 us
    ppermute x14, starting transfers between devices, permute(): return lax.ppermute(block, axis, route)  26.8 us
    pallas_call x1, Pallas kernels, body(): pl.pallas_call(kernel, grid_spec=grid_spec, out_shape=jax.ShapeDtypeStruc...  24.5 us
    all_to_all x1, waiting for transfers between devices, body(): lax.all_to_all(value_states, 'head', split_axis=1, concat_axis=0, tiled=T...  20.1 us
    all_to_all x1, blocking collectives, body(): return lax.all_to_all(out, 'head', split_axis=0, concat_axis=1, tiled=True)  18.6 us
  transfers between devices with their start and end apart: 17, of which 7 were waited for; matrix products, arithmetic and copies ran while one was open for 3% of the time, Pallas kernels for 0%

profile of v7, /device:TPU:128, one launch (start us, length us, event | category | flops | bytes accessed | tf_op | source)
XLA Modules:
  0.0 366.6 jit_solution(15722438066762288081)
XLA Ops:
  0.0 2.7 copy.30
  2.7 5.1 %all-to-all-start.2 = ((bf16[128,8,768]{2,0,1:T(8,128)(2,1)}), bf16[128,8,768]{2,0,1:T(8,128)(2,1)S(1)}, u32[]{:S(2)}, u32[]{:S(2)}) async-start(bf16[128,8,768]{2,0,1:T(8,128)(2,1)} %bitcast.33), calls=%async_computation.2 | async-start | bytes 3145728 | tf_op jit(solution)/shard_map/all_to_all | solution.py:104
  7.8 1.2 copy.31
  9.0 20.1 %all-to-all-done.2 = bf16[128,8,768]{2,0,1:T(8,128)(2,1)S(1)} async-done(((bf16[128,8,768]{2,0,1:T(8,128)(2,1)}), bf16[128,8,768]{2,0,1:T(8,128)(2,1)S(1)}, u32[]{:S(2)}, u32[]{:S(2)}) %all-to-all-start.2) | async-done | bytes 1572896 | tf_op jit(solution)/shard_map/all_to_all | solution.py:104
  29.1 3.6 all-to-all-start
  32.7 2.8 collective-permute-start.8
  35.5 53.6 %all-to-all-done = bf16[128,8,768]{2,0,1:T(8,128)(2,1)S(1)} async-done(((bf16[128,8,768]{2,0,1:T(8,128)(2,1)}), bf16[128,8,768]{2,0,1:T(8,128)(2,1)S(1)}, u32[]{:S(2)}, u32[]{:S(2)}) %all-to-all-start) | async-done | bytes 1572896 | tf_op jit(solution)/shard_map/all_to_all | solution.py:100
  89.2 3.2 copy.18
  92.3 4.3 %all-to-all-start.1 = ((bf16[128,8,768]{0,2,1:T(8,128)(2,1)}), bf16[128,8,768]{0,2,1:T(8,128)(2,1)}, u32[]{:S(2)}, u32[]{:S(2)}) async-start(bf16[128,8,768]{0,2,1:T(8,128)(2,1)} %bitcast.40), calls=%async_computation.1 | async-start | bytes 3145728 | tf_op jit(solution)/shard_map/all_to_all | solution.py:102
  97.3 8.9 %collective-permute-start.11 = (bf16[1024,768]{1,0:T(8,128)(2,1)}, bf16[1024,768]{1,0:T(8,128)(2,1)}, u32[]{:S(2)}, u32[]{:S(2)}) collective-permute-start(bf16[1024,768]{1,0:T(8,128)(2,1)} %collective-permute-done.8.args_14_), channel_id=1, source_target_pairs={{0,31},{2,1},{4,3},{6,5},{8,7},{10,9},{12,11},{14,13},{16,15},{18,... | collective-permute-start | bytes 4718600 | tf_op jit(solution)/shard_map/ppermute | solution.py:19
  106.2 48.3 %all-to-all-done.1 = bf16[128,8,768]{0,2,1:T(8,128)(2,1)} async-done(((bf16[128,8,768]{0,2,1:T(8,128)(2,1)}), bf16[128,8,768]{0,2,1:T(8,128)(2,1)}, u32[]{:S(2)}, u32[]{:S(2)}) %all-to-all-start.1) | async-done | bytes 1572896 | tf_op jit(solution)/shard_map/all_to_all | solution.py:102
  154.5 1.6 bitcast_bitcast_fusion.args_4_
  156.3 10.3 %collective-permute-done.7.args_13_ = bf16[1024,768]{1,0:T(8,128)(2,1)} collective-permute-done((bf16[1024,768]{1,0:T(8,128)(2,1)S(1)}, bf16[1024,768]{1,0:T(8,128)(2,1)}, u32[]{:S(2)}, u32[]{:S(2)}) %collective-permute-start.7) | collective-permute-done | bytes 1572896 | tf_op jit(solution)/shard_map/ppermute | solution.py:19
  166.6 1.3 collective-permute-start.10
  168.0 1.7 collective-permute-start.2
  169.6 65.4 %collective-permute-done.1.args_6_ = bf16[768,1024]{1,0:T(8,128)(2,1)} collective-permute-done((bf16[768,1024]{1,0:T(8,128)(2,1)S(1)}, bf16[768,1024]{1,0:T(8,128)(2,1)}, u32[]{:S(2)}, u32[]{:S(2)}) %collective-permute-start.1) | collective-permute-done | bytes 1572896 | tf_op jit(solution)/shard_map/ppermute | solution.py:19
  235.0 10.0 %collective-permute-start.4 = (bf16[768,1024]{1,0:T(8,128)(2,1)}, bf16[768,1024]{1,0:T(8,128)(2,1)}, u32[]{:S(2)}, u32[]{:S(2)}) collective-permute-start(bf16[768,1024]{1,0:T(8,128)(2,1)} %collective-permute-done.1.args_6_), channel_id=1, source_target_pairs={{0,31},{2,1},{4,3},{6,5},{8,7},{10,9},{12,11},{14,13},{16,15},{18,... | collective-permute-start | bytes 4718600 | tf_op jit(solution)/shard_map/ppermute | solution.py:19
  245.1 30.3 %collective-permute-done.10.args_16_ = bf16[1024,768]{1,0:T(8,128)(2,1)} collective-permute-done((bf16[1024,768]{1,0:T(8,128)(2,1)}, bf16[1024,768]{1,0:T(8,128)(2,1)}, u32[]{:S(2)}, u32[]{:S(2)}) %collective-permute-start.10) | collective-permute-done | bytes 1572896 | tf_op jit(solution)/shard_map/ppermute | solution.py:19
  275.4 1.3 collective-permute-start.3
  280.3 0.9 copy.21.args_2_
  281.1 41.0 %collective-permute-done.3.args_8_ = bf16[768,1024]{1,0:T(8,128)(2,1)} collective-permute-done((bf16[768,1024]{1,0:T(8,128)(2,1)S(1)}, bf16[768,1024]{1,0:T(8,128)(2,1)}, u32[]{:S(2)}, u32[]{:S(2)}) %collective-permute-start.3) | collective-permute-done | bytes 1572896 | tf_op jit(solution)/shard_map/ppermute | solution.py:19
  322.2 24.5 %shard_map.73 = bf16[1024,768]{1,0:T(8,128)(2,1)} custom-call(s32[64]{0:T(128)} %reshape.68.args_0_, s32[8]{0:T(128)} %args_1_.4, f32[8,6,1024]{2,1,0:T(8,128)} %copy.21.args_2_, bf16[1024,768]{1,0:T(8,128)(2,1)} %bitcast.39, bf16[768,1024]{1,0:T(8,128)(2,1)} %copy-done.3, bf16[768,1024]{1,0:T(8,128)(2,1)} %copy-done.4, ...), custom_call_target="tpu_custom_call" | custom-call | tf_op jit(solution)/shard_map/pallas_call | solution.py:149
  346.6 18.6 %all_to_all.76 = bf16[8,128,768]{2,1,0:T(8,128)(2,1)S(1)} all-to-all(bf16[8,128,768]{2,1,0:T(8,128)(2,1)} %bitcast.41), channel_id=1, replica_groups=mesh['head'=8,'blk'=32] {'head'}, dimensions={0} | all-to-all | bytes 3145728 | tf_op jit(solution)/shard_map/all_to_all | solution.py:162
  365.3 1.3 copy.26
  (55 shorter events, 4.3 us)
Async XLA Ops:
  0.0 278.4 %copy-start = (s32[256]{0:T(256)S(1)}, s32[256]{0:T(256)}, u32[]{:S(2)}) copy-start(s32[256]{0:T(256)} %param.12) | copy-start | bytes 3076
  2.7 5.1 %copy-start.5 = (bf16[128,6144]{1,0:T(8,128)(2,1)S(1)}, bf16[128,6144]{1,0:T(8,128)(2,1)}, u32[]{:S(2)}) copy-start(bf16[128,6144]{1,0:T(8,128)(2,1)} %param.7) | copy-start | bytes 4718596
  2.7 26.4 %all-to-all-start.2 = ((bf16[128,8,768]{2,0,1:T(8,128)(2,1)}), bf16[128,8,768]{2,0,1:T(8,128)(2,1)S(1)}, u32[]{:S(2)}, u32[]{:S(2)}) async-start(bf16[128,8,768]{2,0,1:T(8,128)(2,1)} %bitcast.33), calls=%async_computation.2 | async-start | bytes 3145728 | tf_op jit(solution)/shard_map/all_to_all | solution.py:104
  29.1 67.6 %copy-start.1 = (bf16[128,8,768]{2,0,1:T(8,128)(2,1)}, bf16[128,8,768]{2,0,1:T(8,128)(2,1)S(1)}, u32[]{:S(2)}) copy-start(bf16[128,8,768]{2,0,1:T(8,128)(2,1)S(1)} %all-to-all-done.2) | copy-start | bytes 4718596
  29.1 60.0 %all-to-all-start = ((bf16[128,8,768]{2,0,1:T(8,128)(2,1)}), bf16[128,8,768]{2,0,1:T(8,128)(2,1)S(1)}, u32[]{:S(2)}, u32[]{:S(2)}) async-start(bf16[128,8,768]{2,0,1:T(8,128)(2,1)} %bitcast.42), calls=%async_computation | async-start | bytes 3145728 | tf_op jit(solution)/shard_map/all_to_all | solution.py:100
  32.7 64.1 %collective-permute-start.8 = (bf16[1024,768]{1,0:T(8,128)(2,1)S(1)}, bf16[1024,768]{1,0:T(8,128)(2,1)}, u32[]{:S(2)}, u32[]{:S(2)}) collective-permute-start(bf16[1024,768]{1,0:T(8,128)(2,1)S(1)} %bitcast.35), channel_id=1, source_target_pairs={{0,30},{1,31},{2,0},{3,1},{4,2},{5,3},{6,4},{7,5},{8,6},{9,7},{10,... | collective-permute-start | bytes 4718600 | tf_op jit(solution)/shard_map/ppermute | solution.py:19
  92.3 62.2 %all-to-all-start.1 = ((bf16[128,8,768]{0,2,1:T(8,128)(2,1)}), bf16[128,8,768]{0,2,1:T(8,128)(2,1)}, u32[]{:S(2)}, u32[]{:S(2)}) async-start(bf16[128,8,768]{0,2,1:T(8,128)(2,1)} %bitcast.40), calls=%async_computation.1 | async-start | bytes 3145728 | tf_op jit(solution)/shard_map/all_to_all | solution.py:102
  96.6 180.1 %copy-start.6 = (s32[8,8]{1,0:T(8,128)S(1)}, s32[8,8]{1,0:T(8,128)}, u32[]{:S(2)}) copy-start(s32[8,8]{1,0:T(8,128)} %param.10) | copy-start | bytes 772
  96.6 180.3 %copy-start.7 = (s32[2,7]{1,0:T(2,128)S(1)}, s32[2,7]{1,0:T(2,128)}, u32[]{:S(2)}) copy-start(s32[2,7]{1,0:T(2,128)} %constant.84.clone) | copy-start | bytes 172
  96.6 70.0 %collective-permute-start.7 = (bf16[1024,768]{1,0:T(8,128)(2,1)S(1)}, bf16[1024,768]{1,0:T(8,128)(2,1)}, u32[]{:S(2)}, u32[]{:S(2)}) collective-permute-start(bf16[1024,768]{1,0:T(8,128)(2,1)S(1)} %bitcast.36), channel_id=1, source_target_pairs={{0,2},{1,3},{2,4},{3,5},{4,6},{5,7},{6,8},{7,9},{8,10},{9,11},{10,... | collective-permute-start | bytes 4718600 | tf_op jit(solution)/shard_map/ppermute | solution.py:19
  96.7 69.9 %collective-permute-start.9 = (bf16[1024,768]{1,0:T(8,128)(2,1)S(1)}, bf16[1024,768]{1,0:T(8,128)(2,1)}, u32[]{:S(2)}, u32[]{:S(2)}) collective-permute-start(bf16[1024,768]{1,0:T(8,128)(2,1)S(1)} %bitcast.37), channel_id=1, source_target_pairs={{0,1},{1,0},{2,3},{3,2},{4,5},{5,4},{6,7},{7,6},{8,9},{9,8},{10,11... | collective-permute-start | bytes 4718600 | tf_op jit(solution)/shard_map/ppermute | solution.py:19
  96.9 69.8 %collective-permute-start.13 = (bf16[1024,768]{1,0:T(8,128)(2,1)}, bf16[1024,768]{1,0:T(8,128)(2,1)}, u32[]{:S(2)}, u32[]{:S(2)}) collective-permute-start(bf16[1024,768]{1,0:T(8,128)(2,1)} %collective-permute-done.8.args_14_), channel_id=1, source_target_pairs={{0,1},{1,0},{2,3},{3,2},{4,5},{5,4},{6,7},{7,6},{8,9},{9,8},{10,11... | collective-permute-start | bytes 4718600 | tf_op jit(solution)/shard_map/ppermute | solution.py:19
  97.3 70.6 %collective-permute-start.11 = (bf16[1024,768]{1,0:T(8,128)(2,1)}, bf16[1024,768]{1,0:T(8,128)(2,1)}, u32[]{:S(2)}, u32[]{:S(2)}) collective-permute-start(bf16[1024,768]{1,0:T(8,128)(2,1)} %collective-permute-done.8.args_14_), channel_id=1, source_target_pairs={{0,31},{2,1},{4,3},{6,5},{8,7},{10,9},{12,11},{14,13},{16,15},{18,... | collective-permute-start | bytes 4718600 | tf_op jit(solution)/shard_map/ppermute | solution.py:19
  156.2 121.5 %copy-start.3 = (bf16[768,1024]{1,0:T(8,128)(2,1)}, bf16[768,1024]{1,0:T(8,128)(2,1)S(1)}, u32[]{:S(2)}) copy-start(bf16[768,1024]{1,0:T(8,128)(2,1)S(1)} %bitcast_bitcast_fusion.args_4_) | copy-start | bytes 4718596
  156.2 78.8 %collective-permute-start.1 = (bf16[768,1024]{1,0:T(8,128)(2,1)S(1)}, bf16[768,1024]{1,0:T(8,128)(2,1)}, u32[]{:S(2)}, u32[]{:S(2)}) collective-permute-start(bf16[768,1024]{1,0:T(8,128)(2,1)S(1)} %bitcast_bitcast_fusion.args_4_), channel_id=1, source_target_pairs={{0,30},{1,31},{2,0},{3,1},{4,2},{5,3},{6,4},{7,5},{8,6},{9,7},{10,... | collective-permute-start | bytes 4718600 | tf_op jit(solution)/shard_map/ppermute | solution.py:19
  166.6 68.4 %collective-permute-start.12 = (bf16[1024,768]{1,0:T(8,128)(2,1)}, bf16[1024,768]{1,0:T(8,128)(2,1)}, u32[]{:S(2)}, u32[]{:S(2)}) collective-permute-start(bf16[1024,768]{1,0:T(8,128)(2,1)} %collective-permute-done.7.args_13_), channel_id=1, source_target_pairs={{0,1},{1,0},{2,3},{3,2},{4,5},{5,4},{6,7},{7,6},{8,9},{9,8},{10,11... | collective-permute-start | bytes 4718600 | tf_op jit(solution)/shard_map/ppermute | solution.py:19
  166.6 78.4 %collective-permute-start = (bf16[768,1024]{1,0:T(8,128)(2,1)S(1)}, bf16[768,1024]{1,0:T(8,128)(2,1)S(1)}, u32[]{:S(2)}, u32[]{:S(2)}) collective-permute-start(bf16[768,1024]{1,0:T(8,128)(2,1)S(1)} %bitcast_bitcast_fusion.args_4_), channel_id=1, source_target_pairs={{0,2},{1,3},{2,4},{3,5},{4,6},{5,7},{6,8},{7,9},{8,10},{9,11},{10,... | collective-permute-start | bytes 4718600 | tf_op jit(solution)/shard_map/ppermute | solution.py:19
  166.6 108.7 %collective-permute-start.10 = (bf16[1024,768]{1,0:T(8,128)(2,1)}, bf16[1024,768]{1,0:T(8,128)(2,1)}, u32[]{:S(2)}, u32[]{:S(2)}) collective-permute-start(bf16[1024,768]{1,0:T(8,128)(2,1)} %collective-permute-done.7.args_13_), channel_id=1, source_target_pairs={{1,2},{3,4},{5,6},{7,8},{9,10},{11,12},{13,14},{15,16},{17,18},{19... | collective-permute-start | bytes 4718600 | tf_op jit(solution)/shard_map/ppermute | solution.py:19
  168.0 113.2 %collective-permute-start.2 = (bf16[768,1024]{1,0:T(8,128)(2,1)S(1)}, bf16[768,1024]{1,0:T(8,128)(2,1)}, u32[]{:S(2)}, u32[]{:S(2)}) collective-permute-start(bf16[768,1024]{1,0:T(8,128)(2,1)S(1)} %bitcast_bitcast_fusion.args_4_), channel_id=1, source_target_pairs={{0,1},{1,0},{2,3},{3,2},{4,5},{5,4},{6,7},{7,6},{8,9},{9,8},{10,11... | collective-permute-start | bytes 4718600 | tf_op jit(solution)/shard_map/ppermute | solution.py:19
  235.0 46.1 %collective-permute-start.6 = (bf16[768,1024]{1,0:T(8,128)(2,1)}, bf16[768,1024]{1,0:T(8,128)(2,1)}, u32[]{:S(2)}, u32[]{:S(2)}) collective-permute-start(bf16[768,1024]{1,0:T(8,128)(2,1)} %collective-permute-done.1.args_6_), channel_id=1, source_target_pairs={{0,1},{1,0},{2,3},{3,2},{4,5},{5,4},{6,7},{7,6},{8,9},{9,8},{10,11... | collective-permute-start | bytes 4718600 | tf_op jit(solution)/shard_map/ppermute | solution.py:19
  235.0 46.1 %collective-permute-start.4 = (bf16[768,1024]{1,0:T(8,128)(2,1)}, bf16[768,1024]{1,0:T(8,128)(2,1)}, u32[]{:S(2)}, u32[]{:S(2)}) collective-permute-start(bf16[768,1024]{1,0:T(8,128)(2,1)} %collective-permute-done.1.args_6_), channel_id=1, source_target_pairs={{0,31},{2,1},{4,3},{6,5},{8,7},{10,9},{12,11},{14,13},{16,15},{18,... | collective-permute-start | bytes 4718600 | tf_op jit(solution)/shard_map/ppermute | solution.py:19
  245.1 32.6 %copy-start.4 = (bf16[768,1024]{1,0:T(8,128)(2,1)}, bf16[768,1024]{1,0:T(8,128)(2,1)S(1)}, u32[]{:S(2)}) copy-start(bf16[768,1024]{1,0:T(8,128)(2,1)S(1)} %collective-permute-done.args_5_) | copy-start | bytes 4718596
  245.1 36.1 %collective-permute-start.5 = (bf16[768,1024]{1,0:T(8,128)(2,1)S(1)}, bf16[768,1024]{1,0:T(8,128)(2,1)}, u32[]{:S(2)}, u32[]{:S(2)}) collective-permute-start(bf16[768,1024]{1,0:T(8,128)(2,1)S(1)} %collective-permute-done.args_5_), channel_id=1, source_target_pairs={{0,1},{1,0},{2,3},{3,2},{4,5},{5,4},{6,7},{7,6},{8,9},{9,8},{10,11... | collective-permute-start | bytes 4718600 | tf_op jit(solution)/shard_map/ppermute | solution.py:19
  275.4 46.8 %collective-permute-start.3 = (bf16[768,1024]{1,0:T(8,128)(2,1)S(1)}, bf16[768,1024]{1,0:T(8,128)(2,1)}, u32[]{:S(2)}, u32[]{:S(2)}) collective-permute-start(bf16[768,1024]{1,0:T(8,128)(2,1)S(1)} %collective-permute-done.args_5_), channel_id=1, source_target_pairs={{1,2},{3,4},{5,6},{7,8},{9,10},{11,12},{13,14},{15,16},{17,18},{19... | collective-permute-start | bytes 4718600 | tf_op jit(solution)/shard_map/ppermute | solution.py:19
  (1 other events, 3.2 us)

commit v8 on v6

--- a/solution.py
+++ b/solution.py
@@ -97,11 +97,10 @@
     cycle_size = lax.axis_size("blk")
     group_size = lax.axis_size("head")
     heads_local = H // group_size
-    k_heads = lax.all_to_all(key_states, "head", split_axis=1, concat_axis=0, tiled=True)
+    stacked = jnp.stack((queries, key_states, value_states))
+    q_heads, k_heads, v_heads = lax.all_to_all(stacked, "head", split_axis=2, concat_axis=1, tiled=True)
     k_window = exchange(k_heads.T, 1, cycle_size)
-    v_heads = lax.all_to_all(value_states, "head", split_axis=1, concat_axis=0, tiled=True)
     v_window = exchange(v_heads, 0, cycle_size)
-    q_heads = lax.all_to_all(queries, "head", split_axis=1, concat_axis=0, tiled=True)
     shard_tok = q_heads.shape[0]
     tile_count = shard_tok // TILE
     width = heads_local * DH

time: 335 us -> 378 us (1.13)
  the two profiles are of different devices: /device:TPU:64 before, /device:TPU:6 now
where the time goes in v8:
time: 378 us; the launch traced here: 377 us
  waiting for transfers between devices  144 us (38%)
  blocking collectives  139 us (37%)
  local copies, waits for them, and re-layouts  33.7 us (9%)
  starting transfers between devices  30.9 us (8%)
  Pallas kernels  24.8 us (7%)
  other arithmetic  5.32 us (1%)
    ppermute x14, waiting for transfers between devices, permute(): return lax.ppermute(block, axis, route)  144 us
    all_to_all x1, blocking collectives, body(): lax.all_to_all(stacked, 'head', split_axis=2, concat_axis=1, tiled=True)  79 us
    all_to_all x1, blocking collectives, body(): return lax.all_to_all(out, 'head', split_axis=0, concat_axis=1, tiled=True)  59.6 us
    ppermute x14, starting transfers between devices, permute(): return lax.ppermute(block, axis, route)  30.9 us
    pallas_call x1, Pallas kernels, body(): pl.pallas_call(kernel, grid_spec=grid_spec, out_shape=jax.ShapeDtypeStruc...  24.8 us
    all_to_all x1, local copies, waits for them, and re-layouts, body(): lax.all_to_all(stacked, 'head', split_axis=2, concat_axis=1, tiled=True)  10.2 us
    another operation x1, local copies, waits for them, and re-layouts, body(): stacked = jnp.stack((queries, key_states, value_states))  10.1 us
  transfers between devices with their start and end apart: 14, of which 4 were waited for; matrix products, arithmetic and copies ran while one was open for 1% of the time, Pallas kernels for 0%

profile of v8, /device:TPU:6, one launch (start us, length us, event | category | flops | bytes accessed | tf_op | source)
XLA Modules:
  0.0 377.1 jit_solution(14559420218987862207)
XLA Ops:
  0.0 5.1 %pad_maximum_fusion = bf16[3,128,6144]{2,1,0:T(8,128)(2,1)} fusion(bf16[1,128,6144]{2,1,0:T(8,128)(2,1)} %bitcast.35, bf16[1,128,6144]{2,1,0:T(8,128)(2,1)} %bitcast.36, bf16[1,128,6144]{2,1,0:T(8,128)(2,1)} %bitcast.37), kind=kLoop, calls=%fused_computation.3 | loop fusion | flops 4718592 | bytes 9437184 | tf_op jit(solution)/shard_map/stack | solution.py:100
  5.1 10.1 %copy.22 = bf16[3,128,6144]{1,0,2:T(4,128)(2,1)} copy(bf16[3,128,6144]{2,1,0:T(8,128)(2,1)} %pad_maximum_fusion) | data formatting | bytes 9437184 | tf_op jit(solution)/shard_map/stack | solution.py:100
  15.3 79.0 %all_to_all.34 = bf16[3,128,6144]{1,0,2:T(4,128)(2,1)} all-to-all(bf16[3,128,6144]{1,0,2:T(4,128)(2,1)} %copy.22), channel_id=1, replica_groups=mesh['head'=8,'blk'=32] {'head'}, dimensions={2} | all-to-all | bytes 9437184 | tf_op jit(solution)/shard_map/all_to_all | solution.py:101
  94.3 10.2 %copy.23 = bf16[3,128,8,768]{3,1,2,0:T(8,128)(2,1)} copy(bf16[3,128,8,768]{1,0,3,2:T(4,128)(2,1)} %bitcast.21) | data formatting | bytes 9437184 | tf_op jit(solution)/shard_map/all_to_all | solution.py:101
  104.4 4.5 %fusion.7 = (bf16[1,8,128,768]{3,2,1,0:T(8,128)(2,1)S(1)}, bf16[1,8,128,768]{3,2,1,0:T(8,128)(2,1)}, bf16[1,8,128,768]{3,2,1,0:T(8,128)(2,1)}) fusion(bf16[3,8,128,768]{3,2,1,0:T(8,128)(2,1)} %bitcast.22), kind=kLoop, calls=%fused_computation.31 | loop fusion | bytes 9437184 | tf_op jit(solution)/shard_map/unstack | solution.py:101
  109.0 2.3 copy.27
  111.4 0.9 collective-permute-start.1
  112.3 4.2 %collective-permute-start = (bf16[768,1024]{1,0:T(8,128)(2,1)S(1)}, bf16[768,1024]{1,0:T(8,128)(2,1)}, u32[]{:S(2)}, u32[]{:S(2)}) collective-permute-start(bf16[768,1024]{1,0:T(8,128)(2,1)S(1)} %bitcast.30), channel_id=1, source_target_pairs={{0,2},{1,3},{2,4},{3,5},{4,6},{5,7},{6,8},{7,9},{8,10},{9,11},{10,... | collective-permute-start | bytes 4718600 | tf_op jit(solution)/shard_map/ppermute | solution.py:19
  116.5 5.1 %collective-permute-start.7 = (bf16[1024,768]{1,0:T(8,128)(2,1)S(1)}, bf16[1024,768]{1,0:T(8,128)(2,1)}, u32[]{:S(2)}, u32[]{:S(2)}) collective-permute-start(bf16[1024,768]{1,0:T(8,128)(2,1)S(1)} %bitcast.25), channel_id=1, source_target_pairs={{0,2},{1,3},{2,4},{3,5},{4,6},{5,7},{6,8},{7,9},{8,10},{9,11},{10,... | collective-permute-start | bytes 4718600 | tf_op jit(solution)/shard_map/ppermute | solution.py:19
  121.6 97.0 %collective-permute-done.1.args_6_ = bf16[768,1024]{1,0:T(8,128)(2,1)} collective-permute-done((bf16[768,1024]{1,0:T(8,128)(2,1)S(1)}, bf16[768,1024]{1,0:T(8,128)(2,1)}, u32[]{:S(2)}, u32[]{:S(2)}) %collective-permute-start.1) | collective-permute-done | bytes 1572896 | tf_op jit(solution)/shard_map/ppermute | solution.py:19
  218.6 2.5 collective-permute-start.4
  221.1 1.2 copy-done.4
  222.3 30.2 %collective-permute-done.8.args_14_ = bf16[1024,768]{1,0:T(8,128)(2,1)} collective-permute-done((bf16[1024,768]{1,0:T(8,128)(2,1)S(1)}, bf16[1024,768]{1,0:T(8,128)(2,1)}, u32[]{:S(2)}, u32[]{:S(2)}) %collective-permute-start.8) | collective-permute-done | bytes 1572896 | tf_op jit(solution)/shard_map/ppermute | solution.py:19
  252.5 1.3 collective-permute-start.3
  253.8 1.3 collective-permute-start.13
  255.1 5.3 %collective-permute-start.11 = (bf16[1024,768]{1,0:T(8,128)(2,1)}, bf16[1024,768]{1,0:T(8,128)(2,1)}, u32[]{:S(2)}, u32[]{:S(2)}) collective-permute-start(bf16[1024,768]{1,0:T(8,128)(2,1)} %collective-permute-done.8.args_14_), channel_id=1, source_target_pairs={{0,31},{2,1},{4,3},{6,5},{8,7},{10,9},{12,11},{14,13},{16,15},{18,... | collective-permute-start | bytes 4718600 | tf_op jit(solution)/shard_map/ppermute | solution.py:19
  260.4 8.9 %collective-permute-start.12 = (bf16[1024,768]{1,0:T(8,128)(2,1)}, bf16[1024,768]{1,0:T(8,128)(2,1)}, u32[]{:S(2)}, u32[]{:S(2)}) collective-permute-start(bf16[1024,768]{1,0:T(8,128)(2,1)} %collective-permute-done.7.args_13_), channel_id=1, source_target_pairs={{0,1},{1,0},{2,3},{3,2},{4,5},{5,4},{6,7},{7,6},{8,9},{9,8},{10,11... | collective-permute-start | bytes 4718600 | tf_op jit(solution)/shard_map/ppermute | solution.py:19
  269.3 1.3 collective-permute-start.10
  274.2 0.8 copy.25.args_2_
  275.0 2.4 collective-permute-done.11.args_17_
  277.4 13.9 %collective-permute-done.10.args_16_ = bf16[1024,768]{1,0:T(8,128)(2,1)} collective-permute-done((bf16[1024,768]{1,0:T(8,128)(2,1)}, bf16[1024,768]{1,0:T(8,128)(2,1)}, u32[]{:S(2)}, u32[]{:S(2)}) %collective-permute-start.10) | collective-permute-done | bytes 1572896 | tf_op jit(solution)/shard_map/ppermute | solution.py:19
  291.4 24.8 %shard_map.73 = bf16[1024,768]{1,0:T(8,128)(2,1)} custom-call(s32[64]{0:T(128)} %reshape.65.args_0_, s32[8]{0:T(128)} %args_1_.4, f32[8,6,1024]{2,1,0:T(8,128)} %copy.25.args_2_, bf16[1024,768]{1,0:T(8,128)(2,1)} %bitcast.27, bf16[768,1024]{1,0:T(8,128)(2,1)} %bitcast.31, bf16[768,1024]{1,0:T(8,128)(2,1)} %collective-permute-done.args_5_, ...), custom_call_target="tpu_custom_call" | custom-call | tf_op jit(solution)/shard_map/pallas_call | solution.py:147
  316.2 59.6 %all_to_all.35 = bf16[8,128,768]{2,1,0:T(8,128)(2,1)S(1)} all-to-all(bf16[8,128,768]{2,1,0:T(8,128)(2,1)} %bitcast.32), channel_id=1, replica_groups=mesh['head'=8,'blk'=32] {'head'}, dimensions={0} | all-to-all | bytes 3145728 | tf_op jit(solution)/shard_map/all_to_all | solution.py:160
  375.8 1.3 copy.28
  (51 shorter events, 3.7 us)
Async XLA Ops:
  0.0 272.3 %copy-start = (s32[256]{0:T(256)S(1)}, s32[256]{0:T(256)}, u32[]{:S(2)}) copy-start(s32[256]{0:T(256)} %param.12) | copy-start | bytes 3076
  108.9 7.6 %copy-start.1 = (bf16[1,8,128,768]{3,2,1,0:T(8,128)(2,1)}, bf16[1,8,128,768]{3,2,1,0:T(8,128)(2,1)S(1)}, u32[]{:S(2)}) copy-start(bf16[1,8,128,768]{3,2,1,0:T(8,128)(2,1)S(1)} %get-tuple-element.5) | copy-start | bytes 4718596
  108.9 161.6 %copy-start.6 = (s32[8,8]{1,0:T(8,128)S(1)}, s32[8,8]{1,0:T(8,128)}, u32[]{:S(2)}) copy-start(s32[8,8]{1,0:T(8,128)} %param.10) | copy-start | bytes 772
  109.0 161.8 %copy-start.7 = (s32[2,7]{1,0:T(2,128)S(1)}, s32[2,7]{1,0:T(2,128)}, u32[]{:S(2)}) copy-start(s32[2,7]{1,0:T(2,128)} %constant.84.clone) | copy-start | bytes 172
  111.3 160.3 %copy-start.2 = (bf16[1024,768]{0,1:T(8,128)(2,1)}, bf16[1024,768]{0,1:T(8,128)(2,1)S(1)}, u32[]{:S(2)}) copy-start(bf16[1024,768]{0,1:T(8,128)(2,1)S(1)} %copy.27) | copy-start | bytes 4718596
  111.3 5.2 %collective-permute-start.2 = (bf16[768,1024]{1,0:T(8,128)(2,1)S(1)}, bf16[768,1024]{1,0:T(8,128)(2,1)S(1)}, u32[]{:S(2)}, u32[]{:S(2)}) collective-permute-start(bf16[768,1024]{1,0:T(8,128)(2,1)S(1)} %bitcast.28), channel_id=1, source_target_pairs={{0,1},{1,0},{2,3},{3,2},{4,5},{5,4},{6,7},{7,6},{8,9},{9,8},{10,11... | collective-permute-start | bytes 4718600 | tf_op jit(solution)/shard_map/ppermute | solution.py:19
  111.4 107.2 %collective-permute-start.1 = (bf16[768,1024]{1,0:T(8,128)(2,1)S(1)}, bf16[768,1024]{1,0:T(8,128)(2,1)}, u32[]{:S(2)}, u32[]{:S(2)}) collective-permute-start(bf16[768,1024]{1,0:T(8,128)(2,1)S(1)} %bitcast.29), channel_id=1, source_target_pairs={{0,30},{1,31},{2,0},{3,1},{4,2},{5,3},{6,4},{7,5},{8,6},{9,7},{10,... | collective-permute-start | bytes 4718600 | tf_op jit(solution)/shard_map/ppermute | solution.py:19
  112.3 106.3 %collective-permute-start = (bf16[768,1024]{1,0:T(8,128)(2,1)S(1)}, bf16[768,1024]{1,0:T(8,128)(2,1)}, u32[]{:S(2)}, u32[]{:S(2)}) collective-permute-start(bf16[768,1024]{1,0:T(8,128)(2,1)S(1)} %bitcast.30), channel_id=1, source_target_pairs={{0,2},{1,3},{2,4},{3,5},{4,6},{5,7},{6,8},{7,9},{8,10},{9,11},{10,... | collective-permute-start | bytes 4718600 | tf_op jit(solution)/shard_map/ppermute | solution.py:19
  116.5 104.6 %collective-permute-start.9 = (bf16[1024,768]{1,0:T(8,128)(2,1)S(1)}, bf16[1024,768]{1,0:T(8,128)(2,1)S(1)}, u32[]{:S(2)}, u32[]{:S(2)}) collective-permute-start(bf16[1024,768]{1,0:T(8,128)(2,1)S(1)} %bitcast.23), channel_id=1, source_target_pairs={{0,1},{1,0},{2,3},{3,2},{4,5},{5,4},{6,7},{7,6},{8,9},{9,8},{10,11... | collective-permute-start | bytes 4718600 | tf_op jit(solution)/shard_map/ppermute | solution.py:19
  116.5 136.0 %collective-permute-start.8 = (bf16[1024,768]{1,0:T(8,128)(2,1)S(1)}, bf16[1024,768]{1,0:T(8,128)(2,1)}, u32[]{:S(2)}, u32[]{:S(2)}) collective-permute-start(bf16[1024,768]{1,0:T(8,128)(2,1)S(1)} %bitcast.24), channel_id=1, source_target_pairs={{0,30},{1,31},{2,0},{3,1},{4,2},{5,3},{6,4},{7,5},{8,6},{9,7},{10,... | collective-permute-start | bytes 4718600 | tf_op jit(solution)/shard_map/ppermute | solution.py:19
  116.5 104.6 %copy-start.3 = (bf16[768,1024]{1,0:T(8,128)(2,1)}, bf16[768,1024]{1,0:T(8,128)(2,1)S(1)}, u32[]{:S(2)}) copy-start(bf16[768,1024]{1,0:T(8,128)(2,1)S(1)} %collective-permute-done.2.args_7_) | copy-start | bytes 4718596
  116.5 137.2 %collective-permute-start.7 = (bf16[1024,768]{1,0:T(8,128)(2,1)S(1)}, bf16[1024,768]{1,0:T(8,128)(2,1)}, u32[]{:S(2)}, u32[]{:S(2)}) collective-permute-start(bf16[1024,768]{1,0:T(8,128)(2,1)S(1)} %bitcast.25), channel_id=1, source_target_pairs={{0,2},{1,3},{2,4},{3,5},{4,6},{5,7},{6,8},{7,9},{8,10},{9,11},{10,... | collective-permute-start | bytes 4718600 | tf_op jit(solution)/shard_map/ppermute | solution.py:19
  218.6 36.5 %collective-permute-start.6 = (bf16[768,1024]{1,0:T(8,128)(2,1)}, bf16[768,1024]{1,0:T(8,128)(2,1)}, u32[]{:S(2)}, u32[]{:S(2)}) collective-permute-start(bf16[768,1024]{1,0:T(8,128)(2,1)} %collective-permute-done.1.args_6_), channel_id=1, source_target_pairs={{0,1},{1,0},{2,3},{3,2},{4,5},{5,4},{6,7},{7,6},{8,9},{9,8},{10,11... | collective-permute-start | bytes 4718600 | tf_op jit(solution)/shard_map/ppermute | solution.py:19
  218.6 41.8 %collective-permute-start.4 = (bf16[768,1024]{1,0:T(8,128)(2,1)}, bf16[768,1024]{1,0:T(8,128)(2,1)}, u32[]{:S(2)}, u32[]{:S(2)}) collective-permute-start(bf16[768,1024]{1,0:T(8,128)(2,1)} %collective-permute-done.1.args_6_), channel_id=1, source_target_pairs={{0,31},{2,1},{4,3},{6,5},{8,7},{10,9},{12,11},{14,13},{16,15},{18,... | collective-permute-start | bytes 4718600 | tf_op jit(solution)/shard_map/ppermute | solution.py:19
  221.1 1.2 copy-start.4
  221.1 48.1 %collective-permute-start.5 = (bf16[768,1024]{1,0:T(8,128)(2,1)}, bf16[768,1024]{1,0:T(8,128)(2,1)}, u32[]{:S(2)}, u32[]{:S(2)}) collective-permute-start(bf16[768,1024]{1,0:T(8,128)(2,1)} %collective-permute-done.args_5_), channel_id=1, source_target_pairs={{0,1},{1,0},{2,3},{3,2},{4,5},{5,4},{6,7},{7,6},{8,9},{9,8},{10,11... | collective-permute-start | bytes 4718600 | tf_op jit(solution)/shard_map/ppermute | solution.py:19
  252.5 22.5 %collective-permute-start.3 = (bf16[768,1024]{1,0:T(8,128)(2,1)}, bf16[768,1024]{1,0:T(8,128)(2,1)}, u32[]{:S(2)}, u32[]{:S(2)}) collective-permute-start(bf16[768,1024]{1,0:T(8,128)(2,1)} %collective-permute-done.args_5_), channel_id=1, source_target_pairs={{1,2},{3,4},{5,6},{7,8},{9,10},{11,12},{13,14},{15,16},{17,18},{19... | collective-permute-start | bytes 4718600 | tf_op jit(solution)/shard_map/ppermute | solution.py:19
  253.8 21.2 %collective-permute-start.13 = (bf16[1024,768]{1,0:T(8,128)(2,1)}, bf16[1024,768]{1,0:T(8,128)(2,1)S(1)}, u32[]{:S(2)}, u32[]{:S(2)}) collective-permute-start(bf16[1024,768]{1,0:T(8,128)(2,1)} %collective-permute-done.8.args_14_), channel_id=1, source_target_pairs={{0,1},{1,0},{2,3},{3,2},{4,5},{5,4},{6,7},{7,6},{8,9},{9,8},{10,11... | collective-permute-start | bytes 4718600 | tf_op jit(solution)/shard_map/ppermute | solution.py:19
  255.1 22.3 %collective-permute-start.11 = (bf16[1024,768]{1,0:T(8,128)(2,1)}, bf16[1024,768]{1,0:T(8,128)(2,1)}, u32[]{:S(2)}, u32[]{:S(2)}) collective-permute-start(bf16[1024,768]{1,0:T(8,128)(2,1)} %collective-permute-done.8.args_14_), channel_id=1, source_target_pairs={{0,31},{2,1},{4,3},{6,5},{8,7},{10,9},{12,11},{14,13},{16,15},{18,... | collective-permute-start | bytes 4718600 | tf_op jit(solution)/shard_map/ppermute | solution.py:19
  260.4 17.1 %collective-permute-start.12 = (bf16[1024,768]{1,0:T(8,128)(2,1)}, bf16[1024,768]{1,0:T(8,128)(2,1)}, u32[]{:S(2)}, u32[]{:S(2)}) collective-permute-start(bf16[1024,768]{1,0:T(8,128)(2,1)} %collective-permute-done.7.args_13_), channel_id=1, source_target_pairs={{0,1},{1,0},{2,3},{3,2},{4,5},{5,4},{6,7},{7,6},{8,9},{9,8},{10,11... | collective-permute-start | bytes 4718600 | tf_op jit(solution)/shard_map/ppermute | solution.py:19
  269.3 22.1 %collective-permute-start.10 = (bf16[1024,768]{1,0:T(8,128)(2,1)}, bf16[1024,768]{1,0:T(8,128)(2,1)}, u32[]{:S(2)}, u32[]{:S(2)}) collective-permute-start(bf16[1024,768]{1,0:T(8,128)(2,1)} %collective-permute-done.7.args_13_), channel_id=1, source_target_pairs={{1,2},{3,4},{5,6},{7,8},{9,10},{11,12},{13,14},{15,16},{17,18},{19... | collective-permute-start | bytes 4718600 | tf_op jit(solution)/shard_map/ppermute | solution.py:19
  275.0 16.4 %copy-start.5 = (bf16[1024,768]{1,0:T(8,128)(2,1)}, bf16[1024,768]{1,0:T(8,128)(2,1)S(1)}, u32[]{:S(2)}) copy-start(bf16[1024,768]{1,0:T(8,128)(2,1)S(1)} %collective-permute-done.13.args_19_) | copy-start | bytes 4718596

commit v9 on v5

--- a/solution.py
+++ b/solution.py
@@ -46,13 +46,14 @@
             p_code = code // TILE_COUNT
             j = code % TILE_COUNT
             for p in range(pieces):
-                @pl.when(p_code == p)
+                @pl.when(jnp.logical_and(p_code == p, c < cnt_ref[step]))
                 def _():
                     for copy in copies(step, slot, c, p, j):
                         copy.start()
 
     @pl.when(i == 0)
     def _():
+        v_buf[...] = jnp.zeros(v_buf.shape, v_buf.dtype)
         start(0, 0)
 
     @pl.when(i + 1 < steps)
@@ -60,8 +61,10 @@
         start(i + 1, 1 - parity)
 
     for c in range(SLOTS):
-        for copy in copies(i, parity, c, 0, 0):
-            copy.wait()
+        @pl.when(c < cnt_ref[i])
+        def _():
+            for copy in copies(i, parity, c, 0, 0):
+                copy.wait()
 
     count = cnt_ref[i]
     keys = SLOTS * TILE

time: 323 us -> 323 us (level)
  no operation moved by 1% of the time
where the time goes in v9:
time: 323 us; the launch traced here: 318 us
  waiting for transfers between devices  228 us (71%)
  starting transfers between devices  26.6 us (8%)
  Pallas kernels  24.3 us (8%)
  blocking collectives  18.8 us (6%)
  local copies, waits for them, and re-layouts  15.2 us (5%)
  other arithmetic  4.36 us (1%)
    ppermute x12, waiting for transfers between devices, permute(): return lax.ppermute(block, axis, route)  113 us
    all_to_all x1, waiting for transfers between devices, body(): lax.all_to_all(key_states, 'head', split_axis=1, concat_axis=0, tiled=True)  53.7 us
    all_to_all x1, waiting for transfers between devices, body(): lax.all_to_all(queries, 'head', split_axis=1, concat_axis=0, tiled=True)  41.1 us
    pallas_call x1, Pallas kernels, body(): pl.pallas_call(kernel, grid_spec=grid_spec, out_shape=jax.ShapeDtypeStruc...  24.3 us
    all_to_all x1, waiting for transfers between devices, body(): lax.all_to_all(value_states, 'head', split_axis=1, concat_axis=0, tiled=T...  19.9 us
    all_to_all x1, blocking collectives, body(): return lax.all_to_all(out, 'head', split_axis=0, concat_axis=1, tiled=True)  18.8 us
    ppermute x12, starting transfers between devices, permute(): return lax.ppermute(block, axis, route)  12.5 us
  transfers between devices with their start and end apart: 15, of which 7 were waited for; matrix products, arithmetic and copies ran while one was open for 5% of the time, Pallas kernels for 0%

profile of v9, /device:TPU:128, one launch (start us, length us, event | category | flops | bytes accessed | tf_op | source)
XLA Modules:
  0.0 317.6 jit_solution(6805269509719564979)
XLA Ops:
  0.0 2.7 copy.30
  2.7 5.1 %all-to-all-start.2 = ((bf16[128,8,768]{2,0,1:T(8,128)(2,1)}), bf16[128,8,768]{2,0,1:T(8,128)(2,1)}, u32[]{:S(2)}, u32[]{:S(2)}) async-start(bf16[128,8,768]{2,0,1:T(8,128)(2,1)} %bitcast.33), calls=%async_computation.2 | async-start | bytes 3145728 | tf_op jit(solution)/shard_map/all_to_all | solution.py:107
  7.7 1.6 copy.18
  9.3 19.9 %all-to-all-done.2 = bf16[128,8,768]{2,0,1:T(8,128)(2,1)} async-done(((bf16[128,8,768]{2,0,1:T(8,128)(2,1)}), bf16[128,8,768]{2,0,1:T(8,128)(2,1)}, u32[]{:S(2)}, u32[]{:S(2)}) %all-to-all-start.2) | async-done | bytes 1572896 | tf_op jit(solution)/shard_map/all_to_all | solution.py:107
  29.2 4.3 %all-to-all-start.1 = ((bf16[128,8,768]{0,2,1:T(8,128)(2,1)}), bf16[128,8,768]{0,2,1:T(8,128)(2,1)}, u32[]{:S(2)}, u32[]{:S(2)}) async-start(bf16[128,8,768]{0,2,1:T(8,128)(2,1)} %bitcast.4), calls=%async_computation.1 | async-start | bytes 3145728 | tf_op jit(solution)/shard_map/all_to_all | solution.py:105
  33.5 2.8 collective-permute-start.7
  36.3 53.7 %all-to-all-done.1 = bf16[128,8,768]{0,2,1:T(8,128)(2,1)} async-done(((bf16[128,8,768]{0,2,1:T(8,128)(2,1)}), bf16[128,8,768]{0,2,1:T(8,128)(2,1)}, u32[]{:S(2)}, u32[]{:S(2)}) %all-to-all-start.1) | async-done | bytes 1572896 | tf_op jit(solution)/shard_map/all_to_all | solution.py:105
  90.0 2.9 bitcast_bitcast_fusion.args_4_
  92.9 2.0 collective-permute-start
  95.4 27.0 %collective-permute-done.6.args_12_ = bf16[1024,768]{1,0:T(8,128)(2,1)S(1)} collective-permute-done((bf16[1024,768]{1,0:T(8,128)(2,1)}, bf16[1024,768]{1,0:T(8,128)(2,1)S(1)}, u32[]{:S(2)}, u32[]{:S(2)}) %collective-permute-start.6) | collective-permute-done | bytes 1572896 | tf_op jit(solution)/shard_map/ppermute | solution.py:19
  122.4 1.4 copy.31
  123.8 4.8 %all-to-all-start = ((bf16[128,8,768]{2,0,1:T(8,128)(2,1)}), bf16[128,8,768]{2,0,1:T(8,128)(2,1)}, u32[]{:S(2)}, u32[]{:S(2)}) async-start(bf16[128,8,768]{2,0,1:T(8,128)(2,1)} %bitcast.35), calls=%async_computation | async-start | bytes 3145728 | tf_op jit(solution)/shard_map/all_to_all | solution.py:109
  128.6 1.3 broadcast_select_fusion
  129.9 53.8 %collective-permute-done.1.args_6_ = bf16[768,1024]{1,0:T(8,128)(2,1)} collective-permute-done((bf16[768,1024]{1,0:T(8,128)(2,1)}, bf16[768,1024]{1,0:T(8,128)(2,1)}, u32[]{:S(2)}, u32[]{:S(2)}) %collective-permute-start.1) | collective-permute-done | bytes 1572896 | tf_op jit(solution)/shard_map/ppermute | solution.py:19
  183.7 6.3 %collective-permute-start.9 = (bf16[1024,768]{1,0:T(8,128)(2,1)}, bf16[1024,768]{1,0:T(8,128)(2,1)}, u32[]{:S(2)}, u32[]{:S(2)}) collective-permute-start(bf16[1024,768]{1,0:T(8,128)(2,1)} %broadcast_select_fusion), channel_id=1, source_target_pairs={{0,31},{1,2},{2,1},{3,4},{4,3},{5,6},{6,5},{7,8},{8,7},{9,10},{10,... | collective-permute-start | bytes 4718600 | tf_op jit(solution)/shard_map/ppermute | solution.py:19
  190.0 2.8 broadcast_select_fusion.1
  197.4 0.8 copy.21.args_2_
  198.2 41.1 %all-to-all-done = bf16[128,8,768]{2,0,1:T(8,128)(2,1)} async-done(((bf16[128,8,768]{2,0,1:T(8,128)(2,1)}), bf16[128,8,768]{2,0,1:T(8,128)(2,1)}, u32[]{:S(2)}, u32[]{:S(2)}) %all-to-all-start) | async-done | bytes 1572896 | tf_op jit(solution)/shard_map/all_to_all | solution.py:109
  239.3 15.8 %collective-permute-done.9.args_15_ = bf16[1024,768]{1,0:T(8,128)(2,1)} collective-permute-done((bf16[1024,768]{1,0:T(8,128)(2,1)}, bf16[1024,768]{1,0:T(8,128)(2,1)}, u32[]{:S(2)}, u32[]{:S(2)}) %collective-permute-start.9) | collective-permute-done | bytes 1572896 | tf_op jit(solution)/shard_map/ppermute | solution.py:19
  255.1 16.8 %collective-permute-done.3.args_8_ = bf16[768,1024]{1,0:T(8,128)(2,1)} collective-permute-done((bf16[768,1024]{1,0:T(8,128)(2,1)}, bf16[768,1024]{1,0:T(8,128)(2,1)}, u32[]{:S(2)}, u32[]{:S(2)}) %collective-permute-start.3) | collective-permute-done | bytes 1572896 | tf_op jit(solution)/shard_map/ppermute | solution.py:19
  272.0 1.1 copy-done.3
  273.1 24.3 %shard_map.73 = bf16[1024,768]{1,0:T(8,128)(2,1)} custom-call(s32[64]{0:T(128)} %reshape.68.args_0_, s32[8]{0:T(128)} %args_1_.4, f32[8,6,1024]{2,1,0:T(8,128)} %copy.21.args_2_, bf16[1024,768]{1,0:T(8,128)(2,1)} %bitcast.3.args_3_, bf16[768,1024]{1,0:T(8,128)(2,1)} %bitcast_bitcast_fusion.args_4_, bf16[768,1024]{1,0:T(8,128)(2,1)} %collective-permute-done.args_5_, ...), custom_call_target="tpu_custom_call" | custom-call | tf_op jit(solution)/shard_map/pallas_call | solution.py:153
  297.5 18.8 %all_to_all.76 = bf16[8,128,768]{2,1,0:T(8,128)(2,1)S(1)} all-to-all(bf16[8,128,768]{2,1,0:T(8,128)(2,1)} %bitcast.36), channel_id=1, replica_groups=mesh['head'=8,'blk'=32] {'head'}, dimensions={0} | all-to-all | bytes 3145728 | tf_op jit(solution)/shard_map/all_to_all | solution.py:166
  316.3 1.3 copy.26
  (53 shorter events, 5.0 us)
Async XLA Ops:
  0.0 195.5 %copy-start = (s32[256]{0:T(256)S(1)}, s32[256]{0:T(256)}, u32[]{:S(2)}) copy-start(s32[256]{0:T(256)} %param.12) | copy-start | bytes 3076
  2.7 5.1 %copy-start.4 = (bf16[128,6144]{1,0:T(8,128)(2,1)S(1)}, bf16[128,6144]{1,0:T(8,128)(2,1)}, u32[]{:S(2)}) copy-start(bf16[128,6144]{1,0:T(8,128)(2,1)} %param.8) | copy-start | bytes 4718596
  2.7 26.5 %all-to-all-start.2 = ((bf16[128,8,768]{2,0,1:T(8,128)(2,1)}), bf16[128,8,768]{2,0,1:T(8,128)(2,1)}, u32[]{:S(2)}, u32[]{:S(2)}) async-start(bf16[128,8,768]{2,0,1:T(8,128)(2,1)} %bitcast.33), calls=%async_computation.2 | async-start | bytes 3145728 | tf_op jit(solution)/shard_map/all_to_all | solution.py:107
  29.2 60.8 %all-to-all-start.1 = ((bf16[128,8,768]{0,2,1:T(8,128)(2,1)}), bf16[128,8,768]{0,2,1:T(8,128)(2,1)}, u32[]{:S(2)}, u32[]{:S(2)}) async-start(bf16[128,8,768]{0,2,1:T(8,128)(2,1)} %bitcast.4), calls=%async_computation.1 | async-start | bytes 3145728 | tf_op jit(solution)/shard_map/all_to_all | solution.py:105
  33.5 61.5 %collective-permute-start.7 = (bf16[1024,768]{1,0:T(8,128)(2,1)}, bf16[1024,768]{1,0:T(8,128)(2,1)S(1)}, u32[]{:S(2)}, u32[]{:S(2)}) collective-permute-start(bf16[1024,768]{1,0:T(8,128)(2,1)} %bitcast.8.args_11_), channel_id=1, source_target_pairs={{0,30},{1,31},{2,0},{3,1},{4,2},{5,3},{6,4},{7,5},{8,6},{9,7},{10,... | collective-permute-start | bytes 4718600 | tf_op jit(solution)/shard_map/ppermute | solution.py:19
  36.3 86.1 %collective-permute-start.6 = (bf16[1024,768]{1,0:T(8,128)(2,1)}, bf16[1024,768]{1,0:T(8,128)(2,1)S(1)}, u32[]{:S(2)}, u32[]{:S(2)}) collective-permute-start(bf16[1024,768]{1,0:T(8,128)(2,1)} %bitcast.8.args_11_), channel_id=1, source_target_pairs={{0,2},{1,3},{2,4},{3,5},{4,6},{5,7},{6,8},{7,9},{8,10},{9,11},{10,... | collective-permute-start | bytes 4718600 | tf_op jit(solution)/shard_map/ppermute | solution.py:19
  90.0 32.4 %copy-start.5 = (bf16[128,6144]{1,0:T(8,128)(2,1)S(1)}, bf16[128,6144]{1,0:T(8,128)(2,1)}, u32[]{:S(2)}) copy-start(bf16[128,6144]{1,0:T(8,128)(2,1)} %param.7) | copy-start | bytes 4718596
  92.9 90.8 %collective-permute-start.1 = (bf16[768,1024]{1,0:T(8,128)(2,1)}, bf16[768,1024]{1,0:T(8,128)(2,1)}, u32[]{:S(2)}, u32[]{:S(2)}) collective-permute-start(bf16[768,1024]{1,0:T(8,128)(2,1)} %bitcast_bitcast_fusion.args_4_), channel_id=1, source_target_pairs={{0,30},{1,31},{2,0},{3,1},{4,2},{5,3},{6,4},{7,5},{8,6},{9,7},{10,... | collective-permute-start | bytes 4718600 | tf_op jit(solution)/shard_map/ppermute | solution.py:19
  92.9 97.1 %collective-permute-start = (bf16[768,1024]{1,0:T(8,128)(2,1)}, bf16[768,1024]{1,0:T(8,128)(2,1)}, u32[]{:S(2)}, u32[]{:S(2)}) collective-permute-start(bf16[768,1024]{1,0:T(8,128)(2,1)} %bitcast_bitcast_fusion.args_4_), channel_id=1, source_target_pairs={{0,2},{1,3},{2,4},{3,5},{4,6},{5,7},{6,8},{7,9},{8,10},{9,11},{10,... | collective-permute-start | bytes 4718600 | tf_op jit(solution)/shard_map/ppermute | solution.py:19
  94.9 97.9 %collective-permute-start.8 = (bf16[1024,768]{1,0:T(8,128)(2,1)}, bf16[1024,768]{1,0:T(8,128)(2,1)}, u32[]{:S(2)}, u32[]{:S(2)}) collective-permute-start(bf16[1024,768]{1,0:T(8,128)(2,1)} %bitcast.8.args_11_), channel_id=1, source_target_pairs={{0,1},{1,0},{2,3},{3,2},{4,5},{5,4},{6,7},{7,6},{8,9},{9,8},{10,11... | collective-permute-start | bytes 4718600 | tf_op jit(solution)/shard_map/ppermute | solution.py:19
  94.9 33.7 %copy-start.1 = (bf16[1024,768]{1,0:T(8,128)(2,1)}, bf16[1024,768]{1,0:T(8,128)(2,1)S(1)}, u32[]{:S(2)}) copy-start(bf16[1024,768]{1,0:T(8,128)(2,1)S(1)} %collective-permute-done.7.args_13_) | copy-start | bytes 4718596
  94.9 98.0 %collective-permute-start.2 = (bf16[768,1024]{1,0:T(8,128)(2,1)}, bf16[768,1024]{1,0:T(8,128)(2,1)}, u32[]{:S(2)}, u32[]{:S(2)}) collective-permute-start(bf16[768,1024]{1,0:T(8,128)(2,1)} %bitcast_bitcast_fusion.args_4_), channel_id=1, source_target_pairs={{0,1},{1,0},{2,3},{3,2},{4,5},{5,4},{6,7},{7,6},{8,9},{9,8},{10,11... | collective-permute-start | bytes 4718600 | tf_op jit(solution)/shard_map/ppermute | solution.py:19
  122.4 70.4 %copy-start.2 = (bf16[1024,768]{1,0:T(8,128)(2,1)}, bf16[1024,768]{1,0:T(8,128)(2,1)S(1)}, u32[]{:S(2)}) copy-start(bf16[1024,768]{1,0:T(8,128)(2,1)S(1)} %collective-permute-done.6.args_12_) | copy-start | bytes 4718596
  122.4 71.0 %collective-permute-start.11 = (bf16[1024,768]{1,0:T(8,128)(2,1)S(1)}, bf16[1024,768]{1,0:T(8,128)(2,1)}, u32[]{:S(2)}, u32[]{:S(2)}) collective-permute-start(bf16[1024,768]{1,0:T(8,128)(2,1)S(1)} %collective-permute-done.7.args_13_), channel_id=1, source_target_pairs={{0,1},{1,0},{2,3},{3,2},{4,5},{5,4},{6,7},{7,6},{8,9},{9,8},{10,11... | collective-permute-start | bytes 4718600 | tf_op jit(solution)/shard_map/ppermute | solution.py:19
  123.8 115.5 %all-to-all-start = ((bf16[128,8,768]{2,0,1:T(8,128)(2,1)}), bf16[128,8,768]{2,0,1:T(8,128)(2,1)}, u32[]{:S(2)}, u32[]{:S(2)}) async-start(bf16[128,8,768]{2,0,1:T(8,128)(2,1)} %bitcast.35), calls=%async_computation | async-start | bytes 3145728 | tf_op jit(solution)/shard_map/all_to_all | solution.py:109
  129.9 63.8 %copy-start.6 = (s32[8,8]{1,0:T(8,128)S(1)}, s32[8,8]{1,0:T(8,128)}, u32[]{:S(2)}) copy-start(s32[8,8]{1,0:T(8,128)} %param.10) | copy-start | bytes 772
  129.9 64.0 %copy-start.7 = (s32[2,7]{1,0:T(2,128)S(1)}, s32[2,7]{1,0:T(2,128)}, u32[]{:S(2)}) copy-start(s32[2,7]{1,0:T(2,128)} %constant.89.clone) | copy-start | bytes 172
  183.7 71.4 %collective-permute-start.9 = (bf16[1024,768]{1,0:T(8,128)(2,1)}, bf16[1024,768]{1,0:T(8,128)(2,1)}, u32[]{:S(2)}, u32[]{:S(2)}) collective-permute-start(bf16[1024,768]{1,0:T(8,128)(2,1)} %broadcast_select_fusion), channel_id=1, source_target_pairs={{0,31},{1,2},{2,1},{3,4},{4,3},{5,6},{6,5},{7,8},{8,7},{9,10},{10,... | collective-permute-start | bytes 4718600 | tf_op jit(solution)/shard_map/ppermute | solution.py:19
  192.8 79.2 %collective-permute-start.3 = (bf16[768,1024]{1,0:T(8,128)(2,1)}, bf16[768,1024]{1,0:T(8,128)(2,1)}, u32[]{:S(2)}, u32[]{:S(2)}) collective-permute-start(bf16[768,1024]{1,0:T(8,128)(2,1)} %broadcast_select_fusion.1), channel_id=1, source_target_pairs={{0,31},{1,2},{2,1},{3,4},{4,3},{5,6},{6,5},{7,8},{8,7},{9,10},{10,... | collective-permute-start | bytes 4718600 | tf_op jit(solution)/shard_map/ppermute | solution.py:19
  192.8 62.3 %collective-permute-start.10 = (bf16[1024,768]{1,0:T(8,128)(2,1)S(1)}, bf16[1024,768]{1,0:T(8,128)(2,1)}, u32[]{:S(2)}, u32[]{:S(2)}) collective-permute-start(bf16[1024,768]{1,0:T(8,128)(2,1)S(1)} %collective-permute-done.6.args_12_), channel_id=1, source_target_pairs={{0,1},{1,0},{2,3},{3,2},{4,5},{5,4},{6,7},{7,6},{8,9},{9,8},{10,11... | collective-permute-start | bytes 4718600 | tf_op jit(solution)/shard_map/ppermute | solution.py:19
  192.9 62.2 %collective-permute-start.5 = (bf16[768,1024]{1,0:T(8,128)(2,1)}, bf16[768,1024]{1,0:T(8,128)(2,1)}, u32[]{:S(2)}, u32[]{:S(2)}) collective-permute-start(bf16[768,1024]{1,0:T(8,128)(2,1)} %collective-permute-done.1.args_6_), channel_id=1, source_target_pairs={{0,1},{1,0},{2,3},{3,2},{4,5},{5,4},{6,7},{7,6},{8,9},{9,8},{10,11... | collective-permute-start | bytes 4718600 | tf_op jit(solution)/shard_map/ppermute | solution.py:19
  193.4 78.6 %collective-permute-start.4 = (bf16[768,1024]{1,0:T(8,128)(2,1)}, bf16[768,1024]{1,0:T(8,128)(2,1)S(1)}, u32[]{:S(2)}, u32[]{:S(2)}) collective-permute-start(bf16[768,1024]{1,0:T(8,128)(2,1)} %collective-permute-done.args_5_), channel_id=1, source_target_pairs={{0,1},{1,0},{2,3},{3,2},{4,5},{5,4},{6,7},{7,6},{8,9},{9,8},{10,11... | collective-permute-start | bytes 4718600 | tf_op jit(solution)/shard_map/ppermute | solution.py:19
  272.0 1.1 copy-start.3

commit v10 on v9

--- a/solution.py
+++ b/solution.py
@@ -84,18 +84,23 @@
         o_ref[:, cols] = (acc / total).astype(o_ref.dtype)
 
 
-def exchange(local, axis, n):
+def step_a(local, n):
     swap = [(i, i ^ 1) for i in range(n)]
     from_left2 = permute(local, "blk", shift_pairs(n, 2))
     from_right2 = permute(local, "blk", shift_pairs(n, -2))
     other_core = permute(local, "blk", swap)
+    return from_left2, from_right2, other_core
+
+
+def step_b(from_left2, from_right2, n):
+    swap = [(i, i ^ 1) for i in range(n)]
     core = lax.axis_index("blk") % 2
     forward = jnp.where(core == 1, from_left2, from_right2)
     cross_route = [((i, (i + 1) % n) if i % 2 == 1 else (i, (i - 1) % n)) for i in range(n)]
     across = permute(forward, "blk", cross_route)
     other_left2 = permute(from_left2, "blk", swap)
     other_right2 = permute(from_right2, "blk", swap)
-    return [local, from_left2, from_right2, other_core, across, other_left2, other_right2]
+    return across, other_left2, other_right2
 
 
 def body(queries, key_states, value_states, block_lists, block_counts, tile_order):
@@ -103,9 +108,13 @@
     group_size = lax.axis_size("head")
     heads_local = H // group_size
     k_heads = lax.all_to_all(key_states, "head", split_axis=1, concat_axis=0, tiled=True)
-    k_window = exchange(k_heads.T, 1, cycle_size)
+    k_local = k_heads.T
+    k_left2, k_right2, k_core = step_a(k_local, cycle_size)
     v_heads = lax.all_to_all(value_states, "head", split_axis=1, concat_axis=0, tiled=True)
-    v_window = exchange(v_heads, 0, cycle_size)
+    v_heads, k_left2, k_right2 = lax.optimization_barrier((v_heads, k_left2, k_right2))
+    k_window = [k_local, k_left2, k_right2, k_core, *step_b(k_left2, k_right2, cycle_size)]
+    v_left2, v_right2, v_core = step_a(v_heads, cycle_size)
+    v_window = [v_heads, v_left2, v_right2, v_core, *step_b(v_left2, v_right2, cycle_size)]
     q_heads = lax.all_to_all(queries, "head", split_axis=1, concat_axis=0, tiled=True)
     shard_tok = q_heads.shape[0]
     tile_count = shard_tok // TILE

time: 323 us -> 328 us (1.015)
  waiting for transfers between devices: 228 us -> 234 us
    ppermute x12, waiting for transfers between devices: 113 us -> 160 us  [permute(): return lax.ppermute(block, axis, route)]
    all_to_all x1, waiting for transfers between devices: 41.1 us -> 1.86 us  [body(): lax.all_to_all(queries, 'head', split_axis=1, concat_axis=0, tiled=True)]
    all_to_all x1, waiting for transfers between devices: 53.7 us -> 20.1 us  [body(): lax.all_to_all(key_states, 'head', split_axis=1, concat_axis=0, tiled=True)]
    all_to_all x1, waiting for transfers between devices: 19.9 us -> 52.4 us  [body(): lax.all_to_all(value_states, 'head', split_axis=1, concat_axis=0, tiled=T...]
    all_to_all x1, starting transfers between devices: 4.78 us -> 8.92 us  [body(): lax.all_to_all(queries, 'head', split_axis=1, concat_axis=0, tiled=True)]
  transfers between devices with their start and end apart: 15 -> 15, of which waited for: 7 -> 8; matrix products, arithmetic and copies ran while one was open for 5% -> 4% of each run, Pallas kernels for 0% -> 0%
where the time goes in v10:
time: 328 us; the launch traced here: 323 us
  waiting for transfers between devices  234 us (71%)
  starting transfers between devices  27.9 us (9%)
  Pallas kernels  24.5 us (7%)
  blocking collectives  18.5 us (6%)
  local copies, waits for them, and re-layouts  13.2 us (4%)
  other arithmetic  4.3 us (1%)
    ppermute x12, waiting for transfers between devices, permute(): return lax.ppermute(block, axis, route)  160 us
    all_to_all x1, waiting for transfers between devices, body(): lax.all_to_all(value_states, 'head', split_axis=1, concat_axis=0, tiled=T...  52.4 us
    pallas_call x1, Pallas kernels, body(): pl.pallas_call(kernel, grid_spec=grid_spec, out_shape=jax.ShapeDtypeStruc...  24.5 us
    all_to_all x1, waiting for transfers between devices, body(): lax.all_to_all(key_states, 'head', split_axis=1, concat_axis=0, tiled=True)  20.1 us
    all_to_all x1, blocking collectives, body(): return lax.all_to_all(out, 'head', split_axis=0, concat_axis=1, tiled=True)  18.5 us
    ppermute x12, starting transfers between devices, permute(): return lax.ppermute(block, axis, route)  9.63 us
    all_to_all x1, starting transfers between devices, body(): lax.all_to_all(queries, 'head', split_axis=1, concat_axis=0, tiled=True)  8.92 us
  transfers between devices with their start and end apart: 15, of which 8 were waited for; matrix products, arithmetic and copies ran while one was open for 4% of the time, Pallas kernels for 0%

profile of v10, /device:TPU:128, one launch (start us, length us, event | category | flops | bytes accessed | tf_op | source)
XLA Modules:
  0.0 322.6 jit_solution(5287756135293252002)
XLA Ops:
  0.0 2.6 copy.18
  2.6 5.1 %all-to-all-start.1 = ((bf16[128,8,768]{0,2,1:T(8,128)(2,1)}), bf16[128,8,768]{0,2,1:T(8,128)(2,1)S(1)}, u32[]{:S(2)}, u32[]{:S(2)}) async-start(bf16[128,8,768]{0,2,1:T(8,128)(2,1)} %bitcast.4), calls=%async_computation.1 | async-start | bytes 3145728 | tf_op jit(solution)/shard_map/all_to_all | solution.py:110
  7.7 1.3 copy.30
  8.9 20.1 %all-to-all-done.1 = bf16[128,8,768]{0,2,1:T(8,128)(2,1)S(1)} async-done(((bf16[128,8,768]{0,2,1:T(8,128)(2,1)}), bf16[128,8,768]{0,2,1:T(8,128)(2,1)S(1)}, u32[]{:S(2)}, u32[]{:S(2)}) %all-to-all-start.1) | async-done | bytes 1572896 | tf_op jit(solution)/shard_map/all_to_all | solution.py:110
  29.0 4.3 %all-to-all-start.2 = ((bf16[128,8,768]{2,0,1:T(8,128)(2,1)}), bf16[128,8,768]{2,0,1:T(8,128)(2,1)}, u32[]{:S(2)}, u32[]{:S(2)}) async-start(bf16[128,8,768]{2,0,1:T(8,128)(2,1)} %bitcast.33), calls=%async_computation.2 | async-start | bytes 3145728 | tf_op jit(solution)/shard_map/all_to_all | solution.py:113
  33.3 1.4 bitcast_bitcast_fusion.args_4_
  34.7 2.7 collective-permute-start.1
  37.4 52.4 %all-to-all-done.2 = bf16[128,8,768]{2,0,1:T(8,128)(2,1)} async-done(((bf16[128,8,768]{2,0,1:T(8,128)(2,1)}), bf16[128,8,768]{2,0,1:T(8,128)(2,1)}, u32[]{:S(2)}, u32[]{:S(2)}) %all-to-all-start.2) | async-done | bytes 1572896 | tf_op jit(solution)/shard_map/all_to_all | solution.py:113
  89.8 30.2 %collective-permute-done.args_5_ = bf16[768,1024]{1,0:T(8,128)(2,1)S(1)} collective-permute-done((bf16[768,1024]{1,0:T(8,128)(2,1)}, bf16[768,1024]{1,0:T(8,128)(2,1)S(1)}, u32[]{:S(2)}, u32[]{:S(2)}) %collective-permute-start) | collective-permute-done | bytes 1572896 | tf_op jit(solution)/shard_map/ppermute | solution.py:19
  120.0 2.0 collective-permute-start.6
  122.0 1.4 broadcast_select_fusion.1
  123.4 4.3 %collective-permute-start.3 = (bf16[768,1024]{1,0:T(8,128)(2,1)}, bf16[768,1024]{1,0:T(8,128)(2,1)}, u32[]{:S(2)}, u32[]{:S(2)}) collective-permute-start(bf16[768,1024]{1,0:T(8,128)(2,1)} %broadcast_select_fusion.1), channel_id=1, source_target_pairs={{0,31},{1,2},{2,1},{3,4},{4,3},{5,6},{6,5},{7,8},{8,7},{9,10},{10,... | collective-permute-start | bytes 4718600 | tf_op jit(solution)/shard_map/ppermute | solution.py:19
  127.7 1.2 copy.31
  129.0 8.9 %all-to-all-start = ((bf16[128,8,768]{2,0,1:T(8,128)(2,1)}), bf16[128,8,768]{2,0,1:T(8,128)(2,1)}, u32[]{:S(2)}, u32[]{:S(2)}) async-start(bf16[128,8,768]{2,0,1:T(8,128)(2,1)} %bitcast.35), calls=%async_computation | async-start | bytes 3145728 | tf_op jit(solution)/shard_map/all_to_all | solution.py:118
  137.9 16.7 %collective-permute-done.7.args_13_ = bf16[1024,768]{1,0:T(8,128)(2,1)} collective-permute-done((bf16[1024,768]{1,0:T(8,128)(2,1)}, bf16[1024,768]{1,0:T(8,128)(2,1)}, u32[]{:S(2)}, u32[]{:S(2)}) %collective-permute-start.7) | collective-permute-done | bytes 1572896 | tf_op jit(solution)/shard_map/ppermute | solution.py:19
  154.7 24.5 %collective-permute-done.6.args_12_ = bf16[1024,768]{1,0:T(8,128)(2,1)} collective-permute-done((bf16[1024,768]{1,0:T(8,128)(2,1)}, bf16[1024,768]{1,0:T(8,128)(2,1)}, u32[]{:S(2)}, u32[]{:S(2)}) %collective-permute-start.6) | collective-permute-done | bytes 1572896 | tf_op jit(solution)/shard_map/ppermute | solution.py:19
  179.1 2.7 broadcast_select_fusion
  181.9 70.0 %collective-permute-done.3.args_8_ = bf16[768,1024]{1,0:T(8,128)(2,1)} collective-permute-done((bf16[768,1024]{1,0:T(8,128)(2,1)}, bf16[768,1024]{1,0:T(8,128)(2,1)}, u32[]{:S(2)}, u32[]{:S(2)}) %collective-permute-start.3) | collective-permute-done | bytes 1572896 | tf_op jit(solution)/shard_map/ppermute | solution.py:19
  256.9 1.9 all-to-all-done
  258.8 18.4 %collective-permute-done.9.args_15_ = bf16[1024,768]{1,0:T(8,128)(2,1)} collective-permute-done((bf16[1024,768]{1,0:T(8,128)(2,1)}, bf16[1024,768]{1,0:T(8,128)(2,1)}, u32[]{:S(2)}, u32[]{:S(2)}) %collective-permute-start.9) | collective-permute-done | bytes 1572896 | tf_op jit(solution)/shard_map/ppermute | solution.py:19
  277.2 1.1 copy-done.3
  278.3 24.5 %shard_map.73 = bf16[1024,768]{1,0:T(8,128)(2,1)} custom-call(s32[64]{0:T(128)} %reshape.68.args_0_, s32[8]{0:T(128)} %args_1_.4, f32[8,6,1024]{2,1,0:T(8,128)} %copy.21.args_2_, bf16[1024,768]{1,0:T(8,128)(2,1)} %bitcast.3.args_3_, bf16[768,1024]{1,0:T(8,128)(2,1)} %bitcast_bitcast_fusion.args_4_, bf16[768,1024]{1,0:T(8,128)(2,1)} %copy-done.2, ...), custom_call_target="tpu_custom_call" | custom-call | tf_op jit(solution)/shard_map/pallas_call | solution.py:162
  302.8 18.5 %all_to_all.76 = bf16[8,128,768]{2,1,0:T(8,128)(2,1)S(1)} all-to-all(bf16[8,128,768]{2,1,0:T(8,128)(2,1)} %bitcast.36), channel_id=1, replica_groups=mesh['head'=8,'blk'=32] {'head'}, dimensions={0} | all-to-all | bytes 3145728 | tf_op jit(solution)/shard_map/all_to_all | solution.py:175
  321.3 1.3 copy.26
  (53 shorter events, 5.0 us)
Async XLA Ops:
  0.0 254.2 %copy-start = (s32[256]{0:T(256)S(1)}, s32[256]{0:T(256)}, u32[]{:S(2)}) copy-start(s32[256]{0:T(256)} %param.12) | copy-start | bytes 3076
  2.6 5.1 %copy-start.4 = (bf16[128,6144]{1,0:T(8,128)(2,1)S(1)}, bf16[128,6144]{1,0:T(8,128)(2,1)}, u32[]{:S(2)}) copy-start(bf16[128,6144]{1,0:T(8,128)(2,1)} %param.9) | copy-start | bytes 4718596
  2.6 26.4 %all-to-all-start.1 = ((bf16[128,8,768]{0,2,1:T(8,128)(2,1)}), bf16[128,8,768]{0,2,1:T(8,128)(2,1)S(1)}, u32[]{:S(2)}, u32[]{:S(2)}) async-start(bf16[128,8,768]{0,2,1:T(8,128)(2,1)} %bitcast.4), calls=%async_computation.1 | async-start | bytes 3145728 | tf_op jit(solution)/shard_map/all_to_all | solution.py:110
  29.0 60.8 %all-to-all-start.2 = ((bf16[128,8,768]{2,0,1:T(8,128)(2,1)}), bf16[128,8,768]{2,0,1:T(8,128)(2,1)}, u32[]{:S(2)}, u32[]{:S(2)}) async-start(bf16[128,8,768]{2,0,1:T(8,128)(2,1)} %bitcast.33), calls=%async_computation.2 | async-start | bytes 3145728 | tf_op jit(solution)/shard_map/all_to_all | solution.py:113
  34.7 55.1 %collective-permute-start.1 = (bf16[768,1024]{1,0:T(8,128)(2,1)}, bf16[768,1024]{1,0:T(8,128)(2,1)S(1)}, u32[]{:S(2)}, u32[]{:S(2)}) collective-permute-start(bf16[768,1024]{1,0:T(8,128)(2,1)} %bitcast_bitcast_fusion.args_4_), channel_id=1, source_target_pairs={{0,30},{1,31},{2,0},{3,1},{4,2},{5,3},{6,4},{7,5},{8,6},{9,7},{10,... | collective-permute-start | bytes 4718600 | tf_op jit(solution)/shard_map/ppermute | solution.py:19
  37.4 82.6 %collective-permute-start = (bf16[768,1024]{1,0:T(8,128)(2,1)}, bf16[768,1024]{1,0:T(8,128)(2,1)S(1)}, u32[]{:S(2)}, u32[]{:S(2)}) collective-permute-start(bf16[768,1024]{1,0:T(8,128)(2,1)} %bitcast_bitcast_fusion.args_4_), channel_id=1, source_target_pairs={{0,2},{1,3},{2,4},{3,5},{4,6},{5,7},{6,8},{7,9},{8,10},{9,11},{10,... | collective-permute-start | bytes 4718600 | tf_op jit(solution)/shard_map/ppermute | solution.py:19
  89.8 64.8 %copy-start.1 = (bf16[768,1024]{1,0:T(8,128)(2,1)}, bf16[768,1024]{1,0:T(8,128)(2,1)S(1)}, u32[]{:S(2)}) copy-start(bf16[768,1024]{1,0:T(8,128)(2,1)S(1)} %collective-permute-done.1.args_6_) | copy-start | bytes 4718596
  120.0 7.7 %copy-start.2 = (bf16[768,1024]{1,0:T(8,128)(2,1)}, bf16[768,1024]{1,0:T(8,128)(2,1)S(1)}, u32[]{:S(2)}) copy-start(bf16[768,1024]{1,0:T(8,128)(2,1)S(1)} %collective-permute-done.args_5_) | copy-start | bytes 4718596
  120.0 34.7 %collective-permute-start.7 = (bf16[1024,768]{1,0:T(8,128)(2,1)}, bf16[1024,768]{1,0:T(8,128)(2,1)}, u32[]{:S(2)}, u32[]{:S(2)}) collective-permute-start(bf16[1024,768]{1,0:T(8,128)(2,1)} %bitcast.8.args_11_), channel_id=1, source_target_pairs={{0,30},{1,31},{2,0},{3,1},{4,2},{5,3},{6,4},{7,5},{8,6},{9,7},{10,... | collective-permute-start | bytes 4718600 | tf_op jit(solution)/shard_map/ppermute | solution.py:19
  120.0 59.1 %collective-permute-start.6 = (bf16[1024,768]{1,0:T(8,128)(2,1)}, bf16[1024,768]{1,0:T(8,128)(2,1)}, u32[]{:S(2)}, u32[]{:S(2)}) collective-permute-start(bf16[1024,768]{1,0:T(8,128)(2,1)} %bitcast.8.args_11_), channel_id=1, source_target_pairs={{0,2},{1,3},{2,4},{3,5},{4,6},{5,7},{6,8},{7,9},{8,10},{9,11},{10,... | collective-permute-start | bytes 4718600 | tf_op jit(solution)/shard_map/ppermute | solution.py:19
  122.0 5.7 %copy-start.5 = (bf16[128,6144]{1,0:T(8,128)(2,1)S(1)}, bf16[128,6144]{1,0:T(8,128)(2,1)}, u32[]{:S(2)}) copy-start(bf16[128,6144]{1,0:T(8,128)(2,1)} %param.7) | copy-start | bytes 4718596
  122.0 59.8 %collective-permute-start.2 = (bf16[768,1024]{1,0:T(8,128)(2,1)}, bf16[768,1024]{1,0:T(8,128)(2,1)}, u32[]{:S(2)}, u32[]{:S(2)}) collective-permute-start(bf16[768,1024]{1,0:T(8,128)(2,1)} %bitcast_bitcast_fusion.args_4_), channel_id=1, source_target_pairs={{0,1},{1,0},{2,3},{3,2},{4,5},{5,4},{6,7},{7,6},{8,9},{9,8},{10,11... | collective-permute-start | bytes 4718600 | tf_op jit(solution)/shard_map/ppermute | solution.py:19
  123.4 128.5 %collective-permute-start.3 = (bf16[768,1024]{1,0:T(8,128)(2,1)}, bf16[768,1024]{1,0:T(8,128)(2,1)}, u32[]{:S(2)}, u32[]{:S(2)}) collective-permute-start(bf16[768,1024]{1,0:T(8,128)(2,1)} %broadcast_select_fusion.1), channel_id=1, source_target_pairs={{0,31},{1,2},{2,1},{3,4},{4,3},{5,6},{6,5},{7,8},{8,7},{9,10},{10,... | collective-permute-start | bytes 4718600 | tf_op jit(solution)/shard_map/ppermute | solution.py:19
  127.7 124.2 %collective-permute-start.4 = (bf16[768,1024]{1,0:T(8,128)(2,1)S(1)}, bf16[768,1024]{1,0:T(8,128)(2,1)}, u32[]{:S(2)}, u32[]{:S(2)}) collective-permute-start(bf16[768,1024]{1,0:T(8,128)(2,1)S(1)} %collective-permute-done.args_5_), channel_id=1, source_target_pairs={{0,1},{1,0},{2,3},{3,2},{4,5},{5,4},{6,7},{7,6},{8,9},{9,8},{10,11... | collective-permute-start | bytes 4718600 | tf_op jit(solution)/shard_map/ppermute | solution.py:19
  129.0 129.8 %all-to-all-start = ((bf16[128,8,768]{2,0,1:T(8,128)(2,1)}), bf16[128,8,768]{2,0,1:T(8,128)(2,1)}, u32[]{:S(2)}, u32[]{:S(2)}) async-start(bf16[128,8,768]{2,0,1:T(8,128)(2,1)} %bitcast.35), calls=%async_computation | async-start | bytes 3145728 | tf_op jit(solution)/shard_map/all_to_all | solution.py:118
  137.9 114.5 %copy-start.6 = (s32[8,8]{1,0:T(8,128)S(1)}, s32[8,8]{1,0:T(8,128)}, u32[]{:S(2)}) copy-start(s32[8,8]{1,0:T(8,128)} %param.10) | copy-start | bytes 772
  137.9 114.7 %copy-start.7 = (s32[2,7]{1,0:T(2,128)S(1)}, s32[2,7]{1,0:T(2,128)}, u32[]{:S(2)}) copy-start(s32[2,7]{1,0:T(2,128)} %constant.89.clone) | copy-start | bytes 172
  154.6 104.1 %collective-permute-start.5 = (bf16[768,1024]{1,0:T(8,128)(2,1)S(1)}, bf16[768,1024]{1,0:T(8,128)(2,1)}, u32[]{:S(2)}, u32[]{:S(2)}) collective-permute-start(bf16[768,1024]{1,0:T(8,128)(2,1)S(1)} %collective-permute-done.1.args_6_), channel_id=1, source_target_pairs={{0,1},{1,0},{2,3},{3,2},{4,5},{5,4},{6,7},{7,6},{8,9},{9,8},{10,11... | collective-permute-start | bytes 4718600 | tf_op jit(solution)/shard_map/ppermute | solution.py:19
  179.1 79.6 %collective-permute-start.8 = (bf16[1024,768]{1,0:T(8,128)(2,1)}, bf16[1024,768]{1,0:T(8,128)(2,1)}, u32[]{:S(2)}, u32[]{:S(2)}) collective-permute-start(bf16[1024,768]{1,0:T(8,128)(2,1)} %bitcast.8.args_11_), channel_id=1, source_target_pairs={{0,1},{1,0},{2,3},{3,2},{4,5},{5,4},{6,7},{7,6},{8,9},{9,8},{10,11... | collective-permute-start | bytes 4718600 | tf_op jit(solution)/shard_map/ppermute | solution.py:19
  181.9 95.3 %collective-permute-start.9 = (bf16[1024,768]{1,0:T(8,128)(2,1)}, bf16[1024,768]{1,0:T(8,128)(2,1)}, u32[]{:S(2)}, u32[]{:S(2)}) collective-permute-start(bf16[1024,768]{1,0:T(8,128)(2,1)} %broadcast_select_fusion), channel_id=1, source_target_pairs={{0,31},{1,2},{2,1},{3,4},{4,3},{5,6},{6,5},{7,8},{8,7},{9,10},{10,... | collective-permute-start | bytes 4718600 | tf_op jit(solution)/shard_map/ppermute | solution.py:19
  251.9 6.9 %collective-permute-start.11 = (bf16[1024,768]{1,0:T(8,128)(2,1)}, bf16[1024,768]{1,0:T(8,128)(2,1)}, u32[]{:S(2)}, u32[]{:S(2)}) collective-permute-start(bf16[1024,768]{1,0:T(8,128)(2,1)} %collective-permute-done.7.args_13_), channel_id=1, source_target_pairs={{0,1},{1,0},{2,3},{3,2},{4,5},{5,4},{6,7},{7,6},{8,9},{9,8},{10,11... | collective-permute-start | bytes 4718600 | tf_op jit(solution)/shard_map/ppermute | solution.py:19
  251.9 25.3 %collective-permute-start.10 = (bf16[1024,768]{1,0:T(8,128)(2,1)}, bf16[1024,768]{1,0:T(8,128)(2,1)S(1)}, u32[]{:S(2)}, u32[]{:S(2)}) collective-permute-start(bf16[1024,768]{1,0:T(8,128)(2,1)} %collective-permute-done.6.args_12_), channel_id=1, source_target_pairs={{0,1},{1,0},{2,3},{3,2},{4,5},{5,4},{6,7},{7,6},{8,9},{9,8},{10,11... | collective-permute-start | bytes 4718600 | tf_op jit(solution)/shard_map/ppermute | solution.py:19
  277.2 1.1 copy-start.3

commit v11 on v9

--- a/solution.py
+++ b/solution.py
@@ -26,7 +26,7 @@
 def attention_kernel(sw_ref, cnt_ref, bias_ref, q_ref, *refs, heads_local, scale, pieces):
     k_hbm = refs[:pieces]
     v_hbm = refs[pieces:2 * pieces]
-    o_ref, k_buf, v_buf, sem = refs[2 * pieces:]
+    o_ref, k_buf, v_buf, sem, s_buf = refs[2 * pieces:]
     i = pl.program_id(0)
     steps = pl.num_programs(0)
     parity = i % 2
@@ -53,7 +53,6 @@
 
     @pl.when(i == 0)
     def _():
-        v_buf[...] = jnp.zeros(v_buf.shape, v_buf.dtype)
         start(0, 0)
 
     @pl.when(i + 1 < steps)
@@ -67,20 +66,32 @@
                 copy.wait()
 
     count = cnt_ref[i]
-    keys = SLOTS * TILE
-    valid = lax.broadcasted_iota(jnp.int32, (TILE, keys), 1) < count * TILE
     k_all = k_buf.at[parity]
     v_all = v_buf.at[parity]
     for h in range(heads_local):
         cols = slice(h * DH, (h + 1) * DH)
-        s = jnp.dot(q_ref[:, cols], k_all[cols, :], preferred_element_type=jnp.float32)
-        s = s * scale
-        s = s - bias_ref[h : h + 1, :]
-        s = jnp.where(valid, s, -1e30)
-        top = s.max(axis=1, keepdims=True)
-        w = jnp.exp(s - top).astype(jnp.bfloat16)
-        total = w.astype(jnp.float32).sum(axis=1, keepdims=True)
-        acc = jnp.dot(w, v_all[:, cols], preferred_element_type=jnp.float32)
+        q = q_ref[:, cols]
+
+        def score_pass(c, top):
+            keys = pl.ds(pl.multiple_of(c * TILE, TILE), TILE)
+            s = jnp.dot(q, k_all[cols, keys], preferred_element_type=jnp.float32)
+            s = s * scale
+            s = s - bias_ref[h : h + 1, keys]
+            s_buf[c] = s
+            return jnp.maximum(top, s.max(axis=1, keepdims=True))
+
+        top = lax.fori_loop(0, count, score_pass, jnp.full((TILE, 1), -jnp.inf, jnp.float32))
+
+        def weight_pass(c, carry):
+            total, acc = carry
+            keys = pl.ds(pl.multiple_of(c * TILE, TILE), TILE)
+            w = jnp.exp(s_buf[c] - top).astype(jnp.bfloat16)
+            total = total + w.astype(jnp.float32).sum(axis=1, keepdims=True)
+            acc = acc + jnp.dot(w, v_all[keys, cols], preferred_element_type=jnp.float32)
+            return total, acc
+
+        zero = (jnp.zeros((TILE, 1), jnp.float32), jnp.zeros((TILE, DH), jnp.float32))
+        total, acc = lax.fori_loop(0, count, weight_pass, zero)
         o_ref[:, cols] = (acc / total).astype(o_ref.dtype)
 
 
@@ -147,6 +158,7 @@
             pltpu.VMEM((2, width, SLOTS * TILE), jnp.bfloat16),
             pltpu.VMEM((2, SLOTS * TILE, width), jnp.bfloat16),
             pltpu.SemaphoreType.DMA((2, 2, SLOTS)),
+            pltpu.VMEM((SLOTS, TILE, TILE), jnp.float32),
         ],
     )
     kernel = lambda *args: attention_kernel(*args, heads_local=heads_local, scale=scale, pieces=pieces)

time: 323 us -> 407 us (1.26)
  Pallas kernels: 24.3 us -> 106 us
    pallas_call x1, Pallas kernels: 24.3 us -> 106 us  [body(): pl.pallas_call(kernel, grid_spec=grid_spec, out_shape=jax.ShapeDtypeStruc...]
  transfers between devices with their start and end apart: 15 -> 15, of which waited for: 7 -> 7; matrix products, arithmetic and copies ran while one was open for 5% -> 4% of each run, Pallas kernels for 0% -> 0%
where the time goes in v11:
time: 407 us; the launch traced here: 399 us
  waiting for transfers between devices  228 us (56%)
  Pallas kernels  106 us (26%)
  starting transfers between devices  26.5 us (7%)
  blocking collectives  18.8 us (5%)
  local copies, waits for them, and re-layouts  15.2 us (4%)
  other arithmetic  4.36 us (1%)
    ppermute x12, waiting for transfers between devices, permute(): return lax.ppermute(block, axis, route)  113 us
    pallas_call x1, Pallas kernels, body(): pl.pallas_call(kernel, grid_spec=grid_spec, out_shape=jax.ShapeDtypeStruc...  106 us
    all_to_all x1, waiting for transfers between devices, body(): lax.all_to_all(key_states, 'head', split_axis=1, concat_axis=0, tiled=True)  53.7 us
    all_to_all x1, waiting for transfers between devices, body(): lax.all_to_all(queries, 'head', split_axis=1, concat_axis=0, tiled=True)  41.3 us
    all_to_all x1, waiting for transfers between devices, body(): lax.all_to_all(value_states, 'head', split_axis=1, concat_axis=0, tiled=T...  19.9 us
    all_to_all x1, blocking collectives, body(): return lax.all_to_all(out, 'head', split_axis=0, concat_axis=1, tiled=True)  18.8 us
    ppermute x12, starting transfers between devices, permute(): return lax.ppermute(block, axis, route)  12.3 us
  transfers between devices with their start and end apart: 15, of which 7 were waited for; matrix products, arithmetic and copies ran while one was open for 4% of the time, Pallas kernels for 0%

profile of v11, /device:TPU:128, one launch (start us, length us, event | category | flops | bytes accessed | tf_op | source)
XLA Modules:
  0.0 399.3 jit_solution(2007437551842062737)
XLA Ops:
  0.0 2.7 copy.30
  2.7 5.1 %all-to-all-start.2 = ((bf16[128,8,768]{2,0,1:T(8,128)(2,1)}), bf16[128,8,768]{2,0,1:T(8,128)(2,1)}, u32[]{:S(2)}, u32[]{:S(2)}) async-start(bf16[128,8,768]{2,0,1:T(8,128)(2,1)} %bitcast.33), calls=%async_computation.2 | async-start | bytes 3145728 | tf_op jit(solution)/shard_map/all_to_all | solution.py:118
  7.7 1.6 copy.18
  9.3 19.9 %all-to-all-done.2 = bf16[128,8,768]{2,0,1:T(8,128)(2,1)} async-done(((bf16[128,8,768]{2,0,1:T(8,128)(2,1)}), bf16[128,8,768]{2,0,1:T(8,128)(2,1)}, u32[]{:S(2)}, u32[]{:S(2)}) %all-to-all-start.2) | async-done | bytes 1572896 | tf_op jit(solution)/shard_map/all_to_all | solution.py:118
  29.2 4.3 %all-to-all-start.1 = ((bf16[128,8,768]{0,2,1:T(8,128)(2,1)}), bf16[128,8,768]{0,2,1:T(8,128)(2,1)}, u32[]{:S(2)}, u32[]{:S(2)}) async-start(bf16[128,8,768]{0,2,1:T(8,128)(2,1)} %bitcast.4), calls=%async_computation.1 | async-start | bytes 3145728 | tf_op jit(solution)/shard_map/all_to_all | solution.py:116
  33.5 2.8 collective-permute-start.7
  36.3 53.7 %all-to-all-done.1 = bf16[128,8,768]{0,2,1:T(8,128)(2,1)} async-done(((bf16[128,8,768]{0,2,1:T(8,128)(2,1)}), bf16[128,8,768]{0,2,1:T(8,128)(2,1)}, u32[]{:S(2)}, u32[]{:S(2)}) %all-to-all-start.1) | async-done | bytes 1572896 | tf_op jit(solution)/shard_map/all_to_all | solution.py:116
  90.0 2.9 bitcast_bitcast_fusion.args_4_
  92.9 2.0 collective-permute-start
  95.4 27.0 %collective-permute-done.6.args_12_ = bf16[1024,768]{1,0:T(8,128)(2,1)S(1)} collective-permute-done((bf16[1024,768]{1,0:T(8,128)(2,1)}, bf16[1024,768]{1,0:T(8,128)(2,1)S(1)}, u32[]{:S(2)}, u32[]{:S(2)}) %collective-permute-start.6) | collective-permute-done | bytes 1572896 | tf_op jit(solution)/shard_map/ppermute | solution.py:19
  122.4 1.4 copy.31
  123.8 4.8 %all-to-all-start = ((bf16[128,8,768]{2,0,1:T(8,128)(2,1)}), bf16[128,8,768]{2,0,1:T(8,128)(2,1)}, u32[]{:S(2)}, u32[]{:S(2)}) async-start(bf16[128,8,768]{2,0,1:T(8,128)(2,1)} %bitcast.35), calls=%async_computation | async-start | bytes 3145728 | tf_op jit(solution)/shard_map/all_to_all | solution.py:120
  128.6 1.3 broadcast_select_fusion
  129.9 53.8 %collective-permute-done.1.args_6_ = bf16[768,1024]{1,0:T(8,128)(2,1)} collective-permute-done((bf16[768,1024]{1,0:T(8,128)(2,1)}, bf16[768,1024]{1,0:T(8,128)(2,1)}, u32[]{:S(2)}, u32[]{:S(2)}) %collective-permute-start.1) | collective-permute-done | bytes 1572896 | tf_op jit(solution)/shard_map/ppermute | solution.py:19
  183.7 6.3 %collective-permute-start.9 = (bf16[1024,768]{1,0:T(8,128)(2,1)}, bf16[1024,768]{1,0:T(8,128)(2,1)}, u32[]{:S(2)}, u32[]{:S(2)}) collective-permute-start(bf16[1024,768]{1,0:T(8,128)(2,1)} %broadcast_select_fusion), channel_id=1, source_target_pairs={{0,31},{1,2},{2,1},{3,4},{4,3},{5,6},{6,5},{7,8},{8,7},{9,10},{10,... | collective-permute-start | bytes 4718600 | tf_op jit(solution)/shard_map/ppermute | solution.py:19
  190.0 2.8 broadcast_select_fusion.1
  197.2 0.8 copy.21.args_2_
  198.0 41.3 %all-to-all-done = bf16[128,8,768]{2,0,1:T(8,128)(2,1)} async-done(((bf16[128,8,768]{2,0,1:T(8,128)(2,1)}), bf16[128,8,768]{2,0,1:T(8,128)(2,1)}, u32[]{:S(2)}, u32[]{:S(2)}) %all-to-all-start) | async-done | bytes 1572896 | tf_op jit(solution)/shard_map/all_to_all | solution.py:120
  239.3 15.8 %collective-permute-done.9.args_15_ = bf16[1024,768]{1,0:T(8,128)(2,1)} collective-permute-done((bf16[1024,768]{1,0:T(8,128)(2,1)}, bf16[1024,768]{1,0:T(8,128)(2,1)}, u32[]{:S(2)}, u32[]{:S(2)}) %collective-permute-start.9) | collective-permute-done | bytes 1572896 | tf_op jit(solution)/shard_map/ppermute | solution.py:19
  255.1 16.8 %collective-permute-done.3.args_8_ = bf16[768,1024]{1,0:T(8,128)(2,1)} collective-permute-done((bf16[768,1024]{1,0:T(8,128)(2,1)}, bf16[768,1024]{1,0:T(8,128)(2,1)}, u32[]{:S(2)}, u32[]{:S(2)}) %collective-permute-start.3) | collective-permute-done | bytes 1572896 | tf_op jit(solution)/shard_map/ppermute | solution.py:19
  272.0 1.1 copy-done.3
  273.1 106.0 %shard_map.73 = bf16[1024,768]{1,0:T(8,128)(2,1)} custom-call(s32[64]{0:T(128)} %reshape.68.args_0_, s32[8]{0:T(128)} %args_1_.4, f32[8,6,1024]{2,1,0:T(8,128)} %copy.21.args_2_, bf16[1024,768]{1,0:T(8,128)(2,1)} %bitcast.3.args_3_, bf16[768,1024]{1,0:T(8,128)(2,1)} %bitcast_bitcast_fusion.args_4_, bf16[768,1024]{1,0:T(8,128)(2,1)} %collective-permute-done.args_5_, ...), custom_call_target="tpu_custom_call" | custom-call | tf_op jit(solution)/shard_map/pallas_call | solution.py:165
  379.2 18.8 %all_to_all.76 = bf16[8,128,768]{2,1,0:T(8,128)(2,1)S(1)} all-to-all(bf16[8,128,768]{2,1,0:T(8,128)(2,1)} %bitcast.36), channel_id=1, replica_groups=mesh['head'=8,'blk'=32] {'head'}, dimensions={0} | all-to-all | bytes 3145728 | tf_op jit(solution)/shard_map/all_to_all | solution.py:178
  398.0 1.3 copy.26
  (53 shorter events, 4.9 us)
Async XLA Ops:
  0.0 195.3 %copy-start = (s32[256]{0:T(256)S(1)}, s32[256]{0:T(256)}, u32[]{:S(2)}) copy-start(s32[256]{0:T(256)} %param.12) | copy-start | bytes 3076
  2.7 5.1 %copy-start.4 = (bf16[128,6144]{1,0:T(8,128)(2,1)S(1)}, bf16[128,6144]{1,0:T(8,128)(2,1)}, u32[]{:S(2)}) copy-start(bf16[128,6144]{1,0:T(8,128)(2,1)} %param.8) | copy-start | bytes 4718596
  2.7 26.5 %all-to-all-start.2 = ((bf16[128,8,768]{2,0,1:T(8,128)(2,1)}), bf16[128,8,768]{2,0,1:T(8,128)(2,1)}, u32[]{:S(2)}, u32[]{:S(2)}) async-start(bf16[128,8,768]{2,0,1:T(8,128)(2,1)} %bitcast.33), calls=%async_computation.2 | async-start | bytes 3145728 | tf_op jit(solution)/shard_map/all_to_all | solution.py:118
  29.2 60.8 %all-to-all-start.1 = ((bf16[128,8,768]{0,2,1:T(8,128)(2,1)}), bf16[128,8,768]{0,2,1:T(8,128)(2,1)}, u32[]{:S(2)}, u32[]{:S(2)}) async-start(bf16[128,8,768]{0,2,1:T(8,128)(2,1)} %bitcast.4), calls=%async_computation.1 | async-start | bytes 3145728 | tf_op jit(solution)/shard_map/all_to_all | solution.py:116
  33.5 61.5 %collective-permute-start.7 = (bf16[1024,768]{1,0:T(8,128)(2,1)}, bf16[1024,768]{1,0:T(8,128)(2,1)S(1)}, u32[]{:S(2)}, u32[]{:S(2)}) collective-permute-start(bf16[1024,768]{1,0:T(8,128)(2,1)} %bitcast.8.args_11_), channel_id=1, source_target_pairs={{0,30},{1,31},{2,0},{3,1},{4,2},{5,3},{6,4},{7,5},{8,6},{9,7},{10,... | collective-permute-start | bytes 4718600 | tf_op jit(solution)/shard_map/ppermute | solution.py:19
  36.3 86.1 %collective-permute-start.6 = (bf16[1024,768]{1,0:T(8,128)(2,1)}, bf16[1024,768]{1,0:T(8,128)(2,1)S(1)}, u32[]{:S(2)}, u32[]{:S(2)}) collective-permute-start(bf16[1024,768]{1,0:T(8,128)(2,1)} %bitcast.8.args_11_), channel_id=1, source_target_pairs={{0,2},{1,3},{2,4},{3,5},{4,6},{5,7},{6,8},{7,9},{8,10},{9,11},{10,... | collective-permute-start | bytes 4718600 | tf_op jit(solution)/shard_map/ppermute | solution.py:19
  90.0 32.4 %copy-start.5 = (bf16[128,6144]{1,0:T(8,128)(2,1)S(1)}, bf16[128,6144]{1,0:T(8,128)(2,1)}, u32[]{:S(2)}) copy-start(bf16[128,6144]{1,0:T(8,128)(2,1)} %param.7) | copy-start | bytes 4718596
  92.9 90.8 %collective-permute-start.1 = (bf16[768,1024]{1,0:T(8,128)(2,1)}, bf16[768,1024]{1,0:T(8,128)(2,1)}, u32[]{:S(2)}, u32[]{:S(2)}) collective-permute-start(bf16[768,1024]{1,0:T(8,128)(2,1)} %bitcast_bitcast_fusion.args_4_), channel_id=1, source_target_pairs={{0,30},{1,31},{2,0},{3,1},{4,2},{5,3},{6,4},{7,5},{8,6},{9,7},{10,... | collective-permute-start | bytes 4718600 | tf_op jit(solution)/shard_map/ppermute | solution.py:19
  92.9 97.1 %collective-permute-start = (bf16[768,1024]{1,0:T(8,128)(2,1)}, bf16[768,1024]{1,0:T(8,128)(2,1)}, u32[]{:S(2)}, u32[]{:S(2)}) collective-permute-start(bf16[768,1024]{1,0:T(8,128)(2,1)} %bitcast_bitcast_fusion.args_4_), channel_id=1, source_target_pairs={{0,2},{1,3},{2,4},{3,5},{4,6},{5,7},{6,8},{7,9},{8,10},{9,11},{10,... | collective-permute-start | bytes 4718600 | tf_op jit(solution)/shard_map/ppermute | solution.py:19
  94.9 97.9 %collective-permute-start.8 = (bf16[1024,768]{1,0:T(8,128)(2,1)}, bf16[1024,768]{1,0:T(8,128)(2,1)}, u32[]{:S(2)}, u32[]{:S(2)}) collective-permute-start(bf16[1024,768]{1,0:T(8,128)(2,1)} %bitcast.8.args_11_), channel_id=1, source_target_pairs={{0,1},{1,0},{2,3},{3,2},{4,5},{5,4},{6,7},{7,6},{8,9},{9,8},{10,11... | collective-permute-start | bytes 4718600 | tf_op jit(solution)/shard_map/ppermute | solution.py:19
  94.9 33.7 %copy-start.1 = (bf16[1024,768]{1,0:T(8,128)(2,1)}, bf16[1024,768]{1,0:T(8,128)(2,1)S(1)}, u32[]{:S(2)}) copy-start(bf16[1024,768]{1,0:T(8,128)(2,1)S(1)} %collective-permute-done.7.args_13_) | copy-start | bytes 4718596
  94.9 98.0 %collective-permute-start.2 = (bf16[768,1024]{1,0:T(8,128)(2,1)}, bf16[768,1024]{1,0:T(8,128)(2,1)}, u32[]{:S(2)}, u32[]{:S(2)}) collective-permute-start(bf16[768,1024]{1,0:T(8,128)(2,1)} %bitcast_bitcast_fusion.args_4_), channel_id=1, source_target_pairs={{0,1},{1,0},{2,3},{3,2},{4,5},{5,4},{6,7},{7,6},{8,9},{9,8},{10,11... | collective-permute-start | bytes 4718600 | tf_op jit(solution)/shard_map/ppermute | solution.py:19
  122.4 70.4 %copy-start.2 = (bf16[1024,768]{1,0:T(8,128)(2,1)}, bf16[1024,768]{1,0:T(8,128)(2,1)S(1)}, u32[]{:S(2)}) copy-start(bf16[1024,768]{1,0:T(8,128)(2,1)S(1)} %collective-permute-done.6.args_12_) | copy-start | bytes 4718596
  122.4 71.0 %collective-permute-start.11 = (bf16[1024,768]{1,0:T(8,128)(2,1)S(1)}, bf16[1024,768]{1,0:T(8,128)(2,1)}, u32[]{:S(2)}, u32[]{:S(2)}) collective-permute-start(bf16[1024,768]{1,0:T(8,128)(2,1)S(1)} %collective-permute-done.7.args_13_), channel_id=1, source_target_pairs={{0,1},{1,0},{2,3},{3,2},{4,5},{5,4},{6,7},{7,6},{8,9},{9,8},{10,11... | collective-permute-start | bytes 4718600 | tf_op jit(solution)/shard_map/ppermute | solution.py:19
  123.8 115.5 %all-to-all-start = ((bf16[128,8,768]{2,0,1:T(8,128)(2,1)}), bf16[128,8,768]{2,0,1:T(8,128)(2,1)}, u32[]{:S(2)}, u32[]{:S(2)}) async-start(bf16[128,8,768]{2,0,1:T(8,128)(2,1)} %bitcast.35), calls=%async_computation | async-start | bytes 3145728 | tf_op jit(solution)/shard_map/all_to_all | solution.py:120
  129.9 63.6 %copy-start.6 = (s32[8,8]{1,0:T(8,128)S(1)}, s32[8,8]{1,0:T(8,128)}, u32[]{:S(2)}) copy-start(s32[8,8]{1,0:T(8,128)} %param.10) | copy-start | bytes 772
  129.9 63.8 %copy-start.7 = (s32[2,7]{1,0:T(2,128)S(1)}, s32[2,7]{1,0:T(2,128)}, u32[]{:S(2)}) copy-start(s32[2,7]{1,0:T(2,128)} %constant.89.clone) | copy-start | bytes 172
  183.7 71.4 %collective-permute-start.9 = (bf16[1024,768]{1,0:T(8,128)(2,1)}, bf16[1024,768]{1,0:T(8,128)(2,1)}, u32[]{:S(2)}, u32[]{:S(2)}) collective-permute-start(bf16[1024,768]{1,0:T(8,128)(2,1)} %broadcast_select_fusion), channel_id=1, source_target_pairs={{0,31},{1,2},{2,1},{3,4},{4,3},{5,6},{6,5},{7,8},{8,7},{9,10},{10,... | collective-permute-start | bytes 4718600 | tf_op jit(solution)/shard_map/ppermute | solution.py:19
  192.8 79.2 %collective-permute-start.3 = (bf16[768,1024]{1,0:T(8,128)(2,1)}, bf16[768,1024]{1,0:T(8,128)(2,1)}, u32[]{:S(2)}, u32[]{:S(2)}) collective-permute-start(bf16[768,1024]{1,0:T(8,128)(2,1)} %broadcast_select_fusion.1), channel_id=1, source_target_pairs={{0,31},{1,2},{2,1},{3,4},{4,3},{5,6},{6,5},{7,8},{8,7},{9,10},{10,... | collective-permute-start | bytes 4718600 | tf_op jit(solution)/shard_map/ppermute | solution.py:19
  192.8 62.3 %collective-permute-start.10 = (bf16[1024,768]{1,0:T(8,128)(2,1)S(1)}, bf16[1024,768]{1,0:T(8,128)(2,1)}, u32[]{:S(2)}, u32[]{:S(2)}) collective-permute-start(bf16[1024,768]{1,0:T(8,128)(2,1)S(1)} %collective-permute-done.6.args_12_), channel_id=1, source_target_pairs={{0,1},{1,0},{2,3},{3,2},{4,5},{5,4},{6,7},{7,6},{8,9},{9,8},{10,11... | collective-permute-start | bytes 4718600 | tf_op jit(solution)/shard_map/ppermute | solution.py:19
  192.9 62.2 %collective-permute-start.5 = (bf16[768,1024]{1,0:T(8,128)(2,1)}, bf16[768,1024]{1,0:T(8,128)(2,1)}, u32[]{:S(2)}, u32[]{:S(2)}) collective-permute-start(bf16[768,1024]{1,0:T(8,128)(2,1)} %collective-permute-done.1.args_6_), channel_id=1, source_target_pairs={{0,1},{1,0},{2,3},{3,2},{4,5},{5,4},{6,7},{7,6},{8,9},{9,8},{10,11... | collective-permute-start | bytes 4718600 | tf_op jit(solution)/shard_map/ppermute | solution.py:19
  193.4 78.6 %collective-permute-start.4 = (bf16[768,1024]{1,0:T(8,128)(2,1)}, bf16[768,1024]{1,0:T(8,128)(2,1)S(1)}, u32[]{:S(2)}, u32[]{:S(2)}) collective-permute-start(bf16[768,1024]{1,0:T(8,128)(2,1)} %collective-permute-done.args_5_), channel_id=1, source_target_pairs={{0,1},{1,0},{2,3},{3,2},{4,5},{5,4},{6,7},{7,6},{8,9},{9,8},{10,11... | collective-permute-start | bytes 4718600 | tf_op jit(solution)/shard_map/ppermute | solution.py:19
  272.0 1.1 copy-start.3

commit v12 on v9

--- a/solution.py
+++ b/solution.py
@@ -23,7 +23,7 @@
     return [(i, (i + distance) % n) for i in range(n)]
 
 
-def attention_kernel(sw_ref, cnt_ref, bias_ref, q_ref, *refs, heads_local, scale, pieces):
+def attention_kernel(sw_ref, cnt_ref, bias_ref, q_ref, *refs, heads_local, scale, pieces, rows):
     k_hbm = refs[:pieces]
     v_hbm = refs[pieces:2 * pieces]
     o_ref, k_buf, v_buf, sem = refs[2 * pieces:]
@@ -68,7 +68,7 @@
 
     count = cnt_ref[i]
     keys = SLOTS * TILE
-    valid = lax.broadcasted_iota(jnp.int32, (TILE, keys), 1) < count * TILE
+    valid = lax.broadcasted_iota(jnp.int32, (rows, keys), 1) < count * TILE
     k_all = k_buf.at[parity]
     v_all = v_buf.at[parity]
     for h in range(heads_local):
@@ -130,40 +130,47 @@
 
     assert tile_count == TILE_COUNT
     pieces = len(k_window)
+    rows = TILE // 2
     any_spec = pl.BlockSpec(memory_space=pl.ANY)
-    in_specs = (
-        [
-            pl.BlockSpec((None, heads_local, SLOTS * TILE), lambda i, sw, cnt: (i, 0, 0)),
-            pl.BlockSpec((TILE, width), lambda i, sw, cnt: (i, 0)),
-        ]
-        + [any_spec] * (2 * pieces)
-    )
-    grid_spec = pltpu.PrefetchScalarGridSpec(
-        num_scalar_prefetch=2,
-        grid=(tile_count,),
-        in_specs=in_specs,
-        out_specs=pl.BlockSpec((TILE, width), lambda i, sw, cnt: (i, 0)),
-        scratch_shapes=[
-            pltpu.VMEM((2, width, SLOTS * TILE), jnp.bfloat16),
-            pltpu.VMEM((2, SLOTS * TILE, width), jnp.bfloat16),
-            pltpu.SemaphoreType.DMA((2, 2, SLOTS)),
-        ],
-    )
-    kernel = lambda *args: attention_kernel(*args, heads_local=heads_local, scale=scale, pieces=pieces)
-    out = pl.pallas_call(
-        kernel,
-        grid_spec=grid_spec,
-        out_shape=jax.ShapeDtypeStruct((shard_tok, width), jnp.bfloat16),
-        compiler_params=pltpu.CompilerParams(dimension_semantics=("arbitrary",)),
-    )(
-        slot_window.reshape(-1),
-        block_counts.astype(jnp.int32),
-        bias,
-        q_heads,
-        *k_window,
-        *v_window,
-    )
-    return lax.all_to_all(out, "head", split_axis=0, concat_axis=1, tiled=True)
+
+    def half_call(half):
+        in_specs = (
+            [
+                pl.BlockSpec((None, heads_local, SLOTS * TILE), lambda i, sw, cnt: (i, 0, 0)),
+                pl.BlockSpec((rows, width), lambda i, sw, cnt: (2 * i + half, 0)),
+            ]
+            + [any_spec] * (2 * pieces)
+        )
+        grid_spec = pltpu.PrefetchScalarGridSpec(
+            num_scalar_prefetch=2,
+            grid=(tile_count,),
+            in_specs=in_specs,
+            out_specs=pl.BlockSpec((rows, width), lambda i, sw, cnt: (i, 0)),
+            scratch_shapes=[
+                pltpu.VMEM((2, width, SLOTS * TILE), jnp.bfloat16),
+                pltpu.VMEM((2, SLOTS * TILE, width), jnp.bfloat16),
+                pltpu.SemaphoreType.DMA((2, 2, SLOTS)),
+            ],
+        )
+        kernel = lambda *args: attention_kernel(
+            *args, heads_local=heads_local, scale=scale, pieces=pieces, rows=rows
+        )
+        out = pl.pallas_call(
+            kernel,
+            grid_spec=grid_spec,
+            out_shape=jax.ShapeDtypeStruct((tile_count * rows, width), jnp.bfloat16),
+            compiler_params=pltpu.CompilerParams(dimension_semantics=("arbitrary",)),
+        )(
+            slot_window.reshape(-1),
+            block_counts.astype(jnp.int32),
+            bias,
+            q_heads,
+            *k_window,
+            *v_window,
+        )
+        return lax.all_to_all(out, "head", split_axis=0, concat_axis=1, tiled=True)
+
+    return jnp.concatenate([half_call(0), half_call(1)], axis=0)
 
 
 def solution(mesh):

time: 323 us -> 345 us (1.068)
  Pallas kernels: 24.3 us -> 44.1 us
  blocking collectives: 18.8 us -> 0 us
  waiting for transfers between devices: 228 us -> 240 us
  starting transfers between devices: 26.6 us -> 37.5 us
    pallas_call x1 -> x2, Pallas kernels: 24.3 us -> 44.1 us  [half_call(): pl.pallas_call(kernel, grid_spec=grid_spec, out_shape=jax.ShapeDtypeStruc...]
    all_to_all x1 -> x0, blocking collectives: 18.8 us -> none  [body(): return lax.all_to_all(out, 'head', split_axis=0, concat_axis=1, tiled=True)]
    all_to_all x0 -> x2, starting transfers between devices: none -> 11 us  [half_call(): return lax.all_to_all(out, 'head', split_axis=0, concat_axis=1, tiled=True)]
    all_to_all x0 -> x2, waiting for transfers between devices: none -> 10.1 us  [half_call(): return lax.all_to_all(out, 'head', split_axis=0, concat_axis=1, tiled=True)]
  transfers between devices with their start and end apart: 15 -> 17, of which waited for: 7 -> 8; matrix products, arithmetic and copies ran while one was open for 5% -> 4% of each run, Pallas kernels for 0% -> 6%
where the time goes in v12:
time: 345 us; the launch traced here: 341 us
  waiting for transfers between devices  240 us (70%)
  Pallas kernels  44.1 us (13%)
  starting transfers between devices  37.5 us (11%)
  local copies, waits for them, and re-layouts  13.9 us (4%)
  other arithmetic  5.63 us (2%)
    ppermute x12, waiting for transfers between devices, permute(): return lax.ppermute(block, axis, route)  115 us
    all_to_all x1, waiting for transfers between devices, body(): lax.all_to_all(key_states, 'head', split_axis=1, concat_axis=0, tiled=True)  53.7 us
    pallas_call x2, Pallas kernels, half_call(): pl.pallas_call(kernel, grid_spec=grid_spec, out_shape=jax.ShapeDtypeStruc...  44.1 us
    all_to_all x1, waiting for transfers between devices, body(): lax.all_to_all(queries, 'head', split_axis=1, concat_axis=0, tiled=True)  41.4 us
    all_to_all x1, waiting for transfers between devices, body(): lax.all_to_all(value_states, 'head', split_axis=1, concat_axis=0, tiled=T...  19.9 us
    ppermute x12, starting transfers between devices, permute(): return lax.ppermute(block, axis, route)  12.3 us
    all_to_all x2, starting transfers between devices, half_call(): return lax.all_to_all(out, 'head', split_axis=0, concat_axis=1, tiled=True)  11 us
    all_to_all x2, waiting for transfers between devices, half_call(): return lax.all_to_all(out, 'head', split_axis=0, concat_axis=1, tiled=True)  10.1 us
  transfers between devices with their start and end apart: 17, of which 8 were waited for; matrix products, arithmetic and copies ran while one was open for 4% of the time, Pallas kernels for 6%

profile of v12, /device:TPU:128, one launch (start us, length us, event | category | flops | bytes accessed | tf_op | source)
XLA Modules:
  0.0 340.8 jit_solution(763178269938360412)
XLA Ops:
  0.0 2.7 copy.36
  2.7 5.1 %all-to-all-start.2 = ((bf16[128,8,768]{2,0,1:T(8,128)(2,1)}), bf16[128,8,768]{2,0,1:T(8,128)(2,1)}, u32[]{:S(2)}, u32[]{:S(2)}) async-start(bf16[128,8,768]{2,0,1:T(8,128)(2,1)} %bitcast.37), calls=%async_computation.2 | async-start | bytes 3145728 | tf_op jit(solution)/shard_map/all_to_all | solution.py:107
  7.7 1.6 copy.21
  9.3 19.9 %all-to-all-done.2 = bf16[128,8,768]{2,0,1:T(8,128)(2,1)} async-done(((bf16[128,8,768]{2,0,1:T(8,128)(2,1)}), bf16[128,8,768]{2,0,1:T(8,128)(2,1)}, u32[]{:S(2)}, u32[]{:S(2)}) %all-to-all-start.2) | async-done | bytes 1572896 | tf_op jit(solution)/shard_map/all_to_all | solution.py:107
  29.2 4.3 %all-to-all-start.1 = ((bf16[128,8,768]{0,2,1:T(8,128)(2,1)}), bf16[128,8,768]{0,2,1:T(8,128)(2,1)}, u32[]{:S(2)}, u32[]{:S(2)}) async-start(bf16[128,8,768]{0,2,1:T(8,128)(2,1)} %bitcast.4), calls=%async_computation.1 | async-start | bytes 3145728 | tf_op jit(solution)/shard_map/all_to_all | solution.py:105
  33.5 2.8 collective-permute-start.7
  36.3 53.7 %all-to-all-done.1 = bf16[128,8,768]{0,2,1:T(8,128)(2,1)} async-done(((bf16[128,8,768]{0,2,1:T(8,128)(2,1)}), bf16[128,8,768]{0,2,1:T(8,128)(2,1)}, u32[]{:S(2)}, u32[]{:S(2)}) %all-to-all-start.1) | async-done | bytes 1572896 | tf_op jit(solution)/shard_map/all_to_all | solution.py:105
  90.0 2.9 bitcast_bitcast_fusion.args_4_
  92.9 2.0 collective-permute-start
  95.5 27.0 %collective-permute-done.6.args_12_ = bf16[1024,768]{1,0:T(8,128)(2,1)S(1)} collective-permute-done((bf16[1024,768]{1,0:T(8,128)(2,1)}, bf16[1024,768]{1,0:T(8,128)(2,1)S(1)}, u32[]{:S(2)}, u32[]{:S(2)}) %collective-permute-start.6) | collective-permute-done | bytes 1572896 | tf_op jit(solution)/shard_map/ppermute | solution.py:19
  122.5 1.4 copy.37
  123.8 4.8 %all-to-all-start = ((bf16[128,8,768]{2,0,1:T(8,128)(2,1)}), bf16[128,8,768]{2,0,1:T(8,128)(2,1)}, u32[]{:S(2)}, u32[]{:S(2)}) async-start(bf16[128,8,768]{2,0,1:T(8,128)(2,1)} %bitcast.39), calls=%async_computation | async-start | bytes 3145728 | tf_op jit(solution)/shard_map/all_to_all | solution.py:109
  128.6 1.3 broadcast_select_fusion
  130.0 53.7 %collective-permute-done.1.args_6_ = bf16[768,1024]{1,0:T(8,128)(2,1)} collective-permute-done((bf16[768,1024]{1,0:T(8,128)(2,1)}, bf16[768,1024]{1,0:T(8,128)(2,1)}, u32[]{:S(2)}, u32[]{:S(2)}) %collective-permute-start.1) | collective-permute-done | bytes 1572896 | tf_op jit(solution)/shard_map/ppermute | solution.py:19
  183.7 6.3 %collective-permute-start.9 = (bf16[1024,768]{1,0:T(8,128)(2,1)}, bf16[1024,768]{1,0:T(8,128)(2,1)}, u32[]{:S(2)}, u32[]{:S(2)}) collective-permute-start(bf16[1024,768]{1,0:T(8,128)(2,1)} %broadcast_select_fusion), channel_id=1, source_target_pairs={{0,31},{1,2},{2,1},{3,4},{4,3},{5,6},{6,5},{7,8},{8,7},{9,10},{10,... | collective-permute-start | bytes 4718600 | tf_op jit(solution)/shard_map/ppermute | solution.py:19
  190.0 2.8 broadcast_select_fusion.1
  197.9 41.4 %all-to-all-done = bf16[128,8,768]{2,0,1:T(8,128)(2,1)} async-done(((bf16[128,8,768]{2,0,1:T(8,128)(2,1)}), bf16[128,8,768]{2,0,1:T(8,128)(2,1)}, u32[]{:S(2)}, u32[]{:S(2)}) %all-to-all-start) | async-done | bytes 1572896 | tf_op jit(solution)/shard_map/all_to_all | solution.py:109
  239.3 15.8 %collective-permute-done.9.args_15_ = bf16[1024,768]{1,0:T(8,128)(2,1)} collective-permute-done((bf16[1024,768]{1,0:T(8,128)(2,1)}, bf16[1024,768]{1,0:T(8,128)(2,1)}, u32[]{:S(2)}, u32[]{:S(2)}) %collective-permute-start.9) | collective-permute-done | bytes 1572896 | tf_op jit(solution)/shard_map/ppermute | solution.py:19
  255.2 18.0 %collective-permute-done.3.args_8_ = bf16[768,1024]{1,0:T(8,128)(2,1)} collective-permute-done((bf16[768,1024]{1,0:T(8,128)(2,1)}, bf16[768,1024]{1,0:T(8,128)(2,1)}, u32[]{:S(2)}, u32[]{:S(2)}) %collective-permute-start.3) | collective-permute-done | bytes 1572896 | tf_op jit(solution)/shard_map/ppermute | solution.py:19
  274.3 22.0 %shard_map.74 = bf16[512,768]{1,0:T(8,128)(2,1)} custom-call(s32[64]{0:T(128)} %reshape.72.args_0_, s32[8]{0:T(128)} %args_1_.6, f32[8,6,1024]{2,1,0:T(8,128)} %copy.24.args_2_, bf16[1024,768]{1,0:T(8,128)(2,1)} %bitcast.3.args_3_, bf16[768,1024]{1,0:T(8,128)(2,1)} %bitcast_bitcast_fusion.args_4_, bf16[768,1024]{1,0:T(8,128)(2,1)} %collective-permute-done.args_5_, ...), custom_call_target="tpu_custom_call" | custom-call | tf_op jit(solution)/shard_map/pallas_call | solution.py:158
  296.3 5.3 %all-to-all-start.4 = ((bf16[8,64,768]{2,1,0:T(8,128)(2,1)}), bf16[8,64,768]{2,1,0:T(8,128)(2,1)S(1)}, u32[]{:S(2)}, u32[]{:S(2)}) async-start(bf16[8,64,768]{2,1,0:T(8,128)(2,1)} %bitcast.41), calls=%async_computation.4 | async-start | bytes 1572864 | tf_op jit(solution)/shard_map/all_to_all | solution.py:171
  301.6 22.0 %shard_map.73 = bf16[512,768]{1,0:T(8,128)(2,1)} custom-call(s32[64]{0:T(128)} %reshape.72.args_0_, s32[8]{0:T(128)} %args_1_.6, f32[8,6,1024]{2,1,0:T(8,128)} %copy.24.args_2_, bf16[1024,768]{1,0:T(8,128)(2,1)} %bitcast.3.args_3_, bf16[768,1024]{1,0:T(8,128)(2,1)} %bitcast_bitcast_fusion.args_4_, bf16[768,1024]{1,0:T(8,128)(2,1)} %collective-permute-done.args_5_, ...), custom_call_target="tpu_custom_call" | custom-call | tf_op jit(solution)/shard_map/pallas_call | solution.py:158
  323.6 5.7 %all-to-all-start.3 = ((bf16[8,64,768]{2,1,0:T(8,128)(2,1)}), bf16[8,64,768]{2,1,0:T(8,128)(2,1)S(1)}, u32[]{:S(2)}, u32[]{:S(2)}) async-start(bf16[8,64,768]{2,1,0:T(8,128)(2,1)} %bitcast.40), calls=%async_computation.3 | async-start | bytes 1572864 | tf_op jit(solution)/shard_map/all_to_all | solution.py:171
  329.4 10.1 %all-to-all-done.3 = bf16[8,64,768]{2,1,0:T(8,128)(2,1)S(1)} async-done(((bf16[8,64,768]{2,1,0:T(8,128)(2,1)}), bf16[8,64,768]{2,1,0:T(8,128)(2,1)S(1)}, u32[]{:S(2)}, u32[]{:S(2)}) %all-to-all-start.3) | async-done | bytes 786464 | tf_op jit(solution)/shard_map/all_to_all | solution.py:171
  (59 shorter events, 8.1 us)
Async XLA Ops:
  0.0 195.2 %copy-start = (s32[256]{0:T(256)S(1)}, s32[256]{0:T(256)}, u32[]{:S(2)}) copy-start(s32[256]{0:T(256)} %param.12) | copy-start | bytes 3076
  2.7 5.1 %copy-start.4 = (bf16[128,6144]{1,0:T(8,128)(2,1)S(1)}, bf16[128,6144]{1,0:T(8,128)(2,1)}, u32[]{:S(2)}) copy-start(bf16[128,6144]{1,0:T(8,128)(2,1)} %param.8) | copy-start | bytes 4718596
  2.7 26.5 %all-to-all-start.2 = ((bf16[128,8,768]{2,0,1:T(8,128)(2,1)}), bf16[128,8,768]{2,0,1:T(8,128)(2,1)}, u32[]{:S(2)}, u32[]{:S(2)}) async-start(bf16[128,8,768]{2,0,1:T(8,128)(2,1)} %bitcast.37), calls=%async_computation.2 | async-start | bytes 3145728 | tf_op jit(solution)/shard_map/all_to_all | solution.py:107
  29.2 60.8 %all-to-all-start.1 = ((bf16[128,8,768]{0,2,1:T(8,128)(2,1)}), bf16[128,8,768]{0,2,1:T(8,128)(2,1)}, u32[]{:S(2)}, u32[]{:S(2)}) async-start(bf16[128,8,768]{0,2,1:T(8,128)(2,1)} %bitcast.4), calls=%async_computation.1 | async-start | bytes 3145728 | tf_op jit(solution)/shard_map/all_to_all | solution.py:105
  33.5 61.5 %collective-permute-start.7 = (bf16[1024,768]{1,0:T(8,128)(2,1)}, bf16[1024,768]{1,0:T(8,128)(2,1)S(1)}, u32[]{:S(2)}, u32[]{:S(2)}) collective-permute-start(bf16[1024,768]{1,0:T(8,128)(2,1)} %bitcast.8.args_11_), channel_id=1, source_target_pairs={{0,30},{1,31},{2,0},{3,1},{4,2},{5,3},{6,4},{7,5},{8,6},{9,7},{10,... | collective-permute-start | bytes 4718600 | tf_op jit(solution)/shard_map/ppermute | solution.py:19
  36.3 86.1 %collective-permute-start.6 = (bf16[1024,768]{1,0:T(8,128)(2,1)}, bf16[1024,768]{1,0:T(8,128)(2,1)S(1)}, u32[]{:S(2)}, u32[]{:S(2)}) collective-permute-start(bf16[1024,768]{1,0:T(8,128)(2,1)} %bitcast.8.args_11_), channel_id=1, source_target_pairs={{0,2},{1,3},{2,4},{3,5},{4,6},{5,7},{6,8},{7,9},{8,10},{9,11},{10,... | collective-permute-start | bytes 4718600 | tf_op jit(solution)/shard_map/ppermute | solution.py:19
  90.0 32.4 %copy-start.5 = (bf16[128,6144]{1,0:T(8,128)(2,1)S(1)}, bf16[128,6144]{1,0:T(8,128)(2,1)}, u32[]{:S(2)}) copy-start(bf16[128,6144]{1,0:T(8,128)(2,1)} %param.7) | copy-start | bytes 4718596
  92.9 90.8 %collective-permute-start.1 = (bf16[768,1024]{1,0:T(8,128)(2,1)}, bf16[768,1024]{1,0:T(8,128)(2,1)}, u32[]{:S(2)}, u32[]{:S(2)}) collective-permute-start(bf16[768,1024]{1,0:T(8,128)(2,1)} %bitcast_bitcast_fusion.args_4_), channel_id=1, source_target_pairs={{0,30},{1,31},{2,0},{3,1},{4,2},{5,3},{6,4},{7,5},{8,6},{9,7},{10,... | collective-permute-start | bytes 4718600 | tf_op jit(solution)/shard_map/ppermute | solution.py:19
  92.9 97.1 %collective-permute-start = (bf16[768,1024]{1,0:T(8,128)(2,1)}, bf16[768,1024]{1,0:T(8,128)(2,1)}, u32[]{:S(2)}, u32[]{:S(2)}) collective-permute-start(bf16[768,1024]{1,0:T(8,128)(2,1)} %bitcast_bitcast_fusion.args_4_), channel_id=1, source_target_pairs={{0,2},{1,3},{2,4},{3,5},{4,6},{5,7},{6,8},{7,9},{8,10},{9,11},{10,... | collective-permute-start | bytes 4718600 | tf_op jit(solution)/shard_map/ppermute | solution.py:19
  94.9 97.9 %collective-permute-start.8 = (bf16[1024,768]{1,0:T(8,128)(2,1)}, bf16[1024,768]{1,0:T(8,128)(2,1)}, u32[]{:S(2)}, u32[]{:S(2)}) collective-permute-start(bf16[1024,768]{1,0:T(8,128)(2,1)} %bitcast.8.args_11_), channel_id=1, source_target_pairs={{0,1},{1,0},{2,3},{3,2},{4,5},{5,4},{6,7},{7,6},{8,9},{9,8},{10,11... | collective-permute-start | bytes 4718600 | tf_op jit(solution)/shard_map/ppermute | solution.py:19
  95.0 33.7 %copy-start.1 = (bf16[1024,768]{1,0:T(8,128)(2,1)}, bf16[1024,768]{1,0:T(8,128)(2,1)S(1)}, u32[]{:S(2)}) copy-start(bf16[1024,768]{1,0:T(8,128)(2,1)S(1)} %collective-permute-done.7.args_13_) | copy-start | bytes 4718596
  95.0 98.0 %collective-permute-start.2 = (bf16[768,1024]{1,0:T(8,128)(2,1)}, bf16[768,1024]{1,0:T(8,128)(2,1)}, u32[]{:S(2)}, u32[]{:S(2)}) collective-permute-start(bf16[768,1024]{1,0:T(8,128)(2,1)} %bitcast_bitcast_fusion.args_4_), channel_id=1, source_target_pairs={{0,1},{1,0},{2,3},{3,2},{4,5},{5,4},{6,7},{7,6},{8,9},{9,8},{10,11... | collective-permute-start | bytes 4718600 | tf_op jit(solution)/shard_map/ppermute | solution.py:19
  122.5 70.4 %copy-start.2 = (bf16[1024,768]{1,0:T(8,128)(2,1)}, bf16[1024,768]{1,0:T(8,128)(2,1)S(1)}, u32[]{:S(2)}) copy-start(bf16[1024,768]{1,0:T(8,128)(2,1)S(1)} %collective-permute-done.6.args_12_) | copy-start | bytes 4718596
  122.5 71.0 %collective-permute-start.11 = (bf16[1024,768]{1,0:T(8,128)(2,1)S(1)}, bf16[1024,768]{1,0:T(8,128)(2,1)}, u32[]{:S(2)}, u32[]{:S(2)}) collective-permute-start(bf16[1024,768]{1,0:T(8,128)(2,1)S(1)} %collective-permute-done.7.args_13_), channel_id=1, source_target_pairs={{0,1},{1,0},{2,3},{3,2},{4,5},{5,4},{6,7},{7,6},{8,9},{9,8},{10,11... | collective-permute-start | bytes 4718600 | tf_op jit(solution)/shard_map/ppermute | solution.py:19
  123.8 115.5 %all-to-all-start = ((bf16[128,8,768]{2,0,1:T(8,128)(2,1)}), bf16[128,8,768]{2,0,1:T(8,128)(2,1)}, u32[]{:S(2)}, u32[]{:S(2)}) async-start(bf16[128,8,768]{2,0,1:T(8,128)(2,1)} %bitcast.39), calls=%async_computation | async-start | bytes 3145728 | tf_op jit(solution)/shard_map/all_to_all | solution.py:109
  130.0 63.6 %copy-start.6 = (s32[8,8]{1,0:T(8,128)S(1)}, s32[8,8]{1,0:T(8,128)}, u32[]{:S(2)}) copy-start(s32[8,8]{1,0:T(8,128)} %param.10) | copy-start | bytes 772
  130.0 63.8 %copy-start.7 = (s32[2,7]{1,0:T(2,128)S(1)}, s32[2,7]{1,0:T(2,128)}, u32[]{:S(2)}) copy-start(s32[2,7]{1,0:T(2,128)} %constant.89.clone) | copy-start | bytes 172
  183.7 71.4 %collective-permute-start.9 = (bf16[1024,768]{1,0:T(8,128)(2,1)}, bf16[1024,768]{1,0:T(8,128)(2,1)}, u32[]{:S(2)}, u32[]{:S(2)}) collective-permute-start(bf16[1024,768]{1,0:T(8,128)(2,1)} %broadcast_select_fusion), channel_id=1, source_target_pairs={{0,31},{1,2},{2,1},{3,4},{4,3},{5,6},{6,5},{7,8},{8,7},{9,10},{10,... | collective-permute-start | bytes 4718600 | tf_op jit(solution)/shard_map/ppermute | solution.py:19
  192.8 80.3 %collective-permute-start.3 = (bf16[768,1024]{1,0:T(8,128)(2,1)}, bf16[768,1024]{1,0:T(8,128)(2,1)}, u32[]{:S(2)}, u32[]{:S(2)}) collective-permute-start(bf16[768,1024]{1,0:T(8,128)(2,1)} %broadcast_select_fusion.1), channel_id=1, source_target_pairs={{0,31},{1,2},{2,1},{3,4},{4,3},{5,6},{6,5},{7,8},{8,7},{9,10},{10,... | collective-permute-start | bytes 4718600 | tf_op jit(solution)/shard_map/ppermute | solution.py:19
  192.8 62.3 %collective-permute-start.10 = (bf16[1024,768]{1,0:T(8,128)(2,1)S(1)}, bf16[1024,768]{1,0:T(8,128)(2,1)}, u32[]{:S(2)}, u32[]{:S(2)}) collective-permute-start(bf16[1024,768]{1,0:T(8,128)(2,1)S(1)} %collective-permute-done.6.args_12_), channel_id=1, source_target_pairs={{0,1},{1,0},{2,3},{3,2},{4,5},{5,4},{6,7},{7,6},{8,9},{9,8},{10,11... | collective-permute-start | bytes 4718600 | tf_op jit(solution)/shard_map/ppermute | solution.py:19
  192.9 62.2 %collective-permute-start.5 = (bf16[768,1024]{1,0:T(8,128)(2,1)}, bf16[768,1024]{1,0:T(8,128)(2,1)}, u32[]{:S(2)}, u32[]{:S(2)}) collective-permute-start(bf16[768,1024]{1,0:T(8,128)(2,1)} %collective-permute-done.1.args_6_), channel_id=1, source_target_pairs={{0,1},{1,0},{2,3},{3,2},{4,5},{5,4},{6,7},{7,6},{8,9},{9,8},{10,11... | collective-permute-start | bytes 4718600 | tf_op jit(solution)/shard_map/ppermute | solution.py:19
  193.4 79.7 %collective-permute-start.4 = (bf16[768,1024]{1,0:T(8,128)(2,1)}, bf16[768,1024]{1,0:T(8,128)(2,1)S(1)}, u32[]{:S(2)}, u32[]{:S(2)}) collective-permute-start(bf16[768,1024]{1,0:T(8,128)(2,1)} %collective-permute-done.args_5_), channel_id=1, source_target_pairs={{0,1},{1,0},{2,3},{3,2},{4,5},{5,4},{6,7},{7,6},{8,9},{9,8},{10,11... | collective-permute-start | bytes 4718600 | tf_op jit(solution)/shard_map/ppermute | solution.py:19
  296.3 27.3 %all-to-all-start.4 = ((bf16[8,64,768]{2,1,0:T(8,128)(2,1)}), bf16[8,64,768]{2,1,0:T(8,128)(2,1)S(1)}, u32[]{:S(2)}, u32[]{:S(2)}) async-start(bf16[8,64,768]{2,1,0:T(8,128)(2,1)} %bitcast.41), calls=%async_computation.4 | async-start | bytes 1572864 | tf_op jit(solution)/shard_map/all_to_all | solution.py:171
  323.6 15.9 %all-to-all-start.3 = ((bf16[8,64,768]{2,1,0:T(8,128)(2,1)}), bf16[8,64,768]{2,1,0:T(8,128)(2,1)S(1)}, u32[]{:S(2)}, u32[]{:S(2)}) async-start(bf16[8,64,768]{2,1,0:T(8,128)(2,1)} %bitcast.40), calls=%async_computation.3 | async-start | bytes 1572864 | tf_op jit(solution)/shard_map/all_to_all | solution.py:171
  (1 other events, 1.1 us)

commit v13 on v6

--- a/solution.py
+++ b/solution.py
@@ -46,13 +46,14 @@
             p_code = code // TILE_COUNT
             j = code % TILE_COUNT
             for p in range(pieces):
-                @pl.when(p_code == p)
+                @pl.when(jnp.logical_and(p_code == p, c < cnt_ref[step]))
                 def _():
                     for copy in copies(step, slot, c, p, j):
                         copy.start()
 
     @pl.when(i == 0)
     def _():
+        v_buf[...] = jnp.zeros(v_buf.shape, v_buf.dtype)
         start(0, 0)
 
     @pl.when(i + 1 < steps)
@@ -60,8 +61,10 @@
         start(i + 1, 1 - parity)
 
     for c in range(SLOTS):
-        for copy in copies(i, parity, c, 0, 0):
-            copy.wait()
+        @pl.when(c < cnt_ref[i])
+        def _():
+            for copy in copies(i, parity, c, 0, 0):
+                copy.wait()
 
     count = cnt_ref[i]
     keys = SLOTS * TILE
@@ -97,11 +100,11 @@
     cycle_size = lax.axis_size("blk")
     group_size = lax.axis_size("head")
     heads_local = H // group_size
-    k_heads = lax.all_to_all(key_states, "head", split_axis=1, concat_axis=0, tiled=True)
+    q_and_k = jnp.stack((queries, key_states))
+    q_heads, k_heads = lax.all_to_all(q_and_k, "head", split_axis=2, concat_axis=1, tiled=True)
     k_window = exchange(k_heads.T, 1, cycle_size)
     v_heads = lax.all_to_all(value_states, "head", split_axis=1, concat_axis=0, tiled=True)
     v_window = exchange(v_heads, 0, cycle_size)
-    q_heads = lax.all_to_all(queries, "head", split_axis=1, concat_axis=0, tiled=True)
     shard_tok = q_heads.shape[0]
     tile_count = shard_tok // TILE
     width = heads_local * DH

time: 335 us -> 346 us (1.033)
  the two profiles are of different devices: /device:TPU:64 before, /device:TPU:128 now
where the time goes in v13:
time: 346 us
  waiting for transfers between devices  209 us (60%)
  blocking collectives  55.7 us (16%)
  starting transfers between devices  35.7 us (10%)
  Pallas kernels  24.7 us (7%)
  local copies, waits for them, and re-layouts  18.1 us (5%)
    ppermute x14, waiting for transfers between devices, permute(): return lax.ppermute(block, axis, route)  151 us
    all_to_all x1, blocking collectives, body(): return lax.all_to_all(out, 'head', split_axis=0, concat_axis=1, tiled=True)  55.7 us
    all_to_all x1, waiting for transfers between devices, body(): lax.all_to_all(q_and_k, 'head', split_axis=2, concat_axis=1, tiled=True)  44.5 us
    ppermute x14, starting transfers between devices, permute(): return lax.ppermute(block, axis, route)  27.1 us
    pallas_call x1, Pallas kernels, body(): pl.pallas_call(kernel, grid_spec=grid_spec, out_shape=jax.ShapeDtypeStruc...  24.7 us
    all_to_all x1, waiting for transfers between devices, body(): lax.all_to_all(value_states, 'head', split_axis=1, concat_axis=0, tiled=T...  13.8 us
  transfers between devices with their start and end apart: 16, of which 8 were waited for; matrix products, arithmetic and copies ran while one was open for 5% of the time, Pallas kernels for 0%

profile of v13, /device:TPU:128, one launch (start us, length us, event | category | flops | bytes accessed | tf_op | source)
XLA Modules:
  0.0 346.1 jit_solution(4903351887845759785)
XLA Ops:
  0.0 2.7 copy.38
  2.7 4.9 %all-to-all-start.1 = ((bf16[128,8,768]{2,0,1:T(8,128)(2,1)}), bf16[128,8,768]{2,0,1:T(8,128)(2,1)}, u32[]{:S(2)}, u32[]{:S(2)}) async-start(bf16[128,8,768]{2,0,1:T(8,128)(2,1)} %bitcast.35), calls=%async_computation.1 | async-start | bytes 3145728 | tf_op jit(solution)/shard_map/all_to_all | solution.py:106
  7.6 2.2 pad_maximum_fusion
  9.8 5.5 %copy.24 = bf16[2,128,6144]{1,0,2:T(2,128)(2,1)} copy(bf16[2,128,6144]{2,1,0:T(8,128)(2,1)S(1)} %pad_maximum_fusion) | data formatting | bytes 6291456 | tf_op jit(solution)/shard_map/stack | solution.py:103
  15.3 13.8 %all-to-all-done.1 = bf16[128,8,768]{2,0,1:T(8,128)(2,1)} async-done(((bf16[128,8,768]{2,0,1:T(8,128)(2,1)}), bf16[128,8,768]{2,0,1:T(8,128)(2,1)}, u32[]{:S(2)}, u32[]{:S(2)}) %all-to-all-start.1) | async-done | bytes 1572896 | tf_op jit(solution)/shard_map/all_to_all | solution.py:106
  29.1 3.6 %all-to-all-start = ((bf16[2,128,6144]{1,0,2:T(2,128)(2,1)}), bf16[2,128,6144]{1,0,2:T(2,128)(2,1)S(1)}, u32[]{:S(2)}, u32[]{:S(2)}) async-start(bf16[2,128,6144]{1,0,2:T(2,128)(2,1)} %copy.24), calls=%async_computation | async-start | bytes 6291456 | tf_op jit(solution)/shard_map/all_to_all | solution.py:104
  32.7 2.8 collective-permute-start.8
  35.6 32.9 %collective-permute-done.8.args_14_ = bf16[1024,768]{1,0:T(8,128)(2,1)} collective-permute-done((bf16[1024,768]{1,0:T(8,128)(2,1)}, bf16[1024,768]{1,0:T(8,128)(2,1)}, u32[]{:S(2)}, u32[]{:S(2)}) %collective-permute-start.8) | collective-permute-done | bytes 1572896 | tf_op jit(solution)/shard_map/ppermute | solution.py:19
  68.4 9.9 %collective-permute-start.11 = (bf16[1024,768]{1,0:T(8,128)(2,1)}, bf16[1024,768]{1,0:T(8,128)(2,1)}, u32[]{:S(2)}, u32[]{:S(2)}) collective-permute-start(bf16[1024,768]{1,0:T(8,128)(2,1)} %collective-permute-done.8.args_14_), channel_id=1, source_target_pairs={{0,31},{2,1},{4,3},{6,5},{8,7},{10,9},{12,11},{14,13},{16,15},{18,... | collective-permute-start | bytes 4718600 | tf_op jit(solution)/shard_map/ppermute | solution.py:19
  78.3 44.5 %all-to-all-done = bf16[2,128,6144]{1,0,2:T(2,128)(2,1)S(1)} async-done(((bf16[2,128,6144]{1,0,2:T(2,128)(2,1)}), bf16[2,128,6144]{1,0,2:T(2,128)(2,1)S(1)}, u32[]{:S(2)}, u32[]{:S(2)}) %all-to-all-start) | async-done | bytes 3145760 | tf_op jit(solution)/shard_map/all_to_all | solution.py:104
  122.9 2.0 copy.36
  125.7 11.0 %collective-permute-done.7.args_13_ = bf16[1024,768]{1,0:T(8,128)(2,1)} collective-permute-done((bf16[1024,768]{1,0:T(8,128)(2,1)}, bf16[1024,768]{1,0:T(8,128)(2,1)}, u32[]{:S(2)}, u32[]{:S(2)}) %collective-permute-start.7) | collective-permute-done | bytes 1572896 | tf_op jit(solution)/shard_map/ppermute | solution.py:19
  136.8 1.3 collective-permute-start.10
  138.1 1.6 collective-permute-start.2
  139.7 45.6 %collective-permute-done.1.args_6_ = bf16[768,1024]{1,0:T(8,128)(2,1)} collective-permute-done((bf16[768,1024]{1,0:T(8,128)(2,1)S(1)}, bf16[768,1024]{1,0:T(8,128)(2,1)}, u32[]{:S(2)}, u32[]{:S(2)}) %collective-permute-start.1) | collective-permute-done | bytes 1572896 | tf_op jit(solution)/shard_map/ppermute | solution.py:19
  185.3 9.9 %collective-permute-start.4 = (bf16[768,1024]{1,0:T(8,128)(2,1)}, bf16[768,1024]{1,0:T(8,128)(2,1)}, u32[]{:S(2)}, u32[]{:S(2)}) collective-permute-start(bf16[768,1024]{1,0:T(8,128)(2,1)} %collective-permute-done.1.args_6_), channel_id=1, source_target_pairs={{0,31},{2,1},{4,3},{6,5},{8,7},{10,9},{12,11},{14,13},{16,15},{18,... | collective-permute-start | bytes 4718600 | tf_op jit(solution)/shard_map/ppermute | solution.py:19
  195.3 15.1 %collective-permute-done.10.args_16_ = bf16[1024,768]{1,0:T(8,128)(2,1)} collective-permute-done((bf16[1024,768]{1,0:T(8,128)(2,1)}, bf16[1024,768]{1,0:T(8,128)(2,1)}, u32[]{:S(2)}, u32[]{:S(2)}) %collective-permute-start.10) | collective-permute-done | bytes 1572896 | tf_op jit(solution)/shard_map/ppermute | solution.py:19
  210.4 1.5 collective-permute-start.3
  216.3 1.8 copy.26
  218.1 35.8 %collective-permute-done.4.args_9_ = bf16[768,1024]{1,0:T(8,128)(2,1)} collective-permute-done((bf16[768,1024]{1,0:T(8,128)(2,1)}, bf16[768,1024]{1,0:T(8,128)(2,1)}, u32[]{:S(2)}, u32[]{:S(2)}) %collective-permute-start.4) | collective-permute-done | bytes 1572896 | tf_op jit(solution)/shard_map/ppermute | solution.py:19
  253.9 10.4 %collective-permute-done.3.args_8_ = bf16[768,1024]{1,0:T(8,128)(2,1)} collective-permute-done((bf16[768,1024]{1,0:T(8,128)(2,1)}, bf16[768,1024]{1,0:T(8,128)(2,1)}, u32[]{:S(2)}, u32[]{:S(2)}) %collective-permute-start.3) | collective-permute-done | bytes 1572896 | tf_op jit(solution)/shard_map/ppermute | solution.py:19
  264.4 24.7 %shard_map.73 = bf16[1024,768]{1,0:T(8,128)(2,1)} custom-call(s32[64]{0:T(128)} %reshape.66.args_0_, s32[8]{0:T(128)} %args_1_.4, f32[8,6,1024]{2,1,0:T(8,128)} %copy.28.args_2_, bf16[1024,768]{1,0:T(8,128)(2,1)} %bitcast.42, bf16[768,1024]{1,0:T(8,128)(2,1)} %bitcast.41, bf16[768,1024]{1,0:T(8,128)(2,1)} %collective-permute-done.args_5_, ...), custom_call_target="tpu_custom_call" | custom-call | tf_op jit(solution)/shard_map/pallas_call | solution.py:151
  289.1 55.7 %all_to_all.53 = bf16[8,128,768]{2,1,0:T(8,128)(2,1)S(1)} all-to-all(bf16[8,128,768]{2,1,0:T(8,128)(2,1)} %bitcast.43), channel_id=1, replica_groups=mesh['head'=8,'blk'=32] {'head'}, dimensions={0} | all-to-all | bytes 3145728 | tf_op jit(solution)/shard_map/all_to_all | solution.py:164
  344.8 1.3 copy.31
  (48 shorter events, 5.1 us)
Async XLA Ops:
  0.0 213.6 %copy-start = (s32[256]{0:T(256)S(1)}, s32[256]{0:T(256)}, u32[]{:S(2)}) copy-start(s32[256]{0:T(256)} %param.12) | copy-start | bytes 3076
  2.7 26.4 %all-to-all-start.1 = ((bf16[128,8,768]{2,0,1:T(8,128)(2,1)}), bf16[128,8,768]{2,0,1:T(8,128)(2,1)}, u32[]{:S(2)}, u32[]{:S(2)}) async-start(bf16[128,8,768]{2,0,1:T(8,128)(2,1)} %bitcast.35), calls=%async_computation.1 | async-start | bytes 3145728 | tf_op jit(solution)/shard_map/all_to_all | solution.py:106
  29.1 93.8 %all-to-all-start = ((bf16[2,128,6144]{1,0,2:T(2,128)(2,1)}), bf16[2,128,6144]{1,0,2:T(2,128)(2,1)S(1)}, u32[]{:S(2)}, u32[]{:S(2)}) async-start(bf16[2,128,6144]{1,0,2:T(2,128)(2,1)} %copy.24), calls=%async_computation | async-start | bytes 6291456 | tf_op jit(solution)/shard_map/all_to_all | solution.py:104
  32.7 35.7 %collective-permute-start.8 = (bf16[1024,768]{1,0:T(8,128)(2,1)}, bf16[1024,768]{1,0:T(8,128)(2,1)}, u32[]{:S(2)}, u32[]{:S(2)}) collective-permute-start(bf16[1024,768]{1,0:T(8,128)(2,1)} %bitcast.9.args_12_), channel_id=1, source_target_pairs={{0,30},{1,31},{2,0},{3,1},{4,2},{5,3},{6,4},{7,5},{8,6},{9,7},{10,... | collective-permute-start | bytes 4718600 | tf_op jit(solution)/shard_map/ppermute | solution.py:19
  35.5 101.2 %collective-permute-start.7 = (bf16[1024,768]{1,0:T(8,128)(2,1)}, bf16[1024,768]{1,0:T(8,128)(2,1)}, u32[]{:S(2)}, u32[]{:S(2)}) collective-permute-start(bf16[1024,768]{1,0:T(8,128)(2,1)} %bitcast.9.args_12_), channel_id=1, source_target_pairs={{0,2},{1,3},{2,4},{3,5},{4,6},{5,7},{6,8},{7,9},{8,10},{9,11},{10,... | collective-permute-start | bytes 4718600 | tf_op jit(solution)/shard_map/ppermute | solution.py:19
  35.6 101.2 %collective-permute-start.9 = (bf16[1024,768]{1,0:T(8,128)(2,1)}, bf16[1024,768]{1,0:T(8,128)(2,1)}, u32[]{:S(2)}, u32[]{:S(2)}) collective-permute-start(bf16[1024,768]{1,0:T(8,128)(2,1)} %bitcast.9.args_12_), channel_id=1, source_target_pairs={{0,1},{1,0},{2,3},{3,2},{4,5},{5,4},{6,7},{7,6},{8,9},{9,8},{10,11... | collective-permute-start | bytes 4718600 | tf_op jit(solution)/shard_map/ppermute | solution.py:19
  68.4 68.3 %collective-permute-start.13 = (bf16[1024,768]{1,0:T(8,128)(2,1)}, bf16[1024,768]{1,0:T(8,128)(2,1)}, u32[]{:S(2)}, u32[]{:S(2)}) collective-permute-start(bf16[1024,768]{1,0:T(8,128)(2,1)} %collective-permute-done.8.args_14_), channel_id=1, source_target_pairs={{0,1},{1,0},{2,3},{3,2},{4,5},{5,4},{6,7},{7,6},{8,9},{9,8},{10,11... | collective-permute-start | bytes 4718600 | tf_op jit(solution)/shard_map/ppermute | solution.py:19
  68.4 69.6 %collective-permute-start.11 = (bf16[1024,768]{1,0:T(8,128)(2,1)}, bf16[1024,768]{1,0:T(8,128)(2,1)}, u32[]{:S(2)}, u32[]{:S(2)}) collective-permute-start(bf16[1024,768]{1,0:T(8,128)(2,1)} %collective-permute-done.8.args_14_), channel_id=1, source_target_pairs={{0,31},{2,1},{4,3},{6,5},{8,7},{10,9},{12,11},{14,13},{16,15},{18,... | collective-permute-start | bytes 4718600 | tf_op jit(solution)/shard_map/ppermute | solution.py:19
  125.1 86.8 %copy-start.2 = (s32[8,8]{1,0:T(8,128)S(1)}, s32[8,8]{1,0:T(8,128)}, u32[]{:S(2)}) copy-start(s32[8,8]{1,0:T(8,128)} %param.10) | copy-start | bytes 772
  125.1 87.0 %copy-start.3 = (s32[2,7]{1,0:T(2,128)S(1)}, s32[2,7]{1,0:T(2,128)}, u32[]{:S(2)}) copy-start(s32[2,7]{1,0:T(2,128)} %constant.84.clone) | copy-start | bytes 172
  125.6 87.3 %copy-start.1 = (bf16[96,8,8,128]{3,1,2,0:T(8,128)(2,1)}, bf16[96,8,8,128]{3,1,2,0:T(8,128)(2,1)S(1)}, u32[]{:S(2)}) copy-start(bf16[96,8,8,128]{3,1,2,0:T(8,128)(2,1)S(1)} %copy.37) | copy-start | bytes 4718596
  125.6 59.7 %collective-permute-start.1 = (bf16[768,1024]{1,0:T(8,128)(2,1)S(1)}, bf16[768,1024]{1,0:T(8,128)(2,1)}, u32[]{:S(2)}, u32[]{:S(2)}) collective-permute-start(bf16[768,1024]{1,0:T(8,128)(2,1)S(1)} %bitcast.38), channel_id=1, source_target_pairs={{0,30},{1,31},{2,0},{3,1},{4,2},{5,3},{6,4},{7,5},{8,6},{9,7},{10,... | collective-permute-start | bytes 4718600 | tf_op jit(solution)/shard_map/ppermute | solution.py:19
  136.7 48.6 %collective-permute-start.12 = (bf16[1024,768]{1,0:T(8,128)(2,1)}, bf16[1024,768]{1,0:T(8,128)(2,1)}, u32[]{:S(2)}, u32[]{:S(2)}) collective-permute-start(bf16[1024,768]{1,0:T(8,128)(2,1)} %collective-permute-done.7.args_13_), channel_id=1, source_target_pairs={{0,1},{1,0},{2,3},{3,2},{4,5},{5,4},{6,7},{7,6},{8,9},{9,8},{10,11... | collective-permute-start | bytes 4718600 | tf_op jit(solution)/shard_map/ppermute | solution.py:19
  136.7 58.5 %collective-permute-start = (bf16[768,1024]{1,0:T(8,128)(2,1)S(1)}, bf16[768,1024]{1,0:T(8,128)(2,1)}, u32[]{:S(2)}, u32[]{:S(2)}) collective-permute-start(bf16[768,1024]{1,0:T(8,128)(2,1)S(1)} %bitcast.39), channel_id=1, source_target_pairs={{0,2},{1,3},{2,4},{3,5},{4,6},{5,7},{6,8},{7,9},{8,10},{9,11},{10,... | collective-permute-start | bytes 4718600 | tf_op jit(solution)/shard_map/ppermute | solution.py:19
  136.8 73.6 %collective-permute-start.10 = (bf16[1024,768]{1,0:T(8,128)(2,1)}, bf16[1024,768]{1,0:T(8,128)(2,1)}, u32[]{:S(2)}, u32[]{:S(2)}) collective-permute-start(bf16[1024,768]{1,0:T(8,128)(2,1)} %collective-permute-done.7.args_13_), channel_id=1, source_target_pairs={{1,2},{3,4},{5,6},{7,8},{9,10},{11,12},{13,14},{15,16},{17,18},{19... | collective-permute-start | bytes 4718600 | tf_op jit(solution)/shard_map/ppermute | solution.py:19
  138.1 80.0 %collective-permute-start.2 = (bf16[768,1024]{1,0:T(8,128)(2,1)S(1)}, bf16[768,1024]{1,0:T(8,128)(2,1)}, u32[]{:S(2)}, u32[]{:S(2)}) collective-permute-start(bf16[768,1024]{1,0:T(8,128)(2,1)S(1)} %bitcast.40), channel_id=1, source_target_pairs={{0,1},{1,0},{2,3},{3,2},{4,5},{5,4},{6,7},{7,6},{8,9},{9,8},{10,11... | collective-permute-start | bytes 4718600 | tf_op jit(solution)/shard_map/ppermute | solution.py:19
  185.3 32.8 %collective-permute-start.6 = (bf16[768,1024]{1,0:T(8,128)(2,1)}, bf16[768,1024]{1,0:T(8,128)(2,1)}, u32[]{:S(2)}, u32[]{:S(2)}) collective-permute-start(bf16[768,1024]{1,0:T(8,128)(2,1)} %collective-permute-done.1.args_6_), channel_id=1, source_target_pairs={{0,1},{1,0},{2,3},{3,2},{4,5},{5,4},{6,7},{7,6},{8,9},{9,8},{10,11... | collective-permute-start | bytes 4718600 | tf_op jit(solution)/shard_map/ppermute | solution.py:19
  185.3 68.6 %collective-permute-start.4 = (bf16[768,1024]{1,0:T(8,128)(2,1)}, bf16[768,1024]{1,0:T(8,128)(2,1)}, u32[]{:S(2)}, u32[]{:S(2)}) collective-permute-start(bf16[768,1024]{1,0:T(8,128)(2,1)} %collective-permute-done.1.args_6_), channel_id=1, source_target_pairs={{0,31},{2,1},{4,3},{6,5},{8,7},{10,9},{12,11},{14,13},{16,15},{18,... | collective-permute-start | bytes 4718600 | tf_op jit(solution)/shard_map/ppermute | solution.py:19
  195.3 58.7 %collective-permute-start.5 = (bf16[768,1024]{1,0:T(8,128)(2,1)}, bf16[768,1024]{1,0:T(8,128)(2,1)}, u32[]{:S(2)}, u32[]{:S(2)}) collective-permute-start(bf16[768,1024]{1,0:T(8,128)(2,1)} %collective-permute-done.args_5_), channel_id=1, source_target_pairs={{0,1},{1,0},{2,3},{3,2},{4,5},{5,4},{6,7},{7,6},{8,9},{9,8},{10,11... | collective-permute-start | bytes 4718600 | tf_op jit(solution)/shard_map/ppermute | solution.py:19
  210.4 54.0 %collective-permute-start.3 = (bf16[768,1024]{1,0:T(8,128)(2,1)}, bf16[768,1024]{1,0:T(8,128)(2,1)}, u32[]{:S(2)}, u32[]{:S(2)}) collective-permute-start(bf16[768,1024]{1,0:T(8,128)(2,1)} %collective-permute-done.args_5_), channel_id=1, source_target_pairs={{1,2},{3,4},{5,6},{7,8},{9,10},{11,12},{13,14},{15,16},{17,18},{19... | collective-permute-start | bytes 4718600 | tf_op jit(solution)/shard_map/ppermute | solution.py:19

commit v14 on v5

--- a/solution.py
+++ b/solution.py
@@ -31,12 +31,12 @@
     steps = pl.num_programs(0)
     parity = i % 2
 
-    def copies(step, slot, c, p, j):
+    def copies(slot, c, p, j):
         k_copy = pltpu.make_async_copy(
-            k_hbm[p].at[:, pl.ds(j * TILE, TILE)], k_buf.at[slot, :, pl.ds(c * TILE, TILE)], sem.at[0, slot, c]
+            k_hbm[p].at[pl.ds(j * TILE, TILE), :], k_buf.at[slot, pl.ds(c * TILE, TILE), :], sem.at[0, slot, c]
         )
         v_copy = pltpu.make_async_copy(
-            v_hbm[p].at[pl.ds(j * TILE, TILE), :], v_buf.at[slot, pl.ds(c * TILE, TILE), :], sem.at[1, slot, c]
+            v_hbm[p].at[:, pl.ds(j * TILE, TILE)], v_buf.at[slot, :, pl.ds(c * TILE, TILE)], sem.at[1, slot, c]
         )
         return k_copy, v_copy
 
@@ -48,7 +48,7 @@
             for p in range(pieces):
                 @pl.when(p_code == p)
                 def _():
-                    for copy in copies(step, slot, c, p, j):
+                    for copy in copies(slot, c, p, j):
                         copy.start()
 
     @pl.when(i == 0)
@@ -60,25 +60,25 @@
         start(i + 1, 1 - parity)
 
     for c in range(SLOTS):
-        for copy in copies(i, parity, c, 0, 0):
+        for copy in copies(parity, c, 0, 0):
             copy.wait()
 
     count = cnt_ref[i]
     keys = SLOTS * TILE
-    valid = lax.broadcasted_iota(jnp.int32, (TILE, keys), 1) < count * TILE
+    valid = lax.broadcasted_iota(jnp.int32, (keys, TILE), 0) < count * TILE
     k_all = k_buf.at[parity]
     v_all = v_buf.at[parity]
     for h in range(heads_local):
         cols = slice(h * DH, (h + 1) * DH)
-        s = jnp.dot(q_ref[:, cols], k_all[cols, :], preferred_element_type=jnp.float32)
+        s = jnp.dot(k_all[:, cols], q_ref[cols, :], preferred_element_type=jnp.float32)
         s = s * scale
-        s = s - bias_ref[h : h + 1, :]
+        s = s - bias_ref[h]
         s = jnp.where(valid, s, -1e30)
-        top = s.max(axis=1, keepdims=True)
+        top = s.max(axis=0, keepdims=True)
         w = jnp.exp(s - top).astype(jnp.bfloat16)
-        total = w.astype(jnp.float32).sum(axis=1, keepdims=True)
-        acc = jnp.dot(w, v_all[:, cols], preferred_element_type=jnp.float32)
-        o_ref[:, cols] = (acc / total).astype(o_ref.dtype)
+        total = w.astype(jnp.float32).sum(axis=0, keepdims=True)
+        acc = jnp.dot(v_all[cols, :], w, preferred_element_type=jnp.float32)
+        o_ref[cols, :] = (acc / total).astype(o_ref.dtype)
 
 
 def exchange(local, axis, n):
@@ -100,9 +100,9 @@
     group_size = lax.axis_size("head")
     heads_local = H // group_size
     k_heads = lax.all_to_all(key_states, "head", split_axis=1, concat_axis=0, tiled=True)
-    k_window = exchange(k_heads.T, 1, cycle_size)
+    k_window = exchange(k_heads, 0, cycle_size)
     v_heads = lax.all_to_all(value_states, "head", split_axis=1, concat_axis=0, tiled=True)
-    v_window = exchange(v_heads, 0, cycle_size)
+    v_window = exchange(v_heads.T, 1, cycle_size)
     q_heads = lax.all_to_all(queries, "head", split_axis=1, concat_axis=0, tiled=True)
     shard_tok = q_heads.shape[0]
     tile_count = shard_tok // TILE
@@ -122,7 +122,7 @@
     head_index = lax.axis_index("head") * heads_local + jnp.arange(heads_local, dtype=jnp.int32)
     slopes = 8.0 * jnp.power(2.0, -8.0 * head_index.astype(jnp.float32) / H)
     bias = slopes[None, :, None, None] * distance[:, None, :, None]
-    bias = jnp.broadcast_to(bias, (tile_count, heads_local, SLOTS, TILE)).reshape(tile_count, heads_local, SLOTS * TILE)
+    bias = jnp.broadcast_to(bias, (tile_count, heads_local, SLOTS, TILE)).reshape(tile_count, heads_local, SLOTS * TILE, 1)
     scale = DH ** (-0.5)
 
     assert tile_count == TILE_COUNT
@@ -130,8 +130,8 @@
     any_spec = pl.BlockSpec(memory_space=pl.ANY)
     in_specs = (
         [
-            pl.BlockSpec((None, heads_local, SLOTS * TILE), lambda i, sw, cnt: (i, 0, 0)),
-            pl.BlockSpec((TILE, width), lambda i, sw, cnt: (i, 0)),
+            pl.BlockSpec((None, heads_local, SLOTS * TILE, 1), lambda i, sw, cnt: (i, 0, 0, 0)),
+            pl.BlockSpec((width, TILE), lambda i, sw, cnt: (0, i)),
         ]
         + [any_spec] * (2 * pieces)
     )
@@ -139,10 +139,10 @@
         num_scalar_prefetch=2,
         grid=(tile_count,),
         in_specs=in_specs,
-        out_specs=pl.BlockSpec((TILE, width), lambda i, sw, cnt: (i, 0)),
+        out_specs=pl.BlockSpec((width, TILE), lambda i, sw, cnt: (0, i)),
         scratch_shapes=[
+            pltpu.VMEM((2, SLOTS * TILE, width), jnp.bfloat16),
             pltpu.VMEM((2, width, SLOTS * TILE), jnp.bfloat16),
-            pltpu.VMEM((2, SLOTS * TILE, width), jnp.bfloat16),
             pltpu.SemaphoreType.DMA((2, 2, SLOTS)),
         ],
     )
@@ -150,17 +150,17 @@
     out = pl.pallas_call(
         kernel,
         grid_spec=grid_spec,
-        out_shape=jax.ShapeDtypeStruct((shard_tok, width), jnp.bfloat16),
+        out_shape=jax.ShapeDtypeStruct((width, shard_tok), jnp.bfloat16),
         compiler_params=pltpu.CompilerParams(dimension_semantics=("arbitrary",)),
     )(
         slot_window.reshape(-1),
         block_counts.astype(jnp.int32),
         bias,
-        q_heads,
+        q_heads.T,
         *k_window,
         *v_window,
     )
-    return lax.all_to_all(out, "head", split_axis=0, concat_axis=1, tiled=True)
+    return lax.all_to_all(out.T, "head", split_axis=0, concat_axis=1, tiled=True)
 
 
 def solution(mesh):

time: 323 us -> 327 us (1.012)
  waiting for transfers between devices: 228 us -> 195 us
  starting transfers between devices: 26.6 us -> 45.7 us
  local copies, waits for them, and re-layouts: 15.2 us -> 31.6 us
    ppermute x12, waiting for transfers between devices: 113 us -> 90 us  [permute(): return lax.ppermute(block, axis, route)]
    all_to_all x1, starting transfers between devices: 4.78 us -> 25.4 us  [body(): lax.all_to_all(queries, 'head', split_axis=1, concat_axis=0, tiled=True)]
    reshape x2, local copies, waits for them, and re-layouts: 0.87 us -> 12.7 us  [body(): jnp.broadcast_to(bias, (tile_count, heads_local, SLOTS, TILE))]
    all_to_all x1, waiting for transfers between devices: 41.1 us -> 31.6 us  [body(): lax.all_to_all(queries, 'head', split_axis=1, concat_axis=0, tiled=True)]
    unnamed x17 -> x18, local copies, waits for them, and re-layouts: 2.74 us -> 6.99 us
  transfers between devices with their start and end apart: 15 -> 15, of which waited for: 7 -> 8; matrix products, arithmetic and copies ran while one was open for 5% -> 9% of each run, Pallas kernels for 0% -> 0%
where the time goes in v14:
time: 327 us; the launch traced here: 322 us
  waiting for transfers between devices  195 us (60%)
  starting transfers between devices  45.7 us (14%)
  local copies, waits for them, and re-layouts  31.6 us (10%)
  Pallas kernels  25.9 us (8%)
  blocking collectives  19.6 us (6%)
  other arithmetic  4.28 us (1%)
    ppermute x12, waiting for transfers between devices, permute(): return lax.ppermute(block, axis, route)  90 us
    all_to_all x1, waiting for transfers between devices, body(): lax.all_to_all(key_states, 'head', split_axis=1, concat_axis=0, tiled=True)  52.9 us
    all_to_all x1, waiting for transfers between devices, body(): lax.all_to_all(queries, 'head', split_axis=1, concat_axis=0, tiled=True)  31.6 us
    pallas_call x1, Pallas kernels, body(): pl.pallas_call(kernel, grid_spec=grid_spec, out_shape=jax.ShapeDtypeStruc...  25.9 us
    all_to_all x1, starting transfers between devices, body(): lax.all_to_all(queries, 'head', split_axis=1, concat_axis=0, tiled=True)  25.4 us
    all_to_all x1, waiting for transfers between devices, body(): lax.all_to_all(value_states, 'head', split_axis=1, concat_axis=0, tiled=T...  20.1 us
    all_to_all x1, blocking collectives, body(): lax.all_to_all(out.T, 'head', split_axis=0, concat_axis=1, tiled=True)  19.6 us
    reshape x2, local copies, waits for them, and re-layouts, body(): jnp.broadcast_to(bias, (tile_count, heads_local, SLOTS, TILE))  12.7 us
  transfers between devices with their start and end apart: 15, of which 8 were waited for; matrix products, arithmetic and copies ran while one was open for 9% of the time, Pallas kernels for 0%

profile of v14, /device:TPU:128, one launch (start us, length us, event | category | flops | bytes accessed | tf_op | source)
XLA Modules:
  0.0 321.9 jit_solution(16702291370285702018)
XLA Ops:
  0.0 2.7 copy.20
  2.7 5.1 %all-to-all-start.2 = ((bf16[128,8,768]{0,2,1:T(8,128)(2,1)}), bf16[128,8,768]{0,2,1:T(8,128)(2,1)S(1)}, u32[]{:S(2)}, u32[]{:S(2)}) async-start(bf16[128,8,768]{0,2,1:T(8,128)(2,1)} %bitcast.8), calls=%async_computation.2 | async-start | bytes 3145728 | tf_op jit(solution)/shard_map/all_to_all | solution.py:104
  9.0 20.1 %all-to-all-done.2 = bf16[128,8,768]{0,2,1:T(8,128)(2,1)S(1)} async-done(((bf16[128,8,768]{0,2,1:T(8,128)(2,1)}), bf16[128,8,768]{0,2,1:T(8,128)(2,1)S(1)}, u32[]{:S(2)}, u32[]{:S(2)}) %all-to-all-start.2) | async-done | bytes 1572896 | tf_op jit(solution)/shard_map/all_to_all | solution.py:104
  29.1 4.3 %all-to-all-start.1 = ((bf16[128,8,768]{2,0,1:T(8,128)(2,1)}), bf16[128,8,768]{2,0,1:T(8,128)(2,1)}, u32[]{:S(2)}, u32[]{:S(2)}) async-start(bf16[128,8,768]{2,0,1:T(8,128)(2,1)} %bitcast.41), calls=%async_computation.1 | async-start | bytes 3145728 | tf_op jit(solution)/shard_map/all_to_all | solution.py:102
  33.4 1.4 bitcast_bitcast_fusion.args_11_
  34.8 2.7 collective-permute-start.7
  37.5 52.9 %all-to-all-done.1 = bf16[128,8,768]{2,0,1:T(8,128)(2,1)} async-done(((bf16[128,8,768]{2,0,1:T(8,128)(2,1)}), bf16[128,8,768]{2,0,1:T(8,128)(2,1)}, u32[]{:S(2)}, u32[]{:S(2)}) %all-to-all-start.1) | async-done | bytes 1572896 | tf_op jit(solution)/shard_map/all_to_all | solution.py:102
  90.4 2.0 collective-permute-start
  92.9 29.4 %collective-permute-done.6.args_12_ = bf16[768,1024]{1,0:T(8,128)(2,1)S(1)} collective-permute-done((bf16[768,1024]{1,0:T(8,128)(2,1)}, bf16[768,1024]{1,0:T(8,128)(2,1)S(1)}, u32[]{:S(2)}, u32[]{:S(2)}) %collective-permute-start.6) | collective-permute-done | bytes 1572896 | tf_op jit(solution)/shard_map/ppermute | solution.py:19
  122.4 3.1 copy.17
  125.5 25.4 %all-to-all-start = ((bf16[128,8,768]{0,2,1:T(8,128)(2,1)}), bf16[128,8,768]{0,2,1:T(8,128)(2,1)}, u32[]{:S(2)}, u32[]{:S(2)}) async-start(bf16[128,8,768]{0,2,1:T(8,128)(2,1)} %bitcast.42), calls=%async_computation | async-start | bytes 3145728 | tf_op jit(solution)/shard_map/all_to_all | solution.py:106
  151.9 1.3 broadcast_select_fusion
  153.2 29.6 %collective-permute-done.1.args_6_ = bf16[1024,768]{1,0:T(8,128)(2,1)} collective-permute-done((bf16[1024,768]{1,0:T(8,128)(2,1)}, bf16[1024,768]{1,0:T(8,128)(2,1)}, u32[]{:S(2)}, u32[]{:S(2)}) %collective-permute-start.1) | collective-permute-done | bytes 1572896 | tf_op jit(solution)/shard_map/ppermute | solution.py:19
  182.8 4.4 %collective-permute-start.9 = (bf16[768,1024]{1,0:T(8,128)(2,1)}, bf16[768,1024]{1,0:T(8,128)(2,1)}, u32[]{:S(2)}, u32[]{:S(2)}) collective-permute-start(bf16[768,1024]{1,0:T(8,128)(2,1)} %broadcast_select_fusion), channel_id=1, source_target_pairs={{0,31},{1,2},{2,1},{3,4},{4,3},{5,6},{6,5},{7,8},{8,7},{9,10},{10,... | collective-permute-start | bytes 4718600 | tf_op jit(solution)/shard_map/ppermute | solution.py:19
  188.4 2.7 broadcast_select_fusion.1
  194.9 12.6 %copy.22.args_2_ = f32[8,6,1024,1]{3,2,1,0:T(8,128)} copy(f32[8,6,1024,1]{2,0,1,3:T(8,128)S(1)} %reshape.69) | data formatting | bytes 393216 | tf_op jit(solution)/shard_map/reshape | solution.py:125
  207.6 31.6 %all-to-all-done = bf16[128,8,768]{0,2,1:T(8,128)(2,1)} async-done(((bf16[128,8,768]{0,2,1:T(8,128)(2,1)}), bf16[128,8,768]{0,2,1:T(8,128)(2,1)}, u32[]{:S(2)}, u32[]{:S(2)}) %all-to-all-start) | async-done | bytes 1572896 | tf_op jit(solution)/shard_map/all_to_all | solution.py:106
  239.2 2.8 bitcast_bitcast_fusion.1.args_3_
  242.0 13.1 %collective-permute-done.9.args_15_ = bf16[768,1024]{1,0:T(8,128)(2,1)} collective-permute-done((bf16[768,1024]{1,0:T(8,128)(2,1)}, bf16[768,1024]{1,0:T(8,128)(2,1)}, u32[]{:S(2)}, u32[]{:S(2)}) %collective-permute-start.9) | collective-permute-done | bytes 1572896 | tf_op jit(solution)/shard_map/ppermute | solution.py:19
  255.1 16.8 %collective-permute-done.3.args_8_ = bf16[1024,768]{1,0:T(8,128)(2,1)} collective-permute-done((bf16[1024,768]{1,0:T(8,128)(2,1)}, bf16[1024,768]{1,0:T(8,128)(2,1)}, u32[]{:S(2)}, u32[]{:S(2)}) %collective-permute-start.3) | collective-permute-done | bytes 1572896 | tf_op jit(solution)/shard_map/ppermute | solution.py:19
  273.1 25.9 %shard_map.73 = bf16[768,1024]{1,0:T(8,128)(2,1)} custom-call(s32[64]{0:T(128)} %reshape.68.args_0_, s32[8]{0:T(128)} %args_1_.4, f32[8,6,1024,1]{3,2,1,0:T(8,128)} %copy.22.args_2_, bf16[768,1024]{1,0:T(8,128)(2,1)} %bitcast_bitcast_fusion.1.args_3_, bf16[1024,768]{1,0:T(8,128)(2,1)} %bitcast.6.args_4_, bf16[1024,768]{1,0:T(8,128)(2,1)} %collective-permute-done.args_5_, ...), custom_call_target="tpu_custom_call" | custom-call | tf_op jit(solution)/shard_map/pallas_call | solution.py:150
  299.0 1.7 copy_bitcast_fusion
  300.7 19.6 %all_to_all.76 = bf16[8,128,768]{1,2,0:T(8,128)(2,1)S(1)} all-to-all(bf16[8,128,768]{1,2,0:T(8,128)(2,1)S(1)} %copy_bitcast_fusion), channel_id=1, replica_groups=mesh['head'=8,'blk'=32] {'head'}, dimensions={0} | all-to-all | bytes 3145728 | tf_op jit(solution)/shard_map/all_to_all | solution.py:163
  320.3 1.6 copy.24
  (55 shorter events, 8.8 us)
Async XLA Ops:
  0.0 193.1 %copy-start = (s32[256]{0:T(256)S(1)}, s32[256]{0:T(256)}, u32[]{:S(2)}) copy-start(s32[256]{0:T(256)} %param.12) | copy-start | bytes 3076
  2.7 5.1 %copy-start.5 = (bf16[128,6144]{1,0:T(8,128)(2,1)S(1)}, bf16[128,6144]{1,0:T(8,128)(2,1)}, u32[]{:S(2)}) copy-start(bf16[128,6144]{1,0:T(8,128)(2,1)} %param.8) | copy-start | bytes 4718596
  2.7 26.4 %all-to-all-start.2 = ((bf16[128,8,768]{0,2,1:T(8,128)(2,1)}), bf16[128,8,768]{0,2,1:T(8,128)(2,1)S(1)}, u32[]{:S(2)}, u32[]{:S(2)}) async-start(bf16[128,8,768]{0,2,1:T(8,128)(2,1)} %bitcast.8), calls=%async_computation.2 | async-start | bytes 3145728 | tf_op jit(solution)/shard_map/all_to_all | solution.py:104
  29.1 61.3 %all-to-all-start.1 = ((bf16[128,8,768]{2,0,1:T(8,128)(2,1)}), bf16[128,8,768]{2,0,1:T(8,128)(2,1)}, u32[]{:S(2)}, u32[]{:S(2)}) async-start(bf16[128,8,768]{2,0,1:T(8,128)(2,1)} %bitcast.41), calls=%async_computation.1 | async-start | bytes 3145728 | tf_op jit(solution)/shard_map/all_to_all | solution.py:102
  34.8 57.6 %collective-permute-start.7 = (bf16[768,1024]{1,0:T(8,128)(2,1)}, bf16[768,1024]{1,0:T(8,128)(2,1)S(1)}, u32[]{:S(2)}, u32[]{:S(2)}) collective-permute-start(bf16[768,1024]{1,0:T(8,128)(2,1)} %bitcast_bitcast_fusion.args_11_), channel_id=1, source_target_pairs={{0,30},{1,31},{2,0},{3,1},{4,2},{5,3},{6,4},{7,5},{8,6},{9,7},{10,... | collective-permute-start | bytes 4718600 | tf_op jit(solution)/shard_map/ppermute | solution.py:19
  37.5 84.8 %collective-permute-start.6 = (bf16[768,1024]{1,0:T(8,128)(2,1)}, bf16[768,1024]{1,0:T(8,128)(2,1)S(1)}, u32[]{:S(2)}, u32[]{:S(2)}) collective-permute-start(bf16[768,1024]{1,0:T(8,128)(2,1)} %bitcast_bitcast_fusion.args_11_), channel_id=1, source_target_pairs={{0,2},{1,3},{2,4},{3,5},{4,6},{5,7},{6,8},{7,9},{8,10},{9,11},{10,... | collective-permute-start | bytes 4718600 | tf_op jit(solution)/shard_map/ppermute | solution.py:19
  90.4 92.4 %collective-permute-start.1 = (bf16[1024,768]{1,0:T(8,128)(2,1)}, bf16[1024,768]{1,0:T(8,128)(2,1)}, u32[]{:S(2)}, u32[]{:S(2)}) collective-permute-start(bf16[1024,768]{1,0:T(8,128)(2,1)} %bitcast.6.args_4_), channel_id=1, source_target_pairs={{0,30},{1,31},{2,0},{3,1},{4,2},{5,3},{6,4},{7,5},{8,6},{9,7},{10,... | collective-permute-start | bytes 4718600 | tf_op jit(solution)/shard_map/ppermute | solution.py:19
  90.4 98.0 %collective-permute-start = (bf16[1024,768]{1,0:T(8,128)(2,1)}, bf16[1024,768]{1,0:T(8,128)(2,1)}, u32[]{:S(2)}, u32[]{:S(2)}) collective-permute-start(bf16[1024,768]{1,0:T(8,128)(2,1)} %bitcast.6.args_4_), channel_id=1, source_target_pairs={{0,2},{1,3},{2,4},{3,5},{4,6},{5,7},{6,8},{7,9},{8,10},{9,11},{10,... | collective-permute-start | bytes 4718600 | tf_op jit(solution)/shard_map/ppermute | solution.py:19
  92.4 99.1 %collective-permute-start.8 = (bf16[768,1024]{1,0:T(8,128)(2,1)}, bf16[768,1024]{1,0:T(8,128)(2,1)}, u32[]{:S(2)}, u32[]{:S(2)}) collective-permute-start(bf16[768,1024]{1,0:T(8,128)(2,1)} %bitcast_bitcast_fusion.args_11_), channel_id=1, source_target_pairs={{0,1},{1,0},{2,3},{3,2},{4,5},{5,4},{6,7},{7,6},{8,9},{9,8},{10,11... | collective-permute-start | bytes 4718600 | tf_op jit(solution)/shard_map/ppermute | solution.py:19
  92.4 59.5 %copy-start.2 = (bf16[768,1024]{1,0:T(8,128)(2,1)}, bf16[768,1024]{1,0:T(8,128)(2,1)S(1)}, u32[]{:S(2)}) copy-start(bf16[768,1024]{1,0:T(8,128)(2,1)S(1)} %collective-permute-done.7.args_13_) | copy-start | bytes 4718596
  92.4 99.1 %collective-permute-start.2 = (bf16[1024,768]{1,0:T(8,128)(2,1)}, bf16[1024,768]{1,0:T(8,128)(2,1)}, u32[]{:S(2)}, u32[]{:S(2)}) collective-permute-start(bf16[1024,768]{1,0:T(8,128)(2,1)} %bitcast.6.args_4_), channel_id=1, source_target_pairs={{0,1},{1,0},{2,3},{3,2},{4,5},{5,4},{6,7},{7,6},{8,9},{9,8},{10,11... | collective-permute-start | bytes 4718600 | tf_op jit(solution)/shard_map/ppermute | solution.py:19
  122.3 69.2 %copy-start.3 = (bf16[768,1024]{1,0:T(8,128)(2,1)}, bf16[768,1024]{1,0:T(8,128)(2,1)S(1)}, u32[]{:S(2)}) copy-start(bf16[768,1024]{1,0:T(8,128)(2,1)S(1)} %collective-permute-done.6.args_12_) | copy-start | bytes 4718596
  122.3 69.7 %collective-permute-start.11 = (bf16[768,1024]{1,0:T(8,128)(2,1)S(1)}, bf16[768,1024]{1,0:T(8,128)(2,1)}, u32[]{:S(2)}, u32[]{:S(2)}) collective-permute-start(bf16[768,1024]{1,0:T(8,128)(2,1)S(1)} %collective-permute-done.7.args_13_), channel_id=1, source_target_pairs={{0,1},{1,0},{2,3},{3,2},{4,5},{5,4},{6,7},{7,6},{8,9},{9,8},{10,11... | collective-permute-start | bytes 4718600 | tf_op jit(solution)/shard_map/ppermute | solution.py:19
  125.5 25.4 %copy-start.6 = (s32[8,8]{1,0:T(8,128)S(1)}, s32[8,8]{1,0:T(8,128)}, u32[]{:S(2)}) copy-start(s32[8,8]{1,0:T(8,128)} %param.10) | copy-start | bytes 772
  125.5 25.6 %copy-start.7 = (s32[2,7]{1,0:T(2,128)S(1)}, s32[2,7]{1,0:T(2,128)}, u32[]{:S(2)}) copy-start(s32[2,7]{1,0:T(2,128)} %constant.89.clone) | copy-start | bytes 172
  125.5 113.7 %all-to-all-start = ((bf16[128,8,768]{0,2,1:T(8,128)(2,1)}), bf16[128,8,768]{0,2,1:T(8,128)(2,1)}, u32[]{:S(2)}, u32[]{:S(2)}) async-start(bf16[128,8,768]{0,2,1:T(8,128)(2,1)} %bitcast.42), calls=%async_computation | async-start | bytes 3145728 | tf_op jit(solution)/shard_map/all_to_all | solution.py:106
  182.8 72.2 %collective-permute-start.9 = (bf16[768,1024]{1,0:T(8,128)(2,1)}, bf16[768,1024]{1,0:T(8,128)(2,1)}, u32[]{:S(2)}, u32[]{:S(2)}) collective-permute-start(bf16[768,1024]{1,0:T(8,128)(2,1)} %broadcast_select_fusion), channel_id=1, source_target_pairs={{0,31},{1,2},{2,1},{3,4},{4,3},{5,6},{6,5},{7,8},{8,7},{9,10},{10,... | collective-permute-start | bytes 4718600 | tf_op jit(solution)/shard_map/ppermute | solution.py:19
  191.1 80.8 %collective-permute-start.3 = (bf16[1024,768]{1,0:T(8,128)(2,1)}, bf16[1024,768]{1,0:T(8,128)(2,1)}, u32[]{:S(2)}, u32[]{:S(2)}) collective-permute-start(bf16[1024,768]{1,0:T(8,128)(2,1)} %broadcast_select_fusion.1), channel_id=1, source_target_pairs={{0,31},{1,2},{2,1},{3,4},{4,3},{5,6},{6,5},{7,8},{8,7},{9,10},{10,... | collective-permute-start | bytes 4718600 | tf_op jit(solution)/shard_map/ppermute | solution.py:19
  191.6 63.5 %collective-permute-start.10 = (bf16[768,1024]{1,0:T(8,128)(2,1)S(1)}, bf16[768,1024]{1,0:T(8,128)(2,1)}, u32[]{:S(2)}, u32[]{:S(2)}) collective-permute-start(bf16[768,1024]{1,0:T(8,128)(2,1)S(1)} %collective-permute-done.6.args_12_), channel_id=1, source_target_pairs={{0,1},{1,0},{2,3},{3,2},{4,5},{5,4},{6,7},{7,6},{8,9},{9,8},{10,11... | collective-permute-start | bytes 4718600 | tf_op jit(solution)/shard_map/ppermute | solution.py:19
  191.6 63.5 %collective-permute-start.5 = (bf16[1024,768]{1,0:T(8,128)(2,1)}, bf16[1024,768]{1,0:T(8,128)(2,1)}, u32[]{:S(2)}, u32[]{:S(2)}) collective-permute-start(bf16[1024,768]{1,0:T(8,128)(2,1)} %collective-permute-done.1.args_6_), channel_id=1, source_target_pairs={{0,1},{1,0},{2,3},{3,2},{4,5},{5,4},{6,7},{7,6},{8,9},{9,8},{10,11... | collective-permute-start | bytes 4718600 | tf_op jit(solution)/shard_map/ppermute | solution.py:19
  192.1 79.8 %collective-permute-start.4 = (bf16[1024,768]{1,0:T(8,128)(2,1)}, bf16[1024,768]{1,0:T(8,128)(2,1)S(1)}, u32[]{:S(2)}, u32[]{:S(2)}) collective-permute-start(bf16[1024,768]{1,0:T(8,128)(2,1)} %collective-permute-done.args_5_), channel_id=1, source_target_pairs={{0,1},{1,0},{2,3},{3,2},{4,5},{5,4},{6,7},{7,6},{8,9},{9,8},{10,11... | collective-permute-start | bytes 4718600 | tf_op jit(solution)/shard_map/ppermute | solution.py:19
  271.9 1.2 copy-start.4
  320.3 1.6 copy-start.1

commit v15 on v4

--- a/solution.py
+++ b/solution.py
@@ -104,6 +104,7 @@
     k_window = exchange(k_heads.T, 1, cycle_size)
     v_heads = lax.all_to_all(value_states, "head", split_axis=1, concat_axis=0, tiled=True)
     v_window = exchange(v_heads, 0, cycle_size)
+    queries, k_window, v_window = lax.optimization_barrier((queries, k_window, v_window))
     q_heads = lax.all_to_all(queries, "head", split_axis=1, concat_axis=0, tiled=True)
     shard_tok = q_heads.shape[0]
     tile_count = shard_tok // TILE

time: 323 us -> 329 us (1.019)
  waiting for transfers between devices: 228 us -> 234 us
  starting transfers between devices: 26.6 us -> 30.2 us
    ppermute x12, waiting for transfers between devices: 113 us -> 155 us  [permute(): return lax.ppermute(block, axis, route)]
    all_to_all x1, waiting for transfers between devices: 53.7 us -> 20.1 us  [body(): lax.all_to_all(key_states, 'head', split_axis=1, concat_axis=0, tiled=True)]
    all_to_all x1, waiting for transfers between devices: 41.5 us -> 10.2 us  [body(): lax.all_to_all(queries, 'head', split_axis=1, concat_axis=0, tiled=True)]
    all_to_all x1, waiting for transfers between devices: 19.9 us -> 48.9 us  [body(): lax.all_to_all(value_states, 'head', split_axis=1, concat_axis=0, tiled=T...]
    unnamed x17 -> x33, local copies, waits for them, and re-layouts: 2.74 us -> 7.49 us
  transfers between devices with their start and end apart: 15 -> 15, of which waited for: 7 -> 7; matrix products, arithmetic and copies ran while one was open for 4% -> 3% of each run, Pallas kernels for 0% -> 0%
where the time goes in v15:
time: 329 us; the launch traced here: 325 us
  waiting for transfers between devices  234 us (71%)
  starting transfers between devices  30.2 us (9%)
  Pallas kernels  24.7 us (8%)
  blocking collectives  17.8 us (5%)
  local copies, waits for them, and re-layouts  16.6 us (5%)
    ppermute x12, waiting for transfers between devices, permute(): return lax.ppermute(block, axis, route)  155 us
    all_to_all x1, waiting for transfers between devices, body(): lax.all_to_all(value_states, 'head', split_axis=1, concat_axis=0, tiled=T...  48.9 us
    pallas_call x1, Pallas kernels, body(): pl.pallas_call(kernel, grid_spec=grid_spec, out_shape=jax.ShapeDtypeStruc...  24.7 us
    all_to_all x1, waiting for transfers between devices, body(): lax.all_to_all(key_states, 'head', split_axis=1, concat_axis=0, tiled=True)  20.1 us
    all_to_all x1, blocking collectives, body(): return lax.all_to_all(out, 'head', split_axis=0, concat_axis=1, tiled=True)  17.8 us
    ppermute x12, starting transfers between devices, permute(): return lax.ppermute(block, axis, route)  14.8 us
    all_to_all x1, waiting for transfers between devices, body(): lax.all_to_all(queries, 'head', split_axis=1, concat_axis=0, tiled=True)  10.2 us
    unnamed x33, local copies, waits for them, and re-layouts  7.49 us
  transfers between devices with their start and end apart: 15, of which 7 were waited for; matrix products, arithmetic and copies ran while one was open for 3% of the time, Pallas kernels for 0%

profile of v15, /device:TPU:128, one launch (start us, length us, event | category | flops | bytes accessed | tf_op | source)
XLA Modules:
  0.0 325.3 jit_solution(7578623816654061711)
XLA Ops:
  0.0 2.6 copy.16
  2.6 5.1 %all-to-all-start = ((bf16[128,8,768]{0,2,1:T(8,128)(2,1)}), bf16[128,8,768]{0,2,1:T(8,128)(2,1)S(1)}, u32[]{:S(2)}, u32[]{:S(2)}) async-start(bf16[128,8,768]{0,2,1:T(8,128)(2,1)} %bitcast.2), calls=%async_computation | async-start | bytes 3145728 | tf_op jit(solution)/shard_map/all_to_all | solution.py:103
  7.7 1.3 copy.29
  8.9 20.1 %all-to-all-done = bf16[128,8,768]{0,2,1:T(8,128)(2,1)S(1)} async-done(((bf16[128,8,768]{0,2,1:T(8,128)(2,1)}), bf16[128,8,768]{0,2,1:T(8,128)(2,1)S(1)}, u32[]{:S(2)}, u32[]{:S(2)}) %all-to-all-start) | async-done | bytes 1572896 | tf_op jit(solution)/shard_map/all_to_all | solution.py:103
  29.0 4.3 %all-to-all-start.1 = ((bf16[128,8,768]{2,0,1:T(8,128)(2,1)}), bf16[128,8,768]{2,0,1:T(8,128)(2,1)}, u32[]{:S(2)}, u32[]{:S(2)}) async-start(bf16[128,8,768]{2,0,1:T(8,128)(2,1)} %bitcast.30), calls=%async_computation.1 | async-start | bytes 3145728 | tf_op jit(solution)/shard_map/all_to_all | solution.py:105
  33.3 1.4 bitcast_bitcast_fusion.args_4_
  34.7 1.5 collective-permute-start
  36.2 4.8 %collective-permute-start.1 = (bf16[768,1024]{1,0:T(8,128)(2,1)}, bf16[768,1024]{1,0:T(8,128)(2,1)S(1)}, u32[]{:S(2)}, u32[]{:S(2)}) collective-permute-start(bf16[768,1024]{1,0:T(8,128)(2,1)} %bitcast_bitcast_fusion.args_4_), channel_id=1, source_target_pairs={{0,30},{1,31},{2,0},{3,1},{4,2},{5,3},{6,4},{7,5},{8,6},{9,7},{10,... | collective-permute-start | bytes 4718600 | tf_op jit(solution)/shard_map/ppermute | solution.py:19
  40.9 48.9 %all-to-all-done.1 = bf16[128,8,768]{2,0,1:T(8,128)(2,1)} async-done(((bf16[128,8,768]{2,0,1:T(8,128)(2,1)}), bf16[128,8,768]{2,0,1:T(8,128)(2,1)}, u32[]{:S(2)}, u32[]{:S(2)}) %all-to-all-start.1) | async-done | bytes 1572896 | tf_op jit(solution)/shard_map/all_to_all | solution.py:105
  89.8 6.2 %collective-permute-start.7 = (bf16[1024,768]{1,0:T(8,128)(2,1)}, bf16[1024,768]{1,0:T(8,128)(2,1)}, u32[]{:S(2)}, u32[]{:S(2)}) collective-permute-start(bf16[1024,768]{1,0:T(8,128)(2,1)} %bitcast.6.args_11_), channel_id=1, source_target_pairs={{0,30},{1,31},{2,0},{3,1},{4,2},{5,3},{6,4},{7,5},{8,6},{9,7},{10,... | collective-permute-start | bytes 4718600 | tf_op jit(solution)/shard_map/ppermute | solution.py:19
  96.1 66.4 %collective-permute-done.args_5_ = bf16[768,1024]{1,0:T(8,128)(2,1)S(1)} collective-permute-done((bf16[768,1024]{1,0:T(8,128)(2,1)}, bf16[768,1024]{1,0:T(8,128)(2,1)S(1)}, u32[]{:S(2)}, u32[]{:S(2)}) %collective-permute-start) | collective-permute-done | bytes 1572896 | tf_op jit(solution)/shard_map/ppermute | solution.py:19
  162.8 60.5 %collective-permute-done.6.args_12_ = bf16[1024,768]{1,0:T(8,128)(2,1)} collective-permute-done((bf16[1024,768]{1,0:T(8,128)(2,1)}, bf16[1024,768]{1,0:T(8,128)(2,1)}, u32[]{:S(2)}, u32[]{:S(2)}) %collective-permute-start.6) | collective-permute-done | bytes 1572896 | tf_op jit(solution)/shard_map/ppermute | solution.py:19
  223.3 1.6 broadcast_select_fusion
  224.9 1.5 collective-permute-start.9
  227.2 10.8 %collective-permute-done.3.args_8_ = bf16[768,1024]{1,0:T(8,128)(2,1)S(1)} collective-permute-done((bf16[768,1024]{1,0:T(8,128)(2,1)S(1)}, bf16[768,1024]{1,0:T(8,128)(2,1)S(1)}, u32[]{:S(2)}, u32[]{:S(2)}) %collective-permute-start.3) | collective-permute-done | bytes 1572896 | tf_op jit(solution)/shard_map/ppermute | solution.py:19
  238.0 16.8 %collective-permute-done.9.args_15_ = bf16[1024,768]{1,0:T(8,128)(2,1)S(1)} collective-permute-done((bf16[1024,768]{1,0:T(8,128)(2,1)S(1)}, bf16[1024,768]{1,0:T(8,128)(2,1)S(1)}, u32[]{:S(2)}, u32[]{:S(2)}) %collective-permute-start.9) | collective-permute-done | bytes 1572896 | tf_op jit(solution)/shard_map/ppermute | solution.py:19
  257.4 1.2 copy-done.11
  258.6 1.2 copy.28
  259.9 6.1 %all-to-all-start.2 = ((bf16[128,8,768]{2,0,1:T(8,128)(2,1)}), bf16[128,8,768]{2,0,1:T(8,128)(2,1)S(1)}, u32[]{:S(2)}, u32[]{:S(2)}) async-start(bf16[128,8,768]{2,0,1:T(8,128)(2,1)} %bitcast.29), calls=%async_computation.2 | async-start | bytes 3145728 | tf_op jit(solution)/shard_map/all_to_all | solution.py:108
  270.1 10.2 %all-to-all-done.2 = bf16[128,8,768]{2,0,1:T(8,128)(2,1)S(1)} async-done(((bf16[128,8,768]{2,0,1:T(8,128)(2,1)}), bf16[128,8,768]{2,0,1:T(8,128)(2,1)S(1)}, u32[]{:S(2)}, u32[]{:S(2)}) %all-to-all-start.2) | async-done | bytes 1572896 | tf_op jit(solution)/shard_map/all_to_all | solution.py:108
  280.3 1.1 copy-done.3
  281.5 24.7 %shard_map.73 = bf16[1024,768]{1,0:T(8,128)(2,1)} custom-call(s32[64]{0:T(128)} %reshape.64.args_0_, s32[8]{0:T(128)} %args_1_.4, f32[384]{0:T(512)} %mul.43.args_2_, bf16[1024,768]{1,0:T(8,128)(2,1)} %bitcast.31, bf16[768,1024]{1,0:T(8,128)(2,1)} %bitcast_bitcast_fusion.args_4_, bf16[768,1024]{1,0:T(8,128)(2,1)} %copy-done.1, bf16[768,1024]{1,0:T(8,128)(2,1)} %copy-done.2, ...), custom_call_target="tpu_custom_call" | custom-call | tf_op jit(solution)/shard_map/pallas_call | solution.py:148
  306.1 17.8 %all_to_all.76 = bf16[8,128,768]{2,1,0:T(8,128)(2,1)S(1)} all-to-all(bf16[8,128,768]{2,1,0:T(8,128)(2,1)} %bitcast.32), channel_id=1, replica_groups=mesh['head'=8,'blk'=32] {'head'}, dimensions={0} | all-to-all | bytes 3145728 | tf_op jit(solution)/shard_map/all_to_all | solution.py:161
  323.9 1.3 copy.24
  (67 shorter events, 7.7 us)
Async XLA Ops:
  0.0 267.7 %copy-start = (s32[256]{0:T(256)S(1)}, s32[256]{0:T(256)}, u32[]{:S(2)}) copy-start(s32[256]{0:T(256)} %param.12) | copy-start | bytes 3076
  2.6 26.4 %all-to-all-start = ((bf16[128,8,768]{0,2,1:T(8,128)(2,1)}), bf16[128,8,768]{0,2,1:T(8,128)(2,1)S(1)}, u32[]{:S(2)}, u32[]{:S(2)}) async-start(bf16[128,8,768]{0,2,1:T(8,128)(2,1)} %bitcast.2), calls=%async_computation | async-start | bytes 3145728 | tf_op jit(solution)/shard_map/all_to_all | solution.py:103
  29.0 60.8 %all-to-all-start.1 = ((bf16[128,8,768]{2,0,1:T(8,128)(2,1)}), bf16[128,8,768]{2,0,1:T(8,128)(2,1)}, u32[]{:S(2)}, u32[]{:S(2)}) async-start(bf16[128,8,768]{2,0,1:T(8,128)(2,1)} %bitcast.30), calls=%async_computation.1 | async-start | bytes 3145728 | tf_op jit(solution)/shard_map/all_to_all | solution.py:105
  34.7 127.8 %collective-permute-start = (bf16[768,1024]{1,0:T(8,128)(2,1)}, bf16[768,1024]{1,0:T(8,128)(2,1)S(1)}, u32[]{:S(2)}, u32[]{:S(2)}) collective-permute-start(bf16[768,1024]{1,0:T(8,128)(2,1)} %bitcast_bitcast_fusion.args_4_), channel_id=1, source_target_pairs={{0,2},{1,3},{2,4},{3,5},{4,6},{5,7},{6,8},{7,9},{8,10},{9,11},{10,... | collective-permute-start | bytes 4718600 | tf_op jit(solution)/shard_map/ppermute | solution.py:19
  36.2 126.3 %collective-permute-start.1 = (bf16[768,1024]{1,0:T(8,128)(2,1)}, bf16[768,1024]{1,0:T(8,128)(2,1)S(1)}, u32[]{:S(2)}, u32[]{:S(2)}) collective-permute-start(bf16[768,1024]{1,0:T(8,128)(2,1)} %bitcast_bitcast_fusion.args_4_), channel_id=1, source_target_pairs={{0,30},{1,31},{2,0},{3,1},{4,2},{5,3},{6,4},{7,5},{8,6},{9,7},{10,... | collective-permute-start | bytes 4718600 | tf_op jit(solution)/shard_map/ppermute | solution.py:19
  89.8 133.5 %collective-permute-start.6 = (bf16[1024,768]{1,0:T(8,128)(2,1)}, bf16[1024,768]{1,0:T(8,128)(2,1)}, u32[]{:S(2)}, u32[]{:S(2)}) collective-permute-start(bf16[1024,768]{1,0:T(8,128)(2,1)} %bitcast.6.args_11_), channel_id=1, source_target_pairs={{0,2},{1,3},{2,4},{3,5},{4,6},{5,7},{6,8},{7,9},{8,10},{9,11},{10,... | collective-permute-start | bytes 4718600 | tf_op jit(solution)/shard_map/ppermute | solution.py:19
  89.8 133.5 %collective-permute-start.7 = (bf16[1024,768]{1,0:T(8,128)(2,1)}, bf16[1024,768]{1,0:T(8,128)(2,1)}, u32[]{:S(2)}, u32[]{:S(2)}) collective-permute-start(bf16[1024,768]{1,0:T(8,128)(2,1)} %bitcast.6.args_11_), channel_id=1, source_target_pairs={{0,30},{1,31},{2,0},{3,1},{4,2},{5,3},{6,4},{7,5},{8,6},{9,7},{10,... | collective-permute-start | bytes 4718600 | tf_op jit(solution)/shard_map/ppermute | solution.py:19
  96.1 130.4 %collective-permute-start.2 = (bf16[768,1024]{1,0:T(8,128)(2,1)}, bf16[768,1024]{1,0:T(8,128)(2,1)S(1)}, u32[]{:S(2)}, u32[]{:S(2)}) collective-permute-start(bf16[768,1024]{1,0:T(8,128)(2,1)} %bitcast_bitcast_fusion.args_4_), channel_id=1, source_target_pairs={{0,1},{1,0},{2,3},{3,2},{4,5},{5,4},{6,7},{7,6},{8,9},{9,8},{10,11... | collective-permute-start | bytes 4718600 | tf_op jit(solution)/shard_map/ppermute | solution.py:19
  162.5 63.9 %copy-start.1 = (bf16[768,1024]{1,0:T(8,128)(2,1)}, bf16[768,1024]{1,0:T(8,128)(2,1)S(1)}, u32[]{:S(2)}) copy-start(bf16[768,1024]{1,0:T(8,128)(2,1)S(1)} %collective-permute-done.args_5_) | copy-start | bytes 4718596
  162.5 64.5 %collective-permute-start.8 = (bf16[1024,768]{1,0:T(8,128)(2,1)}, bf16[1024,768]{1,0:T(8,128)(2,1)S(1)}, u32[]{:S(2)}, u32[]{:S(2)}) collective-permute-start(bf16[1024,768]{1,0:T(8,128)(2,1)} %bitcast.6.args_11_), channel_id=1, source_target_pairs={{0,1},{1,0},{2,3},{3,2},{4,5},{5,4},{6,7},{7,6},{8,9},{9,8},{10,11... | collective-permute-start | bytes 4718600 | tf_op jit(solution)/shard_map/ppermute | solution.py:19
  162.5 63.9 %copy-start.2 = (bf16[768,1024]{1,0:T(8,128)(2,1)}, bf16[768,1024]{1,0:T(8,128)(2,1)S(1)}, u32[]{:S(2)}) copy-start(bf16[768,1024]{1,0:T(8,128)(2,1)S(1)} %collective-permute-done.1.args_6_) | copy-start | bytes 4718596
  162.7 95.9 %copy-start.13 = (bf16[128,6144]{1,0:T(8,128)(2,1)S(1)}, bf16[128,6144]{1,0:T(8,128)(2,1)}, u32[]{:S(2)}) copy-start(bf16[128,6144]{1,0:T(8,128)(2,1)} %param.7) | copy-start | bytes 4718596
  162.7 75.3 %collective-permute-start.3 = (bf16[768,1024]{1,0:T(8,128)(2,1)S(1)}, bf16[768,1024]{1,0:T(8,128)(2,1)S(1)}, u32[]{:S(2)}, u32[]{:S(2)}) collective-permute-start(bf16[768,1024]{1,0:T(8,128)(2,1)S(1)} %broadcast_select_fusion.1), channel_id=1, source_target_pairs={{0,31},{1,2},{2,1},{3,4},{4,3},{5,6},{6,5},{7,8},{8,7},{9,10},{10,... | collective-permute-start | bytes 4718600 | tf_op jit(solution)/shard_map/ppermute | solution.py:19
  224.9 29.9 %collective-permute-start.9 = (bf16[1024,768]{1,0:T(8,128)(2,1)S(1)}, bf16[1024,768]{1,0:T(8,128)(2,1)S(1)}, u32[]{:S(2)}, u32[]{:S(2)}) collective-permute-start(bf16[1024,768]{1,0:T(8,128)(2,1)S(1)} %broadcast_select_fusion), channel_id=1, source_target_pairs={{0,31},{1,2},{2,1},{3,4},{4,3},{5,6},{6,5},{7,8},{8,7},{9,10},{10,... | collective-permute-start | bytes 4718600 | tf_op jit(solution)/shard_map/ppermute | solution.py:19
  226.5 28.4 %collective-permute-start.4 = (bf16[768,1024]{1,0:T(8,128)(2,1)S(1)}, bf16[768,1024]{1,0:T(8,128)(2,1)S(1)}, u32[]{:S(2)}, u32[]{:S(2)}) collective-permute-start(bf16[768,1024]{1,0:T(8,128)(2,1)S(1)} %collective-permute-done.args_5_), channel_id=1, source_target_pairs={{0,1},{1,0},{2,3},{3,2},{4,5},{5,4},{6,7},{7,6},{8,9},{9,8},{10,11... | collective-permute-start | bytes 4718600 | tf_op jit(solution)/shard_map/ppermute | solution.py:19
  226.5 33.4 %copy-start.4 = (bf16[768,1024]{1,0:T(8,128)(2,1)}, bf16[768,1024]{1,0:T(8,128)(2,1)S(1)}, u32[]{:S(2)}) copy-start(bf16[768,1024]{1,0:T(8,128)(2,1)S(1)} %collective-permute-done.2.args_7_) | copy-start | bytes 4718596
  226.5 28.4 %collective-permute-start.5 = (bf16[768,1024]{1,0:T(8,128)(2,1)S(1)}, bf16[768,1024]{1,0:T(8,128)(2,1)S(1)}, u32[]{:S(2)}, u32[]{:S(2)}) collective-permute-start(bf16[768,1024]{1,0:T(8,128)(2,1)S(1)} %collective-permute-done.1.args_6_), channel_id=1, source_target_pairs={{0,1},{1,0},{2,3},{3,2},{4,5},{5,4},{6,7},{7,6},{8,9},{9,8},{10,11... | collective-permute-start | bytes 4718600 | tf_op jit(solution)/shard_map/ppermute | solution.py:19
  227.1 32.8 %copy-start.5 = (bf16[1024,768]{1,0:T(8,128)(2,1)}, bf16[1024,768]{1,0:T(8,128)(2,1)S(1)}, u32[]{:S(2)}) copy-start(bf16[1024,768]{1,0:T(8,128)(2,1)S(1)} %collective-permute-done.8.args_14_) | copy-start | bytes 4718596
  227.1 27.8 %collective-permute-start.10 = (bf16[1024,768]{1,0:T(8,128)(2,1)}, bf16[1024,768]{1,0:T(8,128)(2,1)S(1)}, u32[]{:S(2)}, u32[]{:S(2)}) collective-permute-start(bf16[1024,768]{1,0:T(8,128)(2,1)} %collective-permute-done.6.args_12_), channel_id=1, source_target_pairs={{0,1},{1,0},{2,3},{3,2},{4,5},{5,4},{6,7},{7,6},{8,9},{9,8},{10,11... | collective-permute-start | bytes 4718600 | tf_op jit(solution)/shard_map/ppermute | solution.py:19
  238.0 16.9 %copy-start.6 = (bf16[768,1024]{1,0:T(8,128)(2,1)}, bf16[768,1024]{1,0:T(8,128)(2,1)S(1)}, u32[]{:S(2)}) copy-start(bf16[768,1024]{1,0:T(8,128)(2,1)S(1)} %collective-permute-done.3.args_8_) | copy-start | bytes 4718596
  238.0 18.0 %collective-permute-start.11 = (bf16[1024,768]{1,0:T(8,128)(2,1)}, bf16[1024,768]{1,0:T(8,128)(2,1)S(1)}, u32[]{:S(2)}, u32[]{:S(2)}) collective-permute-start(bf16[1024,768]{1,0:T(8,128)(2,1)} %collective-permute-done.7.args_13_), channel_id=1, source_target_pairs={{0,1},{1,0},{2,3},{3,2},{4,5},{5,4},{6,7},{7,6},{8,9},{9,8},{10,11... | collective-permute-start | bytes 4718600 | tf_op jit(solution)/shard_map/ppermute | solution.py:19
  259.9 6.1 %copy-start.14 = (s32[8,8]{1,0:T(8,128)S(1)}, s32[8,8]{1,0:T(8,128)}, u32[]{:S(2)}) copy-start(s32[8,8]{1,0:T(8,128)} %param.10) | copy-start | bytes 772
  259.9 6.2 %copy-start.15 = (s32[2,7]{1,0:T(2,128)S(1)}, s32[2,7]{1,0:T(2,128)}, u32[]{:S(2)}) copy-start(s32[2,7]{1,0:T(2,128)} %constant.89.clone) | copy-start | bytes 172
  259.9 20.4 %all-to-all-start.2 = ((bf16[128,8,768]{2,0,1:T(8,128)(2,1)}), bf16[128,8,768]{2,0,1:T(8,128)(2,1)S(1)}, u32[]{:S(2)}, u32[]{:S(2)}) async-start(bf16[128,8,768]{2,0,1:T(8,128)(2,1)} %bitcast.29), calls=%async_computation.2 | async-start | bytes 3145728 | tf_op jit(solution)/shard_map/all_to_all | solution.py:108
  (7 other events, 13.8 us)

commit v16 on v4

--- a/solution.py
+++ b/solution.py
@@ -104,6 +104,7 @@
     k_window = exchange(k_heads.T, 1, cycle_size)
     v_heads = lax.all_to_all(value_states, "head", split_axis=1, concat_axis=0, tiled=True)
     v_window = exchange(v_heads, 0, cycle_size)
+    queries, k_window = lax.optimization_barrier((queries, k_window))
     q_heads = lax.all_to_all(queries, "head", split_axis=1, concat_axis=0, tiled=True)
     shard_tok = q_heads.shape[0]
     tile_count = shard_tok // TILE

time: 323 us -> 327 us (1.012)
  starting transfers between devices: 26.6 us -> 44.3 us
  waiting for transfers between devices: 228 us -> 215 us
    ppermute x12, waiting for transfers between devices: 113 us -> 195 us  [permute(): return lax.ppermute(block, axis, route)]
    all_to_all x1, waiting for transfers between devices: 41.5 us -> 0.01 us  [body(): lax.all_to_all(queries, 'head', split_axis=1, concat_axis=0, tiled=True)]
    all_to_all x1, waiting for transfers between devices: 53.7 us -> 20.1 us  [body(): lax.all_to_all(key_states, 'head', split_axis=1, concat_axis=0, tiled=True)]
    all_to_all x1, waiting for transfers between devices: 19.9 us -> 0.01 us  [body(): lax.all_to_all(value_states, 'head', split_axis=1, concat_axis=0, tiled=T...]
    ppermute x12, starting transfers between devices: 12.5 us -> 30.7 us  [permute(): return lax.ppermute(block, axis, route)]
  transfers between devices with their start and end apart: 15 -> 15, of which waited for: 7 -> 4; matrix products, arithmetic and copies ran while one was open for 4% -> 4% of each run, Pallas kernels for 0% -> 0%
where the time goes in v16:
time: 327 us; the launch traced here: 324 us
  waiting for transfers between devices  215 us (66%)
  starting transfers between devices  44.3 us (14%)
  Pallas kernels  24.8 us (8%)
  blocking collectives  20.5 us (6%)
  local copies, waits for them, and re-layouts  14.9 us (5%)
  other arithmetic  4.43 us (1%)
    ppermute x12, waiting for transfers between devices, permute(): return lax.ppermute(block, axis, route)  195 us
    ppermute x12, starting transfers between devices, permute(): return lax.ppermute(block, axis, route)  30.7 us
    pallas_call x1, Pallas kernels, body(): pl.pallas_call(kernel, grid_spec=grid_spec, out_shape=jax.ShapeDtypeStruc...  24.8 us
    all_to_all x1, blocking collectives, body(): return lax.all_to_all(out, 'head', split_axis=0, concat_axis=1, tiled=True)  20.5 us
    all_to_all x1, waiting for transfers between devices, body(): lax.all_to_all(key_states, 'head', split_axis=1, concat_axis=0, tiled=True)  20.1 us
  transfers between devices with their start and end apart: 15, of which 4 were waited for; matrix products, arithmetic and copies ran while one was open for 4% of the time, Pallas kernels for 0%

profile of v16, /device:TPU:128, one launch (start us, length us, event | category | flops | bytes accessed | tf_op | source)
XLA Modules:
  0.0 324.5 jit_solution(10319343692964629412)
XLA Ops:
  0.0 2.6 copy.16
  2.6 5.1 %all-to-all-start = ((bf16[128,8,768]{0,2,1:T(8,128)(2,1)}), bf16[128,8,768]{0,2,1:T(8,128)(2,1)S(1)}, u32[]{:S(2)}, u32[]{:S(2)}) async-start(bf16[128,8,768]{0,2,1:T(8,128)(2,1)} %bitcast.2), calls=%async_computation | async-start | bytes 3145728 | tf_op jit(solution)/shard_map/all_to_all | solution.py:103
  7.7 1.3 copy.28
  8.9 20.1 %all-to-all-done = bf16[128,8,768]{0,2,1:T(8,128)(2,1)S(1)} async-done(((bf16[128,8,768]{0,2,1:T(8,128)(2,1)}), bf16[128,8,768]{0,2,1:T(8,128)(2,1)S(1)}, u32[]{:S(2)}, u32[]{:S(2)}) %all-to-all-start) | async-done | bytes 1572896 | tf_op jit(solution)/shard_map/all_to_all | solution.py:103
  29.0 4.3 %all-to-all-start.2 = ((bf16[128,8,768]{2,0,1:T(8,128)(2,1)}), bf16[128,8,768]{2,0,1:T(8,128)(2,1)}, u32[]{:S(2)}, u32[]{:S(2)}) async-start(bf16[128,8,768]{2,0,1:T(8,128)(2,1)} %bitcast.29), calls=%async_computation.2 | async-start | bytes 3145728 | tf_op jit(solution)/shard_map/all_to_all | solution.py:105
  33.3 1.4 bitcast_bitcast_fusion.args_4_
  34.7 1.5 collective-permute-start
  36.2 4.8 %collective-permute-start.1 = (bf16[768,1024]{1,0:T(8,128)(2,1)}, bf16[768,1024]{1,0:T(8,128)(2,1)S(1)}, u32[]{:S(2)}, u32[]{:S(2)}) collective-permute-start(bf16[768,1024]{1,0:T(8,128)(2,1)} %bitcast_bitcast_fusion.args_4_), channel_id=1, source_target_pairs={{0,30},{1,31},{2,0},{3,1},{4,2},{5,3},{6,4},{7,5},{8,6},{9,7},{10,... | collective-permute-start | bytes 4718600 | tf_op jit(solution)/shard_map/ppermute | solution.py:19
  40.9 79.1 %collective-permute-done.args_5_ = bf16[768,1024]{1,0:T(8,128)(2,1)S(1)} collective-permute-done((bf16[768,1024]{1,0:T(8,128)(2,1)}, bf16[768,1024]{1,0:T(8,128)(2,1)S(1)}, u32[]{:S(2)}, u32[]{:S(2)}) %collective-permute-start) | collective-permute-done | bytes 1572896 | tf_op jit(solution)/shard_map/ppermute | solution.py:19
  120.0 1.5 broadcast_select_fusion.1
  122.2 6.2 %collective-permute-start.7 = (bf16[1024,768]{1,0:T(8,128)(2,1)}, bf16[1024,768]{1,0:T(8,128)(2,1)}, u32[]{:S(2)}, u32[]{:S(2)}) collective-permute-start(bf16[1024,768]{1,0:T(8,128)(2,1)} %bitcast.8.args_11_), channel_id=1, source_target_pairs={{0,30},{1,31},{2,0},{3,1},{4,2},{5,3},{6,4},{7,5},{8,6},{9,7},{10,... | collective-permute-start | bytes 4718600 | tf_op jit(solution)/shard_map/ppermute | solution.py:19
  128.5 80.7 %collective-permute-done.3.args_8_ = bf16[768,1024]{1,0:T(8,128)(2,1)} collective-permute-done((bf16[768,1024]{1,0:T(8,128)(2,1)}, bf16[768,1024]{1,0:T(8,128)(2,1)}, u32[]{:S(2)}, u32[]{:S(2)}) %collective-permute-start.3) | collective-permute-done | bytes 1572896 | tf_op jit(solution)/shard_map/ppermute | solution.py:19
  209.2 2.7 copy.29
  211.9 4.3 %all-to-all-start.1 = ((bf16[128,8,768]{2,0,1:T(8,128)(2,1)}), bf16[128,8,768]{2,0,1:T(8,128)(2,1)S(1)}, u32[]{:S(2)}, u32[]{:S(2)}) async-start(bf16[128,8,768]{2,0,1:T(8,128)(2,1)} %bitcast.30), calls=%async_computation.1 | async-start | bytes 3145728 | tf_op jit(solution)/shard_map/all_to_all | solution.py:108
  216.3 2.7 broadcast_select_fusion
  219.0 17.5 %collective-permute-start.9 = (bf16[1024,768]{1,0:T(8,128)(2,1)}, bf16[1024,768]{1,0:T(8,128)(2,1)}, u32[]{:S(2)}, u32[]{:S(2)}) collective-permute-start(bf16[1024,768]{1,0:T(8,128)(2,1)} %broadcast_select_fusion), channel_id=1, source_target_pairs={{0,31},{1,2},{2,1},{3,4},{4,3},{5,6},{6,5},{7,8},{8,7},{9,10},{10,... | collective-permute-start | bytes 4718600 | tf_op jit(solution)/shard_map/ppermute | solution.py:19
  237.2 0.8 gather_fusion
  238.8 0.8 gather_fusion.2
  240.5 0.7 mul.43.args_2_
  241.2 35.5 %collective-permute-done.9.args_15_ = bf16[1024,768]{1,0:T(8,128)(2,1)} collective-permute-done((bf16[1024,768]{1,0:T(8,128)(2,1)}, bf16[1024,768]{1,0:T(8,128)(2,1)}, u32[]{:S(2)}, u32[]{:S(2)}) %collective-permute-start.9) | collective-permute-done | bytes 1572896 | tf_op jit(solution)/shard_map/ppermute | solution.py:19
  276.8 1.1 copy-done.3
  277.9 24.8 %shard_map.73 = bf16[1024,768]{1,0:T(8,128)(2,1)} custom-call(s32[64]{0:T(128)} %reshape.64.args_0_, s32[8]{0:T(128)} %args_1_.4, f32[384]{0:T(512)} %mul.43.args_2_, bf16[1024,768]{1,0:T(8,128)(2,1)} %bitcast.31, bf16[768,1024]{1,0:T(8,128)(2,1)} %bitcast_bitcast_fusion.args_4_, bf16[768,1024]{1,0:T(8,128)(2,1)} %copy-done.1, bf16[768,1024]{1,0:T(8,128)(2,1)} %copy-done.2, ...), custom_call_target="tpu_custom_call" | custom-call | tf_op jit(solution)/shard_map/pallas_call | solution.py:148
  302.7 20.5 %all_to_all.76 = bf16[8,128,768]{2,1,0:T(8,128)(2,1)S(1)} all-to-all(bf16[8,128,768]{2,1,0:T(8,128)(2,1)} %bitcast.32), channel_id=1, replica_groups=mesh['head'=8,'blk'=32] {'head'}, dimensions={0} | all-to-all | bytes 3145728 | tf_op jit(solution)/shard_map/all_to_all | solution.py:161
  323.2 1.3 copy.24
  (51 shorter events, 3.3 us)
Async XLA Ops:
  0.0 238.8 %copy-start = (s32[256]{0:T(256)S(1)}, s32[256]{0:T(256)}, u32[]{:S(2)}) copy-start(s32[256]{0:T(256)} %param.12) | copy-start | bytes 3076
  2.6 5.1 %copy-start.5 = (bf16[128,6144]{1,0:T(8,128)(2,1)S(1)}, bf16[128,6144]{1,0:T(8,128)(2,1)}, u32[]{:S(2)}) copy-start(bf16[128,6144]{1,0:T(8,128)(2,1)} %param.9) | copy-start | bytes 4718596
  2.6 26.4 %all-to-all-start = ((bf16[128,8,768]{0,2,1:T(8,128)(2,1)}), bf16[128,8,768]{0,2,1:T(8,128)(2,1)S(1)}, u32[]{:S(2)}, u32[]{:S(2)}) async-start(bf16[128,8,768]{0,2,1:T(8,128)(2,1)} %bitcast.2), calls=%async_computation | async-start | bytes 3145728 | tf_op jit(solution)/shard_map/all_to_all | solution.py:103
  29.0 93.2 %all-to-all-start.2 = ((bf16[128,8,768]{2,0,1:T(8,128)(2,1)}), bf16[128,8,768]{2,0,1:T(8,128)(2,1)}, u32[]{:S(2)}, u32[]{:S(2)}) async-start(bf16[128,8,768]{2,0,1:T(8,128)(2,1)} %bitcast.29), calls=%async_computation.2 | async-start | bytes 3145728 | tf_op jit(solution)/shard_map/all_to_all | solution.py:105
  34.7 85.3 %collective-permute-start = (bf16[768,1024]{1,0:T(8,128)(2,1)}, bf16[768,1024]{1,0:T(8,128)(2,1)S(1)}, u32[]{:S(2)}, u32[]{:S(2)}) collective-permute-start(bf16[768,1024]{1,0:T(8,128)(2,1)} %bitcast_bitcast_fusion.args_4_), channel_id=1, source_target_pairs={{0,2},{1,3},{2,4},{3,5},{4,6},{5,7},{6,8},{7,9},{8,10},{9,11},{10,... | collective-permute-start | bytes 4718600 | tf_op jit(solution)/shard_map/ppermute | solution.py:19
  36.2 83.8 %collective-permute-start.1 = (bf16[768,1024]{1,0:T(8,128)(2,1)}, bf16[768,1024]{1,0:T(8,128)(2,1)S(1)}, u32[]{:S(2)}, u32[]{:S(2)}) collective-permute-start(bf16[768,1024]{1,0:T(8,128)(2,1)} %bitcast_bitcast_fusion.args_4_), channel_id=1, source_target_pairs={{0,30},{1,31},{2,0},{3,1},{4,2},{5,3},{6,4},{7,5},{8,6},{9,7},{10,... | collective-permute-start | bytes 4718600 | tf_op jit(solution)/shard_map/ppermute | solution.py:19
  40.9 81.3 %collective-permute-start.2 = (bf16[768,1024]{1,0:T(8,128)(2,1)}, bf16[768,1024]{1,0:T(8,128)(2,1)}, u32[]{:S(2)}, u32[]{:S(2)}) collective-permute-start(bf16[768,1024]{1,0:T(8,128)(2,1)} %bitcast_bitcast_fusion.args_4_), channel_id=1, source_target_pairs={{0,1},{1,0},{2,3},{3,2},{4,5},{5,4},{6,7},{7,6},{8,9},{9,8},{10,11... | collective-permute-start | bytes 4718600 | tf_op jit(solution)/shard_map/ppermute | solution.py:19
  120.0 1.7 copy-start.1
  120.0 2.2 copy-start.2
  121.5 87.7 %collective-permute-start.3 = (bf16[768,1024]{1,0:T(8,128)(2,1)}, bf16[768,1024]{1,0:T(8,128)(2,1)}, u32[]{:S(2)}, u32[]{:S(2)}) collective-permute-start(bf16[768,1024]{1,0:T(8,128)(2,1)} %broadcast_select_fusion.1), channel_id=1, source_target_pairs={{0,31},{1,2},{2,1},{3,4},{4,3},{5,6},{6,5},{7,8},{8,7},{9,10},{10,... | collective-permute-start | bytes 4718600 | tf_op jit(solution)/shard_map/ppermute | solution.py:19
  121.7 87.5 %collective-permute-start.4 = (bf16[768,1024]{1,0:T(8,128)(2,1)S(1)}, bf16[768,1024]{1,0:T(8,128)(2,1)}, u32[]{:S(2)}, u32[]{:S(2)}) collective-permute-start(bf16[768,1024]{1,0:T(8,128)(2,1)S(1)} %collective-permute-done.args_5_), channel_id=1, source_target_pairs={{0,1},{1,0},{2,3},{3,2},{4,5},{5,4},{6,7},{7,6},{8,9},{9,8},{10,11... | collective-permute-start | bytes 4718600 | tf_op jit(solution)/shard_map/ppermute | solution.py:19
  122.2 87.0 %collective-permute-start.5 = (bf16[768,1024]{1,0:T(8,128)(2,1)S(1)}, bf16[768,1024]{1,0:T(8,128)(2,1)}, u32[]{:S(2)}, u32[]{:S(2)}) collective-permute-start(bf16[768,1024]{1,0:T(8,128)(2,1)S(1)} %collective-permute-done.1.args_6_), channel_id=1, source_target_pairs={{0,1},{1,0},{2,3},{3,2},{4,5},{5,4},{6,7},{7,6},{8,9},{9,8},{10,11... | collective-permute-start | bytes 4718600 | tf_op jit(solution)/shard_map/ppermute | solution.py:19
  122.2 94.0 %collective-permute-start.6 = (bf16[1024,768]{1,0:T(8,128)(2,1)}, bf16[1024,768]{1,0:T(8,128)(2,1)}, u32[]{:S(2)}, u32[]{:S(2)}) collective-permute-start(bf16[1024,768]{1,0:T(8,128)(2,1)} %bitcast.8.args_11_), channel_id=1, source_target_pairs={{0,2},{1,3},{2,4},{3,5},{4,6},{5,7},{6,8},{7,9},{8,10},{9,11},{10,... | collective-permute-start | bytes 4718600 | tf_op jit(solution)/shard_map/ppermute | solution.py:19
  122.2 94.0 %collective-permute-start.7 = (bf16[1024,768]{1,0:T(8,128)(2,1)}, bf16[1024,768]{1,0:T(8,128)(2,1)}, u32[]{:S(2)}, u32[]{:S(2)}) collective-permute-start(bf16[1024,768]{1,0:T(8,128)(2,1)} %bitcast.8.args_11_), channel_id=1, source_target_pairs={{0,30},{1,31},{2,0},{3,1},{4,2},{5,3},{6,4},{7,5},{8,6},{9,7},{10,... | collective-permute-start | bytes 4718600 | tf_op jit(solution)/shard_map/ppermute | solution.py:19
  211.9 64.9 %all-to-all-start.1 = ((bf16[128,8,768]{2,0,1:T(8,128)(2,1)}), bf16[128,8,768]{2,0,1:T(8,128)(2,1)S(1)}, u32[]{:S(2)}, u32[]{:S(2)}) async-start(bf16[128,8,768]{2,0,1:T(8,128)(2,1)} %bitcast.30), calls=%async_computation.1 | async-start | bytes 3145728 | tf_op jit(solution)/shard_map/all_to_all | solution.py:108
  216.1 21.0 %copy-start.6 = (s32[8,8]{1,0:T(8,128)S(1)}, s32[8,8]{1,0:T(8,128)}, u32[]{:S(2)}) copy-start(s32[8,8]{1,0:T(8,128)} %param.10) | copy-start | bytes 772
  216.1 21.1 %copy-start.7 = (s32[2,7]{1,0:T(2,128)S(1)}, s32[2,7]{1,0:T(2,128)}, u32[]{:S(2)}) copy-start(s32[2,7]{1,0:T(2,128)} %constant.89.clone) | copy-start | bytes 172
  216.2 25.1 %collective-permute-start.8 = (bf16[1024,768]{1,0:T(8,128)(2,1)}, bf16[1024,768]{1,0:T(8,128)(2,1)S(1)}, u32[]{:S(2)}, u32[]{:S(2)}) collective-permute-start(bf16[1024,768]{1,0:T(8,128)(2,1)} %bitcast.8.args_11_), channel_id=1, source_target_pairs={{0,1},{1,0},{2,3},{3,2},{4,5},{5,4},{6,7},{7,6},{8,9},{9,8},{10,11... | collective-permute-start | bytes 4718600 | tf_op jit(solution)/shard_map/ppermute | solution.py:19
  219.0 57.7 %collective-permute-start.9 = (bf16[1024,768]{1,0:T(8,128)(2,1)}, bf16[1024,768]{1,0:T(8,128)(2,1)}, u32[]{:S(2)}, u32[]{:S(2)}) collective-permute-start(bf16[1024,768]{1,0:T(8,128)(2,1)} %broadcast_select_fusion), channel_id=1, source_target_pairs={{0,31},{1,2},{2,1},{3,4},{4,3},{5,6},{6,5},{7,8},{8,7},{9,10},{10,... | collective-permute-start | bytes 4718600 | tf_op jit(solution)/shard_map/ppermute | solution.py:19
  236.5 40.2 %collective-permute-start.10 = (bf16[1024,768]{1,0:T(8,128)(2,1)}, bf16[1024,768]{1,0:T(8,128)(2,1)}, u32[]{:S(2)}, u32[]{:S(2)}) collective-permute-start(bf16[1024,768]{1,0:T(8,128)(2,1)} %collective-permute-done.6.args_12_), channel_id=1, source_target_pairs={{0,1},{1,0},{2,3},{3,2},{4,5},{5,4},{6,7},{7,6},{8,9},{9,8},{10,11... | collective-permute-start | bytes 4718600 | tf_op jit(solution)/shard_map/ppermute | solution.py:19
  237.1 39.7 %collective-permute-start.11 = (bf16[1024,768]{1,0:T(8,128)(2,1)}, bf16[1024,768]{1,0:T(8,128)(2,1)}, u32[]{:S(2)}, u32[]{:S(2)}) collective-permute-start(bf16[1024,768]{1,0:T(8,128)(2,1)} %collective-permute-done.7.args_13_), channel_id=1, source_target_pairs={{0,1},{1,0},{2,3},{3,2},{4,5},{5,4},{6,7},{7,6},{8,9},{9,8},{10,11... | collective-permute-start | bytes 4718600 | tf_op jit(solution)/shard_map/ppermute | solution.py:19
  241.2 35.6 %copy-start.4 = (bf16[1024,768]{1,0:T(8,128)(2,1)}, bf16[1024,768]{1,0:T(8,128)(2,1)S(1)}, u32[]{:S(2)}) copy-start(bf16[1024,768]{1,0:T(8,128)(2,1)S(1)} %collective-permute-done.8.args_14_) | copy-start | bytes 4718596
  276.8 1.1 copy-start.3

commit v17 on v4

--- a/solution.py
+++ b/solution.py
@@ -102,9 +102,9 @@
     heads_local = H // group_size
     k_heads = lax.all_to_all(key_states, "head", split_axis=1, concat_axis=0, tiled=True)
     k_window = exchange(k_heads.T, 1, cycle_size)
-    v_heads = lax.all_to_all(value_states, "head", split_axis=1, concat_axis=0, tiled=True)
+    v_and_q = jnp.stack((value_states, queries))
+    v_heads, q_heads = lax.all_to_all(v_and_q, "head", split_axis=2, concat_axis=1, tiled=True)
     v_window = exchange(v_heads, 0, cycle_size)
-    q_heads = lax.all_to_all(queries, "head", split_axis=1, concat_axis=0, tiled=True)
     shard_tok = q_heads.shape[0]
     tile_count = shard_tok // TILE
     width = heads_local * DH

time: 323 us -> 321 us (level)
  local copies, waits for them, and re-layouts: 14.9 us -> 27 us
  waiting for transfers between devices: 228 us -> 219 us
  starting transfers between devices: 26.6 us -> 20.7 us
    all_to_all x1, waiting for transfers between devices: 53.7 us -> 13.7 us  [body(): lax.all_to_all(key_states, 'head', split_axis=1, concat_axis=0, tiled=True)]
    ppermute x12, waiting for transfers between devices: 113 us -> 138 us  [permute(): return lax.ppermute(block, axis, route)]
    another operation x0 -> x2, local copies, waits for them, and re-layouts: none -> 9.49 us  [the longest x1 5.54 us: body(): v_and_q = jnp.stack((value_states, queries))]
    all_to_all x2 -> x1, waiting for transfers between devices: 61.4 us -> 67.7 us  [body(): lax.all_to_all(v_and_q, 'head', split_axis=2, concat_axis=1, tiled=True)]
    all_to_all x2 -> x1, starting transfers between devices: 9.83 us -> 3.65 us  [body(): lax.all_to_all(v_and_q, 'head', split_axis=2, concat_axis=1, tiled=True)]
  transfers between devices with their start and end apart: 15 -> 14, of which waited for: 7 -> 6; matrix products, arithmetic and copies ran while one was open for 4% -> 9% of each run, Pallas kernels for 0% -> 0%
where the time goes in v17:
time: 321 us; the launch traced here: 316 us
  waiting for transfers between devices  219 us (68%)
  local copies, waits for them, and re-layouts  27 us (8%)
  Pallas kernels  24.5 us (8%)
  starting transfers between devices  20.7 us (6%)
  blocking collectives  18.7 us (6%)
  other arithmetic  5.58 us (2%)
    ppermute x12, waiting for transfers between devices, permute(): return lax.ppermute(block, axis, route)  138 us
    all_to_all x1, waiting for transfers between devices, body(): lax.all_to_all(v_and_q, 'head', split_axis=2, concat_axis=1, tiled=True)  67.7 us
    pallas_call x1, Pallas kernels, body(): pl.pallas_call(kernel, grid_spec=grid_spec, out_shape=jax.ShapeDtypeStruc...  24.5 us
    all_to_all x1, blocking collectives, body(): return lax.all_to_all(out, 'head', split_axis=0, concat_axis=1, tiled=True)  18.7 us
    all_to_all x1, waiting for transfers between devices, body(): lax.all_to_all(key_states, 'head', split_axis=1, concat_axis=0, tiled=True)  13.7 us
    ppermute x12, starting transfers between devices, permute(): return lax.ppermute(block, axis, route)  12.2 us
  transfers between devices with their start and end apart: 14, of which 6 were waited for; matrix products, arithmetic and copies ran while one was open for 9% of the time, Pallas kernels for 0%

profile of v17, /device:TPU:128, one launch (start us, length us, event | category | flops | bytes accessed | tf_op | source)
XLA Modules:
  0.0 316.1 jit_solution(15357180939247907796)
XLA Ops:
  0.0 2.6 copy.22
  2.6 4.9 %all-to-all-start.1 = ((bf16[128,8,768]{0,2,1:T(8,128)(2,1)}), bf16[128,8,768]{0,2,1:T(8,128)(2,1)}, u32[]{:S(2)}, u32[]{:S(2)}) async-start(bf16[128,8,768]{0,2,1:T(8,128)(2,1)} %bitcast.7), calls=%async_computation.1 | async-start | bytes 3145728 | tf_op jit(solution)/shard_map/all_to_all | solution.py:103
  7.5 2.2 pad_maximum_fusion
  9.7 5.5 %copy.20 = bf16[2,128,6144]{1,0,2:T(2,128)(2,1)} copy(bf16[2,128,6144]{2,1,0:T(8,128)(2,1)S(1)} %pad_maximum_fusion) | data formatting | bytes 6291456 | tf_op jit(solution)/shard_map/stack | solution.py:105
  15.2 13.7 %all-to-all-done.1 = bf16[128,8,768]{0,2,1:T(8,128)(2,1)} async-done(((bf16[128,8,768]{0,2,1:T(8,128)(2,1)}), bf16[128,8,768]{0,2,1:T(8,128)(2,1)}, u32[]{:S(2)}, u32[]{:S(2)}) %all-to-all-start.1) | async-done | bytes 1572896 | tf_op jit(solution)/shard_map/all_to_all | solution.py:103
  29.0 3.6 %all-to-all-start = ((bf16[2,128,6144]{1,0,2:T(2,128)(2,1)}), bf16[2,128,6144]{1,0,2:T(2,128)(2,1)S(1)}, u32[]{:S(2)}, u32[]{:S(2)}) async-start(bf16[2,128,6144]{1,0,2:T(2,128)(2,1)} %copy.20), calls=%async_computation | async-start | bytes 6291456 | tf_op jit(solution)/shard_map/all_to_all | solution.py:106
  32.6 2.8 bitcast_bitcast_fusion.args_4_
  35.4 2.7 collective-permute-start.1
  38.2 67.7 %all-to-all-done = bf16[2,128,6144]{1,0,2:T(2,128)(2,1)S(1)} async-done(((bf16[2,128,6144]{1,0,2:T(2,128)(2,1)}), bf16[2,128,6144]{1,0,2:T(2,128)(2,1)S(1)}, u32[]{:S(2)}, u32[]{:S(2)}) %all-to-all-start) | async-done | bytes 3145760 | tf_op jit(solution)/shard_map/all_to_all | solution.py:106
  105.9 5.7 %copy.21 = bf16[2,128,8,768]{3,1,2,0:T(8,128)(2,1)} copy(bf16[2,128,8,768]{1,0,3,2:T(2,128)(2,1)S(1)} %bitcast.23) | data formatting | bytes 6291456 | tf_op jit(solution)/shard_map/all_to_all | solution.py:106
  111.7 3.9 %fusion.7 = (bf16[1,8,128,768]{3,2,1,0:T(8,128)(2,1)}, bf16[1,8,128,768]{3,2,1,0:T(8,128)(2,1)}) fusion(bf16[2,8,128,768]{3,2,1,0:T(8,128)(2,1)} %bitcast.24), kind=kLoop, calls=%fused_computation.34 | loop fusion | bytes 6291456 | tf_op jit(solution)/shard_map/unstack | solution.py:106
  115.6 2.0 collective-permute-start.6
  118.1 20.6 %collective-permute-done.args_5_ = bf16[768,1024]{1,0:T(8,128)(2,1)} collective-permute-done((bf16[768,1024]{1,0:T(8,128)(2,1)}, bf16[768,1024]{1,0:T(8,128)(2,1)}, u32[]{:S(2)}, u32[]{:S(2)}) %collective-permute-start) | collective-permute-done | bytes 1572896 | tf_op jit(solution)/shard_map/ppermute | solution.py:19
  138.8 1.6 broadcast_select_fusion.1
  140.5 78.3 %collective-permute-done.7.args_13_ = bf16[1024,768]{1,0:T(8,128)(2,1)S(1)} collective-permute-done((bf16[1024,768]{1,0:T(8,128)(2,1)}, bf16[1024,768]{1,0:T(8,128)(2,1)S(1)}, u32[]{:S(2)}, u32[]{:S(2)}) %collective-permute-start.7) | collective-permute-done | bytes 1572896 | tf_op jit(solution)/shard_map/ppermute | solution.py:19
  219.3 1.6 broadcast_select_fusion
  220.9 6.2 %collective-permute-start.9 = (bf16[1024,768]{1,0:T(8,128)(2,1)}, bf16[1024,768]{1,0:T(8,128)(2,1)}, u32[]{:S(2)}, u32[]{:S(2)}) collective-permute-start(bf16[1024,768]{1,0:T(8,128)(2,1)} %broadcast_select_fusion), channel_id=1, source_target_pairs={{0,31},{1,2},{2,1},{3,4},{4,3},{5,6},{6,5},{7,8},{8,7},{9,10},{10,... | collective-permute-start | bytes 4718600 | tf_op jit(solution)/shard_map/ppermute | solution.py:19
  227.2 27.5 %collective-permute-done.3.args_8_ = bf16[768,1024]{1,0:T(8,128)(2,1)S(1)} collective-permute-done((bf16[768,1024]{1,0:T(8,128)(2,1)S(1)}, bf16[768,1024]{1,0:T(8,128)(2,1)S(1)}, u32[]{:S(2)}, u32[]{:S(2)}) %collective-permute-start.3) | collective-permute-done | bytes 1572896 | tf_op jit(solution)/shard_map/ppermute | solution.py:19
  254.7 1.1 copy-done.5
  258.2 0.8 gather_fusion.2
  260.0 11.6 %collective-permute-done.9.args_15_ = bf16[1024,768]{1,0:T(8,128)(2,1)} collective-permute-done((bf16[1024,768]{1,0:T(8,128)(2,1)}, bf16[1024,768]{1,0:T(8,128)(2,1)}, u32[]{:S(2)}, u32[]{:S(2)}) %collective-permute-start.9) | collective-permute-done | bytes 1572896 | tf_op jit(solution)/shard_map/ppermute | solution.py:19
  271.6 24.5 %shard_map.73 = bf16[1024,768]{1,0:T(8,128)(2,1)} custom-call(s32[64]{0:T(128)} %reshape.62.args_0_, s32[8]{0:T(128)} %args_1_.4, f32[384]{0:T(512)} %mul.43.args_2_, bf16[1024,768]{1,0:T(8,128)(2,1)} %bitcast.25, bf16[768,1024]{1,0:T(8,128)(2,1)} %bitcast_bitcast_fusion.args_4_, bf16[768,1024]{1,0:T(8,128)(2,1)} %collective-permute-done.args_5_, ...), custom_call_target="tpu_custom_call" | custom-call | tf_op jit(solution)/shard_map/pallas_call | solution.py:147
  296.1 18.7 %all_to_all.53 = bf16[8,128,768]{2,1,0:T(8,128)(2,1)S(1)} all-to-all(bf16[8,128,768]{2,1,0:T(8,128)(2,1)} %bitcast.26), channel_id=1, replica_groups=mesh['head'=8,'blk'=32] {'head'}, dimensions={0} | all-to-all | bytes 3145728 | tf_op jit(solution)/shard_map/all_to_all | solution.py:160
  314.8 1.3 copy.26
  (51 shorter events, 4.6 us)
Async XLA Ops:
  0.0 257.6 %copy-start = (s32[256]{0:T(256)S(1)}, s32[256]{0:T(256)}, u32[]{:S(2)}) copy-start(s32[256]{0:T(256)} %param.12) | copy-start | bytes 3076
  2.6 26.4 %all-to-all-start.1 = ((bf16[128,8,768]{0,2,1:T(8,128)(2,1)}), bf16[128,8,768]{0,2,1:T(8,128)(2,1)}, u32[]{:S(2)}, u32[]{:S(2)}) async-start(bf16[128,8,768]{0,2,1:T(8,128)(2,1)} %bitcast.7), calls=%async_computation.1 | async-start | bytes 3145728 | tf_op jit(solution)/shard_map/all_to_all | solution.py:103
  29.0 76.9 %all-to-all-start = ((bf16[2,128,6144]{1,0,2:T(2,128)(2,1)}), bf16[2,128,6144]{1,0,2:T(2,128)(2,1)S(1)}, u32[]{:S(2)}, u32[]{:S(2)}) async-start(bf16[2,128,6144]{1,0,2:T(2,128)(2,1)} %copy.20), calls=%async_computation | async-start | bytes 6291456 | tf_op jit(solution)/shard_map/all_to_all | solution.py:106
  35.4 82.2 %collective-permute-start.1 = (bf16[768,1024]{1,0:T(8,128)(2,1)}, bf16[768,1024]{1,0:T(8,128)(2,1)}, u32[]{:S(2)}, u32[]{:S(2)}) collective-permute-start(bf16[768,1024]{1,0:T(8,128)(2,1)} %bitcast_bitcast_fusion.args_4_), channel_id=1, source_target_pairs={{0,30},{1,31},{2,0},{3,1},{4,2},{5,3},{6,4},{7,5},{8,6},{9,7},{10,... | collective-permute-start | bytes 4718600 | tf_op jit(solution)/shard_map/ppermute | solution.py:19
  38.2 100.6 %collective-permute-start = (bf16[768,1024]{1,0:T(8,128)(2,1)}, bf16[768,1024]{1,0:T(8,128)(2,1)}, u32[]{:S(2)}, u32[]{:S(2)}) collective-permute-start(bf16[768,1024]{1,0:T(8,128)(2,1)} %bitcast_bitcast_fusion.args_4_), channel_id=1, source_target_pairs={{0,2},{1,3},{2,4},{3,5},{4,6},{5,7},{6,8},{7,9},{8,10},{9,11},{10,... | collective-permute-start | bytes 4718600 | tf_op jit(solution)/shard_map/ppermute | solution.py:19
  115.6 103.2 %collective-permute-start.7 = (bf16[1024,768]{1,0:T(8,128)(2,1)}, bf16[1024,768]{1,0:T(8,128)(2,1)S(1)}, u32[]{:S(2)}, u32[]{:S(2)}) collective-permute-start(bf16[1024,768]{1,0:T(8,128)(2,1)} %bitcast.10.args_11_), channel_id=1, source_target_pairs={{0,30},{1,31},{2,0},{3,1},{4,2},{5,3},{6,4},{7,5},{8,6},{9,7},{10,... | collective-permute-start | bytes 4718600 | tf_op jit(solution)/shard_map/ppermute | solution.py:19
  115.6 103.2 %collective-permute-start.6 = (bf16[1024,768]{1,0:T(8,128)(2,1)}, bf16[1024,768]{1,0:T(8,128)(2,1)S(1)}, u32[]{:S(2)}, u32[]{:S(2)}) collective-permute-start(bf16[1024,768]{1,0:T(8,128)(2,1)} %bitcast.10.args_11_), channel_id=1, source_target_pairs={{0,2},{1,3},{2,4},{3,5},{4,6},{5,7},{6,8},{7,9},{8,10},{9,11},{10,... | collective-permute-start | bytes 4718600 | tf_op jit(solution)/shard_map/ppermute | solution.py:19
  117.6 103.3 %collective-permute-start.2 = (bf16[768,1024]{1,0:T(8,128)(2,1)}, bf16[768,1024]{1,0:T(8,128)(2,1)S(1)}, u32[]{:S(2)}, u32[]{:S(2)}) collective-permute-start(bf16[768,1024]{1,0:T(8,128)(2,1)} %bitcast_bitcast_fusion.args_4_), channel_id=1, source_target_pairs={{0,1},{1,0},{2,3},{3,2},{4,5},{5,4},{6,7},{7,6},{8,9},{9,8},{10,11... | collective-permute-start | bytes 4718600 | tf_op jit(solution)/shard_map/ppermute | solution.py:19
  117.6 109.5 %collective-permute-start.5 = (bf16[768,1024]{1,0:T(8,128)(2,1)}, bf16[768,1024]{1,0:T(8,128)(2,1)S(1)}, u32[]{:S(2)}, u32[]{:S(2)}) collective-permute-start(bf16[768,1024]{1,0:T(8,128)(2,1)} %collective-permute-done.1.args_6_), channel_id=1, source_target_pairs={{0,1},{1,0},{2,3},{3,2},{4,5},{5,4},{6,7},{7,6},{8,9},{9,8},{10,11... | collective-permute-start | bytes 4718600 | tf_op jit(solution)/shard_map/ppermute | solution.py:19
  140.3 115.5 %copy-start.6 = (s32[8,8]{1,0:T(8,128)S(1)}, s32[8,8]{1,0:T(8,128)}, u32[]{:S(2)}) copy-start(s32[8,8]{1,0:T(8,128)} %param.10) | copy-start | bytes 772
  140.4 115.7 %copy-start.7 = (s32[2,7]{1,0:T(2,128)S(1)}, s32[2,7]{1,0:T(2,128)}, u32[]{:S(2)}) copy-start(s32[2,7]{1,0:T(2,128)} %constant.89.clone) | copy-start | bytes 172
  140.4 114.3 %collective-permute-start.3 = (bf16[768,1024]{1,0:T(8,128)(2,1)S(1)}, bf16[768,1024]{1,0:T(8,128)(2,1)S(1)}, u32[]{:S(2)}, u32[]{:S(2)}) collective-permute-start(bf16[768,1024]{1,0:T(8,128)(2,1)S(1)} %broadcast_select_fusion.1), channel_id=1, source_target_pairs={{0,31},{1,2},{2,1},{3,4},{4,3},{5,6},{6,5},{7,8},{8,7},{9,10},{10,... | collective-permute-start | bytes 4718600 | tf_op jit(solution)/shard_map/ppermute | solution.py:19
  218.8 8.3 %copy-start.1 = (bf16[1024,768]{1,0:T(8,128)(2,1)}, bf16[1024,768]{1,0:T(8,128)(2,1)S(1)}, u32[]{:S(2)}) copy-start(bf16[1024,768]{1,0:T(8,128)(2,1)S(1)} %collective-permute-done.7.args_13_) | copy-start | bytes 4718596
  218.8 41.3 %collective-permute-start.4 = (bf16[768,1024]{1,0:T(8,128)(2,1)}, bf16[768,1024]{1,0:T(8,128)(2,1)}, u32[]{:S(2)}, u32[]{:S(2)}) collective-permute-start(bf16[768,1024]{1,0:T(8,128)(2,1)} %collective-permute-done.args_5_), channel_id=1, source_target_pairs={{0,1},{1,0},{2,3},{3,2},{4,5},{5,4},{6,7},{7,6},{8,9},{9,8},{10,11... | collective-permute-start | bytes 4718600 | tf_op jit(solution)/shard_map/ppermute | solution.py:19
  218.8 35.9 %copy-start.2 = (bf16[1024,768]{1,0:T(8,128)(2,1)}, bf16[1024,768]{1,0:T(8,128)(2,1)S(1)}, u32[]{:S(2)}) copy-start(bf16[1024,768]{1,0:T(8,128)(2,1)S(1)} %collective-permute-done.6.args_12_) | copy-start | bytes 4718596
  218.8 41.3 %collective-permute-start.8 = (bf16[1024,768]{1,0:T(8,128)(2,1)}, bf16[1024,768]{1,0:T(8,128)(2,1)}, u32[]{:S(2)}, u32[]{:S(2)}) collective-permute-start(bf16[1024,768]{1,0:T(8,128)(2,1)} %bitcast.10.args_11_), channel_id=1, source_target_pairs={{0,1},{1,0},{2,3},{3,2},{4,5},{5,4},{6,7},{7,6},{8,9},{9,8},{10,11... | collective-permute-start | bytes 4718600 | tf_op jit(solution)/shard_map/ppermute | solution.py:19
  220.9 33.8 %copy-start.3 = (bf16[768,1024]{1,0:T(8,128)(2,1)}, bf16[768,1024]{1,0:T(8,128)(2,1)S(1)}, u32[]{:S(2)}) copy-start(bf16[768,1024]{1,0:T(8,128)(2,1)S(1)} %collective-permute-done.2.args_7_) | copy-start | bytes 4718596
  220.9 50.7 %collective-permute-start.9 = (bf16[1024,768]{1,0:T(8,128)(2,1)}, bf16[1024,768]{1,0:T(8,128)(2,1)}, u32[]{:S(2)}, u32[]{:S(2)}) collective-permute-start(bf16[1024,768]{1,0:T(8,128)(2,1)} %broadcast_select_fusion), channel_id=1, source_target_pairs={{0,31},{1,2},{2,1},{3,4},{4,3},{5,6},{6,5},{7,8},{8,7},{9,10},{10,... | collective-permute-start | bytes 4718600 | tf_op jit(solution)/shard_map/ppermute | solution.py:19
  227.1 27.6 %copy-start.4 = (bf16[768,1024]{1,0:T(8,128)(2,1)}, bf16[768,1024]{1,0:T(8,128)(2,1)S(1)}, u32[]{:S(2)}) copy-start(bf16[768,1024]{1,0:T(8,128)(2,1)S(1)} %collective-permute-done.5.args_10_) | copy-start | bytes 4718596
  227.1 32.9 %collective-permute-start.11 = (bf16[1024,768]{1,0:T(8,128)(2,1)S(1)}, bf16[1024,768]{1,0:T(8,128)(2,1)}, u32[]{:S(2)}, u32[]{:S(2)}) collective-permute-start(bf16[1024,768]{1,0:T(8,128)(2,1)S(1)} %collective-permute-done.7.args_13_), channel_id=1, source_target_pairs={{0,1},{1,0},{2,3},{3,2},{4,5},{5,4},{6,7},{7,6},{8,9},{9,8},{10,11... | collective-permute-start | bytes 4718600 | tf_op jit(solution)/shard_map/ppermute | solution.py:19
  254.7 1.2 copy-start.5
  254.7 17.0 %collective-permute-start.10 = (bf16[1024,768]{1,0:T(8,128)(2,1)S(1)}, bf16[1024,768]{1,0:T(8,128)(2,1)}, u32[]{:S(2)}, u32[]{:S(2)}) collective-permute-start(bf16[1024,768]{1,0:T(8,128)(2,1)S(1)} %collective-permute-done.6.args_12_), channel_id=1, source_target_pairs={{0,1},{1,0},{2,3},{3,2},{4,5},{5,4},{6,7},{7,6},{8,9},{9,8},{10,11... | collective-permute-start | bytes 4718600 | tf_op jit(solution)/shard_map/ppermute | solution.py:19

commit v18 on v17

--- a/solution.py
+++ b/solution.py
@@ -12,7 +12,7 @@
 SLOTS = 8
 TILE_COUNT = 8
 
-PIECE_OF_OFFSET = ((4, 1, 5, 0, 3, 2, 6), (5, 1, 3, 0, 6, 2, 4))
+PIECE_OF_OFFSET = ((4, 1, 6, 0, 3, 2, 7), (6, 1, 3, 0, 7, 2, 5))
 
 
 def permute(block, axis, route):
@@ -87,13 +87,11 @@
     from_left2 = permute(local, "blk", shift_pairs(n, 2))
     from_right2 = permute(local, "blk", shift_pairs(n, -2))
     other_core = permute(local, "blk", swap)
-    core = lax.axis_index("blk") % 2
-    forward = jnp.where(core == 1, from_left2, from_right2)
-    cross_route = [((i, (i + 1) % n) if i % 2 == 1 else (i, (i - 1) % n)) for i in range(n)]
-    across = permute(forward, "blk", cross_route)
+    odd_ahead = permute(from_left2, "blk", [(i, (i + 1) % n) for i in range(1, n, 2)])
+    even_back = permute(from_right2, "blk", [(i, (i - 1) % n) for i in range(0, n, 2)])
     other_left2 = permute(from_left2, "blk", swap)
     other_right2 = permute(from_right2, "blk", swap)
-    return [local, from_left2, from_right2, other_core, across, other_left2, other_right2]
+    return [local, from_left2, from_right2, other_core, odd_ahead, even_back, other_left2, other_right2]
 
 
 def body(queries, key_states, value_states, block_lists, block_counts, tile_order):

time: 321 us -> 350 us (1.090); the launches traced: 316 us -> 350 us
  blocking collectives: 18.7 us -> 38.8 us
  starting transfers between devices: 20.7 us -> 35.4 us
  waiting for transfers between devices: 219 us -> 223 us
    ppermute x12 -> x14, waiting for transfers between devices: 138 us -> 167 us  [permute(): return lax.ppermute(block, axis, route)]
    all_to_all x1, waiting for transfers between devices: 67.7 us -> 41.7 us  [body(): lax.all_to_all(v_and_q, 'head', split_axis=2, concat_axis=1, tiled=True)]
    all_to_all x1, blocking collectives: 18.7 us -> 38.8 us  [body(): return lax.all_to_all(out, 'head', split_axis=0, concat_axis=1, tiled=True)]
    ppermute x12 -> x14, starting transfers between devices: 12.2 us -> 26.8 us  [permute(): return lax.ppermute(block, axis, route)]
  transfers between devices with their start and end apart: 14 -> 16, of which waited for: 6 -> 8; matrix products, arithmetic and copies ran while one was open for 9% -> 7% of each run, Pallas kernels for 0% -> 0%
where the time goes in v18:
time: 350 us
  waiting for transfers between devices  223 us (64%)
  blocking collectives  38.8 us (11%)
  starting transfers between devices  35.4 us (10%)
  local copies, waits for them, and re-layouts  25.2 us (7%)
  Pallas kernels  25 us (7%)
    ppermute x14, waiting for transfers between devices, permute(): return lax.ppermute(block, axis, route)  167 us
    all_to_all x1, waiting for transfers between devices, body(): lax.all_to_all(v_and_q, 'head', split_axis=2, concat_axis=1, tiled=True)  41.7 us
    all_to_all x1, blocking collectives, body(): return lax.all_to_all(out, 'head', split_axis=0, concat_axis=1, tiled=True)  38.8 us
    ppermute x14, starting transfers between devices, permute(): return lax.ppermute(block, axis, route)  26.8 us
    pallas_call x1, Pallas kernels, body(): pl.pallas_call(kernel, grid_spec=grid_spec, out_shape=jax.ShapeDtypeStruc...  25 us
    all_to_all x1, waiting for transfers between devices, body(): lax.all_to_all(key_states, 'head', split_axis=1, concat_axis=0, tiled=True)  13.7 us
  transfers between devices with their start and end apart: 16, of which 8 were waited for; matrix products, arithmetic and copies ran while one was open for 7% of the time, Pallas kernels for 0%

profile of v18, /device:TPU:128, one launch (start us, length us, event | category | flops | bytes accessed | tf_op | source)
XLA Modules:
  0.0 349.8 jit_solution(10991418857392181685)
XLA Ops:
  0.0 2.6 copy.22
  2.6 4.9 %all-to-all-start.1 = ((bf16[128,8,768]{0,2,1:T(8,128)(2,1)}), bf16[128,8,768]{0,2,1:T(8,128)(2,1)}, u32[]{:S(2)}, u32[]{:S(2)}) async-start(bf16[128,8,768]{0,2,1:T(8,128)(2,1)} %bitcast.7), calls=%async_computation.1 | async-start | bytes 3145728 | tf_op jit(solution)/shard_map/all_to_all | solution.py:101
  7.5 2.2 pad_maximum_fusion
  9.7 5.6 %copy.20 = bf16[2,128,6144]{1,0,2:T(2,128)(2,1)} copy(bf16[2,128,6144]{2,1,0:T(8,128)(2,1)S(1)} %pad_maximum_fusion) | data formatting | bytes 6291456 | tf_op jit(solution)/shard_map/stack | solution.py:103
  15.3 13.7 %all-to-all-done.1 = bf16[128,8,768]{0,2,1:T(8,128)(2,1)} async-done(((bf16[128,8,768]{0,2,1:T(8,128)(2,1)}), bf16[128,8,768]{0,2,1:T(8,128)(2,1)}, u32[]{:S(2)}, u32[]{:S(2)}) %all-to-all-start.1) | async-done | bytes 1572896 | tf_op jit(solution)/shard_map/all_to_all | solution.py:101
  29.0 3.6 %all-to-all-start = ((bf16[2,128,6144]{1,0,2:T(2,128)(2,1)}), bf16[2,128,6144]{1,0,2:T(2,128)(2,1)S(1)}, u32[]{:S(2)}, u32[]{:S(2)}) async-start(bf16[2,128,6144]{1,0,2:T(2,128)(2,1)} %copy.20), calls=%async_computation | async-start | bytes 6291456 | tf_op jit(solution)/shard_map/all_to_all | solution.py:104
  32.6 2.8 bitcast_bitcast_fusion.args_4_
  35.4 2.7 collective-permute-start.1
  38.2 32.9 %collective-permute-done.1.args_6_ = bf16[768,1024]{1,0:T(8,128)(2,1)} collective-permute-done((bf16[768,1024]{1,0:T(8,128)(2,1)}, bf16[768,1024]{1,0:T(8,128)(2,1)}, u32[]{:S(2)}, u32[]{:S(2)}) %collective-permute-start.1) | collective-permute-done | bytes 1572896 | tf_op jit(solution)/shard_map/ppermute | solution.py:19
  71.1 9.9 %collective-permute-start.4 = (bf16[768,1024]{1,0:T(8,128)(2,1)}, bf16[768,1024]{1,0:T(8,128)(2,1)}, u32[]{:S(2)}, u32[]{:S(2)}) collective-permute-start(bf16[768,1024]{1,0:T(8,128)(2,1)} %collective-permute-done.1.args_6_), channel_id=1, source_target_pairs={{0,31},{2,1},{4,3},{6,5},{8,7},{10,9},{12,11},{14,13},{16,15},{18,... | collective-permute-start | bytes 4718600 | tf_op jit(solution)/shard_map/ppermute | solution.py:19
  81.1 41.7 %all-to-all-done = bf16[2,128,6144]{1,0,2:T(2,128)(2,1)S(1)} async-done(((bf16[2,128,6144]{1,0,2:T(2,128)(2,1)}), bf16[2,128,6144]{1,0,2:T(2,128)(2,1)S(1)}, u32[]{:S(2)}, u32[]{:S(2)}) %all-to-all-start) | async-done | bytes 3145760 | tf_op jit(solution)/shard_map/all_to_all | solution.py:104
  122.8 5.7 %copy.21 = bf16[2,128,8,768]{3,1,2,0:T(8,128)(2,1)} copy(bf16[2,128,8,768]{1,0,3,2:T(2,128)(2,1)S(1)} %bitcast.23) | data formatting | bytes 6291456 | tf_op jit(solution)/shard_map/all_to_all | solution.py:104
  128.5 3.3 fusion.7
  131.8 4.8 %collective-permute-done.args_5_ = bf16[768,1024]{1,0:T(8,128)(2,1)} collective-permute-done((bf16[768,1024]{1,0:T(8,128)(2,1)}, bf16[768,1024]{1,0:T(8,128)(2,1)}, u32[]{:S(2)}, u32[]{:S(2)}) %collective-permute-start) | collective-permute-done | bytes 1572896 | tf_op jit(solution)/shard_map/ppermute | solution.py:19
  136.7 1.3 collective-permute-start.3
  138.0 1.6 collective-permute-start.9
  139.6 45.1 %collective-permute-done.8.args_14_ = bf16[1024,768]{1,0:T(8,128)(2,1)S(1)} collective-permute-done((bf16[1024,768]{1,0:T(8,128)(2,1)S(1)}, bf16[1024,768]{1,0:T(8,128)(2,1)S(1)}, u32[]{:S(2)}, u32[]{:S(2)}) %collective-permute-start.8) | collective-permute-done | bytes 1572896 | tf_op jit(solution)/shard_map/ppermute | solution.py:19
  184.7 9.9 %collective-permute-start.11 = (bf16[1024,768]{1,0:T(8,128)(2,1)S(1)}, bf16[1024,768]{1,0:T(8,128)(2,1)}, u32[]{:S(2)}, u32[]{:S(2)}) collective-permute-start(bf16[1024,768]{1,0:T(8,128)(2,1)S(1)} %collective-permute-done.8.args_14_), channel_id=1, source_target_pairs={{0,31},{2,1},{4,3},{6,5},{8,7},{10,9},{12,11},{14,13},{16,15},{18,... | collective-permute-start | bytes 4718600 | tf_op jit(solution)/shard_map/ppermute | solution.py:19
  194.7 15.6 %collective-permute-done.3.args_8_ = bf16[768,1024]{1,0:T(8,128)(2,1)} collective-permute-done((bf16[768,1024]{1,0:T(8,128)(2,1)}, bf16[768,1024]{1,0:T(8,128)(2,1)}, u32[]{:S(2)}, u32[]{:S(2)}) %collective-permute-start.3) | collective-permute-done | bytes 1572896 | tf_op jit(solution)/shard_map/ppermute | solution.py:19
  215.8 37.8 %collective-permute-done.11.args_17_ = bf16[1024,768]{1,0:T(8,128)(2,1)} collective-permute-done((bf16[1024,768]{1,0:T(8,128)(2,1)S(1)}, bf16[1024,768]{1,0:T(8,128)(2,1)}, u32[]{:S(2)}, u32[]{:S(2)}) %collective-permute-start.11) | collective-permute-done | bytes 1572896 | tf_op jit(solution)/shard_map/ppermute | solution.py:19
  253.6 31.1 %collective-permute-done.10.args_16_ = bf16[1024,768]{1,0:T(8,128)(2,1)} collective-permute-done((bf16[1024,768]{1,0:T(8,128)(2,1)}, bf16[1024,768]{1,0:T(8,128)(2,1)}, u32[]{:S(2)}, u32[]{:S(2)}) %collective-permute-start.10) | collective-permute-done | bytes 1572896 | tf_op jit(solution)/shard_map/ppermute | solution.py:19
  284.7 25.0 %shard_map.73 = bf16[1024,768]{1,0:T(8,128)(2,1)} custom-call(s32[64]{0:T(128)} %reshape.62.args_0_, s32[8]{0:T(128)} %args_1_.4, f32[384]{0:T(512)} %mul.43.args_2_, bf16[1024,768]{1,0:T(8,128)(2,1)} %bitcast.29, bf16[768,1024]{1,0:T(8,128)(2,1)} %bitcast_bitcast_fusion.args_4_, bf16[768,1024]{1,0:T(8,128)(2,1)} %collective-permute-done.args_5_, ...), custom_call_target="tpu_custom_call" | custom-call | tf_op jit(solution)/shard_map/pallas_call | solution.py:145
  309.7 38.8 %all_to_all.53 = bf16[8,128,768]{2,1,0:T(8,128)(2,1)S(1)} all-to-all(bf16[8,128,768]{2,1,0:T(8,128)(2,1)} %bitcast.30), channel_id=1, replica_groups=mesh['head'=8,'blk'=32] {'head'}, dimensions={0} | all-to-all | bytes 3145728 | tf_op jit(solution)/shard_map/all_to_all | solution.py:158
  348.5 1.3 copy.26
  (47 shorter events, 5.4 us)
Async XLA Ops:
  0.0 213.3 %copy-start = (s32[256]{0:T(256)S(1)}, s32[256]{0:T(256)}, u32[]{:S(2)}) copy-start(s32[256]{0:T(256)} %param.12) | copy-start | bytes 3076
  2.6 26.4 %all-to-all-start.1 = ((bf16[128,8,768]{0,2,1:T(8,128)(2,1)}), bf16[128,8,768]{0,2,1:T(8,128)(2,1)}, u32[]{:S(2)}, u32[]{:S(2)}) async-start(bf16[128,8,768]{0,2,1:T(8,128)(2,1)} %bitcast.7), calls=%async_computation.1 | async-start | bytes 3145728 | tf_op jit(solution)/shard_map/all_to_all | solution.py:101
  29.0 93.8 %all-to-all-start = ((bf16[2,128,6144]{1,0,2:T(2,128)(2,1)}), bf16[2,128,6144]{1,0,2:T(2,128)(2,1)S(1)}, u32[]{:S(2)}, u32[]{:S(2)}) async-start(bf16[2,128,6144]{1,0,2:T(2,128)(2,1)} %copy.20), calls=%async_computation | async-start | bytes 6291456 | tf_op jit(solution)/shard_map/all_to_all | solution.py:104
  35.4 35.7 %collective-permute-start.1 = (bf16[768,1024]{1,0:T(8,128)(2,1)}, bf16[768,1024]{1,0:T(8,128)(2,1)}, u32[]{:S(2)}, u32[]{:S(2)}) collective-permute-start(bf16[768,1024]{1,0:T(8,128)(2,1)} %bitcast_bitcast_fusion.args_4_), channel_id=1, source_target_pairs={{0,30},{1,31},{2,0},{3,1},{4,2},{5,3},{6,4},{7,5},{8,6},{9,7},{10,... | collective-permute-start | bytes 4718600 | tf_op jit(solution)/shard_map/ppermute | solution.py:19
  38.2 98.5 %collective-permute-start = (bf16[768,1024]{1,0:T(8,128)(2,1)}, bf16[768,1024]{1,0:T(8,128)(2,1)}, u32[]{:S(2)}, u32[]{:S(2)}) collective-permute-start(bf16[768,1024]{1,0:T(8,128)(2,1)} %bitcast_bitcast_fusion.args_4_), channel_id=1, source_target_pairs={{0,2},{1,3},{2,4},{3,5},{4,6},{5,7},{6,8},{7,9},{8,10},{9,11},{10,... | collective-permute-start | bytes 4718600 | tf_op jit(solution)/shard_map/ppermute | solution.py:19
  38.2 98.5 %collective-permute-start.2 = (bf16[768,1024]{1,0:T(8,128)(2,1)}, bf16[768,1024]{1,0:T(8,128)(2,1)}, u32[]{:S(2)}, u32[]{:S(2)}) collective-permute-start(bf16[768,1024]{1,0:T(8,128)(2,1)} %bitcast_bitcast_fusion.args_4_), channel_id=1, source_target_pairs={{0,1},{1,0},{2,3},{3,2},{4,5},{5,4},{6,7},{7,6},{8,9},{9,8},{10,11... | collective-permute-start | bytes 4718600 | tf_op jit(solution)/shard_map/ppermute | solution.py:19
  71.1 65.5 %collective-permute-start.6 = (bf16[768,1024]{1,0:T(8,128)(2,1)}, bf16[768,1024]{1,0:T(8,128)(2,1)}, u32[]{:S(2)}, u32[]{:S(2)}) collective-permute-start(bf16[768,1024]{1,0:T(8,128)(2,1)} %collective-permute-done.1.args_6_), channel_id=1, source_target_pairs={{0,1},{1,0},{2,3},{3,2},{4,5},{5,4},{6,7},{7,6},{8,9},{9,8},{10,11... | collective-permute-start | bytes 4718600 | tf_op jit(solution)/shard_map/ppermute | solution.py:19
  71.1 66.8 %collective-permute-start.4 = (bf16[768,1024]{1,0:T(8,128)(2,1)}, bf16[768,1024]{1,0:T(8,128)(2,1)}, u32[]{:S(2)}, u32[]{:S(2)}) collective-permute-start(bf16[768,1024]{1,0:T(8,128)(2,1)} %collective-permute-done.1.args_6_), channel_id=1, source_target_pairs={{0,31},{2,1},{4,3},{6,5},{8,7},{10,9},{12,11},{14,13},{16,15},{18,... | collective-permute-start | bytes 4718600 | tf_op jit(solution)/shard_map/ppermute | solution.py:19
  128.5 83.1 %copy-start.3 = (s32[8,8]{1,0:T(8,128)S(1)}, s32[8,8]{1,0:T(8,128)}, u32[]{:S(2)}) copy-start(s32[8,8]{1,0:T(8,128)} %param.10) | copy-start | bytes 772
  128.5 83.3 %copy-start.4 = (s32[2,7]{1,0:T(2,128)S(1)}, s32[2,7]{1,0:T(2,128)}, u32[]{:S(2)}) copy-start(s32[2,7]{1,0:T(2,128)} %constant.84.clone) | copy-start | bytes 172
  131.8 80.8 %copy-start.1 = (bf16[1,8,128,768]{3,2,1,0:T(8,128)(2,1)}, bf16[1,8,128,768]{3,2,1,0:T(8,128)(2,1)S(1)}, u32[]{:S(2)}) copy-start(bf16[1,8,128,768]{3,2,1,0:T(8,128)(2,1)S(1)} %get-tuple-element.5) | copy-start | bytes 4718596
  131.8 52.9 %collective-permute-start.8 = (bf16[1024,768]{1,0:T(8,128)(2,1)S(1)}, bf16[1024,768]{1,0:T(8,128)(2,1)S(1)}, u32[]{:S(2)}, u32[]{:S(2)}) collective-permute-start(bf16[1024,768]{1,0:T(8,128)(2,1)S(1)} %bitcast.25), channel_id=1, source_target_pairs={{0,30},{1,31},{2,0},{3,1},{4,2},{5,3},{6,4},{7,5},{8,6},{9,7},{10,... | collective-permute-start | bytes 4718600 | tf_op jit(solution)/shard_map/ppermute | solution.py:19
  136.6 48.1 %collective-permute-start.5 = (bf16[768,1024]{1,0:T(8,128)(2,1)}, bf16[768,1024]{1,0:T(8,128)(2,1)}, u32[]{:S(2)}, u32[]{:S(2)}) collective-permute-start(bf16[768,1024]{1,0:T(8,128)(2,1)} %collective-permute-done.args_5_), channel_id=1, source_target_pairs={{0,1},{1,0},{2,3},{3,2},{4,5},{5,4},{6,7},{7,6},{8,9},{9,8},{10,11... | collective-permute-start | bytes 4718600 | tf_op jit(solution)/shard_map/ppermute | solution.py:19
  136.7 58.0 %collective-permute-start.7 = (bf16[1024,768]{1,0:T(8,128)(2,1)S(1)}, bf16[1024,768]{1,0:T(8,128)(2,1)}, u32[]{:S(2)}, u32[]{:S(2)}) collective-permute-start(bf16[1024,768]{1,0:T(8,128)(2,1)S(1)} %bitcast.26), channel_id=1, source_target_pairs={{0,2},{1,3},{2,4},{3,5},{4,6},{5,7},{6,8},{7,9},{8,10},{9,11},{10,... | collective-permute-start | bytes 4718600 | tf_op jit(solution)/shard_map/ppermute | solution.py:19
  136.7 73.6 %collective-permute-start.3 = (bf16[768,1024]{1,0:T(8,128)(2,1)}, bf16[768,1024]{1,0:T(8,128)(2,1)}, u32[]{:S(2)}, u32[]{:S(2)}) collective-permute-start(bf16[768,1024]{1,0:T(8,128)(2,1)} %collective-permute-done.args_5_), channel_id=1, source_target_pairs={{1,2},{3,4},{5,6},{7,8},{9,10},{11,12},{13,14},{15,16},{17,18},{19... | collective-permute-start | bytes 4718600 | tf_op jit(solution)/shard_map/ppermute | solution.py:19
  138.0 77.8 %collective-permute-start.9 = (bf16[1024,768]{1,0:T(8,128)(2,1)S(1)}, bf16[1024,768]{1,0:T(8,128)(2,1)}, u32[]{:S(2)}, u32[]{:S(2)}) collective-permute-start(bf16[1024,768]{1,0:T(8,128)(2,1)S(1)} %bitcast.27), channel_id=1, source_target_pairs={{0,1},{1,0},{2,3},{3,2},{4,5},{5,4},{6,7},{7,6},{8,9},{9,8},{10,11... | collective-permute-start | bytes 4718600 | tf_op jit(solution)/shard_map/ppermute | solution.py:19
  184.7 27.9 %copy-start.2 = (bf16[1024,768]{1,0:T(8,128)(2,1)}, bf16[1024,768]{1,0:T(8,128)(2,1)S(1)}, u32[]{:S(2)}) copy-start(bf16[1024,768]{1,0:T(8,128)(2,1)S(1)} %collective-permute-done.8.args_14_) | copy-start | bytes 4718596
  184.7 31.1 %collective-permute-start.13 = (bf16[1024,768]{1,0:T(8,128)(2,1)S(1)}, bf16[1024,768]{1,0:T(8,128)(2,1)}, u32[]{:S(2)}, u32[]{:S(2)}) collective-permute-start(bf16[1024,768]{1,0:T(8,128)(2,1)S(1)} %collective-permute-done.8.args_14_), channel_id=1, source_target_pairs={{0,1},{1,0},{2,3},{3,2},{4,5},{5,4},{6,7},{7,6},{8,9},{9,8},{10,11... | collective-permute-start | bytes 4718600 | tf_op jit(solution)/shard_map/ppermute | solution.py:19
  184.7 68.9 %collective-permute-start.11 = (bf16[1024,768]{1,0:T(8,128)(2,1)S(1)}, bf16[1024,768]{1,0:T(8,128)(2,1)}, u32[]{:S(2)}, u32[]{:S(2)}) collective-permute-start(bf16[1024,768]{1,0:T(8,128)(2,1)S(1)} %collective-permute-done.8.args_14_), channel_id=1, source_target_pairs={{0,31},{2,1},{4,3},{6,5},{8,7},{10,9},{12,11},{14,13},{16,15},{18,... | collective-permute-start | bytes 4718600 | tf_op jit(solution)/shard_map/ppermute | solution.py:19
  194.7 59.0 %collective-permute-start.12 = (bf16[1024,768]{1,0:T(8,128)(2,1)}, bf16[1024,768]{1,0:T(8,128)(2,1)}, u32[]{:S(2)}, u32[]{:S(2)}) collective-permute-start(bf16[1024,768]{1,0:T(8,128)(2,1)} %collective-permute-done.7.args_13_), channel_id=1, source_target_pairs={{0,1},{1,0},{2,3},{3,2},{4,5},{5,4},{6,7},{7,6},{8,9},{9,8},{10,11... | collective-permute-start | bytes 4718600 | tf_op jit(solution)/shard_map/ppermute | solution.py:19
  210.3 74.4 %collective-permute-start.10 = (bf16[1024,768]{1,0:T(8,128)(2,1)}, bf16[1024,768]{1,0:T(8,128)(2,1)}, u32[]{:S(2)}, u32[]{:S(2)}) collective-permute-start(bf16[1024,768]{1,0:T(8,128)(2,1)} %collective-permute-done.7.args_13_), channel_id=1, source_target_pairs={{1,2},{3,4},{5,6},{7,8},{9,10},{11,12},{13,14},{15,16},{17,18},{19... | collective-permute-start | bytes 4718600 | tf_op jit(solution)/shard_map/ppermute | solution.py:19

commit v19 on v17

--- a/solution.py
+++ b/solution.py
@@ -101,8 +101,9 @@
     group_size = lax.axis_size("head")
     heads_local = H // group_size
     k_heads = lax.all_to_all(key_states, "head", split_axis=1, concat_axis=0, tiled=True)
+    k_heads, value_states, queries = lax.optimization_barrier((k_heads, value_states, queries))
+    v_and_q = jnp.stack((value_states, queries))
     k_window = exchange(k_heads.T, 1, cycle_size)
-    v_and_q = jnp.stack((value_states, queries))
     v_heads, q_heads = lax.all_to_all(v_and_q, "head", split_axis=2, concat_axis=1, tiled=True)
     v_window = exchange(v_heads, 0, cycle_size)
     shard_tok = q_heads.shape[0]

time: 321 us -> 329 us (1.025)
  blocking collectives: 18.7 us -> 44.9 us
  waiting for transfers between devices: 219 us -> 208 us
  starting transfers between devices: 20.7 us -> 15.9 us
    all_to_all x0 -> x1, blocking collectives: none -> 26.3 us  [body(): lax.all_to_all(key_states, 'head', split_axis=1, concat_axis=0, tiled=True)]
    all_to_all x1 -> x0, waiting for transfers between devices: 13.7 us -> none  [body(): lax.all_to_all(key_states, 'head', split_axis=1, concat_axis=0, tiled=True)]
    all_to_all x1 -> x0, starting transfers between devices: 4.93 us -> none  [body(): lax.all_to_all(key_states, 'head', split_axis=1, concat_axis=0, tiled=True)]
  transfers between devices with their start and end apart: 14 -> 13, of which waited for: 6 -> 5; matrix products, arithmetic and copies ran while one was open for 9% -> 5% of each run, Pallas kernels for 0% -> 0%
where the time goes in v19:
time: 329 us; the launch traced here: 323 us
  waiting for transfers between devices  208 us (63%)
  blocking collectives  44.9 us (14%)
  local copies, waits for them, and re-layouts  26 us (8%)
  Pallas kernels  24.5 us (7%)
  starting transfers between devices  15.9 us (5%)
  other arithmetic  3.7 us (1%)
    ppermute x12, waiting for transfers between devices, permute(): return lax.ppermute(block, axis, route)  138 us
    all_to_all x1, waiting for transfers between devices, body(): lax.all_to_all(v_and_q, 'head', split_axis=2, concat_axis=1, tiled=True)  70.5 us
    all_to_all x1, blocking collectives, body(): lax.all_to_all(key_states, 'head', split_axis=1, concat_axis=0, tiled=True)  26.3 us
    pallas_call x1, Pallas kernels, body(): pl.pallas_call(kernel, grid_spec=grid_spec, out_shape=jax.ShapeDtypeStruc...  24.5 us
    all_to_all x1, blocking collectives, body(): return lax.all_to_all(out, 'head', split_axis=0, concat_axis=1, tiled=True)  18.7 us
    ppermute x12, starting transfers between devices, permute(): return lax.ppermute(block, axis, route)  12.3 us
  transfers between devices with their start and end apart: 13, of which 5 were waited for; matrix products, arithmetic and copies ran while one was open for 5% of the time, Pallas kernels for 0%

profile of v19, /device:TPU:128, one launch (start us, length us, event | category | flops | bytes accessed | tf_op | source)
XLA Modules:
  0.0 323.4 jit_solution(17244457402376433318)
XLA Ops:
  0.0 1.9 copy.20
  1.9 26.3 %all_to_all.53 = bf16[128,8,768]{0,2,1:T(8,128)(2,1)S(1)} all-to-all(bf16[128,8,768]{0,2,1:T(8,128)(2,1)S(1)} %bitcast.31), channel_id=1, replica_groups=mesh['head'=8,'blk'=32] {'head'}, dimensions={1} | all-to-all | bytes 3145728 | tf_op jit(solution)/shard_map/all_to_all | solution.py:103
  28.2 1.4 copy_bitcast_fusion
  30.9 5.5 %copy.22 = bf16[2,128,6144]{1,0,2:T(2,128)(2,1)} copy(bf16[2,128,6144]{2,1,0:T(8,128)(2,1)S(1)} %pad_maximum_fusion) | data formatting | bytes 6291456 | tf_op jit(solution)/shard_map/stack | solution.py:105
  36.5 3.6 %all-to-all-start.1 = ((bf16[2,128,6144]{1,0,2:T(2,128)(2,1)}), bf16[2,128,6144]{1,0,2:T(2,128)(2,1)S(1)}, u32[]{:S(2)}, u32[]{:S(2)}) async-start(bf16[2,128,6144]{1,0,2:T(2,128)(2,1)} %copy.22), calls=%async_computation.1 | async-start | bytes 6291456 | tf_op jit(solution)/shard_map/all_to_all | solution.py:107
  40.1 2.8 collective-permute-start.1
  43.0 70.5 %all-to-all-done.1 = bf16[2,128,6144]{1,0,2:T(2,128)(2,1)S(1)} async-done(((bf16[2,128,6144]{1,0,2:T(2,128)(2,1)}), bf16[2,128,6144]{1,0,2:T(2,128)(2,1)S(1)}, u32[]{:S(2)}, u32[]{:S(2)}) %all-to-all-start.1) | async-done | bytes 3145760 | tf_op jit(solution)/shard_map/all_to_all | solution.py:107
  113.4 5.7 %copy.23 = bf16[2,128,8,768]{3,1,2,0:T(8,128)(2,1)} copy(bf16[2,128,8,768]{1,0,3,2:T(2,128)(2,1)S(1)} %bitcast.22) | data formatting | bytes 6291456 | tf_op jit(solution)/shard_map/all_to_all | solution.py:107
  119.1 3.9 %fusion.7 = (bf16[1,8,128,768]{3,2,1,0:T(8,128)(2,1)}, bf16[1,8,128,768]{3,2,1,0:T(8,128)(2,1)}) fusion(bf16[2,8,128,768]{3,2,1,0:T(8,128)(2,1)} %bitcast.23), kind=kLoop, calls=%fused_computation.34 | loop fusion | bytes 6291456 | tf_op jit(solution)/shard_map/unstack | solution.py:107
  123.1 2.0 collective-permute-start.6
  125.6 20.6 %collective-permute-done.args_5_ = bf16[768,1024]{1,0:T(8,128)(2,1)} collective-permute-done((bf16[768,1024]{1,0:T(8,128)(2,1)}, bf16[768,1024]{1,0:T(8,128)(2,1)}, u32[]{:S(2)}, u32[]{:S(2)}) %collective-permute-start) | collective-permute-done | bytes 1572896 | tf_op jit(solution)/shard_map/ppermute | solution.py:19
  146.2 1.6 broadcast_select_fusion.1
  147.9 78.1 %collective-permute-done.7.args_13_ = bf16[1024,768]{1,0:T(8,128)(2,1)S(1)} collective-permute-done((bf16[1024,768]{1,0:T(8,128)(2,1)}, bf16[1024,768]{1,0:T(8,128)(2,1)S(1)}, u32[]{:S(2)}, u32[]{:S(2)}) %collective-permute-start.7) | collective-permute-done | bytes 1572896 | tf_op jit(solution)/shard_map/ppermute | solution.py:19
  226.6 1.6 broadcast_select_fusion
  228.2 6.2 %collective-permute-start.9 = (bf16[1024,768]{1,0:T(8,128)(2,1)}, bf16[1024,768]{1,0:T(8,128)(2,1)}, u32[]{:S(2)}, u32[]{:S(2)}) collective-permute-start(bf16[1024,768]{1,0:T(8,128)(2,1)} %broadcast_select_fusion), channel_id=1, source_target_pairs={{0,31},{1,2},{2,1},{3,4},{4,3},{5,6},{6,5},{7,8},{8,7},{9,10},{10,... | collective-permute-start | bytes 4718600 | tf_op jit(solution)/shard_map/ppermute | solution.py:19
  234.5 27.5 %collective-permute-done.3.args_8_ = bf16[768,1024]{1,0:T(8,128)(2,1)S(1)} collective-permute-done((bf16[768,1024]{1,0:T(8,128)(2,1)S(1)}, bf16[768,1024]{1,0:T(8,128)(2,1)S(1)}, u32[]{:S(2)}, u32[]{:S(2)}) %collective-permute-start.3) | collective-permute-done | bytes 1572896 | tf_op jit(solution)/shard_map/ppermute | solution.py:19
  262.0 1.1 copy-done.5
  263.3 0.8 gather_fusion
  265.5 0.8 gather_fusion.2
  266.6 0.7 mul.43.args_2_
  267.3 11.6 %collective-permute-done.9.args_15_ = bf16[1024,768]{1,0:T(8,128)(2,1)} collective-permute-done((bf16[1024,768]{1,0:T(8,128)(2,1)}, bf16[1024,768]{1,0:T(8,128)(2,1)}, u32[]{:S(2)}, u32[]{:S(2)}) %collective-permute-start.9) | collective-permute-done | bytes 1572896 | tf_op jit(solution)/shard_map/ppermute | solution.py:19
  278.9 24.5 %shard_map.73 = bf16[1024,768]{1,0:T(8,128)(2,1)} custom-call(s32[64]{0:T(128)} %reshape.62.args_0_, s32[8]{0:T(128)} %args_1_.4, f32[384]{0:T(512)} %mul.43.args_2_, bf16[1024,768]{1,0:T(8,128)(2,1)} %bitcast.28, bf16[768,1024]{1,0:T(8,128)(2,1)} %bitcast.27, bf16[768,1024]{1,0:T(8,128)(2,1)} %collective-permute-done.args_5_, ...), custom_call_target="tpu_custom_call" | custom-call | tf_op jit(solution)/shard_map/pallas_call | solution.py:148
  303.4 18.7 %all_to_all.54 = bf16[8,128,768]{2,1,0:T(8,128)(2,1)S(1)} all-to-all(bf16[8,128,768]{2,1,0:T(8,128)(2,1)} %bitcast.29), channel_id=1, replica_groups=mesh['head'=8,'blk'=32] {'head'}, dimensions={0} | all-to-all | bytes 3145728 | tf_op jit(solution)/shard_map/all_to_all | solution.py:161
  322.0 1.3 copy.26
  (54 shorter events, 4.4 us)
Async XLA Ops:
  0.0 264.9 %copy-start = (s32[256]{0:T(256)S(1)}, s32[256]{0:T(256)}, u32[]{:S(2)}) copy-start(s32[256]{0:T(256)} %param.12) | copy-start | bytes 3076
  28.2 2.0 copy-start.6
  28.2 2.4 copy-start.7
  36.5 76.9 %all-to-all-start.1 = ((bf16[2,128,6144]{1,0,2:T(2,128)(2,1)}), bf16[2,128,6144]{1,0,2:T(2,128)(2,1)S(1)}, u32[]{:S(2)}, u32[]{:S(2)}) async-start(bf16[2,128,6144]{1,0,2:T(2,128)(2,1)} %copy.22), calls=%async_computation.1 | async-start | bytes 6291456 | tf_op jit(solution)/shard_map/all_to_all | solution.py:107
  40.1 85.0 %collective-permute-start.1 = (bf16[768,1024]{1,0:T(8,128)(2,1)}, bf16[768,1024]{1,0:T(8,128)(2,1)}, u32[]{:S(2)}, u32[]{:S(2)}) collective-permute-start(bf16[768,1024]{1,0:T(8,128)(2,1)} %bitcast.24), channel_id=1, source_target_pairs={{0,30},{1,31},{2,0},{3,1},{4,2},{5,3},{6,4},{7,5},{8,6},{9,7},{10,... | collective-permute-start | bytes 4718600 | tf_op jit(solution)/shard_map/ppermute | solution.py:19
  43.0 103.2 %collective-permute-start = (bf16[768,1024]{1,0:T(8,128)(2,1)}, bf16[768,1024]{1,0:T(8,128)(2,1)}, u32[]{:S(2)}, u32[]{:S(2)}) collective-permute-start(bf16[768,1024]{1,0:T(8,128)(2,1)} %bitcast.25), channel_id=1, source_target_pairs={{0,2},{1,3},{2,4},{3,5},{4,6},{5,7},{6,8},{7,9},{8,10},{9,11},{10,... | collective-permute-start | bytes 4718600 | tf_op jit(solution)/shard_map/ppermute | solution.py:19
  123.1 102.9 %collective-permute-start.7 = (bf16[1024,768]{1,0:T(8,128)(2,1)}, bf16[1024,768]{1,0:T(8,128)(2,1)S(1)}, u32[]{:S(2)}, u32[]{:S(2)}) collective-permute-start(bf16[1024,768]{1,0:T(8,128)(2,1)} %bitcast.10.args_11_), channel_id=1, source_target_pairs={{0,30},{1,31},{2,0},{3,1},{4,2},{5,3},{6,4},{7,5},{8,6},{9,7},{10,... | collective-permute-start | bytes 4718600 | tf_op jit(solution)/shard_map/ppermute | solution.py:19
  123.1 103.0 %collective-permute-start.6 = (bf16[1024,768]{1,0:T(8,128)(2,1)}, bf16[1024,768]{1,0:T(8,128)(2,1)S(1)}, u32[]{:S(2)}, u32[]{:S(2)}) collective-permute-start(bf16[1024,768]{1,0:T(8,128)(2,1)} %bitcast.10.args_11_), channel_id=1, source_target_pairs={{0,2},{1,3},{2,4},{3,5},{4,6},{5,7},{6,8},{7,9},{8,10},{9,11},{10,... | collective-permute-start | bytes 4718600 | tf_op jit(solution)/shard_map/ppermute | solution.py:19
  125.1 103.1 %collective-permute-start.2 = (bf16[768,1024]{1,0:T(8,128)(2,1)}, bf16[768,1024]{1,0:T(8,128)(2,1)S(1)}, u32[]{:S(2)}, u32[]{:S(2)}) collective-permute-start(bf16[768,1024]{1,0:T(8,128)(2,1)} %bitcast.26), channel_id=1, source_target_pairs={{0,1},{1,0},{2,3},{3,2},{4,5},{5,4},{6,7},{7,6},{8,9},{9,8},{10,11... | collective-permute-start | bytes 4718600 | tf_op jit(solution)/shard_map/ppermute | solution.py:19
  125.1 109.3 %collective-permute-start.5 = (bf16[768,1024]{1,0:T(8,128)(2,1)}, bf16[768,1024]{1,0:T(8,128)(2,1)S(1)}, u32[]{:S(2)}, u32[]{:S(2)}) collective-permute-start(bf16[768,1024]{1,0:T(8,128)(2,1)} %collective-permute-done.1.args_6_), channel_id=1, source_target_pairs={{0,1},{1,0},{2,3},{3,2},{4,5},{5,4},{6,7},{7,6},{8,9},{9,8},{10,11... | collective-permute-start | bytes 4718600 | tf_op jit(solution)/shard_map/ppermute | solution.py:19
  147.8 115.3 %copy-start.8 = (s32[8,8]{1,0:T(8,128)S(1)}, s32[8,8]{1,0:T(8,128)}, u32[]{:S(2)}) copy-start(s32[8,8]{1,0:T(8,128)} %param.10) | copy-start | bytes 772
  147.8 115.5 %copy-start.9 = (s32[2,7]{1,0:T(2,128)S(1)}, s32[2,7]{1,0:T(2,128)}, u32[]{:S(2)}) copy-start(s32[2,7]{1,0:T(2,128)} %constant.89.clone) | copy-start | bytes 172
  147.8 114.1 %collective-permute-start.3 = (bf16[768,1024]{1,0:T(8,128)(2,1)S(1)}, bf16[768,1024]{1,0:T(8,128)(2,1)S(1)}, u32[]{:S(2)}, u32[]{:S(2)}) collective-permute-start(bf16[768,1024]{1,0:T(8,128)(2,1)S(1)} %broadcast_select_fusion.1), channel_id=1, source_target_pairs={{0,31},{1,2},{2,1},{3,4},{4,3},{5,6},{6,5},{7,8},{8,7},{9,10},{10,... | collective-permute-start | bytes 4718600 | tf_op jit(solution)/shard_map/ppermute | solution.py:19
  226.0 8.3 %copy-start.1 = (bf16[1024,768]{1,0:T(8,128)(2,1)}, bf16[1024,768]{1,0:T(8,128)(2,1)S(1)}, u32[]{:S(2)}) copy-start(bf16[1024,768]{1,0:T(8,128)(2,1)S(1)} %collective-permute-done.7.args_13_) | copy-start | bytes 4718596
  226.0 41.3 %collective-permute-start.4 = (bf16[768,1024]{1,0:T(8,128)(2,1)}, bf16[768,1024]{1,0:T(8,128)(2,1)}, u32[]{:S(2)}, u32[]{:S(2)}) collective-permute-start(bf16[768,1024]{1,0:T(8,128)(2,1)} %collective-permute-done.args_5_), channel_id=1, source_target_pairs={{0,1},{1,0},{2,3},{3,2},{4,5},{5,4},{6,7},{7,6},{8,9},{9,8},{10,11... | collective-permute-start | bytes 4718600 | tf_op jit(solution)/shard_map/ppermute | solution.py:19
  226.0 35.9 %copy-start.2 = (bf16[1024,768]{1,0:T(8,128)(2,1)}, bf16[1024,768]{1,0:T(8,128)(2,1)S(1)}, u32[]{:S(2)}) copy-start(bf16[1024,768]{1,0:T(8,128)(2,1)S(1)} %collective-permute-done.6.args_12_) | copy-start | bytes 4718596
  226.1 41.3 %collective-permute-start.8 = (bf16[1024,768]{1,0:T(8,128)(2,1)}, bf16[1024,768]{1,0:T(8,128)(2,1)}, u32[]{:S(2)}, u32[]{:S(2)}) collective-permute-start(bf16[1024,768]{1,0:T(8,128)(2,1)} %bitcast.10.args_11_), channel_id=1, source_target_pairs={{0,1},{1,0},{2,3},{3,2},{4,5},{5,4},{6,7},{7,6},{8,9},{9,8},{10,11... | collective-permute-start | bytes 4718600 | tf_op jit(solution)/shard_map/ppermute | solution.py:19
  228.2 33.8 %copy-start.3 = (bf16[768,1024]{1,0:T(8,128)(2,1)}, bf16[768,1024]{1,0:T(8,128)(2,1)S(1)}, u32[]{:S(2)}) copy-start(bf16[768,1024]{1,0:T(8,128)(2,1)S(1)} %collective-permute-done.2.args_7_) | copy-start | bytes 4718596
  228.2 50.7 %collective-permute-start.9 = (bf16[1024,768]{1,0:T(8,128)(2,1)}, bf16[1024,768]{1,0:T(8,128)(2,1)}, u32[]{:S(2)}, u32[]{:S(2)}) collective-permute-start(bf16[1024,768]{1,0:T(8,128)(2,1)} %broadcast_select_fusion), channel_id=1, source_target_pairs={{0,31},{1,2},{2,1},{3,4},{4,3},{5,6},{6,5},{7,8},{8,7},{9,10},{10,... | collective-permute-start | bytes 4718600 | tf_op jit(solution)/shard_map/ppermute | solution.py:19
  234.4 27.6 %copy-start.4 = (bf16[768,1024]{1,0:T(8,128)(2,1)}, bf16[768,1024]{1,0:T(8,128)(2,1)S(1)}, u32[]{:S(2)}) copy-start(bf16[768,1024]{1,0:T(8,128)(2,1)S(1)} %collective-permute-done.5.args_10_) | copy-start | bytes 4718596
  234.4 32.9 %collective-permute-start.11 = (bf16[1024,768]{1,0:T(8,128)(2,1)S(1)}, bf16[1024,768]{1,0:T(8,128)(2,1)}, u32[]{:S(2)}, u32[]{:S(2)}) collective-permute-start(bf16[1024,768]{1,0:T(8,128)(2,1)S(1)} %collective-permute-done.7.args_13_), channel_id=1, source_target_pairs={{0,1},{1,0},{2,3},{3,2},{4,5},{5,4},{6,7},{7,6},{8,9},{9,8},{10,11... | collective-permute-start | bytes 4718600 | tf_op jit(solution)/shard_map/ppermute | solution.py:19
  262.0 1.2 copy-start.5
  262.0 17.0 %collective-permute-start.10 = (bf16[1024,768]{1,0:T(8,128)(2,1)S(1)}, bf16[1024,768]{1,0:T(8,128)(2,1)}, u32[]{:S(2)}, u32[]{:S(2)}) collective-permute-start(bf16[1024,768]{1,0:T(8,128)(2,1)S(1)} %collective-permute-done.6.args_12_), channel_id=1, source_target_pairs={{0,1},{1,0},{2,3},{3,2},{4,5},{5,4},{6,7},{7,6},{8,9},{9,8},{10,11... | collective-permute-start | bytes 4718600 | tf_op jit(solution)/shard_map/ppermute | solution.py:19

commit v20 on v4

--- a/solution.py
+++ b/solution.py
@@ -100,11 +100,11 @@
     cycle_size = lax.axis_size("blk")
     group_size = lax.axis_size("head")
     heads_local = H // group_size
-    k_heads = lax.all_to_all(key_states, "head", split_axis=1, concat_axis=0, tiled=True)
-    k_window = exchange(k_heads.T, 1, cycle_size)
     v_heads = lax.all_to_all(value_states, "head", split_axis=1, concat_axis=0, tiled=True)
     v_window = exchange(v_heads, 0, cycle_size)
-    q_heads = lax.all_to_all(queries, "head", split_axis=1, concat_axis=0, tiled=True)
+    k_and_q = jnp.stack((key_states, queries))
+    k_heads, q_heads = lax.all_to_all(k_and_q, "head", split_axis=2, concat_axis=1, tiled=True)
+    k_window = exchange(k_heads.T, 1, cycle_size)
     shard_tok = q_heads.shape[0]
     tile_count = shard_tok // TILE
     width = heads_local * DH

time: 323 us -> 321 us (level)
  local copies, waits for them, and re-layouts: 14.9 us -> 22.6 us
  starting transfers between devices: 26.6 us -> 20.8 us
  waiting for transfers between devices: 228 us -> 224 us
    ppermute x12, waiting for transfers between devices: 113 us -> 140 us  [permute(): return lax.ppermute(block, axis, route)]
    all_to_all x2 -> x1, waiting for transfers between devices: 95.1 us -> 70.5 us  [body(): lax.all_to_all(k_and_q, 'head', split_axis=2, concat_axis=1, tiled=True)]
    another operation x0 -> x3, local copies, waits for them, and re-layouts: none -> 9.81 us  [the longest x1 5.54 us: body(): k_and_q = jnp.stack((key_states, queries))]
    all_to_all x1, waiting for transfers between devices: 19.9 us -> 13.7 us  [body(): lax.all_to_all(value_states, 'head', split_axis=1, concat_axis=0, tiled=T...]
    all_to_all x2 -> x1, starting transfers between devices: 9.06 us -> 3.65 us  [body(): lax.all_to_all(k_and_q, 'head', split_axis=2, concat_axis=1, tiled=True)]
  transfers between devices with their start and end apart: 15 -> 14, of which waited for: 7 -> 6; matrix products, arithmetic and copies ran while one was open for 4% -> 7% of each run, Pallas kernels for 0% -> 0%
where the time goes in v20:
time: 321 us; the launch traced here: 316 us
  waiting for transfers between devices  224 us (70%)
  Pallas kernels  24.5 us (8%)
  local copies, waits for them, and re-layouts  22.6 us (7%)
  starting transfers between devices  20.8 us (6%)
  blocking collectives  18.7 us (6%)
  other arithmetic  5.68 us (2%)
    ppermute x12, waiting for transfers between devices, permute(): return lax.ppermute(block, axis, route)  140 us
    all_to_all x1, waiting for transfers between devices, body(): lax.all_to_all(k_and_q, 'head', split_axis=2, concat_axis=1, tiled=True)  70.5 us
    pallas_call x1, Pallas kernels, body(): pl.pallas_call(kernel, grid_spec=grid_spec, out_shape=jax.ShapeDtypeStruc...  24.5 us
    all_to_all x1, blocking collectives, body(): return lax.all_to_all(out, 'head', split_axis=0, concat_axis=1, tiled=True)  18.7 us
    all_to_all x1, waiting for transfers between devices, body(): lax.all_to_all(value_states, 'head', split_axis=1, concat_axis=0, tiled=T...  13.7 us
    ppermute x12, starting transfers between devices, permute(): return lax.ppermute(block, axis, route)  12.2 us
  transfers between devices with their start and end apart: 14, of which 6 were waited for; matrix products, arithmetic and copies ran while one was open for 7% of the time, Pallas kernels for 0%

profile of v20, /device:TPU:128, one launch (start us, length us, event | category | flops | bytes accessed | tf_op | source)
XLA Modules:
  0.0 316.2 jit_solution(835762271769098724)
XLA Ops:
  0.0 2.7 copy.35
  2.7 4.9 %all-to-all-start.1 = ((bf16[128,8,768]{2,0,1:T(8,128)(2,1)}), bf16[128,8,768]{2,0,1:T(8,128)(2,1)}, u32[]{:S(2)}, u32[]{:S(2)}) async-start(bf16[128,8,768]{2,0,1:T(8,128)(2,1)} %bitcast.31), calls=%async_computation.1 | async-start | bytes 3145728 | tf_op jit(solution)/shard_map/all_to_all | solution.py:103
  7.6 2.2 pad_maximum_fusion
  9.8 5.5 %copy.22 = bf16[2,128,6144]{1,0,2:T(2,128)(2,1)} copy(bf16[2,128,6144]{2,1,0:T(8,128)(2,1)S(1)} %pad_maximum_fusion) | data formatting | bytes 6291456 | tf_op jit(solution)/shard_map/stack | solution.py:105
  15.3 13.7 %all-to-all-done.1 = bf16[128,8,768]{2,0,1:T(8,128)(2,1)} async-done(((bf16[128,8,768]{2,0,1:T(8,128)(2,1)}), bf16[128,8,768]{2,0,1:T(8,128)(2,1)}, u32[]{:S(2)}, u32[]{:S(2)}) %all-to-all-start.1) | async-done | bytes 1572896 | tf_op jit(solution)/shard_map/all_to_all | solution.py:103
  29.1 3.6 %all-to-all-start = ((bf16[2,128,6144]{1,0,2:T(2,128)(2,1)}), bf16[2,128,6144]{1,0,2:T(2,128)(2,1)S(1)}, u32[]{:S(2)}, u32[]{:S(2)}) async-start(bf16[2,128,6144]{1,0,2:T(2,128)(2,1)} %copy.22), calls=%async_computation | async-start | bytes 6291456 | tf_op jit(solution)/shard_map/all_to_all | solution.py:106
  32.7 2.8 collective-permute-start.7
  35.6 70.5 %all-to-all-done = bf16[2,128,6144]{1,0,2:T(2,128)(2,1)S(1)} async-done(((bf16[2,128,6144]{1,0,2:T(2,128)(2,1)}), bf16[2,128,6144]{1,0,2:T(2,128)(2,1)S(1)}, u32[]{:S(2)}, u32[]{:S(2)}) %all-to-all-start) | async-done | bytes 3145760 | tf_op jit(solution)/shard_map/all_to_all | solution.py:106
  106.0 2.0 copy.33
  108.0 1.3 fusion.7
  109.4 1.6 copy.34
  111.0 2.0 collective-permute-start
  113.6 25.3 %collective-permute-done.6.args_12_ = bf16[1024,768]{1,0:T(8,128)(2,1)} collective-permute-done((bf16[1024,768]{1,0:T(8,128)(2,1)}, bf16[1024,768]{1,0:T(8,128)(2,1)}, u32[]{:S(2)}, u32[]{:S(2)}) %collective-permute-start.6) | collective-permute-done | bytes 1572896 | tf_op jit(solution)/shard_map/ppermute | solution.py:19
  138.8 1.6 broadcast_select_fusion
  140.6 78.3 %collective-permute-done.1.args_6_ = bf16[768,1024]{1,0:T(8,128)(2,1)S(1)} collective-permute-done((bf16[768,1024]{1,0:T(8,128)(2,1)}, bf16[768,1024]{1,0:T(8,128)(2,1)S(1)}, u32[]{:S(2)}, u32[]{:S(2)}) %collective-permute-start.1) | collective-permute-done | bytes 1572896 | tf_op jit(solution)/shard_map/ppermute | solution.py:19
  219.4 1.7 broadcast_select_fusion.1
  221.1 6.2 %collective-permute-start.3 = (bf16[768,1024]{1,0:T(8,128)(2,1)}, bf16[768,1024]{1,0:T(8,128)(2,1)}, u32[]{:S(2)}, u32[]{:S(2)}) collective-permute-start(bf16[768,1024]{1,0:T(8,128)(2,1)} %broadcast_select_fusion.1), channel_id=1, source_target_pairs={{0,31},{1,2},{2,1},{3,4},{4,3},{5,6},{6,5},{7,8},{8,7},{9,10},{10,... | collective-permute-start | bytes 4718600 | tf_op jit(solution)/shard_map/ppermute | solution.py:19
  227.4 27.4 %collective-permute-done.9.args_15_ = bf16[1024,768]{1,0:T(8,128)(2,1)S(1)} collective-permute-done((bf16[1024,768]{1,0:T(8,128)(2,1)S(1)}, bf16[1024,768]{1,0:T(8,128)(2,1)S(1)}, u32[]{:S(2)}, u32[]{:S(2)}) %collective-permute-start.9) | collective-permute-done | bytes 1572896 | tf_op jit(solution)/shard_map/ppermute | solution.py:19
  254.8 1.2 copy-done.5
  260.2 2.9 copy.24
  263.1 8.6 %collective-permute-done.3.args_8_ = bf16[768,1024]{1,0:T(8,128)(2,1)} collective-permute-done((bf16[768,1024]{1,0:T(8,128)(2,1)}, bf16[768,1024]{1,0:T(8,128)(2,1)}, u32[]{:S(2)}, u32[]{:S(2)}) %collective-permute-start.3) | collective-permute-done | bytes 1572896 | tf_op jit(solution)/shard_map/ppermute | solution.py:19
  271.7 24.5 %shard_map.73 = bf16[1024,768]{1,0:T(8,128)(2,1)} custom-call(s32[64]{0:T(128)} %reshape.62.args_0_, s32[8]{0:T(128)} %args_1_.4, f32[384]{0:T(512)} %mul.43.args_2_, bf16[1024,768]{1,0:T(8,128)(2,1)} %bitcast.34, bf16[768,1024]{1,0:T(8,128)(2,1)} %bitcast.30.args_4_, bf16[768,1024]{1,0:T(8,128)(2,1)} %copy-done.2, bf16[768,1024]{1,0:T(8,128)(2,1)} %copy-done.1, ...), custom_call_target="tpu_custom_call" | custom-call | tf_op jit(solution)/shard_map/pallas_call | solution.py:147
  296.2 18.7 %all_to_all.53 = bf16[8,128,768]{2,1,0:T(8,128)(2,1)S(1)} all-to-all(bf16[8,128,768]{2,1,0:T(8,128)(2,1)} %bitcast.35), channel_id=1, replica_groups=mesh['head'=8,'blk'=32] {'head'}, dimensions={0} | all-to-all | bytes 3145728 | tf_op jit(solution)/shard_map/all_to_all | solution.py:160
  314.8 1.3 copy.28
  (52 shorter events, 5.4 us)
Async XLA Ops:
  0.0 257.7 %copy-start = (s32[256]{0:T(256)S(1)}, s32[256]{0:T(256)}, u32[]{:S(2)}) copy-start(s32[256]{0:T(256)} %param.12) | copy-start | bytes 3076
  2.7 26.4 %all-to-all-start.1 = ((bf16[128,8,768]{2,0,1:T(8,128)(2,1)}), bf16[128,8,768]{2,0,1:T(8,128)(2,1)}, u32[]{:S(2)}, u32[]{:S(2)}) async-start(bf16[128,8,768]{2,0,1:T(8,128)(2,1)} %bitcast.31), calls=%async_computation.1 | async-start | bytes 3145728 | tf_op jit(solution)/shard_map/all_to_all | solution.py:103
  29.1 76.9 %all-to-all-start = ((bf16[2,128,6144]{1,0,2:T(2,128)(2,1)}), bf16[2,128,6144]{1,0,2:T(2,128)(2,1)S(1)}, u32[]{:S(2)}, u32[]{:S(2)}) async-start(bf16[2,128,6144]{1,0,2:T(2,128)(2,1)} %copy.22), calls=%async_computation | async-start | bytes 6291456 | tf_op jit(solution)/shard_map/all_to_all | solution.py:106
  32.7 80.3 %collective-permute-start.7 = (bf16[1024,768]{1,0:T(8,128)(2,1)}, bf16[1024,768]{1,0:T(8,128)(2,1)}, u32[]{:S(2)}, u32[]{:S(2)}) collective-permute-start(bf16[1024,768]{1,0:T(8,128)(2,1)} %bitcast.9.args_11_), channel_id=1, source_target_pairs={{0,30},{1,31},{2,0},{3,1},{4,2},{5,3},{6,4},{7,5},{8,6},{9,7},{10,... | collective-permute-start | bytes 4718600 | tf_op jit(solution)/shard_map/ppermute | solution.py:19
  35.5 103.3 %collective-permute-start.6 = (bf16[1024,768]{1,0:T(8,128)(2,1)}, bf16[1024,768]{1,0:T(8,128)(2,1)}, u32[]{:S(2)}, u32[]{:S(2)}) collective-permute-start(bf16[1024,768]{1,0:T(8,128)(2,1)} %bitcast.9.args_11_), channel_id=1, source_target_pairs={{0,2},{1,3},{2,4},{3,5},{4,6},{5,7},{6,8},{7,9},{8,10},{9,11},{10,... | collective-permute-start | bytes 4718600 | tf_op jit(solution)/shard_map/ppermute | solution.py:19
  111.0 107.8 %collective-permute-start.1 = (bf16[768,1024]{1,0:T(8,128)(2,1)}, bf16[768,1024]{1,0:T(8,128)(2,1)S(1)}, u32[]{:S(2)}, u32[]{:S(2)}) collective-permute-start(bf16[768,1024]{1,0:T(8,128)(2,1)} %bitcast.30.args_4_), channel_id=1, source_target_pairs={{0,30},{1,31},{2,0},{3,1},{4,2},{5,3},{6,4},{7,5},{8,6},{9,7},{10,... | collective-permute-start | bytes 4718600 | tf_op jit(solution)/shard_map/ppermute | solution.py:19
  111.0 107.8 %collective-permute-start = (bf16[768,1024]{1,0:T(8,128)(2,1)}, bf16[768,1024]{1,0:T(8,128)(2,1)S(1)}, u32[]{:S(2)}, u32[]{:S(2)}) collective-permute-start(bf16[768,1024]{1,0:T(8,128)(2,1)} %bitcast.30.args_4_), channel_id=1, source_target_pairs={{0,2},{1,3},{2,4},{3,5},{4,6},{5,7},{6,8},{7,9},{8,10},{9,11},{10,... | collective-permute-start | bytes 4718600 | tf_op jit(solution)/shard_map/ppermute | solution.py:19
  113.0 108.0 %collective-permute-start.8 = (bf16[1024,768]{1,0:T(8,128)(2,1)}, bf16[1024,768]{1,0:T(8,128)(2,1)S(1)}, u32[]{:S(2)}, u32[]{:S(2)}) collective-permute-start(bf16[1024,768]{1,0:T(8,128)(2,1)} %bitcast.9.args_11_), channel_id=1, source_target_pairs={{0,1},{1,0},{2,3},{3,2},{4,5},{5,4},{6,7},{7,6},{8,9},{9,8},{10,11... | collective-permute-start | bytes 4718600 | tf_op jit(solution)/shard_map/ppermute | solution.py:19
  113.0 114.2 %collective-permute-start.11 = (bf16[1024,768]{1,0:T(8,128)(2,1)}, bf16[1024,768]{1,0:T(8,128)(2,1)S(1)}, u32[]{:S(2)}, u32[]{:S(2)}) collective-permute-start(bf16[1024,768]{1,0:T(8,128)(2,1)} %collective-permute-done.7.args_13_), channel_id=1, source_target_pairs={{0,1},{1,0},{2,3},{3,2},{4,5},{5,4},{6,7},{7,6},{8,9},{9,8},{10,11... | collective-permute-start | bytes 4718600 | tf_op jit(solution)/shard_map/ppermute | solution.py:19
  140.4 115.5 %copy-start.6 = (s32[8,8]{1,0:T(8,128)S(1)}, s32[8,8]{1,0:T(8,128)}, u32[]{:S(2)}) copy-start(s32[8,8]{1,0:T(8,128)} %param.10) | copy-start | bytes 772
  140.4 115.7 %copy-start.7 = (s32[2,7]{1,0:T(2,128)S(1)}, s32[2,7]{1,0:T(2,128)}, u32[]{:S(2)}) copy-start(s32[2,7]{1,0:T(2,128)} %constant.89.clone) | copy-start | bytes 172
  140.5 114.3 %collective-permute-start.9 = (bf16[1024,768]{1,0:T(8,128)(2,1)S(1)}, bf16[1024,768]{1,0:T(8,128)(2,1)S(1)}, u32[]{:S(2)}, u32[]{:S(2)}) collective-permute-start(bf16[1024,768]{1,0:T(8,128)(2,1)S(1)} %broadcast_select_fusion), channel_id=1, source_target_pairs={{0,31},{1,2},{2,1},{3,4},{4,3},{5,6},{6,5},{7,8},{8,7},{9,10},{10,... | collective-permute-start | bytes 4718600 | tf_op jit(solution)/shard_map/ppermute | solution.py:19
  218.8 8.4 %copy-start.1 = (bf16[768,1024]{1,0:T(8,128)(2,1)}, bf16[768,1024]{1,0:T(8,128)(2,1)S(1)}, u32[]{:S(2)}) copy-start(bf16[768,1024]{1,0:T(8,128)(2,1)S(1)} %collective-permute-done.1.args_6_) | copy-start | bytes 4718596
  218.8 44.2 %collective-permute-start.10 = (bf16[1024,768]{1,0:T(8,128)(2,1)}, bf16[1024,768]{1,0:T(8,128)(2,1)}, u32[]{:S(2)}, u32[]{:S(2)}) collective-permute-start(bf16[1024,768]{1,0:T(8,128)(2,1)} %collective-permute-done.6.args_12_), channel_id=1, source_target_pairs={{0,1},{1,0},{2,3},{3,2},{4,5},{5,4},{6,7},{7,6},{8,9},{9,8},{10,11... | collective-permute-start | bytes 4718600 | tf_op jit(solution)/shard_map/ppermute | solution.py:19
  218.8 35.9 %copy-start.2 = (bf16[768,1024]{1,0:T(8,128)(2,1)}, bf16[768,1024]{1,0:T(8,128)(2,1)S(1)}, u32[]{:S(2)}) copy-start(bf16[768,1024]{1,0:T(8,128)(2,1)S(1)} %collective-permute-done.args_5_) | copy-start | bytes 4718596
  218.9 44.2 %collective-permute-start.2 = (bf16[768,1024]{1,0:T(8,128)(2,1)}, bf16[768,1024]{1,0:T(8,128)(2,1)}, u32[]{:S(2)}, u32[]{:S(2)}) collective-permute-start(bf16[768,1024]{1,0:T(8,128)(2,1)} %bitcast.30.args_4_), channel_id=1, source_target_pairs={{0,1},{1,0},{2,3},{3,2},{4,5},{5,4},{6,7},{7,6},{8,9},{9,8},{10,11... | collective-permute-start | bytes 4718600 | tf_op jit(solution)/shard_map/ppermute | solution.py:19
  221.1 33.7 %copy-start.3 = (bf16[1024,768]{1,0:T(8,128)(2,1)}, bf16[1024,768]{1,0:T(8,128)(2,1)S(1)}, u32[]{:S(2)}) copy-start(bf16[1024,768]{1,0:T(8,128)(2,1)S(1)} %collective-permute-done.8.args_14_) | copy-start | bytes 4718596
  221.1 50.6 %collective-permute-start.3 = (bf16[768,1024]{1,0:T(8,128)(2,1)}, bf16[768,1024]{1,0:T(8,128)(2,1)}, u32[]{:S(2)}, u32[]{:S(2)}) collective-permute-start(bf16[768,1024]{1,0:T(8,128)(2,1)} %broadcast_select_fusion.1), channel_id=1, source_target_pairs={{0,31},{1,2},{2,1},{3,4},{4,3},{5,6},{6,5},{7,8},{8,7},{9,10},{10,... | collective-permute-start | bytes 4718600 | tf_op jit(solution)/shard_map/ppermute | solution.py:19
  227.3 27.5 %copy-start.4 = (bf16[1024,768]{1,0:T(8,128)(2,1)}, bf16[1024,768]{1,0:T(8,128)(2,1)S(1)}, u32[]{:S(2)}) copy-start(bf16[1024,768]{1,0:T(8,128)(2,1)S(1)} %collective-permute-done.11.args_17_) | copy-start | bytes 4718596
  227.3 35.8 %collective-permute-start.5 = (bf16[768,1024]{1,0:T(8,128)(2,1)S(1)}, bf16[768,1024]{1,0:T(8,128)(2,1)}, u32[]{:S(2)}, u32[]{:S(2)}) collective-permute-start(bf16[768,1024]{1,0:T(8,128)(2,1)S(1)} %collective-permute-done.1.args_6_), channel_id=1, source_target_pairs={{0,1},{1,0},{2,3},{3,2},{4,5},{5,4},{6,7},{7,6},{8,9},{9,8},{10,11... | collective-permute-start | bytes 4718600 | tf_op jit(solution)/shard_map/ppermute | solution.py:19
  254.7 1.2 copy-start.5
  254.7 17.0 %collective-permute-start.4 = (bf16[768,1024]{1,0:T(8,128)(2,1)S(1)}, bf16[768,1024]{1,0:T(8,128)(2,1)}, u32[]{:S(2)}, u32[]{:S(2)}) collective-permute-start(bf16[768,1024]{1,0:T(8,128)(2,1)S(1)} %collective-permute-done.args_5_), channel_id=1, source_target_pairs={{0,1},{1,0},{2,3},{3,2},{4,5},{5,4},{6,7},{7,6},{8,9},{9,8},{10,11... | collective-permute-start | bytes 4718600 | tf_op jit(solution)/shard_map/ppermute | solution.py:19
